TPU v7x, 32 devices: a whole 2x2x4 slice. The times are simulated.
32 devices in a mesh: space: 16 (over z, y, x), tm: 2 (over core).
Axes of the slice: x: 2, y: 2, z: 4, core: 2. Of those that a mesh axis runs over, the one named last changes fastest.
Arguments:
- initial: float32 [32, 256, 128], P('space'), may hold values from -6 to 6
- guesses: float32 [2, 32, 256, 128], P('tm', 'space'), may hold values from -6 to 6
- diffusivity: float32 [32, 256, 128], P('space'), may hold values from 0.4 to 1.2
- reaction: float32 [32, 256, 128], P('space'), may hold values from 0.1 to 1
Outputs:
- corrected: float32 [2, 32, 256, 128], P('tm', 'space')
- residual: float32 [2, 32, 256, 128], P('tm', 'space')
All inputs are finite; a program needn't handle non-finite values.
Results may differ from a plain program's by a relative error of at most 0.0001.
Values sent between devices are 32-bit elements; how exact they have to be, the bound alone decides.
No kernel may reach another device: no remote copies, remote signals or barrier semaphores. Data moves between devices by JAX's collectives and lax.ppermute only.
A program may use at most 64 MiB of HBM per device.

v0:
```python
import jax
import jax.numpy as jnp
from jax import lax
from jax.sharding import PartitionSpec as P

STEPS = 4


def extended(block, sides, width):
    for axis, dim in sides:
        count = lax.axis_size(axis)
        forward = [(i, i + 1) for i in range(count - 1)]
        backward = [(target, source) for source, target in forward]
        low = lax.ppermute(
            lax.slice_in_dim(block, block.shape[dim] - width, None, axis=dim), axis, forward
        )
        high = lax.ppermute(lax.slice_in_dim(block, 0, width, axis=dim), axis, backward)
        block = jnp.concatenate([low, block, high], axis=dim)
    return block


def from_behind(block, axis, distance):
    devices = range(lax.axis_size(axis))
    route = [(i - distance, i) for i in devices if i - distance in devices]
    return lax.ppermute(block, axis, route)


def advance(field, conduct, absorb, diffuse_scale, react_scale):
    center = field[1:-1]
    middle = conduct[1:-1]
    padded = jnp.pad(center, ((0, 0), (1, 1), (1, 1)))
    conduct_pad = jnp.pad(middle, ((0, 0), (1, 1), (1, 1)))
    inflow = 0.5 * (conduct[2:] + middle) * (field[2:] - center)
    inflow = inflow + 0.5 * (conduct[:-2] + middle) * (field[:-2] - center)
    inflow = inflow + 0.5 * (conduct_pad[:, 2:, 1:-1] + middle) * (padded[:, 2:, 1:-1] - center)
    inflow = inflow + 0.5 * (conduct_pad[:, :-2, 1:-1] + middle) * (padded[:, :-2, 1:-1] - center)
    inflow = inflow + 0.5 * (conduct_pad[:, 1:-1, 2:] + middle) * (padded[:, 1:-1, 2:] - center)
    inflow = inflow + 0.5 * (conduct_pad[:, 1:-1, :-2] + middle) * (padded[:, 1:-1, :-2] - center)
    return center + diffuse_scale * inflow - react_scale * absorb[1:-1] * center


def restrict(field):
    first, second, third = field.shape
    blocks = field.reshape(first // 2, 2, second // 2, 2, third // 2, 2)
    return jnp.mean(blocks, axis=(1, 3, 5))


def prolong(field):
    first, second, third = field.shape
    spread = jnp.broadcast_to(field[:, None, :, None, :, None], (first, 2, second, 2, third, 2))
    return spread.reshape(first * 2, second * 2, third * 2)


def shards(initial, guesses, diffusivity, reaction):
    start = guesses[0]
    coefs = jnp.stack([diffusivity, reaction])
    rimmed = extended(coefs, (("space", 1),), 1)

    def fine_prop(field):
        for number in range(STEPS):
            widened = extended(field, (("space", 0),), 1)
            field = advance(widened, rimmed[0], rimmed[1], 0.1, 0.1)
        return field

    advanced = fine_prop(start)
    received = from_behind(advanced, "tm", 1)
    relaxed = jnp.where(lax.axis_index("tm") == 0, initial, received)
    residual = fine_prop(relaxed) - advanced
    coarse_coefs = jnp.stack([restrict(diffusivity), restrict(reaction)])
    source = restrict(residual)
    coarse_rimmed = extended(coarse_coefs, (("space", 1),), 1)
    partial_error = source
    for turn in range(lax.axis_size("tm") - 1):
        coarse_field = partial_error
        coarse_widened = extended(coarse_field, (("space", 0),), 1)
        coarse_field = advance(coarse_widened, coarse_rimmed[0], coarse_rimmed[1], 0.1, 0.4)
        partial_error = source + from_behind(coarse_field, "tm", 1)
    corrected = advanced + prolong(partial_error)
    return (corrected[None], residual[None])


def solution(mesh):
    in_specs = (
        P("space", None, None),
        P("tm", "space", None, None),
        P("space", None, None),
        P("space", None, None),
    )
    out_specs = (P("tm", "space", None, None), P("tm", "space", None, None))
    return jax.shard_map(shards, mesh=mesh, in_specs=in_specs, out_specs=out_specs, check_vma=False)
```

profile of v0, /device:TPU:7, one launch (start us, length us, event | category | flops | bytes accessed | tf_op | source)
XLA Modules:
  0.0 181.2 jit_solution(2274903968149523676)
XLA Ops:
  4.0 4.9 %collective-permute-start.2 = (f32[2,1,256,128]{3,2,1,0:T(8,128)S(1)}, f32[2,1,256,128]{3,2,1,0:T(8,128)S(1)}, u32[]{:S(2)}, u32[]{:S(2)}) collective-permute-start(f32[2,1,256,128]{3,2,1,0:T(8,128)S(1)} %get-tuple-element.11), channel_id=1, source_target_pairs={{0,2},{2,4},{4,6},{6,8},{8,10},{10,12},{12,14},{14,16},{16,18},{18... | collective-permute-start | bytes 786440 | tf_op jit(solution)/shard_map/ppermute | solution.py:14
  11.9 3.4 %collective-permute-start.1 = (f32[1,256,128]{2,1,0:T(8,128)S(1)}, f32[1,256,128]{2,1,0:T(8,128)S(1)}, u32[]{:S(2)}, u32[]{:S(2)}) collective-permute-start(f32[1,256,128]{2,1,0:T(8,128)S(1)} %get-tuple-element.30), channel_id=1, source_target_pairs={{2,0},{4,2},{6,4},{8,6},{10,8},{12,10},{14,12},{16,14},{18,16},{20... | collective-permute-start | bytes 393224 | tf_op jit(solution)/shard_map/ppermute | solution.py:17
  15.2 4.1 %collective-permute-done.3 = f32[1,256,128]{2,1,0:T(8,128)S(1)} collective-permute-done((f32[1,256,128]{2,1,0:T(8,128)S(1)}, f32[1,256,128]{2,1,0:T(8,128)S(1)}, u32[]{:S(2)}, u32[]{:S(2)}) %collective-permute-start.3) | collective-permute-done | bytes 131104 | tf_op jit(solution)/shard_map/ppermute | solution.py:14
  19.5 3.4 %fusion.17 = (f32[2,256,128]{2,1,0:T(8,128)S(1)}, f32[2,256,128]{2,1,0:T(8,128)S(1)}, f32[2,256,128]{2,1,0:T(8,128)S(1)}, f32[2,256,128]{2,1,0:T(8,128)S(1)}, f3...) fusion(f32[2,256,128]{2,1,0:T(8,128)} %bitcast.80, ...), kind=kLoop, calls=%fused_computation.55 | loop fusion | flops 2654208 | bytes 4063232 | tf_op jit(solution)/shard_map/sub | solution.py:39
  22.9 7.7 %collective-permute-start.5 = (f32[1,256,128]{2,1,0:T(8,128)S(1)}, f32[1,256,128]{2,1,0:T(8,128)S(1)}, u32[]{:S(2)}, u32[]{:S(2)}) collective-permute-start(f32[1,256,128]{2,1,0:T(8,128)S(1)} %get-tuple-element.29), channel_id=1, source_target_pairs={{0,2},{2,4},{4,6},{6,8},{8,10},{10,12},{12,14},{14,16},{16,18},{18... | collective-permute-start | bytes 393224 | tf_op jit(solution)/shard_map/ppermute | solution.py:14
  33.0 5.6 %collective-permute-done.4 = f32[1,256,128]{2,1,0:T(8,128)S(1)} collective-permute-done((f32[1,256,128]{2,1,0:T(8,128)S(1)}, f32[1,256,128]{2,1,0:T(8,128)S(1)}, u32[]{:S(2)}, u32[]{:S(2)}) %collective-permute-start.4) | collective-permute-done | bytes 131104 | tf_op jit(solution)/shard_map/ppermute | solution.py:17
  39.8 2.3 %collective-permute-start.7 = (f32[1,256,128]{2,1,0:T(8,128)S(1)}, f32[1,256,128]{2,1,0:T(8,128)S(1)}, u32[]{:S(2)}, u32[]{:S(2)}) collective-permute-start(f32[1,256,128]{2,1,0:T(8,128)S(1)} %get-tuple-element.27), channel_id=1, source_target_pairs={{0,2},{2,4},{4,6},{6,8},{8,10},{10,12},{12,14},{14,16},{16,18},{18... | collective-permute-start | bytes 393224 | tf_op jit(solution)/shard_map/ppermute | solution.py:14
  42.1 3.0 %collective-permute-start.6 = (f32[1,256,128]{2,1,0:T(8,128)S(1)}, f32[1,256,128]{2,1,0:T(8,128)S(1)}, u32[]{:S(2)}, u32[]{:S(2)}) collective-permute-start(f32[1,256,128]{2,1,0:T(8,128)S(1)} %get-tuple-element.26), channel_id=1, source_target_pairs={{2,0},{4,2},{6,4},{8,6},{10,8},{12,10},{14,12},{16,14},{18,16},{20... | collective-permute-start | bytes 393224 | tf_op jit(solution)/shard_map/ppermute | solution.py:17
  45.5 4.1 %collective-permute-done.6 = f32[1,256,128]{2,1,0:T(8,128)S(1)} collective-permute-done((f32[1,256,128]{2,1,0:T(8,128)S(1)}, f32[1,256,128]{2,1,0:T(8,128)S(1)}, u32[]{:S(2)}, u32[]{:S(2)}) %collective-permute-start.6) | collective-permute-done | bytes 131104 | tf_op jit(solution)/shard_map/ppermute | solution.py:17
  50.0 3.4 %collective-permute-start.9 = (f32[1,256,128]{2,1,0:T(8,128)S(1)}, f32[1,256,128]{2,1,0:T(8,128)S(1)}, u32[]{:S(2)}, u32[]{:S(2)}) collective-permute-start(f32[1,256,128]{2,1,0:T(8,128)S(1)} %get-tuple-element.25), channel_id=1, source_target_pairs={{0,2},{2,4},{4,6},{6,8},{8,10},{10,12},{12,14},{14,16},{16,18},{18... | collective-permute-start | bytes 393224 | tf_op jit(solution)/shard_map/ppermute | solution.py:14
  55.7 5.2 %collective-permute-done.8 = f32[1,256,128]{2,1,0:T(8,128)S(1)} collective-permute-done((f32[1,256,128]{2,1,0:T(8,128)S(1)}, f32[1,256,128]{2,1,0:T(8,128)S(1)}, u32[]{:S(2)}, u32[]{:S(2)}) %collective-permute-start.8) | collective-permute-done | bytes 131104 | tf_op jit(solution)/shard_map/ppermute | solution.py:17
  62.5 3.8 %collective-permute-done.10 = f32[2,256,128]{2,1,0:T(8,128)S(1)} collective-permute-done((f32[2,256,128]{2,1,0:T(8,128)S(1)}, f32[2,256,128]{2,1,0:T(8,128)S(1)}, u32[]{:S(2)}, u32[]{:S(2)}) %collective-permute-start.10) | collective-permute-done | bytes 262176 | tf_op jit(solution)/shard_map/ppermute | solution.py:25
  66.3 2.2 %collective-permute-start.12 = (f32[1,256,128]{2,1,0:T(8,128)S(1)}, f32[1,256,128]{2,1,0:T(8,128)S(1)}, u32[]{:S(2)}, u32[]{:S(2)}) collective-permute-start(f32[1,256,128]{2,1,0:T(8,128)S(1)} %get-tuple-element.23), channel_id=1, source_target_pairs={{0,2},{2,4},{4,6},{6,8},{8,10},{10,12},{12,14},{14,16},{16,18},{18... | collective-permute-start | bytes 393224 | tf_op jit(solution)/shard_map/ppermute | solution.py:14
  68.5 3.1 %collective-permute-start.11 = (f32[1,256,128]{2,1,0:T(8,128)S(1)}, f32[1,256,128]{2,1,0:T(8,128)S(1)}, u32[]{:S(2)}, u32[]{:S(2)}) collective-permute-start(f32[1,256,128]{2,1,0:T(8,128)S(1)} %get-tuple-element.22), channel_id=1, source_target_pairs={{2,0},{4,2},{6,4},{8,6},{10,8},{12,10},{14,12},{16,14},{18,16},{20... | collective-permute-start | bytes 393224 | tf_op jit(solution)/shard_map/ppermute | solution.py:17
  73.2 3.7 %collective-permute-done.11 = f32[1,256,128]{2,1,0:T(8,128)S(1)} collective-permute-done((f32[1,256,128]{2,1,0:T(8,128)S(1)}, f32[1,256,128]{2,1,0:T(8,128)S(1)}, u32[]{:S(2)}, u32[]{:S(2)}) %collective-permute-start.11) | collective-permute-done | bytes 131104 | tf_op jit(solution)/shard_map/ppermute | solution.py:17
  77.2 2.9 %collective-permute-start.14 = (f32[1,256,128]{2,1,0:T(8,128)S(1)}, f32[1,256,128]{2,1,0:T(8,128)S(1)}, u32[]{:S(2)}, u32[]{:S(2)}) collective-permute-start(f32[1,256,128]{2,1,0:T(8,128)S(1)} %get-tuple-element.21), channel_id=1, source_target_pairs={{0,2},{2,4},{4,6},{6,8},{8,10},{10,12},{12,14},{14,16},{16,18},{18... | collective-permute-start | bytes 393224 | tf_op jit(solution)/shard_map/ppermute | solution.py:14
  80.1 2.4 %collective-permute-start.13 = (f32[1,256,128]{2,1,0:T(8,128)S(1)}, f32[1,256,128]{2,1,0:T(8,128)S(1)}, u32[]{:S(2)}, u32[]{:S(2)}) collective-permute-start(f32[1,256,128]{2,1,0:T(8,128)S(1)} %get-tuple-element.20), channel_id=1, source_target_pairs={{2,0},{4,2},{6,4},{8,6},{10,8},{12,10},{14,12},{16,14},{18,16},{20... | collective-permute-start | bytes 393224 | tf_op jit(solution)/shard_map/ppermute | solution.py:17
  82.9 4.7 %collective-permute-done.13 = f32[1,256,128]{2,1,0:T(8,128)S(1)} collective-permute-done((f32[1,256,128]{2,1,0:T(8,128)S(1)}, f32[1,256,128]{2,1,0:T(8,128)S(1)}, u32[]{:S(2)}, u32[]{:S(2)}) %collective-permute-start.13) | collective-permute-done | bytes 131104 | tf_op jit(solution)/shard_map/ppermute | solution.py:17
  89.8 3.4 %collective-permute-start.15 = (f32[1,256,128]{2,1,0:T(8,128)S(1)}, f32[1,256,128]{2,1,0:T(8,128)S(1)}, u32[]{:S(2)}, u32[]{:S(2)}) collective-permute-start(f32[1,256,128]{2,1,0:T(8,128)S(1)} %get-tuple-element.18), channel_id=1, source_target_pairs={{2,0},{4,2},{6,4},{8,6},{10,8},{12,10},{14,12},{16,14},{18,16},{20... | collective-permute-start | bytes 393224 | tf_op jit(solution)/shard_map/ppermute | solution.py:17
  93.2 9.8 %reduce_sum.40 = f32[128,2,64,2]{3,2,1,0:T(8,128)} reshape(f32[256,128]{1,0:T(8,128)S(1)} %get-tuple-element.15) | data formatting | bytes 262144 | tf_op jit(solution)/shard_map/reduce_sum | solution.py:45
  103.0 4.5 %reduce_sum.44 = f32[128,64]{1,0:T(8,128)S(1)} reduce(f32[128,2,64,2]{3,2,1,0:T(8,128)} %reduce_sum.40, f32[]{:T(128)} %constant.8.clone.1), dimensions={1,3}, to_apply=%region_3.4 | reduce | flops 24576 | bytes 163844 | tf_op jit(solution)/shard_map/reduce_sum | solution.py:45
  107.5 9.8 %reduce_sum.55 = f32[128,2,64,2]{3,2,1,0:T(8,128)} reshape(f32[256,128]{1,0:T(8,128)S(1)} %get-tuple-element.13) | data formatting | bytes 262144 | tf_op jit(solution)/shard_map/reduce_sum | solution.py:45
  117.3 4.5 %reduce_sum.56 = f32[128,64]{1,0:T(8,128)S(1)} reduce(f32[128,2,64,2]{3,2,1,0:T(8,128)} %reduce_sum.55, f32[]{:T(128)} %constant.8.clone.1), dimensions={1,3}, to_apply=%region_5.6 | reduce | flops 24576 | bytes 163844 | tf_op jit(solution)/shard_map/reduce_sum | solution.py:45
  122.1 3.7 %collective-permute-start.18 = (f32[1,256,128]{2,1,0:T(8,128)S(1)}, f32[1,256,128]{2,1,0:T(8,128)S(1)}, u32[]{:S(2)}, u32[]{:S(2)}) collective-permute-start(f32[1,256,128]{2,1,0:T(8,128)S(1)} %get-tuple-element.17), channel_id=1, source_target_pairs={{0,2},{2,4},{4,6},{6,8},{8,10},{10,12},{12,14},{14,16},{16,18},{18... | collective-permute-start | bytes 393224 | tf_op jit(solution)/shard_map/ppermute | solution.py:14
  127.8 5.2 %collective-permute-start.21 = (f32[2,1,128,64]{3,2,1,0:T(8,128)S(1)}, f32[2,1,128,64]{3,2,1,0:T(8,128)S(1)}, u32[]{:S(2)}, u32[]{:S(2)}) collective-permute-start(f32[2,1,128,64]{3,2,1,0:T(8,128)S(1)} %pad_maximum_fusion.21), channel_id=1, source_target_pairs={{0,2},{2,4},{4,6},{6,8},{8,10},{10,12},{12,14},{14,16},{16,18},{18... | collective-permute-start | bytes 196616 | tf_op jit(solution)/shard_map/ppermute | solution.py:14
  136.0 9.7 %reduce_sum.37 = f32[128,2,64,2]{3,2,1,0:T(8,128)} reshape(f32[256,128]{1,0:T(8,128)S(1)} %get-tuple-element.2) | data formatting | bytes 262144 | tf_op jit(solution)/shard_map/reduce_sum | solution.py:45
  145.7 4.5 %reduce_sum.38 = f32[128,64]{1,0:T(8,128)S(1)} reduce(f32[128,2,64,2]{3,2,1,0:T(8,128)} %reduce_sum.37, f32[]{:T(128)} %constant.8.clone.1), dimensions={1,3}, to_apply=%region_1.2 | reduce | flops 24576 | bytes 163844 | tf_op jit(solution)/shard_map/reduce_sum | solution.py:45
  150.3 5.2 %collective-permute-start.22 = (f32[1,128,64]{2,1,0:T(8,128)S(1)}, f32[1,128,64]{2,1,0:T(8,128)S(1)}, u32[]{:S(2)}, u32[]{:S(2)}) collective-permute-start(f32[1,128,64]{2,1,0:T(8,128)S(1)} %multiply_bitcast_fusion.1), channel_id=1, source_target_pairs={{0,2},{2,4},{4,6},{6,8},{8,10},{10,12},{12,14},{14,16},{16,18},{18... | collective-permute-start | bytes 98312 | tf_op jit(solution)/shard_map/ppermute | solution.py:14
  157.4 4.8 %collective-permute-done.20 = f32[1,128,64]{2,1,0:T(8,128)S(1)} collective-permute-done((f32[1,128,64]{2,1,0:T(8,128)S(1)}, f32[1,128,64]{2,1,0:T(8,128)S(1)}, u32[]{:S(2)}, u32[]{:S(2)}) %collective-permute-start.20) | collective-permute-done | bytes 32800 | tf_op jit(solution)/shard_map/ppermute | solution.py:17
  163.7 6.0 %collective-permute-done.23 = f32[1,128,64]{2,1,0:T(8,128)S(1)} collective-permute-done((f32[1,128,64]{2,1,0:T(8,128)S(1)}, f32[1,128,64]{2,1,0:T(8,128)S(1)}, u32[]{:S(2)}, u32[]{:S(2)}) %collective-permute-start.23) | collective-permute-done | bytes 32800 | tf_op jit(solution)/shard_map/ppermute | solution.py:25
  169.7 3.9 %broadcast_in_dim.19 = f32[128,2,64,2]{3,2,1,0:T(8,128)} broadcast(f32[128,64]{1,0:T(8,128)S(1)} %add_bitcast_fusion.1), dimensions={0,2} | broadcast | bytes 163840 | tf_op jit(solution)/shard_map/broadcast_in_dim | solution.py:50
  173.5 6.9 %broadcast_in_dim.20 = f32[256,128]{1,0:T(8,128)S(1)} reshape(f32[128,2,64,2]{3,2,1,0:T(8,128)} %broadcast_in_dim.19) | data formatting | bytes 262144 | tf_op jit(solution)/shard_map/broadcast_in_dim | solution.py:50
  (52 shorter events, 28.6 us)
Async XLA Ops:
  0.6 49.0 %copy-start = (f32[2,256,128]{2,1,0:T(8,128)S(1)}, f32[2,256,128]{2,1,0:T(8,128)}, u32[]{:S(2)}) copy-start(f32[2,256,128]{2,1,0:T(8,128)} %param.7) | copy-start | bytes 786436
  0.6 65.6 %copy-start.1 = (f32[2,256,128]{2,1,0:T(8,128)S(1)}, f32[2,256,128]{2,1,0:T(8,128)}, u32[]{:S(2)}) copy-start(f32[2,256,128]{2,1,0:T(8,128)} %param.4) | copy-start | bytes 786436
  1.8 17.6 %collective-permute-start = (f32[2,1,256,128]{3,2,1,0:T(8,128)S(1)}, f32[2,1,256,128]{3,2,1,0:T(8,128)S(1)}, u32[]{:S(2)}, u32[]{:S(2)}) collective-permute-start(f32[2,1,256,128]{3,2,1,0:T(8,128)S(1)} %get-tuple-element.12), channel_id=1, source_target_pairs={{2,0},{4,2},{6,4},{8,6},{10,8},{12,10},{14,12},{16,14},{18,16},{20... | collective-permute-start | bytes 786440 | tf_op jit(solution)/shard_map/ppermute | solution.py:17
  4.0 15.5 %collective-permute-start.2 = (f32[2,1,256,128]{3,2,1,0:T(8,128)S(1)}, f32[2,1,256,128]{3,2,1,0:T(8,128)S(1)}, u32[]{:S(2)}, u32[]{:S(2)}) collective-permute-start(f32[2,1,256,128]{3,2,1,0:T(8,128)S(1)} %get-tuple-element.11), channel_id=1, source_target_pairs={{0,2},{2,4},{4,6},{6,8},{8,10},{10,12},{12,14},{14,16},{16,18},{18... | collective-permute-start | bytes 786440 | tf_op jit(solution)/shard_map/ppermute | solution.py:14
  9.9 9.3 %collective-permute-start.3 = (f32[1,256,128]{2,1,0:T(8,128)S(1)}, f32[1,256,128]{2,1,0:T(8,128)S(1)}, u32[]{:S(2)}, u32[]{:S(2)}) collective-permute-start(f32[1,256,128]{2,1,0:T(8,128)S(1)} %get-tuple-element.31), channel_id=1, source_target_pairs={{0,2},{2,4},{4,6},{6,8},{8,10},{10,12},{12,14},{14,16},{16,18},{18... | collective-permute-start | bytes 393224 | tf_op jit(solution)/shard_map/ppermute | solution.py:14
  11.9 7.6 %collective-permute-start.1 = (f32[1,256,128]{2,1,0:T(8,128)S(1)}, f32[1,256,128]{2,1,0:T(8,128)S(1)}, u32[]{:S(2)}, u32[]{:S(2)}) collective-permute-start(f32[1,256,128]{2,1,0:T(8,128)S(1)} %get-tuple-element.30), channel_id=1, source_target_pairs={{2,0},{4,2},{6,4},{8,6},{10,8},{12,10},{14,12},{16,14},{18,16},{20... | collective-permute-start | bytes 393224 | tf_op jit(solution)/shard_map/ppermute | solution.py:17
  22.9 10.1 %collective-permute-start.5 = (f32[1,256,128]{2,1,0:T(8,128)S(1)}, f32[1,256,128]{2,1,0:T(8,128)S(1)}, u32[]{:S(2)}, u32[]{:S(2)}) collective-permute-start(f32[1,256,128]{2,1,0:T(8,128)S(1)} %get-tuple-element.29), channel_id=1, source_target_pairs={{0,2},{2,4},{4,6},{6,8},{8,10},{10,12},{12,14},{14,16},{16,18},{18... | collective-permute-start | bytes 393224 | tf_op jit(solution)/shard_map/ppermute | solution.py:14
  30.6 7.9 %collective-permute-start.4 = (f32[1,256,128]{2,1,0:T(8,128)S(1)}, f32[1,256,128]{2,1,0:T(8,128)S(1)}, u32[]{:S(2)}, u32[]{:S(2)}) collective-permute-start(f32[1,256,128]{2,1,0:T(8,128)S(1)} %get-tuple-element.28), channel_id=1, source_target_pairs={{2,0},{4,2},{6,4},{8,6},{10,8},{12,10},{14,12},{16,14},{18,16},{20... | collective-permute-start | bytes 393224 | tf_op jit(solution)/shard_map/ppermute | solution.py:17
  39.8 5.7 %collective-permute-start.7 = (f32[1,256,128]{2,1,0:T(8,128)S(1)}, f32[1,256,128]{2,1,0:T(8,128)S(1)}, u32[]{:S(2)}, u32[]{:S(2)}) collective-permute-start(f32[1,256,128]{2,1,0:T(8,128)S(1)} %get-tuple-element.27), channel_id=1, source_target_pairs={{0,2},{2,4},{4,6},{6,8},{8,10},{10,12},{12,14},{14,16},{16,18},{18... | collective-permute-start | bytes 393224 | tf_op jit(solution)/shard_map/ppermute | solution.py:14
  42.1 7.5 %collective-permute-start.6 = (f32[1,256,128]{2,1,0:T(8,128)S(1)}, f32[1,256,128]{2,1,0:T(8,128)S(1)}, u32[]{:S(2)}, u32[]{:S(2)}) collective-permute-start(f32[1,256,128]{2,1,0:T(8,128)S(1)} %get-tuple-element.26), channel_id=1, source_target_pairs={{2,0},{4,2},{6,4},{8,6},{10,8},{12,10},{14,12},{16,14},{18,16},{20... | collective-permute-start | bytes 393224 | tf_op jit(solution)/shard_map/ppermute | solution.py:17
  50.0 5.7 %collective-permute-start.9 = (f32[1,256,128]{2,1,0:T(8,128)S(1)}, f32[1,256,128]{2,1,0:T(8,128)S(1)}, u32[]{:S(2)}, u32[]{:S(2)}) collective-permute-start(f32[1,256,128]{2,1,0:T(8,128)S(1)} %get-tuple-element.25), channel_id=1, source_target_pairs={{0,2},{2,4},{4,6},{6,8},{8,10},{10,12},{12,14},{14,16},{16,18},{18... | collective-permute-start | bytes 393224 | tf_op jit(solution)/shard_map/ppermute | solution.py:14
  53.4 7.5 %collective-permute-start.8 = (f32[1,256,128]{2,1,0:T(8,128)S(1)}, f32[1,256,128]{2,1,0:T(8,128)S(1)}, u32[]{:S(2)}, u32[]{:S(2)}) collective-permute-start(f32[1,256,128]{2,1,0:T(8,128)S(1)} %get-tuple-element.24), channel_id=1, source_target_pairs={{2,0},{4,2},{6,4},{8,6},{10,8},{12,10},{14,12},{16,14},{18,16},{20... | collective-permute-start | bytes 393224 | tf_op jit(solution)/shard_map/ppermute | solution.py:17
  61.2 5.1 %collective-permute-start.10 = (f32[2,256,128]{2,1,0:T(8,128)S(1)}, f32[2,256,128]{2,1,0:T(8,128)S(1)}, u32[]{:S(2)}, u32[]{:S(2)}) collective-permute-start(f32[2,256,128]{2,1,0:T(8,128)S(1)} %fusion.62), channel_id=1, source_target_pairs={{0,1},{2,3},{4,5},{6,7},{8,9},{10,11},{12,13},{14,15},{16,17},{18,... | collective-permute-start | bytes 786440 | tf_op jit(solution)/shard_map/ppermute | solution.py:25
  66.3 6.9 %collective-permute-start.12 = (f32[1,256,128]{2,1,0:T(8,128)S(1)}, f32[1,256,128]{2,1,0:T(8,128)S(1)}, u32[]{:S(2)}, u32[]{:S(2)}) collective-permute-start(f32[1,256,128]{2,1,0:T(8,128)S(1)} %get-tuple-element.23), channel_id=1, source_target_pairs={{0,2},{2,4},{4,6},{6,8},{8,10},{10,12},{12,14},{14,16},{16,18},{18... | collective-permute-start | bytes 393224 | tf_op jit(solution)/shard_map/ppermute | solution.py:14
  68.5 8.3 %collective-permute-start.11 = (f32[1,256,128]{2,1,0:T(8,128)S(1)}, f32[1,256,128]{2,1,0:T(8,128)S(1)}, u32[]{:S(2)}, u32[]{:S(2)}) collective-permute-start(f32[1,256,128]{2,1,0:T(8,128)S(1)} %get-tuple-element.22), channel_id=1, source_target_pairs={{2,0},{4,2},{6,4},{8,6},{10,8},{12,10},{14,12},{16,14},{18,16},{20... | collective-permute-start | bytes 393224 | tf_op jit(solution)/shard_map/ppermute | solution.py:17
  77.2 5.7 %collective-permute-start.14 = (f32[1,256,128]{2,1,0:T(8,128)S(1)}, f32[1,256,128]{2,1,0:T(8,128)S(1)}, u32[]{:S(2)}, u32[]{:S(2)}) collective-permute-start(f32[1,256,128]{2,1,0:T(8,128)S(1)} %get-tuple-element.21), channel_id=1, source_target_pairs={{0,2},{2,4},{4,6},{6,8},{8,10},{10,12},{12,14},{14,16},{16,18},{18... | collective-permute-start | bytes 393224 | tf_op jit(solution)/shard_map/ppermute | solution.py:14
  80.1 7.5 %collective-permute-start.13 = (f32[1,256,128]{2,1,0:T(8,128)S(1)}, f32[1,256,128]{2,1,0:T(8,128)S(1)}, u32[]{:S(2)}, u32[]{:S(2)}) collective-permute-start(f32[1,256,128]{2,1,0:T(8,128)S(1)} %get-tuple-element.20), channel_id=1, source_target_pairs={{2,0},{4,2},{6,4},{8,6},{10,8},{12,10},{14,12},{16,14},{18,16},{20... | collective-permute-start | bytes 393224 | tf_op jit(solution)/shard_map/ppermute | solution.py:17
  87.9 33.9 %collective-permute-start.16 = (f32[1,256,128]{2,1,0:T(8,128)S(1)}, f32[1,256,128]{2,1,0:T(8,128)S(1)}, u32[]{:S(2)}, u32[]{:S(2)}) collective-permute-start(f32[1,256,128]{2,1,0:T(8,128)S(1)} %get-tuple-element.19), channel_id=1, source_target_pairs={{0,2},{2,4},{4,6},{6,8},{8,10},{10,12},{12,14},{14,16},{16,18},{18... | collective-permute-start | bytes 393224 | tf_op jit(solution)/shard_map/ppermute | solution.py:14
  89.8 32.0 %collective-permute-start.15 = (f32[1,256,128]{2,1,0:T(8,128)S(1)}, f32[1,256,128]{2,1,0:T(8,128)S(1)}, u32[]{:S(2)}, u32[]{:S(2)}) collective-permute-start(f32[1,256,128]{2,1,0:T(8,128)S(1)} %get-tuple-element.18), channel_id=1, source_target_pairs={{2,0},{4,2},{6,4},{8,6},{10,8},{12,10},{14,12},{16,14},{18,16},{20... | collective-permute-start | bytes 393224 | tf_op jit(solution)/shard_map/ppermute | solution.py:17
  122.1 12.8 %collective-permute-start.18 = (f32[1,256,128]{2,1,0:T(8,128)S(1)}, f32[1,256,128]{2,1,0:T(8,128)S(1)}, u32[]{:S(2)}, u32[]{:S(2)}) collective-permute-start(f32[1,256,128]{2,1,0:T(8,128)S(1)} %get-tuple-element.17), channel_id=1, source_target_pairs={{0,2},{2,4},{4,6},{6,8},{8,10},{10,12},{12,14},{14,16},{16,18},{18... | collective-permute-start | bytes 393224 | tf_op jit(solution)/shard_map/ppermute | solution.py:14
  125.9 9.1 %collective-permute-start.17 = (f32[1,256,128]{2,1,0:T(8,128)S(1)}, f32[1,256,128]{2,1,0:T(8,128)S(1)}, u32[]{:S(2)}, u32[]{:S(2)}) collective-permute-start(f32[1,256,128]{2,1,0:T(8,128)S(1)} %get-tuple-element.16), channel_id=1, source_target_pairs={{2,0},{4,2},{6,4},{8,6},{10,8},{12,10},{14,12},{16,14},{18,16},{20... | collective-permute-start | bytes 393224 | tf_op jit(solution)/shard_map/ppermute | solution.py:17
  127.8 29.5 %collective-permute-start.21 = (f32[2,1,128,64]{3,2,1,0:T(8,128)S(1)}, f32[2,1,128,64]{3,2,1,0:T(8,128)S(1)}, u32[]{:S(2)}, u32[]{:S(2)}) collective-permute-start(f32[2,1,128,64]{3,2,1,0:T(8,128)S(1)} %pad_maximum_fusion.21), channel_id=1, source_target_pairs={{0,2},{2,4},{4,6},{6,8},{8,10},{10,12},{12,14},{14,16},{16,18},{18... | collective-permute-start | bytes 196616 | tf_op jit(solution)/shard_map/ppermute | solution.py:14
  133.0 24.4 %collective-permute-start.19 = (f32[2,1,128,64]{3,2,1,0:T(8,128)S(1)}, f32[2,1,128,64]{3,2,1,0:T(8,128)S(1)}, u32[]{:S(2)}, u32[]{:S(2)}) collective-permute-start(f32[2,1,128,64]{3,2,1,0:T(8,128)S(1)} %pad_maximum_fusion.21), channel_id=1, source_target_pairs={{2,0},{4,2},{6,4},{8,6},{10,8},{12,10},{14,12},{16,14},{18,16},{20... | collective-permute-start | bytes 196616 | tf_op jit(solution)/shard_map/ppermute | solution.py:17
  150.3 7.1 %collective-permute-start.22 = (f32[1,128,64]{2,1,0:T(8,128)S(1)}, f32[1,128,64]{2,1,0:T(8,128)S(1)}, u32[]{:S(2)}, u32[]{:S(2)}) collective-permute-start(f32[1,128,64]{2,1,0:T(8,128)S(1)} %multiply_bitcast_fusion.1), channel_id=1, source_target_pairs={{0,2},{2,4},{4,6},{6,8},{8,10},{10,12},{12,14},{14,16},{16,18},{18... | collective-permute-start | bytes 98312 | tf_op jit(solution)/shard_map/ppermute | solution.py:14
  155.4 6.8 %collective-permute-start.20 = (f32[1,128,64]{2,1,0:T(8,128)S(1)}, f32[1,128,64]{2,1,0:T(8,128)S(1)}, u32[]{:S(2)}, u32[]{:S(2)}) collective-permute-start(f32[1,128,64]{2,1,0:T(8,128)S(1)} %multiply_bitcast_fusion.1), channel_id=1, source_target_pairs={{2,0},{4,2},{6,4},{8,6},{10,8},{12,10},{14,12},{16,14},{18,16},{20... | collective-permute-start | bytes 98312 | tf_op jit(solution)/shard_map/ppermute | solution.py:17
  162.4 7.3 %collective-permute-start.23 = (f32[1,128,64]{2,1,0:T(8,128)S(1)}, f32[1,128,64]{2,1,0:T(8,128)S(1)}, u32[]{:S(2)}, u32[]{:S(2)}) collective-permute-start(f32[1,128,64]{2,1,0:T(8,128)S(1)} %fusion.186), channel_id=1, source_target_pairs={{0,1},{2,3},{4,5},{6,7},{8,9},{10,11},{12,13},{14,15},{16,17},{18,... | collective-permute-start | bytes 98312 | tf_op jit(solution)/shard_map/ppermute | solution.py:25
where the time goes:
time: 182 us; the launch traced here: 181 us
  starting transfers between devices  70.8 us (39%)
  waiting for transfers between devices  45.3 us (25%)
  local copies, waits for them, and re-layouts  41.2 us (23%)
  other arithmetic  22.8 us (13%)
    ppermute x11, starting transfers between devices, extended(): lax.ppermute(lax.slice_in_dim(block, block.shape[dim] - width, None, axis...  41.3 us
    reduce_sum x3, local copies, waits for them, and re-layouts, restrict(): return jnp.mean(blocks, axis=(1, 3, 5))  29.3 us
    ppermute x11, waiting for transfers between devices, extended(): lax.ppermute(lax.slice_in_dim(block, 0, width, axis=dim), axis, backward)  28.3 us
    ppermute x11, starting transfers between devices, extended(): lax.ppermute(lax.slice_in_dim(block, 0, width, axis=dim), axis, backward)  26.9 us
    reduce_sum x5, other arithmetic, restrict(): return jnp.mean(blocks, axis=(1, 3, 5))  15.9 us
    broadcast_in_dim x2, local copies, waits for them, and re-layouts, prolong(): jnp.broadcast_to(field[:, None, :, None, :, None], (first, 2, second, 2,...  10.8 us
    ppermute x2, waiting for transfers between devices, from_behind(): return lax.ppermute(block, axis, route)  9.75 us
    ppermute x11, waiting for transfers between devices, extended(): lax.ppermute(lax.slice_in_dim(block, block.shape[dim] - width, None, axis...  7.27 us
  transfers between devices with their start and end apart: 24, of which 15 were waited for; matrix products, arithmetic and copies ran while one was open for 25% of the time, Pallas kernels for 0%

commit v1 on v0

v1 whole, which is shorter than its diff:
```python
import jax
import jax.numpy as jnp
import numpy as np
from jax import lax
from jax.sharding import PartitionSpec as P

STEPS = 4
COARSE_STEPS = STEPS // 4


def advance(field, conduct, absorb, diffuse_scale, react_scale):
    center = field[1:-1]
    middle = conduct[1:-1]
    padded = jnp.pad(center, ((0, 0), (1, 1), (1, 1)))
    conduct_pad = jnp.pad(middle, ((0, 0), (1, 1), (1, 1)))
    inflow = 0.5 * (conduct[2:] + middle) * (field[2:] - center)
    inflow = inflow + 0.5 * (conduct[:-2] + middle) * (field[:-2] - center)
    inflow = inflow + 0.5 * (conduct_pad[:, 2:, 1:-1] + middle) * (padded[:, 2:, 1:-1] - center)
    inflow = inflow + 0.5 * (conduct_pad[:, :-2, 1:-1] + middle) * (padded[:, :-2, 1:-1] - center)
    inflow = inflow + 0.5 * (conduct_pad[:, 1:-1, 2:] + middle) * (padded[:, 1:-1, 2:] - center)
    inflow = inflow + 0.5 * (conduct_pad[:, 1:-1, :-2] + middle) * (padded[:, 1:-1, :-2] - center)
    return center + diffuse_scale * inflow - react_scale * absorb[1:-1] * center


def pair_matrix(fine):
    rows = np.arange(fine)[:, None] // 2 == np.arange(fine // 2)[None, :]
    return jnp.asarray(rows.astype(np.float32))


def restrict(field):
    first, second, third = field.shape
    planes = field.reshape(first // 2, 2, second, third).sum(axis=1)
    rows = pair_matrix(second)
    cols = pair_matrix(third)
    out = jnp.einsum("Yy,mYZ,Zz->myz", rows, planes, cols, precision=lax.Precision.HIGHEST)
    return out * 0.125


def prolong(field):
    first, second, third = field.shape
    rows = pair_matrix(second * 2)
    cols = pair_matrix(third * 2)
    out = jnp.einsum("Yy,myz,Zz->mYZ", rows, field, cols, precision=lax.Precision.HIGHEST)
    return jnp.repeat(out, 2, axis=0)


def gather_planes(block, axis_names, pairs_of, distances):
    pieces = {}
    for d in distances:
        if d == 0 and pairs_of(0) is None:
            pieces[d] = block
            continue
        pieces[d] = lax.ppermute(block, axis_names, pairs_of(d))
    return pieces


def shards(initial, guesses, diffusivity, reaction):
    space = lax.axis_size("space")
    times = lax.axis_size("tm")
    me_s = lax.axis_index("space")
    me_t = lax.axis_index("tm")
    n = initial.shape[0]
    halo = STEPS
    reach = -(-halo // n)

    def space_pairs(d):
        return [(s + d, s) for s in range(space) if 0 <= s + d < space]

    def joint(s, t):
        return s * times + t

    def prev_pairs(d):
        return [
            (joint(s + d, (t - 1) % times), joint(s, t))
            for s in range(space)
            for t in range(times)
            if 0 <= s + d < space
        ]

    start = guesses[0]
    local = jnp.stack([diffusivity, reaction, start])
    distances = [d for d in range(-reach, reach + 1)]
    got = gather_planes(local, "space", lambda d: None if d == 0 else space_pairs(d), distances)
    wide = jnp.concatenate([got[d] for d in distances], axis=1)
    lo = reach * n - halo
    hi = reach * n + n + halo
    wide = wide[:, lo:hi]
    conduct, absorb, field0 = wide[0], wide[1], wide[2]
    plane_ids = me_s * n - halo + jnp.arange(n + 2 * halo)
    inside = ((plane_ids >= 0) & (plane_ids < space * n)).astype(jnp.float32)[:, None, None]

    def fine_prop(field):
        for number in range(STEPS):
            cut = number
            k = conduct[cut : conduct.shape[0] - cut]
            c = absorb[cut : absorb.shape[0] - cut]
            field = advance(field, k, c, 0.1, 0.1)
            if number < STEPS - 1:
                m = inside[cut + 1 : inside.shape[0] - cut - 1]
                field = jnp.where(m > 0, field, 0.0)
        return field

    advanced = fine_prop(field0)
    payload = jnp.where(me_t == times - 1, initial, advanced)
    got2 = gather_planes(payload, ("space", "tm"), prev_pairs, distances)
    relaxed = jnp.concatenate([got2[d] for d in distances], axis=0)[lo:hi]
    residual = fine_prop(relaxed) - advanced

    cn = n // 2
    creach = -(-1 // cn)
    cdist = [d for d in range(-creach, creach + 1)]
    coarse_k = restrict(conduct[halo - 2 * creach * cn : halo + n + 2 * creach * cn])
    coarse_c = restrict(absorb[halo - 2 * creach * cn : halo + n + 2 * creach * cn])
    ck = coarse_k[creach * cn - 1 : creach * cn + cn + 1]
    cc = coarse_c[creach * cn - 1 : creach * cn + cn + 1]
    source = restrict(residual)

    def chain_pairs(d):
        return [
            (joint(s + d, t - 1), joint(s, t))
            for s in range(space)
            for t in range(1, times)
            if 0 <= s + d < space
        ]

    partial_error = source
    for turn in range(times - 1):
        got3 = gather_planes(partial_error, ("space", "tm"), chain_pairs, cdist)
        behind = jnp.concatenate([got3[d] for d in cdist], axis=0)
        behind = behind[creach * cn - 1 : creach * cn + cn + 1]
        for number in range(COARSE_STEPS):
            behind = advance(behind, ck, cc, 0.1, 0.4)
        partial_error = source + behind
    corrected = advanced + prolong(partial_error)
    return (corrected[None], residual[None])


def solution(mesh):
    in_specs = (
        P("space", None, None),
        P("tm", "space", None, None),
        P("space", None, None),
        P("space", None, None),
    )
    out_specs = (P("tm", "space", None, None), P("tm", "space", None, None))
    return jax.shard_map(shards, mesh=mesh, in_specs=in_specs, out_specs=out_specs, check_vma=False)
```

time: 182 us -> 120 us (0.66)
  starting transfers between devices: 70.8 us -> 30.8 us
  local copies, waits for them, and re-layouts: 41.2 us -> 9.47 us
  matrix products: 0 us -> 5.18 us
  waiting for transfers between devices: 45.3 us -> 48.9 us
    ppermute x24 -> x12, starting transfers between devices: 70.8 us -> 30.8 us  [gather_planes(): pieces[d] = lax.ppermute(block, axis_names, pairs_of(d))]
    reduce_sum x3 -> x0, local copies, waits for them, and re-layouts: 29.3 us -> none  [restrict(): return jnp.mean(blocks, axis=(1, 3, 5))]
    select_n x1 -> x7, other arithmetic: 0.03 us -> 13.4 us  [the longest x6 12.2 us: fine_prop(): field = jnp.where(m > 0, field, 0.0)]
    reduce_sum x5 -> x3, other arithmetic: 15.9 us -> 5.1 us  [restrict(): planes = field.reshape(first // 2, 2, second, third).sum(axis=1)]
    broadcast_in_dim x2 -> x0, local copies, waits for them, and re-layouts: 10.8 us -> none  [prolong(): jnp.broadcast_to(field[:, None, :, None, :, None], (first, 2, second, 2,...]
    dot_general x0 -> x8, matrix products: none -> 5.18 us  [the longest x6 4.5 us: restrict(): jnp.einsum('Yy,mYZ,Zz->myz', rows, planes, cols, precision=lax.Precision....]
    unnamed x4 -> x41, local copies, waits for them, and re-layouts: 0.01 us -> 5.09 us
    sub x7 -> x0, other arithmetic: 4.92 us -> none  [advance(): return center + diffuse_scale * inflow - react_scale * absorb[1:-1] * center]
  transfers between devices with their start and end apart: 24 -> 12, of which waited for: 15 -> 4; matrix products, arithmetic and copies ran while one was open for 25% -> 12% of each run, Pallas kernels for 0% -> 0%
where the time goes in v1:
time: 120 us; the launch traced here: 119 us
  waiting for transfers between devices  48.9 us (41%)
  starting transfers between devices  30.8 us (26%)
  other arithmetic  24 us (20%)
  local copies, waits for them, and re-layouts  9.47 us (8%)
  matrix products  5.18 us (4%)
  between operations  1.22 us (1%)
    ppermute x12, waiting for transfers between devices, gather_planes(): pieces[d] = lax.ppermute(block, axis_names, pairs_of(d))  48.9 us
    ppermute x12, starting transfers between devices, gather_planes(): pieces[d] = lax.ppermute(block, axis_names, pairs_of(d))  30.8 us
    select_n x6, other arithmetic, fine_prop(): field = jnp.where(m > 0, field, 0.0)  12.2 us
    reduce_sum x3, other arithmetic, restrict(): planes = field.reshape(first // 2, 2, second, third).sum(axis=1)  5.1 us
    unnamed x41, local copies, waits for them, and re-layouts  5.09 us
    dot_general x6, matrix products, restrict(): jnp.einsum('Yy,mYZ,Zz->myz', rows, planes, cols, precision=lax.Precision....  4.5 us
  transfers between devices with their start and end apart: 12, of which 4 were waited for; matrix products, arithmetic and copies ran while one was open for 12% of the time, Pallas kernels for 0%

profile of v1, /device:TPU:7, one launch (start us, length us, event | category | flops | bytes accessed | tf_op | source)
XLA Modules:
  0.0 119.5 jit_solution(10179962779391824194)
XLA Ops:
  0.7 2.2 %pad_maximum_fusion.3 = f32[3,2,256,128]{3,2,1,0:T(8,128)} fusion(f32[1,2,256,128]{3,2,1,0:T(8,128)} %param.13, f32[1,2,256,128]{3,2,1,0:T(8,128)} %bitcast.164, f32[1,2,256,128]{3,2,1,0:T(8,128)} %bitcast.175), kind=kLoop, calls=%fused_computation.175 | loop fusion | flops 393216 | bytes 1572864 | tf_op jit(solution)/shard_map/stack | solution.py:81
  2.8 3.1 %collective-permute-start = (f32[3,2,256,128]{3,2,1,0:T(8,128)}, f32[3,2,256,128]{3,2,1,0:T(8,128)S(1)}, u32[]{:S(2)}, u32[]{:S(2)}) collective-permute-start(f32[3,2,256,128]{3,2,1,0:T(8,128)} %pad_maximum_fusion.3), channel_id=1, source_target_pairs={{0,4},{2,6},{4,8},{6,10},{8,12},{10,14},{12,16},{14,18},{16,20},{1... | collective-permute-start | bytes 2359304 | tf_op jit(solution)/shard_map/ppermute | solution.py:53
  6.0 2.2 %collective-permute-start.3 = (f32[3,2,256,128]{3,2,1,0:T(8,128)}, f32[3,2,256,128]{3,2,1,0:T(8,128)}, u32[]{:S(2)}, u32[]{:S(2)}) collective-permute-start(f32[3,2,256,128]{3,2,1,0:T(8,128)} %pad_maximum_fusion.3), channel_id=1, source_target_pairs={{4,0},{6,2},{8,4},{10,6},{12,8},{14,10},{16,12},{18,14},{20,16},{2... | collective-permute-start | bytes 2359304 | tf_op jit(solution)/shard_map/ppermute | solution.py:53
  8.2 2.2 %collective-permute-start.2 = (f32[3,2,256,128]{3,2,1,0:T(8,128)}, f32[3,2,256,128]{3,2,1,0:T(8,128)S(1)}, u32[]{:S(2)}, u32[]{:S(2)}) collective-permute-start(f32[3,2,256,128]{3,2,1,0:T(8,128)} %pad_maximum_fusion.3), channel_id=1, source_target_pairs={{2,0},{4,2},{6,4},{8,6},{10,8},{12,10},{14,12},{16,14},{18,16},{20... | collective-permute-start | bytes 2359304 | tf_op jit(solution)/shard_map/ppermute | solution.py:53
  10.3 4.9 %collective-permute-start.1 = (f32[3,2,256,128]{3,2,1,0:T(8,128)}, f32[3,2,256,128]{3,2,1,0:T(8,128)S(1)}, u32[]{:S(2)}, u32[]{:S(2)}) collective-permute-start(f32[3,2,256,128]{3,2,1,0:T(8,128)} %pad_maximum_fusion.3), channel_id=1, source_target_pairs={{0,2},{2,4},{4,6},{6,8},{8,10},{10,12},{12,14},{14,16},{16,18},{18... | collective-permute-start | bytes 2359304 | tf_op jit(solution)/shard_map/ppermute | solution.py:53
  15.5 41.5 %collective-permute-done = f32[3,2,256,128]{3,2,1,0:T(8,128)S(1)} collective-permute-done((f32[3,2,256,128]{3,2,1,0:T(8,128)}, f32[3,2,256,128]{3,2,1,0:T(8,128)S(1)}, u32[]{:S(2)}, u32[]{:S(2)}) %collective-permute-start) | collective-permute-done | bytes 786464 | tf_op jit(solution)/shard_map/ppermute | solution.py:53
  57.6 1.5 %fusion.251 = (f32[1,6,256,128]{3,2,1,0:T(8,128)}, f32[6,256,128]{2,1,0:T(8,128)S(1)}, f32[1,6,256,128]{3,2,1,0:T(8,128)}) fusion(f32[3,6,256,128]{3,2,1,0:T(8,128)S(1)} %pad_maximum_fusion.2), kind=kLoop, calls=%fused_computation.366 | loop fusion | bytes 3932160 | tf_op jit(solution)/shard_map/slice | solution.py:22
  59.0 1.5 %constant_dynamic-update-slice_fusion = f32[3,10,256,128]{3,2,1,0:T(8,128)S(1)} fusion(f32[3,10,256,128]{3,2,1,0:T(8,128)S(1)} %constant_dynamic-update-slice_fusion.1, f32[3,2,256,128]{3,2,1,0:T(8,128)} %collective-permute-done.3), kind=kLoop, calls=%fused_computation.343 | loop fusion | bytes 1572864 | tf_op jit(solution)/shard_map/concatenate | solution.py:84
  60.7 2.1 %pad_maximum_fusion = (f32[3,8,256,128]{3,2,1,0:T(8,128)S(1)}, f32[3,8,256,128]{3,2,1,0:T(8,128)S(1)}) fusion(f32[3,2,256,128]{3,2,1,0:T(8,128)} %collective-permute-done.3, f32[3,2,256,128]{3,2,1,0:T(8,128)S(1)} %collective-permute-done.2, f32[1,2,256,128]{3,2,1,0:T(8,128)S(1)} %copy-done.2, f32[1,2,256,128]{3,2,1,0:T(8,128)S(1)} %bitcast.167, ...), kind=kLoop, calls=%fused_computation.12 | loop fusion | flops 7864320 | bytes 10223616 | tf_op jit(solution)/shard_map/concatenate | solution.py:84
  62.8 1.9 %fusion.20 = f32[8,256,128]{2,1,0:T(8,128)S(1)} fusion(f32[8,256,128]{2,1,0:T(8,128)S(1)} %get-tuple-element.7, f32[3,8,256,128]{3,2,1,0:T(8,128)S(1)} %get-tuple-element.12, f32[3,8,256,128]{3,2,1,0:T(8,128)S(1)} %get-tuple-element.11, f32[3,10,256,128]{3,2,1,0:T(8,128)S(1)} %constant_dynamic-update-slice_fusion, pred[8]{0:T(512)(128)(4,1)S(1)} %slice_compare_fusion, ...), kind=kLoop, calls=%fused_computation.62 | loop fusion | flops 9175040 | bytes 8388616 | tf_op jit(solution)/shard_map/jit(_where)/select_n | solution.py:100
  65.5 2.3 %fusion.73 = f32[6,256,128]{2,1,0:T(8,128)S(1)} fusion(f32[6,256,128]{2,1,0:T(8,128)S(1)} %slice.569, f32[8,256,128]{2,1,0:T(8,128)S(1)} %fusion.20, pred[6]{0:T(512)(128)(4,1)S(1)} %slice_compare_fusion.1, f32[6,256,128]{2,1,0:T(8,128)S(1)} %get-tuple-element.9, f32[3,2,256,128]{3,2,1,0:T(8,128)} %collective-permute-done.3, ...), kind=kLoop, calls=%fused_computation.136 | loop fusion | flops 8847360 | bytes 8650758 | tf_op jit(solution)/shard_map/jit(_where)/select_n | solution.py:100
  69.1 1.1 broadcast_select_fusion
  70.2 2.7 %collective-permute-start.8 = (f32[2,256,128]{2,1,0:T(8,128)}, f32[2,256,128]{2,1,0:T(8,128)}, u32[]{:S(2)}, u32[]{:S(2)}) collective-permute-start(f32[2,256,128]{2,1,0:T(8,128)} %get-tuple-element.4), channel_id=1, source_target_pairs={{5,0},{4,1},{7,2},{6,3},{9,4},{8,5},{11,6},{10,7},{13,8},{12,9},{1... | collective-permute-start | bytes 786440 | tf_op jit(solution)/shard_map/ppermute | solution.py:53
  72.9 2.8 %collective-permute-start.7 = (f32[2,256,128]{2,1,0:T(8,128)}, f32[2,256,128]{2,1,0:T(8,128)}, u32[]{:S(2)}, u32[]{:S(2)}) collective-permute-start(f32[2,256,128]{2,1,0:T(8,128)} %get-tuple-element.4), channel_id=1, source_target_pairs={{3,0},{2,1},{5,2},{4,3},{7,4},{6,5},{9,6},{8,7},{11,8},{10,9},{13,... | collective-permute-start | bytes 786440 | tf_op jit(solution)/shard_map/ppermute | solution.py:53
  75.8 5.3 %collective-permute-start.5 = (f32[2,256,128]{2,1,0:T(8,128)}, f32[2,256,128]{2,1,0:T(8,128)}, u32[]{:S(2)}, u32[]{:S(2)}) collective-permute-start(f32[2,256,128]{2,1,0:T(8,128)} %get-tuple-element.4), channel_id=1, source_target_pairs={{1,2},{0,3},{3,4},{2,5},{5,6},{4,7},{7,8},{6,9},{9,10},{8,11},{11,... | collective-permute-start | bytes 786440 | tf_op jit(solution)/shard_map/ppermute | solution.py:53
  81.1 3.6 %collective-permute-start.4 = (f32[2,256,128]{2,1,0:T(8,128)}, f32[2,256,128]{2,1,0:T(8,128)}, u32[]{:S(2)}, u32[]{:S(2)}) collective-permute-start(f32[2,256,128]{2,1,0:T(8,128)} %get-tuple-element.4), channel_id=1, source_target_pairs={{1,4},{0,5},{3,6},{2,7},{5,8},{4,9},{7,10},{6,11},{9,12},{8,13},{1... | collective-permute-start | bytes 786440 | tf_op jit(solution)/shard_map/ppermute | solution.py:53
  84.8 2.0 %reduce_sum.29 = f32[3,256,128]{2,1,0:T(8,128)} reduce(f32[3,2,256,128]{3,2,1,0:T(8,128)} %bitcast.187, f32[]{:T(128)} %constant.20.clone.1), dimensions={1}, to_apply=%region_2.3 | reduce | flops 98304 | bytes 1179652 | tf_op jit(solution)/shard_map/reduce_sum | solution.py:32
  86.8 2.0 %reduce_sum.28 = f32[3,256,128]{2,1,0:T(8,128)} reduce(f32[3,2,256,128]{3,2,1,0:T(8,128)} %bitcast.186, f32[]{:T(128)} %constant.20.clone.1), dimensions={1}, to_apply=%region_1.2 | reduce | flops 98304 | bytes 1179652 | tf_op jit(solution)/shard_map/reduce_sum | solution.py:32
  88.8 1.7 %fusion.254 = f32[64,3,256]{2,0,1:T(8,128)S(1)} fusion(f32[128,64,1]{1,0,2:T(8,128)} %constant.81, f32[3,256,128]{2,1,0:T(8,128)} %reduce_sum.29), kind=kOutput, calls=%fused_computation.369 | convolution fusion | flops 75497472 | bytes 622592 | tf_op jit(solution)/shard_map/Yy,mYZ,Zz->myz/dot_general | solution.py:35
  90.4 1.6 %fusion.253 = f32[64,3,256]{2,0,1:T(8,128)S(1)} fusion(f32[128,64,1]{1,0,2:T(8,128)} %constant.81, f32[3,256,128]{2,1,0:T(8,128)} %reduce_sum.28), kind=kOutput, calls=%fused_computation.368 | convolution fusion | flops 75497472 | bytes 622592 | tf_op jit(solution)/shard_map/Yy,mYZ,Zz->myz/dot_general | solution.py:35
  92.3 2.2 %collective-permute-done.4 = f32[2,256,128]{2,1,0:T(8,128)} collective-permute-done((f32[2,256,128]{2,1,0:T(8,128)}, f32[2,256,128]{2,1,0:T(8,128)}, u32[]{:S(2)}, u32[]{:S(2)}) %collective-permute-start.4) | collective-permute-done | bytes 262176 | tf_op jit(solution)/shard_map/ppermute | solution.py:53
  96.5 1.0 constant_dynamic-update-slice_fusion.7
  97.5 1.0 constant_dynamic-update-slice_fusion.6
  98.4 1.0 constant_dynamic-update-slice_fusion.5
  99.5 3.8 %fusion.36 = f32[8,256,128]{2,1,0:T(8,128)S(1)} fusion(f32[8,256,128]{2,1,0:T(8,128)S(1)} %slice.580, f32[2,256,128]{2,1,0:T(8,128)} %collective-permute-done.8, f32[2,256,128]{2,1,0:T(8,128)} %collective-permute-done.7, f32[2,256,128]{2,1,0:T(8,128)} %collective-permute-done.6, f32[2,256,128]{2,1,0:T(8,128)} %collective-permute-done.5, ...), kind=kLoop, calls=%fused_computation.78 | loop fusion | flops 10747904 | bytes 7602184 | tf_op jit(solution)/shard_map/jit(_where)/select_n | solution.py:100
  103.4 2.6 %fusion.89 = f32[6,256,128]{2,1,0:T(8,128)S(1)} fusion(f32[6,256,128]{2,1,0:T(8,128)S(1)} %slice.581, f32[8,256,128]{2,1,0:T(8,128)S(1)} %fusion.36, pred[6]{0:T(512)(128)(4,1)S(1)} %slice_compare_fusion.1, f32[6,256,128]{2,1,0:T(8,128)S(1)} %copy-done.9, f32[3,2,256,128]{3,2,1,0:T(8,128)} %collective-permute-done.3, ...), kind=kLoop, calls=%fused_computation.152 | loop fusion | flops 8847360 | bytes 8650758 | tf_op jit(solution)/shard_map/jit(_where)/select_n | solution.py:100
  106.9 1.1 fusion.248
  108.7 1.3 %collective-permute-start.11 = (f32[1,128,64]{1,2,0:T(8,128)S(1)}, f32[1,128,64]{1,2,0:T(8,128)S(1)}, u32[]{:S(2)}, u32[]{:S(2)}) collective-permute-start(f32[1,128,64]{1,2,0:T(8,128)S(1)} %fusion.2), channel_id=1, source_target_pairs={{0,3},{2,5},{4,7},{6,9},{8,11},{10,13},{12,15},{14,17},{16,19},{18... | collective-permute-start | bytes 98312 | tf_op jit(solution)/shard_map/ppermute | solution.py:53
  110.0 1.3 %collective-permute-start.10 = (f32[1,128,64]{1,2,0:T(8,128)S(1)}, f32[1,128,64]{1,2,0:T(8,128)S(1)}, u32[]{:S(2)}, u32[]{:S(2)}) collective-permute-start(f32[1,128,64]{1,2,0:T(8,128)S(1)} %fusion.2), channel_id=1, source_target_pairs={{2,1},{4,3},{6,5},{8,7},{10,9},{12,11},{14,13},{16,15},{18,17},{20... | collective-permute-start | bytes 98312 | tf_op jit(solution)/shard_map/ppermute | solution.py:53
  111.3 1.3 %collective-permute-start.9 = (f32[1,128,64]{1,2,0:T(8,128)S(1)}, f32[1,128,64]{1,2,0:T(8,128)S(1)}, u32[]{:S(2)}, u32[]{:S(2)}) collective-permute-start(f32[1,128,64]{1,2,0:T(8,128)S(1)} %fusion.2), channel_id=1, source_target_pairs={{0,1},{2,3},{4,5},{6,7},{8,9},{10,11},{12,13},{14,15},{16,17},{18,... | collective-permute-start | bytes 98312 | tf_op jit(solution)/shard_map/ppermute | solution.py:53
  113.0 1.0 collective-permute-done.11
  113.9 4.1 %collective-permute-done.10 = f32[1,128,64]{1,2,0:T(8,128)S(1)} collective-permute-done((f32[1,128,64]{1,2,0:T(8,128)S(1)}, f32[1,128,64]{1,2,0:T(8,128)S(1)}, u32[]{:S(2)}, u32[]{:S(2)}) %collective-permute-start.10) | collective-permute-done | bytes 32800 | tf_op jit(solution)/shard_map/ppermute | solution.py:53
  (73 shorter events, 8.6 us)
Async XLA Ops:
  0.6 56.5 %copy-start.2 = (f32[1,2,256,128]{3,2,1,0:T(8,128)S(1)}, f32[1,2,256,128]{3,2,1,0:T(8,128)}, u32[]{:S(2)}) copy-start(f32[1,2,256,128]{3,2,1,0:T(8,128)} %param.13) | copy-start | bytes 786436
  0.6 56.5 %copy-start = (f32[2,256,128]{2,1,0:T(8,128)S(1)}, f32[2,256,128]{2,1,0:T(8,128)}, u32[]{:S(2)}) copy-start(f32[2,256,128]{2,1,0:T(8,128)} %param.15) | copy-start | bytes 786436
  0.7 56.5 %copy-start.1 = (f32[2,256,128]{2,1,0:T(8,128)S(1)}, f32[2,256,128]{2,1,0:T(8,128)}, u32[]{:S(2)}) copy-start(f32[2,256,128]{2,1,0:T(8,128)} %param.14) | copy-start | bytes 786436
  2.8 54.2 %collective-permute-start = (f32[3,2,256,128]{3,2,1,0:T(8,128)}, f32[3,2,256,128]{3,2,1,0:T(8,128)S(1)}, u32[]{:S(2)}, u32[]{:S(2)}) collective-permute-start(f32[3,2,256,128]{3,2,1,0:T(8,128)} %pad_maximum_fusion.3), channel_id=1, source_target_pairs={{0,4},{2,6},{4,8},{6,10},{8,12},{10,14},{12,16},{14,18},{16,20},{1... | collective-permute-start | bytes 2359304 | tf_op jit(solution)/shard_map/ppermute | solution.py:53
  6.0 53.1 %collective-permute-start.3 = (f32[3,2,256,128]{3,2,1,0:T(8,128)}, f32[3,2,256,128]{3,2,1,0:T(8,128)}, u32[]{:S(2)}, u32[]{:S(2)}) collective-permute-start(f32[3,2,256,128]{3,2,1,0:T(8,128)} %pad_maximum_fusion.3), channel_id=1, source_target_pairs={{4,0},{6,2},{8,4},{10,6},{12,8},{14,10},{16,12},{18,14},{20,16},{2... | collective-permute-start | bytes 2359304 | tf_op jit(solution)/shard_map/ppermute | solution.py:53
  8.2 49.1 %collective-permute-start.2 = (f32[3,2,256,128]{3,2,1,0:T(8,128)}, f32[3,2,256,128]{3,2,1,0:T(8,128)S(1)}, u32[]{:S(2)}, u32[]{:S(2)}) collective-permute-start(f32[3,2,256,128]{3,2,1,0:T(8,128)} %pad_maximum_fusion.3), channel_id=1, source_target_pairs={{2,0},{4,2},{6,4},{8,6},{10,8},{12,10},{14,12},{16,14},{18,16},{20... | collective-permute-start | bytes 2359304 | tf_op jit(solution)/shard_map/ppermute | solution.py:53
  10.3 46.8 %collective-permute-start.1 = (f32[3,2,256,128]{3,2,1,0:T(8,128)}, f32[3,2,256,128]{3,2,1,0:T(8,128)S(1)}, u32[]{:S(2)}, u32[]{:S(2)}) collective-permute-start(f32[3,2,256,128]{3,2,1,0:T(8,128)} %pad_maximum_fusion.3), channel_id=1, source_target_pairs={{0,2},{2,4},{4,6},{6,8},{8,10},{10,12},{12,14},{14,16},{16,18},{18... | collective-permute-start | bytes 2359304 | tf_op jit(solution)/shard_map/ppermute | solution.py:53
  57.5 8.0 %copy-start.3 = (f32[3,6,256,128]{3,2,1,0:T(8,128)}, f32[3,6,256,128]{3,2,1,0:T(8,128)S(1)}, u32[]{:S(2)}) copy-start(f32[3,6,256,128]{3,2,1,0:T(8,128)S(1)} %pad_maximum_fusion.2) | copy-start | bytes 7077892
  59.0 6.5 %copy-start.8 = (f32[6,256,128]{2,1,0:T(8,128)}, f32[6,256,128]{2,1,0:T(8,128)S(1)}, u32[]{:S(2)}) copy-start(f32[6,256,128]{2,1,0:T(8,128)S(1)} %get-tuple-element.9) | copy-start | bytes 2359300
  60.5 2.3 %copy-start.10 = (f32[3,10,256,128]{3,2,1,0:T(8,128)}, f32[3,10,256,128]{3,2,1,0:T(8,128)S(1)}, u32[]{:S(2)}) copy-start(f32[3,10,256,128]{3,2,1,0:T(8,128)S(1)} %constant_dynamic-update-slice_fusion) | copy-start | bytes 11796484
  60.7 2.1 %copy-start.6 = (f32[8,256,128]{2,1,0:T(8,128)}, f32[8,256,128]{2,1,0:T(8,128)S(1)}, u32[]{:S(2)}) copy-start(f32[8,256,128]{2,1,0:T(8,128)S(1)} %get-tuple-element.6) | copy-start | bytes 3145732
  62.8 1.9 %copy-start.4 = (f32[3,8,256,128]{3,2,1,0:T(8,128)}, f32[3,8,256,128]{3,2,1,0:T(8,128)S(1)}, u32[]{:S(2)}) copy-start(f32[3,8,256,128]{3,2,1,0:T(8,128)S(1)} %get-tuple-element.11) | copy-start | bytes 9437188
  62.8 2.6 %copy-start.5 = (f32[3,8,256,128]{3,2,1,0:T(8,128)}, f32[3,8,256,128]{3,2,1,0:T(8,128)S(1)}, u32[]{:S(2)}) copy-start(f32[3,8,256,128]{3,2,1,0:T(8,128)S(1)} %get-tuple-element.12) | copy-start | bytes 9437188
  67.9 2.3 %copy-start.11 = (f32[4,256,128]{2,1,0:T(8,128)}, f32[4,256,128]{2,1,0:T(8,128)S(1)}, u32[]{:S(2)}) copy-start(f32[4,256,128]{2,1,0:T(8,128)S(1)} %maximum_bitcast_fusion.3) | copy-start | bytes 1572868
  67.9 1.1 copy-start.15
  69.1 22.9 %copy-start.14 = (f32[256,128,1]{1,0,2:T(8,128)S(1)}, f32[256,128,1]{1,0,2:T(8,128)}, u32[]{:S(2)}) copy-start(f32[256,128,1]{1,0,2:T(8,128)} %constant.82) | copy-start | bytes 393220
  70.2 28.2 %collective-permute-start.8 = (f32[2,256,128]{2,1,0:T(8,128)}, f32[2,256,128]{2,1,0:T(8,128)}, u32[]{:S(2)}, u32[]{:S(2)}) collective-permute-start(f32[2,256,128]{2,1,0:T(8,128)} %get-tuple-element.4), channel_id=1, source_target_pairs={{5,0},{4,1},{7,2},{6,3},{9,4},{8,5},{11,6},{10,7},{13,8},{12,9},{1... | collective-permute-start | bytes 786440 | tf_op jit(solution)/shard_map/ppermute | solution.py:53
  72.9 24.5 %collective-permute-start.7 = (f32[2,256,128]{2,1,0:T(8,128)}, f32[2,256,128]{2,1,0:T(8,128)}, u32[]{:S(2)}, u32[]{:S(2)}) collective-permute-start(f32[2,256,128]{2,1,0:T(8,128)} %get-tuple-element.4), channel_id=1, source_target_pairs={{3,0},{2,1},{5,2},{4,3},{7,4},{6,5},{9,6},{8,7},{11,8},{10,9},{13,... | collective-permute-start | bytes 786440 | tf_op jit(solution)/shard_map/ppermute | solution.py:53
  75.8 20.7 %collective-permute-start.6 = (f32[2,256,128]{2,1,0:T(8,128)}, f32[2,256,128]{2,1,0:T(8,128)}, u32[]{:S(2)}, u32[]{:S(2)}) collective-permute-start(f32[2,256,128]{2,1,0:T(8,128)} %get-tuple-element.4), channel_id=1, source_target_pairs={{1,0},{0,1},{3,2},{2,3},{5,4},{4,5},{7,6},{6,7},{9,8},{8,9},{11,10... | collective-permute-start | bytes 786440 | tf_op jit(solution)/shard_map/ppermute | solution.py:53
  75.8 19.6 %collective-permute-start.5 = (f32[2,256,128]{2,1,0:T(8,128)}, f32[2,256,128]{2,1,0:T(8,128)}, u32[]{:S(2)}, u32[]{:S(2)}) collective-permute-start(f32[2,256,128]{2,1,0:T(8,128)} %get-tuple-element.4), channel_id=1, source_target_pairs={{1,2},{0,3},{3,4},{2,5},{5,6},{4,7},{7,8},{6,9},{9,10},{8,11},{11,... | collective-permute-start | bytes 786440 | tf_op jit(solution)/shard_map/ppermute | solution.py:53
  81.1 13.4 %collective-permute-start.4 = (f32[2,256,128]{2,1,0:T(8,128)}, f32[2,256,128]{2,1,0:T(8,128)}, u32[]{:S(2)}, u32[]{:S(2)}) collective-permute-start(f32[2,256,128]{2,1,0:T(8,128)} %get-tuple-element.4), channel_id=1, source_target_pairs={{1,4},{0,5},{3,6},{2,7},{5,8},{4,9},{7,10},{6,11},{9,12},{8,13},{1... | collective-permute-start | bytes 786440 | tf_op jit(solution)/shard_map/ppermute | solution.py:53
  88.8 10.7 %copy-start.7 = (f32[8,256,128]{2,1,0:T(8,128)S(1)}, f32[8,256,128]{2,1,0:T(8,128)}, u32[]{:S(2)}) copy-start(f32[8,256,128]{2,1,0:T(8,128)} %copy-done.6) | copy-start | bytes 3145732
  99.5 3.9 %copy-start.9 = (f32[6,256,128]{2,1,0:T(8,128)S(1)}, f32[6,256,128]{2,1,0:T(8,128)}, u32[]{:S(2)}) copy-start(f32[6,256,128]{2,1,0:T(8,128)} %copy-done.8) | copy-start | bytes 2359300
  103.4 2.6 %copy-start.12 = (f32[4,256,128]{2,1,0:T(8,128)S(1)}, f32[4,256,128]{2,1,0:T(8,128)}, u32[]{:S(2)}) copy-start(f32[4,256,128]{2,1,0:T(8,128)} %copy-done.11) | copy-start | bytes 1572868
  106.9 1.2 copy-start.16
  106.9 1.4 %copy-start.13 = (f32[256,128]{1,0:T(8,128)S(1)}, f32[256,128]{1,0:T(8,128)}, u32[]{:S(2)}) copy-start(f32[256,128]{1,0:T(8,128)} %constant.26.clone) | copy-start | bytes 393220
  108.7 5.2 %collective-permute-start.11 = (f32[1,128,64]{1,2,0:T(8,128)S(1)}, f32[1,128,64]{1,2,0:T(8,128)S(1)}, u32[]{:S(2)}, u32[]{:S(2)}) collective-permute-start(f32[1,128,64]{1,2,0:T(8,128)S(1)} %fusion.2), channel_id=1, source_target_pairs={{0,3},{2,5},{4,7},{6,9},{8,11},{10,13},{12,15},{14,17},{16,19},{18... | collective-permute-start | bytes 98312 | tf_op jit(solution)/shard_map/ppermute | solution.py:53
  110.0 8.1 %collective-permute-start.10 = (f32[1,128,64]{1,2,0:T(8,128)S(1)}, f32[1,128,64]{1,2,0:T(8,128)S(1)}, u32[]{:S(2)}, u32[]{:S(2)}) collective-permute-start(f32[1,128,64]{1,2,0:T(8,128)S(1)} %fusion.2), channel_id=1, source_target_pairs={{2,1},{4,3},{6,5},{8,7},{10,9},{12,11},{14,13},{16,15},{18,17},{20... | collective-permute-start | bytes 98312 | tf_op jit(solution)/shard_map/ppermute | solution.py:53
  111.3 6.8 %collective-permute-start.9 = (f32[1,128,64]{1,2,0:T(8,128)S(1)}, f32[1,128,64]{1,2,0:T(8,128)S(1)}, u32[]{:S(2)}, u32[]{:S(2)}) collective-permute-start(f32[1,128,64]{1,2,0:T(8,128)S(1)} %fusion.2), channel_id=1, source_target_pairs={{0,1},{2,3},{4,5},{6,7},{8,9},{10,11},{12,13},{14,15},{16,17},{18,... | collective-permute-start | bytes 98312 | tf_op jit(solution)/shard_map/ppermute | solution.py:53

commit v2 on v1

--- a/solution.py
+++ b/solution.py
@@ -78,14 +78,30 @@
         ]
 
     start = guesses[0]
-    local = jnp.stack([diffusivity, reaction, start])
     distances = [d for d in range(-reach, reach + 1)]
+    lo = reach * n - halo
+    hi = reach * n + n + halo
+    split = times % 2 == 0
+    if split:
+        even = me_t % 2 == 0
+        local = jnp.stack([jnp.where(even, diffusivity, reaction), start])
+    else:
+        local = jnp.stack([diffusivity, reaction, start])
     got = gather_planes(local, "space", lambda d: None if d == 0 else space_pairs(d), distances)
     wide = jnp.concatenate([got[d] for d in distances], axis=1)
-    lo = reach * n - halo
-    hi = reach * n + n + halo
     wide = wide[:, lo:hi]
-    conduct, absorb, field0 = wide[0], wide[1], wide[2]
+    if split:
+        mine = wide[0]
+        rim = jnp.concatenate([mine[:halo], mine[halo + n :]], axis=0)
+        partner = [(t, t ^ 1) for t in range(times)]
+        theirs_rim = lax.ppermute(rim, "tm", partner)
+        theirs_own = jnp.where(even, reaction, diffusivity)
+        theirs = jnp.concatenate([theirs_rim[:halo], theirs_own, theirs_rim[halo:]], axis=0)
+        conduct = jnp.where(even, mine, theirs)
+        absorb = jnp.where(even, theirs, mine)
+        field0 = wide[1]
+    else:
+        conduct, absorb, field0 = wide[0], wide[1], wide[2]
     plane_ids = me_s * n - halo + jnp.arange(n + 2 * halo)
     inside = ((plane_ids >= 0) & (plane_ids < space * n)).astype(jnp.float32)[:, None, None]
 

time: 120 us -> 103 us (0.86)
  the two profiles are of different devices: /device:TPU:7 before, /device:TPU:23 now
where the time goes in v2:
time: 103 us; the launch traced here: 102 us
  waiting for transfers between devices  37.1 us (36%)
  starting transfers between devices  30.1 us (29%)
  other arithmetic  19.1 us (19%)
  local copies, waits for them, and re-layouts  9.4 us (9%)
  matrix products  5.11 us (5%)
  between operations  1.22 us (1%)
    ppermute x12, waiting for transfers between devices, gather_planes(): pieces[d] = lax.ppermute(block, axis_names, pairs_of(d))  35.5 us
    ppermute x12, starting transfers between devices, gather_planes(): pieces[d] = lax.ppermute(block, axis_names, pairs_of(d))  29.6 us
    select_n x5, other arithmetic, fine_prop(): field = jnp.where(m > 0, field, 0.0)  8.33 us
    unnamed x51, local copies, waits for them, and re-layouts  7.7 us
    dot_general x6, matrix products, restrict(): jnp.einsum('Yy,mYZ,Zz->myz', rows, planes, cols, precision=lax.Precision....  4.43 us
    reduce_sum x3, other arithmetic, restrict(): planes = field.reshape(first // 2, 2, second, third).sum(axis=1)  3.95 us
    slice x1, other arithmetic, advance(): return center + diffuse_scale * inflow - react_scale * absorb[1:-1] * center  2.07 us
  transfers between devices with their start and end apart: 13, of which 8 were waited for; matrix products, arithmetic and copies ran while one was open for 11% of the time, Pallas kernels for 0%

profile of v2, /device:TPU:23, one launch (start us, length us, event | category | flops | bytes accessed | tf_op | source)
XLA Modules:
  0.0 102.1 jit_solution(4998776054111230537)
XLA Ops:
  0.6 1.1 %broadcast_select_fusion.1 = (f32[2,256,128]{2,1,0:T(8,128)S(1)}, f32[1,2,256,128]{3,2,1,0:T(8,128)S(1)}) fusion(f32[2,256,128]{2,1,0:T(8,128)} %param.15, f32[2,256,128]{2,1,0:T(8,128)} %param.14, pred[]{:T(512)S(6)} %eq.8), kind=kLoop, calls=%fused_computation.296 | loop fusion | flops 131072 | bytes 1048577 | tf_op jit(solution)/shard_map/jit(_where)/select_n | solution.py:98
  1.7 1.1 %pad_maximum_fusion.11 = f32[2,2,256,128]{3,2,1,0:T(8,128)S(1)} fusion(f32[1,2,256,128]{3,2,1,0:T(8,128)} %param.13, f32[1,2,256,128]{3,2,1,0:T(8,128)S(1)} %get-tuple-element.13), kind=kLoop, calls=%fused_computation.238 | loop fusion | flops 131072 | bytes 1048576 | tf_op jit(solution)/shard_map/stack | solution.py:87
  2.8 2.1 %collective-permute-start.3 = (f32[2,2,256,128]{3,2,1,0:T(8,128)S(1)}, f32[2,2,256,128]{3,2,1,0:T(8,128)S(1)}, u32[]{:S(2)}, u32[]{:S(2)}) collective-permute-start(f32[2,2,256,128]{3,2,1,0:T(8,128)S(1)} %pad_maximum_fusion.11), channel_id=1, source_target_pairs={{4,0},{6,2},{8,4},{10,6},{12,8},{14,10},{16,12},{18,14},{20,16},{2... | collective-permute-start | bytes 1572872 | tf_op jit(solution)/shard_map/ppermute | solution.py:53
  5.0 2.2 %collective-permute-start.2 = (f32[2,2,256,128]{3,2,1,0:T(8,128)S(1)}, f32[2,2,256,128]{3,2,1,0:T(8,128)S(1)}, u32[]{:S(2)}, u32[]{:S(2)}) collective-permute-start(f32[2,2,256,128]{3,2,1,0:T(8,128)S(1)} %pad_maximum_fusion.11), channel_id=1, source_target_pairs={{2,0},{4,2},{6,4},{8,6},{10,8},{12,10},{14,12},{16,14},{18,16},{20... | collective-permute-start | bytes 1572872 | tf_op jit(solution)/shard_map/ppermute | solution.py:53
  7.1 4.9 %collective-permute-start.1 = (f32[2,2,256,128]{3,2,1,0:T(8,128)S(1)}, f32[2,2,256,128]{3,2,1,0:T(8,128)S(1)}, u32[]{:S(2)}, u32[]{:S(2)}) collective-permute-start(f32[2,2,256,128]{3,2,1,0:T(8,128)S(1)} %pad_maximum_fusion.11), channel_id=1, source_target_pairs={{0,2},{2,4},{4,6},{6,8},{8,10},{10,12},{12,14},{14,16},{16,18},{18... | collective-permute-start | bytes 1572872 | tf_op jit(solution)/shard_map/ppermute | solution.py:53
  12.1 3.1 %collective-permute-start = (f32[2,2,256,128]{3,2,1,0:T(8,128)S(1)}, f32[2,2,256,128]{3,2,1,0:T(8,128)S(1)}, u32[]{:S(2)}, u32[]{:S(2)}) collective-permute-start(f32[2,2,256,128]{3,2,1,0:T(8,128)S(1)} %pad_maximum_fusion.11), channel_id=1, source_target_pairs={{0,4},{2,6},{4,8},{6,10},{8,12},{10,14},{12,16},{14,18},{16,20},{1... | collective-permute-start | bytes 1572872 | tf_op jit(solution)/shard_map/ppermute | solution.py:53
  15.4 11.4 %collective-permute-done.3 = f32[2,2,256,128]{3,2,1,0:T(8,128)S(1)} collective-permute-done((f32[2,2,256,128]{3,2,1,0:T(8,128)S(1)}, f32[2,2,256,128]{3,2,1,0:T(8,128)S(1)}, u32[]{:S(2)}, u32[]{:S(2)}) %collective-permute-start.3) | collective-permute-done | bytes 524320 | tf_op jit(solution)/shard_map/ppermute | solution.py:53
  26.8 2.9 %collective-permute-done.2 = f32[2,2,256,128]{3,2,1,0:T(8,128)S(1)} collective-permute-done((f32[2,2,256,128]{3,2,1,0:T(8,128)S(1)}, f32[2,2,256,128]{3,2,1,0:T(8,128)S(1)}, u32[]{:S(2)}, u32[]{:S(2)}) %collective-permute-start.2) | collective-permute-done | bytes 524320 | tf_op jit(solution)/shard_map/ppermute | solution.py:53
  29.7 1.8 %collective-permute-done.1 = f32[2,2,256,128]{3,2,1,0:T(8,128)S(1)} collective-permute-done((f32[2,2,256,128]{3,2,1,0:T(8,128)S(1)}, f32[2,2,256,128]{3,2,1,0:T(8,128)S(1)}, u32[]{:S(2)}, u32[]{:S(2)}) %collective-permute-start.1) | collective-permute-done | bytes 524320 | tf_op jit(solution)/shard_map/ppermute | solution.py:53
  31.5 10.4 %collective-permute-done = f32[2,2,256,128]{3,2,1,0:T(8,128)S(1)} collective-permute-done((f32[2,2,256,128]{3,2,1,0:T(8,128)S(1)}, f32[2,2,256,128]{3,2,1,0:T(8,128)S(1)}, u32[]{:S(2)}, u32[]{:S(2)}) %collective-permute-start) | collective-permute-done | bytes 524320 | tf_op jit(solution)/shard_map/ppermute | solution.py:53
  43.3 1.6 %collective-permute-done.4 = f32[8,256,128]{2,1,0:T(8,128)S(1)} collective-permute-done((f32[8,256,128]{2,1,0:T(8,128)S(1)}, f32[8,256,128]{2,1,0:T(8,128)S(1)}, u32[]{:S(2)}, u32[]{:S(2)}) %collective-permute-start.4) | collective-permute-done | bytes 1048608 | tf_op jit(solution)/shard_map/ppermute | solution.py:97
  47.5 2.2 %fusion.22 = f32[8,256,128]{2,1,0:T(8,128)S(1)} fusion(f32[8,256,128]{2,1,0:T(8,128)S(1)} %slice_bitcast_fusion.1, f32[2,2,256,128]{3,2,1,0:T(8,128)S(1)} %copy-done.7, f32[1,2,256,128]{3,2,1,0:T(8,128)S(1)} %copy-done.14, f32[1,2,256,128]{3,2,1,0:T(8,128)S(1)} %copy-done.13, f32[2,2,256,128]{3,2,1,0:T(8,128)S(1)} %copy-done.9, ...), kind=kLoop, calls=%fused_computation.63 | loop fusion | flops 11272192 | bytes 8912904 | tf_op jit(solution)/shard_map/jit(_where)/select_n | solution.py:116
  49.7 2.1 %fusion.246 = (f32[6,256,128]{2,1,0:T(8,128)}, f32[6,256,128]{2,1,0:T(8,128)S(1)}) fusion(f32[10,256,128]{2,1,0:T(8,128)S(1)} %get-tuple-element.7, f32[6,256,128]{2,1,0:T(8,128)S(1)} %slice.530, f32[6,256,128]{2,1,0:T(8,128)S(1)} %slice.532, f32[8,256,128]{2,1,0:T(8,128)S(1)} %fusion.22, f32[10,256,128]{2,1,0:T(8,128)S(1)} %get-tuple-element.6, ...), kind=kLoop, calls=%fused_computation.362 | loop fusion | flops 6881280 | bytes 7077894 | tf_op jit(solution)/shard_map/slice | solution.py:22
  52.8 1.2 %broadcast_select_fusion = (f32[2,256,128]{2,1,0:T(8,128)}, f32[2,256,128]{2,1,0:T(8,128)}) fusion(f32[2,256,128]{2,1,0:T(8,128)S(1)} %copy-done.21, pred[]{:T(512)S(6)} %eq.9, f32[2,256,128]{2,1,0:T(8,128)S(1)} %slice.544, f32[10,256,128]{2,1,0:T(8,128)S(1)} %get-tuple-element.7, f32[2,256,128]{2,1,0:T(8,128)S(1)} %slice.546, ...), kind=kLoop, calls=%fused_computation.295 | loop fusion | flops 2293760 | bytes 2621441 | tf_op jit(solution)/shard_map/jit(_where)/select_n | solution.py:120
  54.1 2.6 %collective-permute-start.9 = (f32[2,256,128]{2,1,0:T(8,128)}, f32[2,256,128]{2,1,0:T(8,128)}, u32[]{:S(2)}, u32[]{:S(2)}) collective-permute-start(f32[2,256,128]{2,1,0:T(8,128)} %get-tuple-element.4), channel_id=1, source_target_pairs={{5,0},{4,1},{7,2},{6,3},{9,4},{8,5},{11,6},{10,7},{13,8},{12,9},{1... | collective-permute-start | bytes 786440 | tf_op jit(solution)/shard_map/ppermute | solution.py:53
  56.6 1.9 %collective-permute-start.8 = (f32[2,256,128]{2,1,0:T(8,128)}, f32[2,256,128]{2,1,0:T(8,128)}, u32[]{:S(2)}, u32[]{:S(2)}) collective-permute-start(f32[2,256,128]{2,1,0:T(8,128)} %get-tuple-element.4), channel_id=1, source_target_pairs={{3,0},{2,1},{5,2},{4,3},{7,4},{6,5},{9,6},{8,7},{11,8},{10,9},{13,... | collective-permute-start | bytes 786440 | tf_op jit(solution)/shard_map/ppermute | solution.py:53
  58.7 5.5 %collective-permute-start.6 = (f32[2,256,128]{2,1,0:T(8,128)}, f32[2,256,128]{2,1,0:T(8,128)}, u32[]{:S(2)}, u32[]{:S(2)}) collective-permute-start(f32[2,256,128]{2,1,0:T(8,128)} %get-tuple-element.4), channel_id=1, source_target_pairs={{1,2},{0,3},{3,4},{2,5},{5,6},{4,7},{7,8},{6,9},{9,10},{8,11},{11,... | collective-permute-start | bytes 786440 | tf_op jit(solution)/shard_map/ppermute | solution.py:53
  64.2 3.2 %collective-permute-start.5 = (f32[2,256,128]{2,1,0:T(8,128)}, f32[2,256,128]{2,1,0:T(8,128)}, u32[]{:S(2)}, u32[]{:S(2)}) collective-permute-start(f32[2,256,128]{2,1,0:T(8,128)} %get-tuple-element.4), channel_id=1, source_target_pairs={{1,4},{0,5},{3,6},{2,7},{5,8},{4,9},{7,10},{6,11},{9,12},{8,13},{1... | collective-permute-start | bytes 786440 | tf_op jit(solution)/shard_map/ppermute | solution.py:53
  68.2 2.0 %reduce_sum.29 = f32[3,256,128]{2,1,0:T(8,128)} reduce(f32[3,2,256,128]{3,2,1,0:T(8,128)} %bitcast.66, f32[]{:T(128)} %constant.20.clone.1), dimensions={1}, to_apply=%region_2.3 | reduce | flops 98304 | bytes 1179652 | tf_op jit(solution)/shard_map/reduce_sum | solution.py:32
  70.2 1.6 %fusion.249 = f32[64,3,256]{2,0,1:T(8,128)S(1)} fusion(f32[128,64,1]{1,0,2:T(8,128)} %constant.90, f32[3,256,128]{2,1,0:T(8,128)} %reduce_sum.28), kind=kOutput, calls=%fused_computation.365 | convolution fusion | flops 75497472 | bytes 622592 | tf_op jit(solution)/shard_map/Yy,mYZ,Zz->myz/dot_general | solution.py:35
  71.8 1.6 %fusion.250 = f32[64,3,256]{2,0,1:T(8,128)S(1)} fusion(f32[128,64,1]{1,0,2:T(8,128)} %constant.90, f32[3,256,128]{2,1,0:T(8,128)} %reduce_sum.29), kind=kOutput, calls=%fused_computation.366 | convolution fusion | flops 75497472 | bytes 622592 | tf_op jit(solution)/shard_map/Yy,mYZ,Zz->myz/dot_general | solution.py:35
  73.7 3.8 %collective-permute-done.5 = f32[2,256,128]{2,1,0:T(8,128)} collective-permute-done((f32[2,256,128]{2,1,0:T(8,128)}, f32[2,256,128]{2,1,0:T(8,128)}, u32[]{:S(2)}, u32[]{:S(2)}) %collective-permute-start.5) | collective-permute-done | bytes 262176 | tf_op jit(solution)/shard_map/ppermute | solution.py:53
  81.4 1.1 %constant_dynamic-update-slice_fusion.5 = f32[10,256,128]{2,1,0:T(8,128)S(1)} fusion(f32[10,256,128]{2,1,0:T(8,128)S(1)} %constant_dynamic-update-slice_fusion.6, f32[2,256,128]{2,1,0:T(8,128)} %collective-permute-done.9), kind=kLoop, calls=%fused_computation.345 | loop fusion | bytes 524288 | tf_op jit(solution)/shard_map/concatenate | solution.py:122
  82.7 3.2 %fusion.38 = f32[8,256,128]{2,1,0:T(8,128)S(1)} fusion(f32[8,256,128]{2,1,0:T(8,128)S(1)} %slice.551, f32[2,256,128]{2,1,0:T(8,128)} %collective-permute-done.9, f32[2,256,128]{2,1,0:T(8,128)} %collective-permute-done.8, f32[2,256,128]{2,1,0:T(8,128)} %collective-permute-done.7, f32[2,256,128]{2,1,0:T(8,128)} %collective-permute-done.6, ...), kind=kLoop, calls=%fused_computation.79 | loop fusion | flops 10747904 | bytes 7602184 | tf_op jit(solution)/shard_map/jit(_where)/select_n | solution.py:116
  86.0 1.2 %fusion.91 = f32[6,256,128]{2,1,0:T(8,128)S(1)} fusion(f32[6,256,128]{2,1,0:T(8,128)S(1)} %slice.552, f32[8,256,128]{2,1,0:T(8,128)S(1)} %fusion.38, pred[6]{0:T(512)(128)(4,1)S(1)} %slice_compare_fusion.1, f32[6,256,128]{2,1,0:T(8,128)S(1)} %slice.532, f32[10,256,128]{2,1,0:T(8,128)S(1)} %get-tuple-element.6, f32[10,256,128]{2,1,0:T(8,128)S(1)} %get-tuple-element.7), kind=kLoop, calls=%fused_computation.158 | loop fusion | flops 6881280 | bytes 6291462 | tf_op jit(solution)/shard_map/jit(_where)/select_n | solution.py:116
  87.3 1.0 copy-done.3
  89.3 1.1 %fusion.243 = (f32[256,128]{1,0:T(8,128)S(1)}, f32[2,256,128]{2,1,0:T(8,128)}) fusion(f32[2,256,128]{2,1,0:T(8,128)S(1)} %copy-done.15, f32[2,256,128]{2,1,0:T(8,128)S(1)} %slice.558, f32[10,256,128]{2,1,0:T(8,128)S(1)} %get-tuple-element.7, f32[2,256,128]{2,1,0:T(8,128)S(1)} %copy-done.17, f32[4,256,128]{2,1,0:T(8,128)S(1)} %fusion.139, ...), kind=kLoop, calls=%fused_computation.361 | loop fusion | flops 2326528 | bytes 2490368 | tf_op jit(solution)/shard_map/reduce_sum | solution.py:32
  91.1 1.3 %collective-permute-start.12 = (f32[1,128,64]{1,2,0:T(8,128)S(1)}, f32[1,128,64]{1,2,0:T(8,128)S(1)}, u32[]{:S(2)}, u32[]{:S(2)}) collective-permute-start(f32[1,128,64]{1,2,0:T(8,128)S(1)} %fusion.4), channel_id=1, source_target_pairs={{0,3},{2,5},{4,7},{6,9},{8,11},{10,13},{12,15},{14,17},{16,19},{18... | collective-permute-start | bytes 98312 | tf_op jit(solution)/shard_map/ppermute | solution.py:53
  92.4 1.3 %collective-permute-start.11 = (f32[1,128,64]{1,2,0:T(8,128)S(1)}, f32[1,128,64]{1,2,0:T(8,128)S(1)}, u32[]{:S(2)}, u32[]{:S(2)}) collective-permute-start(f32[1,128,64]{1,2,0:T(8,128)S(1)} %fusion.4), channel_id=1, source_target_pairs={{2,1},{4,3},{6,5},{8,7},{10,9},{12,11},{14,13},{16,15},{18,17},{20... | collective-permute-start | bytes 98312 | tf_op jit(solution)/shard_map/ppermute | solution.py:53
  93.7 1.3 %collective-permute-start.10 = (f32[1,128,64]{1,2,0:T(8,128)S(1)}, f32[1,128,64]{1,2,0:T(8,128)S(1)}, u32[]{:S(2)}, u32[]{:S(2)}) collective-permute-start(f32[1,128,64]{1,2,0:T(8,128)S(1)} %fusion.4), channel_id=1, source_target_pairs={{0,1},{2,3},{4,5},{6,7},{8,9},{10,11},{12,13},{14,15},{16,17},{18,... | collective-permute-start | bytes 98312 | tf_op jit(solution)/shard_map/ppermute | solution.py:53
  95.4 1.0 collective-permute-done.12
  96.4 4.3 %collective-permute-done.11 = f32[1,128,64]{1,2,0:T(8,128)S(1)} collective-permute-done((f32[1,128,64]{1,2,0:T(8,128)S(1)}, f32[1,128,64]{1,2,0:T(8,128)S(1)}, u32[]{:S(2)}, u32[]{:S(2)}) %collective-permute-start.11) | collective-permute-done | bytes 32800 | tf_op jit(solution)/shard_map/ppermute | solution.py:53
  (91 shorter events, 13.9 us)
Async XLA Ops:
  1.7 41.1 %copy-start.12 = (f32[1,2,256,128]{3,2,1,0:T(8,128)}, f32[1,2,256,128]{3,2,1,0:T(8,128)S(1)}, u32[]{:S(2)}) copy-start(f32[1,2,256,128]{3,2,1,0:T(8,128)S(1)} %get-tuple-element.13) | copy-start | bytes 786436
  2.8 23.9 %collective-permute-start.3 = (f32[2,2,256,128]{3,2,1,0:T(8,128)S(1)}, f32[2,2,256,128]{3,2,1,0:T(8,128)S(1)}, u32[]{:S(2)}, u32[]{:S(2)}) collective-permute-start(f32[2,2,256,128]{3,2,1,0:T(8,128)S(1)} %pad_maximum_fusion.11), channel_id=1, source_target_pairs={{4,0},{6,2},{8,4},{10,6},{12,8},{14,10},{16,12},{18,14},{20,16},{2... | collective-permute-start | bytes 1572872 | tf_op jit(solution)/shard_map/ppermute | solution.py:53
  5.0 24.7 %collective-permute-start.2 = (f32[2,2,256,128]{3,2,1,0:T(8,128)S(1)}, f32[2,2,256,128]{3,2,1,0:T(8,128)S(1)}, u32[]{:S(2)}, u32[]{:S(2)}) collective-permute-start(f32[2,2,256,128]{3,2,1,0:T(8,128)S(1)} %pad_maximum_fusion.11), channel_id=1, source_target_pairs={{2,0},{4,2},{6,4},{8,6},{10,8},{12,10},{14,12},{16,14},{18,16},{20... | collective-permute-start | bytes 1572872 | tf_op jit(solution)/shard_map/ppermute | solution.py:53
  7.1 24.4 %collective-permute-start.1 = (f32[2,2,256,128]{3,2,1,0:T(8,128)S(1)}, f32[2,2,256,128]{3,2,1,0:T(8,128)S(1)}, u32[]{:S(2)}, u32[]{:S(2)}) collective-permute-start(f32[2,2,256,128]{3,2,1,0:T(8,128)S(1)} %pad_maximum_fusion.11), channel_id=1, source_target_pairs={{0,2},{2,4},{4,6},{6,8},{8,10},{10,12},{12,14},{14,16},{16,18},{18... | collective-permute-start | bytes 1572872 | tf_op jit(solution)/shard_map/ppermute | solution.py:53
  12.1 29.9 %collective-permute-start = (f32[2,2,256,128]{3,2,1,0:T(8,128)S(1)}, f32[2,2,256,128]{3,2,1,0:T(8,128)S(1)}, u32[]{:S(2)}, u32[]{:S(2)}) collective-permute-start(f32[2,2,256,128]{3,2,1,0:T(8,128)S(1)} %pad_maximum_fusion.11), channel_id=1, source_target_pairs={{0,4},{2,6},{4,8},{6,10},{8,12},{10,14},{12,16},{14,18},{16,20},{1... | collective-permute-start | bytes 1572872 | tf_op jit(solution)/shard_map/ppermute | solution.py:53
  26.8 16.4 %copy-start.4 = (f32[2,2,256,128]{3,2,1,0:T(8,128)}, f32[2,2,256,128]{3,2,1,0:T(8,128)S(1)}, u32[]{:S(2)}) copy-start(f32[2,2,256,128]{3,2,1,0:T(8,128)S(1)} %collective-permute-done.3) | copy-start | bytes 1572868
  29.7 13.4 %copy-start.6 = (f32[2,2,256,128]{3,2,1,0:T(8,128)}, f32[2,2,256,128]{3,2,1,0:T(8,128)S(1)}, u32[]{:S(2)}) copy-start(f32[2,2,256,128]{3,2,1,0:T(8,128)S(1)} %collective-permute-done.2) | copy-start | bytes 1572868
  31.5 11.3 %copy-start.8 = (f32[2,2,256,128]{3,2,1,0:T(8,128)}, f32[2,2,256,128]{3,2,1,0:T(8,128)S(1)}, u32[]{:S(2)}) copy-start(f32[2,2,256,128]{3,2,1,0:T(8,128)S(1)} %collective-permute-done.1) | copy-start | bytes 1572868
  42.0 1.0 %copy-start.14 = (f32[1,2,256,128]{3,2,1,0:T(8,128)S(1)}, f32[1,2,256,128]{3,2,1,0:T(8,128)}, u32[]{:S(2)}) copy-start(f32[1,2,256,128]{3,2,1,0:T(8,128)} %param.13) | copy-start | bytes 786436
  42.1 2.8 %collective-permute-start.4 = (f32[8,256,128]{2,1,0:T(8,128)S(1)}, f32[8,256,128]{2,1,0:T(8,128)S(1)}, u32[]{:S(2)}, u32[]{:S(2)}) collective-permute-start(f32[8,256,128]{2,1,0:T(8,128)S(1)} %pad_maximum_fusion.8), channel_id=1, source_target_pairs={{0,1},{1,0},{2,3},{3,2},{4,5},{5,4},{6,7},{7,6},{8,9},{9,8},{10,11... | collective-permute-start | bytes 3145736 | tf_op jit(solution)/shard_map/ppermute | solution.py:97
  45.2 7.5 %copy-start.16 = (f32[2,256,128]{2,1,0:T(8,128)}, f32[2,256,128]{2,1,0:T(8,128)S(1)}, u32[]{:S(2)}) copy-start(f32[2,256,128]{2,1,0:T(8,128)S(1)} %slice.546) | copy-start | bytes 786436
  45.3 6.6 %copy-start.2 = (f32[4,256,128]{2,1,0:T(8,128)}, f32[4,256,128]{2,1,0:T(8,128)S(1)}, u32[]{:S(2)}) copy-start(f32[4,256,128]{2,1,0:T(8,128)S(1)} %slice.539) | copy-start | bytes 1572868
  45.3 1.2 %copy-start.13 = (f32[1,2,256,128]{3,2,1,0:T(8,128)S(1)}, f32[1,2,256,128]{3,2,1,0:T(8,128)}, u32[]{:S(2)}) copy-start(f32[1,2,256,128]{3,2,1,0:T(8,128)} %copy-done.12) | copy-start | bytes 786436
  45.3 1.6 %copy-start.5 = (f32[2,2,256,128]{3,2,1,0:T(8,128)S(1)}, f32[2,2,256,128]{3,2,1,0:T(8,128)}, u32[]{:S(2)}) copy-start(f32[2,2,256,128]{3,2,1,0:T(8,128)} %copy-done.4) | copy-start | bytes 1572868
  45.4 1.8 %copy-start.7 = (f32[2,2,256,128]{3,2,1,0:T(8,128)S(1)}, f32[2,2,256,128]{3,2,1,0:T(8,128)}, u32[]{:S(2)}) copy-start(f32[2,2,256,128]{3,2,1,0:T(8,128)} %copy-done.6) | copy-start | bytes 1572868
  45.4 2.0 %copy-start.9 = (f32[2,2,256,128]{3,2,1,0:T(8,128)S(1)}, f32[2,2,256,128]{3,2,1,0:T(8,128)}, u32[]{:S(2)}) copy-start(f32[2,2,256,128]{3,2,1,0:T(8,128)} %copy-done.8) | copy-start | bytes 1572868
  45.4 2.1 %copy-start.11 = (f32[2,2,256,128]{3,2,1,0:T(8,128)S(1)}, f32[2,2,256,128]{3,2,1,0:T(8,128)}, u32[]{:S(2)}) copy-start(f32[2,2,256,128]{3,2,1,0:T(8,128)} %copy-done.10) | copy-start | bytes 1572868
  45.5 4.2 %copy-start = (f32[8,256,128]{2,1,0:T(8,128)}, f32[8,256,128]{2,1,0:T(8,128)S(1)}, u32[]{:S(2)}) copy-start(f32[8,256,128]{2,1,0:T(8,128)S(1)} %slice.527) | copy-start | bytes 3145732
  54.1 27.4 %collective-permute-start.9 = (f32[2,256,128]{2,1,0:T(8,128)}, f32[2,256,128]{2,1,0:T(8,128)}, u32[]{:S(2)}, u32[]{:S(2)}) collective-permute-start(f32[2,256,128]{2,1,0:T(8,128)} %get-tuple-element.4), channel_id=1, source_target_pairs={{5,0},{4,1},{7,2},{6,3},{9,4},{8,5},{11,6},{10,7},{13,8},{12,9},{1... | collective-permute-start | bytes 786440 | tf_op jit(solution)/shard_map/ppermute | solution.py:53
  56.6 23.8 %collective-permute-start.8 = (f32[2,256,128]{2,1,0:T(8,128)}, f32[2,256,128]{2,1,0:T(8,128)}, u32[]{:S(2)}, u32[]{:S(2)}) collective-permute-start(f32[2,256,128]{2,1,0:T(8,128)} %get-tuple-element.4), channel_id=1, source_target_pairs={{3,0},{2,1},{5,2},{4,3},{7,4},{6,5},{9,6},{8,7},{11,8},{10,9},{13,... | collective-permute-start | bytes 786440 | tf_op jit(solution)/shard_map/ppermute | solution.py:53
  58.5 20.9 %collective-permute-start.7 = (f32[2,256,128]{2,1,0:T(8,128)}, f32[2,256,128]{2,1,0:T(8,128)}, u32[]{:S(2)}, u32[]{:S(2)}) collective-permute-start(f32[2,256,128]{2,1,0:T(8,128)} %get-tuple-element.4), channel_id=1, source_target_pairs={{1,0},{0,1},{3,2},{2,3},{5,4},{4,5},{7,6},{6,7},{9,8},{8,9},{11,10... | collective-permute-start | bytes 786440 | tf_op jit(solution)/shard_map/ppermute | solution.py:53
  58.7 19.7 %collective-permute-start.6 = (f32[2,256,128]{2,1,0:T(8,128)}, f32[2,256,128]{2,1,0:T(8,128)}, u32[]{:S(2)}, u32[]{:S(2)}) collective-permute-start(f32[2,256,128]{2,1,0:T(8,128)} %get-tuple-element.4), channel_id=1, source_target_pairs={{1,2},{0,3},{3,4},{2,5},{5,6},{4,7},{7,8},{6,9},{9,10},{8,11},{11,... | collective-permute-start | bytes 786440 | tf_op jit(solution)/shard_map/ppermute | solution.py:53
  64.2 13.3 %collective-permute-start.5 = (f32[2,256,128]{2,1,0:T(8,128)}, f32[2,256,128]{2,1,0:T(8,128)}, u32[]{:S(2)}, u32[]{:S(2)}) collective-permute-start(f32[2,256,128]{2,1,0:T(8,128)} %get-tuple-element.4), channel_id=1, source_target_pairs={{1,4},{0,5},{3,6},{2,7},{5,8},{4,9},{7,10},{6,11},{9,12},{8,13},{1... | collective-permute-start | bytes 786440 | tf_op jit(solution)/shard_map/ppermute | solution.py:53
  68.2 5.2 %copy-start.19 = (f32[256,128,1]{1,0,2:T(8,128)S(1)}, f32[256,128,1]{1,0,2:T(8,128)}, u32[]{:S(2)}) copy-start(f32[256,128,1]{1,0,2:T(8,128)} %constant.91) | copy-start | bytes 393220
  81.4 1.3 %copy-start.1 = (f32[8,256,128]{2,1,0:T(8,128)S(1)}, f32[8,256,128]{2,1,0:T(8,128)}, u32[]{:S(2)}) copy-start(f32[8,256,128]{2,1,0:T(8,128)} %copy-done) | copy-start | bytes 3145732
  87.3 1.0 %copy-start.3 = (f32[4,256,128]{2,1,0:T(8,128)S(1)}, f32[4,256,128]{2,1,0:T(8,128)}, u32[]{:S(2)}) copy-start(f32[4,256,128]{2,1,0:T(8,128)} %copy-done.2) | copy-start | bytes 1572868
  88.3 1.0 %copy-start.17 = (f32[2,256,128]{2,1,0:T(8,128)S(1)}, f32[2,256,128]{2,1,0:T(8,128)}, u32[]{:S(2)}) copy-start(f32[2,256,128]{2,1,0:T(8,128)} %copy-done.16) | copy-start | bytes 786436
  89.2 1.3 %copy-start.20 = (f32[128,64]{1,0:T(8,128)S(1)}, f32[128,64]{1,0:T(8,128)}, u32[]{:S(2)}) copy-start(f32[128,64]{1,0:T(8,128)} %constant.27.clone) | copy-start | bytes 98308
  89.3 1.4 %copy-start.18 = (f32[256,128]{1,0:T(8,128)S(1)}, f32[256,128]{1,0:T(8,128)}, u32[]{:S(2)}) copy-start(f32[256,128]{1,0:T(8,128)} %constant.26.clone) | copy-start | bytes 393220
  91.1 5.2 %collective-permute-start.12 = (f32[1,128,64]{1,2,0:T(8,128)S(1)}, f32[1,128,64]{1,2,0:T(8,128)S(1)}, u32[]{:S(2)}, u32[]{:S(2)}) collective-permute-start(f32[1,128,64]{1,2,0:T(8,128)S(1)} %fusion.4), channel_id=1, source_target_pairs={{0,3},{2,5},{4,7},{6,9},{8,11},{10,13},{12,15},{14,17},{16,19},{18... | collective-permute-start | bytes 98312 | tf_op jit(solution)/shard_map/ppermute | solution.py:53
  92.4 8.2 %collective-permute-start.11 = (f32[1,128,64]{1,2,0:T(8,128)S(1)}, f32[1,128,64]{1,2,0:T(8,128)S(1)}, u32[]{:S(2)}, u32[]{:S(2)}) collective-permute-start(f32[1,128,64]{1,2,0:T(8,128)S(1)} %fusion.4), channel_id=1, source_target_pairs={{2,1},{4,3},{6,5},{8,7},{10,9},{12,11},{14,13},{16,15},{18,17},{20... | collective-permute-start | bytes 98312 | tf_op jit(solution)/shard_map/ppermute | solution.py:53
  93.7 6.9 %collective-permute-start.10 = (f32[1,128,64]{1,2,0:T(8,128)S(1)}, f32[1,128,64]{1,2,0:T(8,128)S(1)}, u32[]{:S(2)}, u32[]{:S(2)}) collective-permute-start(f32[1,128,64]{1,2,0:T(8,128)S(1)} %fusion.4), channel_id=1, source_target_pairs={{0,1},{2,3},{4,5},{6,7},{8,9},{10,11},{12,13},{14,15},{16,17},{18,... | collective-permute-start | bytes 98312 | tf_op jit(solution)/shard_map/ppermute | solution.py:53
  (3 other events, 2.7 us)

commit v3 on v2

--- a/solution.py
+++ b/solution.py
@@ -6,6 +6,7 @@
 
 STEPS = 4
 COARSE_STEPS = STEPS // 4
+HALO = 2
 
 
 def advance(field, conduct, absorb, diffuse_scale, react_scale):
@@ -60,8 +61,11 @@
     me_s = lax.axis_index("space")
     me_t = lax.axis_index("tm")
     n = initial.shape[0]
-    halo = STEPS
+    halo = HALO
     reach = -(-halo // n)
+    distances = [d for d in range(-reach, reach + 1)]
+    lo = reach * n - halo
+    hi = reach * n + n + halo
 
     def space_pairs(d):
         return [(s + d, s) for s in range(space) if 0 <= s + d < space]
@@ -77,20 +81,16 @@
             if 0 <= s + d < space
         ]
 
+    def widen(block, axis):
+        got = gather_planes(block, "space", lambda d: None if d == 0 else space_pairs(d), distances)
+        wide = jnp.concatenate([got[d] for d in distances], axis=axis)
+        return lax.slice_in_dim(wide, lo, hi, axis=axis)
+
     start = guesses[0]
-    distances = [d for d in range(-reach, reach + 1)]
-    lo = reach * n - halo
-    hi = reach * n + n + halo
     split = times % 2 == 0
     if split:
         even = me_t % 2 == 0
-        local = jnp.stack([jnp.where(even, diffusivity, reaction), start])
-    else:
-        local = jnp.stack([diffusivity, reaction, start])
-    got = gather_planes(local, "space", lambda d: None if d == 0 else space_pairs(d), distances)
-    wide = jnp.concatenate([got[d] for d in distances], axis=1)
-    wide = wide[:, lo:hi]
-    if split:
+        wide = widen(jnp.stack([jnp.where(even, diffusivity, reaction), start]), 1)
         mine = wide[0]
         rim = jnp.concatenate([mine[:halo], mine[halo + n :]], axis=0)
         partner = [(t, t ^ 1) for t in range(times)]
@@ -101,19 +101,22 @@
         absorb = jnp.where(even, theirs, mine)
         field0 = wide[1]
     else:
+        wide = widen(jnp.stack([diffusivity, reaction, start]), 1)
         conduct, absorb, field0 = wide[0], wide[1], wide[2]
     plane_ids = me_s * n - halo + jnp.arange(n + 2 * halo)
-    inside = ((plane_ids >= 0) & (plane_ids < space * n)).astype(jnp.float32)[:, None, None]
+    inside = (plane_ids >= 0) & (plane_ids < space * n)
 
     def fine_prop(field):
         for number in range(STEPS):
-            cut = number
+            cut = number % halo
+            if number > 0 and cut == 0:
+                field = widen(field, 0)
             k = conduct[cut : conduct.shape[0] - cut]
             c = absorb[cut : absorb.shape[0] - cut]
             field = advance(field, k, c, 0.1, 0.1)
-            if number < STEPS - 1:
-                m = inside[cut + 1 : inside.shape[0] - cut - 1]
-                field = jnp.where(m > 0, field, 0.0)
+            if cut < halo - 1:
+                m = inside[cut + 1 : inside.shape[0] - cut - 1][:, None, None]
+                field = jnp.where(m, field, 0.0)
         return field
 
     advanced = fine_prop(field0)

time: 103 us -> 105 us (1.019)
  the two profiles are of different devices: /device:TPU:23 before, /device:TPU:1 now
where the time goes in v3:
time: 105 us; the launch traced here: 104 us
  waiting for transfers between devices  55.9 us (53%)
  starting transfers between devices  29.1 us (28%)
  other arithmetic  12.2 us (12%)
  matrix products  3.04 us (3%)
  local copies, waits for them, and re-layouts  2.33 us (2%)
  between operations  1.19 us (1%)
    ppermute x12, waiting for transfers between devices, gather_planes(): pieces[d] = lax.ppermute(block, axis_names, pairs_of(d))  54.5 us
    ppermute x12, starting transfers between devices, gather_planes(): pieces[d] = lax.ppermute(block, axis_names, pairs_of(d))  28.5 us
    select_n x4, other arithmetic, fine_prop(): field = jnp.where(m, field, 0.0)  4.59 us
    dot_general x6, matrix products, restrict(): jnp.einsum('Yy,mYZ,Zz->myz', rows, planes, cols, precision=lax.Precision....  2.36 us
  transfers between devices with their start and end apart: 13, of which 10 were waited for; matrix products, arithmetic and copies ran while one was open for 2% of the time, Pallas kernels for 0%

profile of v3, /device:TPU:1, one launch (start us, length us, event | category | flops | bytes accessed | tf_op | source)
XLA Modules:
  0.0 103.8 jit_solution(16494039470461354115)
XLA Ops:
  0.7 1.1 %broadcast_select_fusion.1 = (f32[2,256,128]{2,1,0:T(8,128)S(1)}, f32[1,2,256,128]{3,2,1,0:T(8,128)S(1)}) fusion(f32[2,256,128]{2,1,0:T(8,128)} %param.15, f32[2,256,128]{2,1,0:T(8,128)} %param.14, pred[]{:T(512)S(6)} %eq.8), kind=kLoop, calls=%fused_computation.265 | loop fusion | flops 131072 | bytes 1048577 | tf_op jit(solution)/shard_map/jit(_where)/select_n | solution.py:98
  1.8 1.3 %collective-permute-start.1 = (f32[2,2,256,128]{3,2,1,0:T(8,128)S(1)}, f32[2,2,256,128]{3,2,1,0:T(8,128)S(1)}, u32[]{:S(2)}, u32[]{:S(2)}) collective-permute-start(f32[2,2,256,128]{3,2,1,0:T(8,128)S(1)} %pad_maximum_fusion.14), channel_id=1, source_target_pairs={{2,0},{4,2},{6,4},{8,6},{10,8},{12,10},{14,12},{16,14},{18,16},{20... | collective-permute-start | bytes 1572872 | tf_op jit(solution)/shard_map/ppermute | solution.py:54
  3.1 4.6 %collective-permute-start = (f32[2,2,256,128]{3,2,1,0:T(8,128)S(1)}, f32[2,2,256,128]{3,2,1,0:T(8,128)S(1)}, u32[]{:S(2)}, u32[]{:S(2)}) collective-permute-start(f32[2,2,256,128]{3,2,1,0:T(8,128)S(1)} %pad_maximum_fusion.14), channel_id=1, source_target_pairs={{0,2},{2,4},{4,6},{6,8},{8,10},{10,12},{12,14},{14,16},{16,18},{18... | collective-permute-start | bytes 1572872 | tf_op jit(solution)/shard_map/ppermute | solution.py:54
  7.7 9.7 %collective-permute-done.1 = f32[2,2,256,128]{3,2,1,0:T(8,128)S(1)} collective-permute-done((f32[2,2,256,128]{3,2,1,0:T(8,128)S(1)}, f32[2,2,256,128]{3,2,1,0:T(8,128)S(1)}, u32[]{:S(2)}, u32[]{:S(2)}) %collective-permute-start.1) | collective-permute-done | bytes 524320 | tf_op jit(solution)/shard_map/ppermute | solution.py:54
  17.4 13.1 %collective-permute-done = f32[2,2,256,128]{3,2,1,0:T(8,128)S(1)} collective-permute-done((f32[2,2,256,128]{3,2,1,0:T(8,128)S(1)}, f32[2,2,256,128]{3,2,1,0:T(8,128)S(1)}, u32[]{:S(2)}, u32[]{:S(2)}) %collective-permute-start) | collective-permute-done | bytes 524320 | tf_op jit(solution)/shard_map/ppermute | solution.py:54
  30.6 0.6 collective-permute-start.2
  31.2 1.4 %collective-permute-done.2 = f32[4,256,128]{2,1,0:T(8,128)S(1)} collective-permute-done((f32[4,256,128]{2,1,0:T(8,128)S(1)}, f32[4,256,128]{2,1,0:T(8,128)S(1)}, u32[]{:S(2)}, u32[]{:S(2)}) %collective-permute-start.2) | collective-permute-done | bytes 524320 | tf_op jit(solution)/shard_map/ppermute | solution.py:97
  32.9 1.1 %pad_maximum_fusion.3 = (f32[6,256,128]{2,1,0:T(8,128)}, f32[6,256,128]{2,1,0:T(8,128)S(1)}) fusion(f32[2,256,128]{2,1,0:T(8,128)S(1)} %get-tuple-element.27, f32[2,256,128]{2,1,0:T(8,128)S(1)} %get-tuple-element.28, f32[2,256,128]{2,1,0:T(8,128)S(1)} %get-tuple-element.26, f32[1,6,256,128]{3,2,1,0:T(8,128)S(1)} %get-tuple-element.23, pred[]{:T(512)S(6)} %eq.8), kind=kLoop, calls=%fused_computation.49 | loop fusion | flops 589824 | bytes 3145729 | tf_op jit(solution)/shard_map/concatenate | solution.py:99
  34.1 0.9 copy-done.4
  35.3 1.6 %fusion.20 = (f32[4,256,128]{2,1,0:T(8,128)S(1)}, f32[4,256,128]{2,1,0:T(8,128)S(1)}, f32[4,256,128]{2,1,0:T(8,128)S(1)}, f32[4,256,128]{2,1,0:T(8,128)S(1)}, f3...) fusion(f32[4,256,128]{2,1,0:T(8,128)S(1)} %maximum_bitcast_fusion, ...), kind=kLoop, calls=%fused_computation.71 | loop fusion | flops 5111808 | bytes 8388612 | tf_op jit(solution)/shard_map/jit(_where)/select_n | solution.py:119
  36.9 1.6 %fusion.109 = (f32[2,256,128]{2,1,0:T(8,128)}, f32[2,256,128]{2,1,0:T(8,128)}, f32[2,256,128]{2,1,0:T(8,128)}, f32[2,256,128]{2,1,0:T(8,128)}, f32[2,256,128]{2,...) fusion(f32[2,256,128]{2,1,0:T(8,128)S(1)} %slice.449, f32[4,256,128]{2,1,0:T(8,128)S(1)} %get-tuple-element.15, ...), kind=kLoop, calls=%fused_computation.182 | loop fusion | flops 2228224 | bytes 3932160 | tf_op jit(solution)/shard_map/sub | solution.py:23
  38.5 1.3 %collective-permute-start.4 = (f32[2,256,128]{2,1,0:T(8,128)}, f32[2,256,128]{2,1,0:T(8,128)}, u32[]{:S(2)}, u32[]{:S(2)}) collective-permute-start(f32[2,256,128]{2,1,0:T(8,128)} %get-tuple-element.8), channel_id=1, source_target_pairs={{2,0},{4,2},{6,4},{8,6},{10,8},{12,10},{14,12},{16,14},{18,16},{20... | collective-permute-start | bytes 786440 | tf_op jit(solution)/shard_map/ppermute | solution.py:54
  39.8 5.4 %collective-permute-start.3 = (f32[2,256,128]{2,1,0:T(8,128)}, f32[2,256,128]{2,1,0:T(8,128)}, u32[]{:S(2)}, u32[]{:S(2)}) collective-permute-start(f32[2,256,128]{2,1,0:T(8,128)} %get-tuple-element.8), channel_id=1, source_target_pairs={{0,2},{2,4},{4,6},{6,8},{8,10},{10,12},{12,14},{14,16},{16,18},{18... | collective-permute-start | bytes 786440 | tf_op jit(solution)/shard_map/ppermute | solution.py:54
  45.3 4.0 %collective-permute-done.4 = f32[2,256,128]{2,1,0:T(8,128)} collective-permute-done((f32[2,256,128]{2,1,0:T(8,128)}, f32[2,256,128]{2,1,0:T(8,128)}, u32[]{:S(2)}, u32[]{:S(2)}) %collective-permute-start.4) | collective-permute-done | bytes 262176 | tf_op jit(solution)/shard_map/ppermute | solution.py:54
  49.3 5.2 %collective-permute-done.3 = f32[2,256,128]{2,1,0:T(8,128)} collective-permute-done((f32[2,256,128]{2,1,0:T(8,128)}, f32[2,256,128]{2,1,0:T(8,128)}, u32[]{:S(2)}, u32[]{:S(2)}) %collective-permute-start.3) | collective-permute-done | bytes 262176 | tf_op jit(solution)/shard_map/ppermute | solution.py:54
  54.5 1.1 %pad_maximum_fusion.8 = f32[4,256,128]{2,1,0:T(8,128)S(1)} fusion(f32[2,256,128]{2,1,0:T(8,128)} %collective-permute-done.4, f32[2,256,128]{2,1,0:T(8,128)} %get-tuple-element.8, f32[2,256,128]{2,1,0:T(8,128)} %collective-permute-done.3), kind=kLoop, calls=%fused_computation.130 | loop fusion | flops 262144 | bytes 1310720 | tf_op jit(solution)/shard_map/concatenate | solution.py:86
  55.7 1.9 %fusion.36 = f32[4,256,128]{2,1,0:T(8,128)S(1)} fusion(f32[4,256,128]{2,1,0:T(8,128)S(1)} %pad_maximum_fusion.8, f32[4,256,128]{2,1,0:T(8,128)S(1)} %copy-done, f32[4,256,128]{2,1,0:T(8,128)S(1)} %get-tuple-element.20, f32[4,256,128]{2,1,0:T(8,128)S(1)} %get-tuple-element.19, f32[4,256,128]{2,1,0:T(8,128)S(1)} %get-tuple-element.18, ...), kind=kLoop, calls=%fused_computation.87 | loop fusion | flops 3276800 | bytes 5505028 | tf_op jit(solution)/shard_map/jit(_where)/select_n | solution.py:119
  58.0 1.4 %collective-permute-start.7 = (f32[2,256,128]{2,1,0:T(8,128)S(1)}, f32[2,256,128]{2,1,0:T(8,128)S(1)}, u32[]{:S(2)}, u32[]{:S(2)}) collective-permute-start(f32[2,256,128]{2,1,0:T(8,128)S(1)} %get-tuple-element.6), channel_id=1, source_target_pairs={{3,0},{2,1},{5,2},{4,3},{7,4},{6,5},{9,6},{8,7},{11,8},{10,9},{13,... | collective-permute-start | bytes 786440 | tf_op jit(solution)/shard_map/ppermute | solution.py:54
  60.0 4.7 %collective-permute-start.5 = (f32[2,256,128]{2,1,0:T(8,128)S(1)}, f32[2,256,128]{2,1,0:T(8,128)S(1)}, u32[]{:S(2)}, u32[]{:S(2)}) collective-permute-start(f32[2,256,128]{2,1,0:T(8,128)S(1)} %get-tuple-element.6), channel_id=1, source_target_pairs={{1,2},{0,3},{3,4},{2,5},{5,6},{4,7},{7,8},{6,9},{9,10},{8,11},{11,... | collective-permute-start | bytes 786440 | tf_op jit(solution)/shard_map/ppermute | solution.py:54
  64.9 0.7 copy-done.21
  66.1 3.2 %collective-permute-done.7 = f32[2,256,128]{2,1,0:T(8,128)S(1)} collective-permute-done((f32[2,256,128]{2,1,0:T(8,128)S(1)}, f32[2,256,128]{2,1,0:T(8,128)S(1)}, u32[]{:S(2)}, u32[]{:S(2)}) %collective-permute-start.7) | collective-permute-done | bytes 262176 | tf_op jit(solution)/shard_map/ppermute | solution.py:54
  69.3 6.3 %collective-permute-done.5 = f32[2,256,128]{2,1,0:T(8,128)S(1)} collective-permute-done((f32[2,256,128]{2,1,0:T(8,128)S(1)}, f32[2,256,128]{2,1,0:T(8,128)S(1)}, u32[]{:S(2)}, u32[]{:S(2)}) %collective-permute-start.5) | collective-permute-done | bytes 262176 | tf_op jit(solution)/shard_map/ppermute | solution.py:54
  76.5 1.3 %collective-permute-start.9 = (f32[2,256,128]{2,1,0:T(8,128)S(1)}, f32[2,256,128]{2,1,0:T(8,128)S(1)}, u32[]{:S(2)}, u32[]{:S(2)}) collective-permute-start(f32[2,256,128]{2,1,0:T(8,128)S(1)} %fusion.139), channel_id=1, source_target_pairs={{2,0},{4,2},{6,4},{8,6},{10,8},{12,10},{14,12},{16,14},{18,16},{20... | collective-permute-start | bytes 786440 | tf_op jit(solution)/shard_map/ppermute | solution.py:54
  77.8 4.7 %collective-permute-start.8 = (f32[2,256,128]{2,1,0:T(8,128)S(1)}, f32[2,256,128]{2,1,0:T(8,128)S(1)}, u32[]{:S(2)}, u32[]{:S(2)}) collective-permute-start(f32[2,256,128]{2,1,0:T(8,128)S(1)} %fusion.139), channel_id=1, source_target_pairs={{0,2},{2,4},{4,6},{6,8},{8,10},{10,12},{12,14},{14,16},{16,18},{18... | collective-permute-start | bytes 786440 | tf_op jit(solution)/shard_map/ppermute | solution.py:54
  83.5 3.5 %collective-permute-done.9 = f32[2,256,128]{2,1,0:T(8,128)S(1)} collective-permute-done((f32[2,256,128]{2,1,0:T(8,128)S(1)}, f32[2,256,128]{2,1,0:T(8,128)S(1)}, u32[]{:S(2)}, u32[]{:S(2)}) %collective-permute-start.9) | collective-permute-done | bytes 262176 | tf_op jit(solution)/shard_map/ppermute | solution.py:54
  87.0 5.6 %collective-permute-done.8 = f32[2,256,128]{2,1,0:T(8,128)S(1)} collective-permute-done((f32[2,256,128]{2,1,0:T(8,128)S(1)}, f32[2,256,128]{2,1,0:T(8,128)S(1)}, u32[]{:S(2)}, u32[]{:S(2)}) %collective-permute-start.8) | collective-permute-done | bytes 262176 | tf_op jit(solution)/shard_map/ppermute | solution.py:54
  93.3 1.0 fusion.216
  94.9 0.7 collective-permute-start.12
  95.6 1.3 %collective-permute-start.11 = (f32[1,128,64]{1,2,0:T(8,128)S(1)}, f32[1,128,64]{1,2,0:T(8,128)S(1)}, u32[]{:S(2)}, u32[]{:S(2)}) collective-permute-start(f32[1,128,64]{1,2,0:T(8,128)S(1)} %fusion.2), channel_id=1, source_target_pairs={{2,1},{4,3},{6,5},{8,7},{10,9},{12,11},{14,13},{16,15},{18,17},{20... | collective-permute-start | bytes 98312 | tf_op jit(solution)/shard_map/ppermute | solution.py:54
  96.9 1.3 %collective-permute-start.10 = (f32[1,128,64]{1,2,0:T(8,128)S(1)}, f32[1,128,64]{1,2,0:T(8,128)S(1)}, u32[]{:S(2)}, u32[]{:S(2)}) collective-permute-start(f32[1,128,64]{1,2,0:T(8,128)S(1)} %fusion.2), channel_id=1, source_target_pairs={{0,1},{2,3},{4,5},{6,7},{8,9},{10,11},{12,13},{14,15},{16,17},{18,... | collective-permute-start | bytes 98312 | tf_op jit(solution)/shard_map/ppermute | solution.py:54
  98.6 3.8 %collective-permute-done.11 = f32[1,128,64]{1,2,0:T(8,128)S(1)} collective-permute-done((f32[1,128,64]{1,2,0:T(8,128)S(1)}, f32[1,128,64]{1,2,0:T(8,128)S(1)}, u32[]{:S(2)}, u32[]{:S(2)}) %collective-permute-start.11) | collective-permute-done | bytes 32800 | tf_op jit(solution)/shard_map/ppermute | solution.py:54
  103.1 0.7 add_bitcast_fusion
  (79 shorter events, 6.5 us)
Async XLA Ops:
  0.6 1.1 %copy-start.9 = (f32[1,2,256,128]{3,2,1,0:T(8,128)S(1)}, f32[1,2,256,128]{3,2,1,0:T(8,128)}, u32[]{:S(2)}) copy-start(f32[1,2,256,128]{3,2,1,0:T(8,128)} %param.13) | copy-start | bytes 786436
  1.8 30.9 %copy-start.3 = (f32[1,2,256,128]{3,2,1,0:T(8,128)}, f32[1,2,256,128]{3,2,1,0:T(8,128)S(1)}, u32[]{:S(2)}) copy-start(f32[1,2,256,128]{3,2,1,0:T(8,128)S(1)} %get-tuple-element.29) | copy-start | bytes 786436
  1.8 15.6 %collective-permute-start.1 = (f32[2,2,256,128]{3,2,1,0:T(8,128)S(1)}, f32[2,2,256,128]{3,2,1,0:T(8,128)S(1)}, u32[]{:S(2)}, u32[]{:S(2)}) collective-permute-start(f32[2,2,256,128]{3,2,1,0:T(8,128)S(1)} %pad_maximum_fusion.14), channel_id=1, source_target_pairs={{2,0},{4,2},{6,4},{8,6},{10,8},{12,10},{14,12},{16,14},{18,16},{20... | collective-permute-start | bytes 1572872 | tf_op jit(solution)/shard_map/ppermute | solution.py:54
  3.1 27.4 %collective-permute-start = (f32[2,2,256,128]{3,2,1,0:T(8,128)S(1)}, f32[2,2,256,128]{3,2,1,0:T(8,128)S(1)}, u32[]{:S(2)}, u32[]{:S(2)}) collective-permute-start(f32[2,2,256,128]{3,2,1,0:T(8,128)S(1)} %pad_maximum_fusion.14), channel_id=1, source_target_pairs={{0,2},{2,4},{4,6},{6,8},{8,10},{10,12},{12,14},{14,16},{16,18},{18... | collective-permute-start | bytes 1572872 | tf_op jit(solution)/shard_map/ppermute | solution.py:54
  17.4 15.3 %copy-start.5 = (f32[2,2,256,128]{3,2,1,0:T(8,128)}, f32[2,2,256,128]{3,2,1,0:T(8,128)S(1)}, u32[]{:S(2)}) copy-start(f32[2,2,256,128]{3,2,1,0:T(8,128)S(1)} %collective-permute-done.1) | copy-start | bytes 1572868
  30.5 2.2 %copy-start.7 = (f32[2,2,256,128]{3,2,1,0:T(8,128)}, f32[2,2,256,128]{3,2,1,0:T(8,128)S(1)}, u32[]{:S(2)}) copy-start(f32[2,2,256,128]{3,2,1,0:T(8,128)S(1)} %collective-permute-done) | copy-start | bytes 1572868
  30.6 2.1 %collective-permute-start.2 = (f32[4,256,128]{2,1,0:T(8,128)S(1)}, f32[4,256,128]{2,1,0:T(8,128)S(1)}, u32[]{:S(2)}, u32[]{:S(2)}) collective-permute-start(f32[4,256,128]{2,1,0:T(8,128)S(1)} %pad_maximum_fusion.15), channel_id=1, source_target_pairs={{0,1},{1,0},{2,3},{3,2},{4,5},{5,4},{6,7},{7,6},{8,9},{9,8},{10,11... | collective-permute-start | bytes 1572872 | tf_op jit(solution)/shard_map/ppermute | solution.py:97
  32.8 1.1 %copy-start.1 = (f32[1,6,256,128]{3,2,1,0:T(8,128)}, f32[1,6,256,128]{3,2,1,0:T(8,128)S(1)}, u32[]{:S(2)}) copy-start(f32[1,6,256,128]{3,2,1,0:T(8,128)S(1)} %get-tuple-element.23) | copy-start | bytes 2359300
  34.0 1.3 %copy-start.8 = (f32[2,2,256,128]{3,2,1,0:T(8,128)S(1)}, f32[2,2,256,128]{3,2,1,0:T(8,128)}, u32[]{:S(2)}) copy-start(f32[2,2,256,128]{3,2,1,0:T(8,128)} %copy-done.7) | copy-start | bytes 1572868
  34.0 1.3 %copy-start.10 = (f32[1,2,256,128]{3,2,1,0:T(8,128)S(1)}, f32[1,2,256,128]{3,2,1,0:T(8,128)}, u32[]{:S(2)}) copy-start(f32[1,2,256,128]{3,2,1,0:T(8,128)} %param.13) | copy-start | bytes 786436
  38.5 10.8 %collective-permute-start.4 = (f32[2,256,128]{2,1,0:T(8,128)}, f32[2,256,128]{2,1,0:T(8,128)}, u32[]{:S(2)}, u32[]{:S(2)}) collective-permute-start(f32[2,256,128]{2,1,0:T(8,128)} %get-tuple-element.8), channel_id=1, source_target_pairs={{2,0},{4,2},{6,4},{8,6},{10,8},{12,10},{14,12},{16,14},{18,16},{20... | collective-permute-start | bytes 786440 | tf_op jit(solution)/shard_map/ppermute | solution.py:54
  39.8 14.7 %collective-permute-start.3 = (f32[2,256,128]{2,1,0:T(8,128)}, f32[2,256,128]{2,1,0:T(8,128)}, u32[]{:S(2)}, u32[]{:S(2)}) collective-permute-start(f32[2,256,128]{2,1,0:T(8,128)} %get-tuple-element.8), channel_id=1, source_target_pairs={{0,2},{2,4},{4,6},{6,8},{8,10},{10,12},{12,14},{14,16},{16,18},{18... | collective-permute-start | bytes 786440 | tf_op jit(solution)/shard_map/ppermute | solution.py:54
  45.3 10.4 %copy-start = (f32[4,256,128]{2,1,0:T(8,128)S(1)}, f32[4,256,128]{2,1,0:T(8,128)}, u32[]{:S(2)}) copy-start(f32[4,256,128]{2,1,0:T(8,128)} %get-tuple-element.21) | copy-start | bytes 1572868
  55.6 2.0 %copy-start.11 = (f32[2,256,128]{2,1,0:T(8,128)S(1)}, f32[2,256,128]{2,1,0:T(8,128)}, u32[]{:S(2)}) copy-start(f32[2,256,128]{2,1,0:T(8,128)} %get-tuple-element.9) | copy-start | bytes 786436
  55.6 2.0 %copy-start.12 = (f32[2,256,128]{2,1,0:T(8,128)S(1)}, f32[2,256,128]{2,1,0:T(8,128)}, u32[]{:S(2)}) copy-start(f32[2,256,128]{2,1,0:T(8,128)} %get-tuple-element.10) | copy-start | bytes 786436
  55.7 2.0 %copy-start.13 = (f32[2,256,128]{2,1,0:T(8,128)S(1)}, f32[2,256,128]{2,1,0:T(8,128)}, u32[]{:S(2)}) copy-start(f32[2,256,128]{2,1,0:T(8,128)} %get-tuple-element.11) | copy-start | bytes 786436
  55.7 2.0 %copy-start.14 = (f32[2,256,128]{2,1,0:T(8,128)S(1)}, f32[2,256,128]{2,1,0:T(8,128)}, u32[]{:S(2)}) copy-start(f32[2,256,128]{2,1,0:T(8,128)} %get-tuple-element.12) | copy-start | bytes 786436
  55.7 2.0 %copy-start.15 = (f32[2,256,128]{2,1,0:T(8,128)S(1)}, f32[2,256,128]{2,1,0:T(8,128)}, u32[]{:S(2)}) copy-start(f32[2,256,128]{2,1,0:T(8,128)} %get-tuple-element.13) | copy-start | bytes 786436
  55.7 2.0 %copy-start.16 = (f32[2,256,128]{2,1,0:T(8,128)S(1)}, f32[2,256,128]{2,1,0:T(8,128)}, u32[]{:S(2)}) copy-start(f32[2,256,128]{2,1,0:T(8,128)} %get-tuple-element.14) | copy-start | bytes 786436
  55.7 2.0 %copy-start.20 = (f32[2,256,128]{2,1,0:T(8,128)S(1)}, f32[2,256,128]{2,1,0:T(8,128)}, u32[]{:S(2)}) copy-start(f32[2,256,128]{2,1,0:T(8,128)} %param.12) | copy-start | bytes 786436
  57.7 7.0 %copy-start.2 = (f32[1,6,256,128]{3,2,1,0:T(8,128)S(1)}, f32[1,6,256,128]{3,2,1,0:T(8,128)}, u32[]{:S(2)}) copy-start(f32[1,6,256,128]{3,2,1,0:T(8,128)} %copy-done.1) | copy-start | bytes 2359300
  57.7 7.0 %copy-start.17 = (f32[6,256,128]{2,1,0:T(8,128)S(1)}, f32[6,256,128]{2,1,0:T(8,128)}, u32[]{:S(2)}) copy-start(f32[6,256,128]{2,1,0:T(8,128)} %get-tuple-element.24) | copy-start | bytes 2359300
  58.0 11.3 %collective-permute-start.7 = (f32[2,256,128]{2,1,0:T(8,128)S(1)}, f32[2,256,128]{2,1,0:T(8,128)S(1)}, u32[]{:S(2)}, u32[]{:S(2)}) collective-permute-start(f32[2,256,128]{2,1,0:T(8,128)S(1)} %get-tuple-element.6), channel_id=1, source_target_pairs={{3,0},{2,1},{5,2},{4,3},{7,4},{6,5},{9,6},{8,7},{11,8},{10,9},{13,... | collective-permute-start | bytes 786440 | tf_op jit(solution)/shard_map/ppermute | solution.py:54
  59.5 9.8 %collective-permute-start.6 = (f32[2,256,128]{2,1,0:T(8,128)S(1)}, f32[2,256,128]{2,1,0:T(8,128)S(1)}, u32[]{:S(2)}, u32[]{:S(2)}) collective-permute-start(f32[2,256,128]{2,1,0:T(8,128)S(1)} %get-tuple-element.6), channel_id=1, source_target_pairs={{1,0},{0,1},{3,2},{2,3},{5,4},{4,5},{7,6},{6,7},{9,8},{8,9},{11,10... | collective-permute-start | bytes 786440 | tf_op jit(solution)/shard_map/ppermute | solution.py:54
  60.0 15.6 %collective-permute-start.5 = (f32[2,256,128]{2,1,0:T(8,128)S(1)}, f32[2,256,128]{2,1,0:T(8,128)S(1)}, u32[]{:S(2)}, u32[]{:S(2)}) collective-permute-start(f32[2,256,128]{2,1,0:T(8,128)S(1)} %get-tuple-element.6), channel_id=1, source_target_pairs={{1,2},{0,3},{3,4},{2,5},{5,6},{4,7},{7,8},{6,9},{9,10},{8,11},{11,... | collective-permute-start | bytes 786440 | tf_op jit(solution)/shard_map/ppermute | solution.py:54
  76.3 6.3 %copy-start.19 = (f32[256,128,1]{1,0,2:T(8,128)S(1)}, f32[256,128,1]{1,0,2:T(8,128)}, u32[]{:S(2)}) copy-start(f32[256,128,1]{1,0,2:T(8,128)} %constant.79) | copy-start | bytes 393220
  76.5 10.5 %collective-permute-start.9 = (f32[2,256,128]{2,1,0:T(8,128)S(1)}, f32[2,256,128]{2,1,0:T(8,128)S(1)}, u32[]{:S(2)}, u32[]{:S(2)}) collective-permute-start(f32[2,256,128]{2,1,0:T(8,128)S(1)} %fusion.139), channel_id=1, source_target_pairs={{2,0},{4,2},{6,4},{8,6},{10,8},{12,10},{14,12},{16,14},{18,16},{20... | collective-permute-start | bytes 786440 | tf_op jit(solution)/shard_map/ppermute | solution.py:54
  77.8 14.8 %collective-permute-start.8 = (f32[2,256,128]{2,1,0:T(8,128)S(1)}, f32[2,256,128]{2,1,0:T(8,128)S(1)}, u32[]{:S(2)}, u32[]{:S(2)}) collective-permute-start(f32[2,256,128]{2,1,0:T(8,128)S(1)} %fusion.139), channel_id=1, source_target_pairs={{0,2},{2,4},{4,6},{6,8},{8,10},{10,12},{12,14},{14,16},{16,18},{18... | collective-permute-start | bytes 786440 | tf_op jit(solution)/shard_map/ppermute | solution.py:54
  93.2 1.3 %copy-start.18 = (f32[256,128]{1,0:T(8,128)S(1)}, f32[256,128]{1,0:T(8,128)}, u32[]{:S(2)}) copy-start(f32[256,128]{1,0:T(8,128)} %constant.48.clone) | copy-start | bytes 393220
  94.9 3.6 %collective-permute-start.12 = (f32[1,128,64]{1,2,0:T(8,128)S(1)}, f32[1,128,64]{1,2,0:T(8,128)S(1)}, u32[]{:S(2)}, u32[]{:S(2)}) collective-permute-start(f32[1,128,64]{1,2,0:T(8,128)S(1)} %fusion.2), channel_id=1, source_target_pairs={{0,3},{2,5},{4,7},{6,9},{8,11},{10,13},{12,15},{14,17},{16,19},{18... | collective-permute-start | bytes 98312 | tf_op jit(solution)/shard_map/ppermute | solution.py:54
  95.6 6.8 %collective-permute-start.11 = (f32[1,128,64]{1,2,0:T(8,128)S(1)}, f32[1,128,64]{1,2,0:T(8,128)S(1)}, u32[]{:S(2)}, u32[]{:S(2)}) collective-permute-start(f32[1,128,64]{1,2,0:T(8,128)S(1)} %fusion.2), channel_id=1, source_target_pairs={{2,1},{4,3},{6,5},{8,7},{10,9},{12,11},{14,13},{16,15},{18,17},{20... | collective-permute-start | bytes 98312 | tf_op jit(solution)/shard_map/ppermute | solution.py:54
  96.9 5.5 %collective-permute-start.10 = (f32[1,128,64]{1,2,0:T(8,128)S(1)}, f32[1,128,64]{1,2,0:T(8,128)S(1)}, u32[]{:S(2)}, u32[]{:S(2)}) collective-permute-start(f32[1,128,64]{1,2,0:T(8,128)S(1)} %fusion.2), channel_id=1, source_target_pairs={{0,1},{2,3},{4,5},{6,7},{8,9},{10,11},{12,13},{14,15},{16,17},{18,... | collective-permute-start | bytes 98312 | tf_op jit(solution)/shard_map/ppermute | solution.py:54
  (4 other events, 4.0 us)

commit v4 on v3

--- a/solution.py
+++ b/solution.py
@@ -2,11 +2,14 @@
 import jax.numpy as jnp
 import numpy as np
 from jax import lax
+from jax.experimental import pallas as pl
+from jax.experimental.pallas import tpu as pltpu
 from jax.sharding import PartitionSpec as P
+import functools
 
 STEPS = 4
 COARSE_STEPS = STEPS // 4
-HALO = 2
+HALO = 4
 
 
 def advance(field, conduct, absorb, diffuse_scale, react_scale):
@@ -21,6 +24,70 @@
     inflow = inflow + 0.5 * (conduct_pad[:, 1:-1, 2:] + middle) * (padded[:, 1:-1, 2:] - center)
     inflow = inflow + 0.5 * (conduct_pad[:, 1:-1, :-2] + middle) * (padded[:, 1:-1, :-2] - center)
     return center + diffuse_scale * inflow - react_scale * absorb[1:-1] * center
+
+
+def stencil_plane(vm, v0, vp, km, k0, kp, c0):
+    rows, cols = v0.shape
+    row = lax.broadcasted_iota(jnp.int32, v0.shape, 0)
+    col = lax.broadcasted_iota(jnp.int32, v0.shape, 1)
+    top = row < rows - 1
+    bottom = row > 0
+    right = col < cols - 1
+    left = col > 0
+    v_yp = jnp.where(top, pltpu.roll(v0, rows - 1, 0), 0.0)
+    k_yp = jnp.where(top, pltpu.roll(k0, rows - 1, 0), 0.0)
+    v_ym = jnp.where(bottom, pltpu.roll(v0, 1, 0), 0.0)
+    k_ym = jnp.where(bottom, pltpu.roll(k0, 1, 0), 0.0)
+    v_zp = jnp.where(right, pltpu.roll(v0, cols - 1, 1), 0.0)
+    k_zp = jnp.where(right, pltpu.roll(k0, cols - 1, 1), 0.0)
+    v_zm = jnp.where(left, pltpu.roll(v0, 1, 1), 0.0)
+    k_zm = jnp.where(left, pltpu.roll(k0, 1, 1), 0.0)
+    inflow = 0.5 * (kp + k0) * (vp - v0)
+    inflow = inflow + 0.5 * (km + k0) * (vm - v0)
+    inflow = inflow + 0.5 * (k_yp + k0) * (v_yp - v0)
+    inflow = inflow + 0.5 * (k_ym + k0) * (v_ym - v0)
+    inflow = inflow + 0.5 * (k_zp + k0) * (v_zp - v0)
+    inflow = inflow + 0.5 * (k_zm + k0) * (v_zm - v0)
+    return v0 + 0.1 * inflow - 0.1 * c0 * v0
+
+
+def fine_kernel(steps, meta_ref, f_ref, k_ref, c_ref, o_ref, buf_a, buf_b):
+    planes = f_ref.shape[0]
+    first = meta_ref[0]
+    total = meta_ref[1]
+    for step in range(steps):
+        src = f_ref if step == 0 else (buf_a if step % 2 == 1 else buf_b)
+        last = step == steps - 1
+        dst = o_ref if last else (buf_a if step % 2 == 0 else buf_b)
+        lo = step + 1
+        hi = planes - step - 1
+
+        def body(p, carry, src=src, dst=dst, last=last, lo=lo):
+            new = stencil_plane(src[p - 1], src[p], src[p + 1], k_ref[p - 1], k_ref[p], k_ref[p + 1], c_ref[p])
+            if last:
+                dst[p - lo] = new
+            else:
+                g = first + p
+                ok = (g >= 0) & (g < total)
+                dst[p] = jnp.where(ok, new, 0.0)
+            return carry
+
+        lax.fori_loop(lo, hi, body, 0)
+
+
+def fine_prop_kernel(field, conduct, absorb, first, total, steps):
+    planes, rows, cols = field.shape
+    out_planes = planes - 2 * steps
+    meta = jnp.stack([first, total]).astype(jnp.int32)
+    cells = rows * cols * sum(planes - 2 * (s + 1) for s in range(steps))
+    return pl.pallas_call(
+        functools.partial(fine_kernel, steps),
+        out_shape=jax.ShapeDtypeStruct((out_planes, rows, cols), jnp.float32),
+        in_specs=[pl.BlockSpec(memory_space=pltpu.SMEM)] + [pl.BlockSpec(memory_space=pltpu.VMEM)] * 3,
+        out_specs=pl.BlockSpec(memory_space=pltpu.VMEM),
+        scratch_shapes=[pltpu.VMEM((planes, rows, cols), jnp.float32)] * 2,
+        cost_estimate=pl.CostEstimate(flops=45 * cells, transcendentals=0, bytes_accessed=4 * rows * cols * (3 * planes + out_planes)),
+    )(meta, field, conduct, absorb)
 
 
 def pair_matrix(fine):
@@ -107,6 +174,8 @@
     inside = (plane_ids >= 0) & (plane_ids < space * n)
 
     def fine_prop(field):
+        if halo == STEPS:
+            return fine_prop_kernel(field, conduct, absorb, me_s * n - halo, jnp.int32(space * n), STEPS)
         for number in range(STEPS):
             cut = number % halo
             if number > 0 and cut == 0:

time: 105 us -> 112 us (1.067)
  the two profiles are of different devices: /device:TPU:1 before, /device:TPU:5 now
where the time goes in v4:
time: 112 us; the launch traced here: 111 us
  waiting for transfers between devices  47.7 us (43%)
  starting transfers between devices  29.9 us (27%)
  Pallas kernels  15.6 us (14%)
  other arithmetic  9.48 us (8%)
  local copies, waits for them, and re-layouts  4.28 us (4%)
  matrix products  3.05 us (3%)
    ppermute x12, waiting for transfers between devices, gather_planes(): pieces[d] = lax.ppermute(block, axis_names, pairs_of(d))  47.5 us
    ppermute x12, starting transfers between devices, gather_planes(): pieces[d] = lax.ppermute(block, axis_names, pairs_of(d))  28 us
    pallas_call x2, Pallas kernels, fine_prop_kernel(): pl.pallas_call(functools.partial(fine_kernel, steps), out_shape=jax.Shape...  15.6 us
    unnamed x29, local copies, waits for them, and re-layouts  2.88 us
    dot_general x6, matrix products, restrict(): jnp.einsum('Yy,mYZ,Zz->myz', rows, planes, cols, precision=lax.Precision....  2.37 us
  transfers between devices with their start and end apart: 13, of which 9 were waited for; matrix products, arithmetic and copies ran while one was open for 4% of the time, Pallas kernels for 0%

profile of v4, /device:TPU:5, one launch (start us, length us, event | category | flops | bytes accessed | tf_op | source)
XLA Modules:
  0.0 111.0 jit_solution(14311309971028359446)
XLA Ops:
  0.6 1.8 %broadcast_select_fusion.1 = (f32[2,256,128]{2,1,0:T(8,128)}, f32[1,2,256,128]{3,2,1,0:T(8,128)S(1)}) fusion(f32[2,256,128]{2,1,0:T(8,128)} %param.15, f32[2,256,128]{2,1,0:T(8,128)} %param.14, pred[]{:T(512)S(6)} %eq.8), kind=kLoop, calls=%fused_computation.20 | loop fusion | flops 131072 | bytes 1048577 | tf_op jit(solution)/shard_map/jit(_where)/select_n | solution.py:165
  2.4 1.0 pad_maximum_fusion.4
  3.4 3.1 %collective-permute-start.2 = (f32[2,2,256,128]{3,2,1,0:T(8,128)S(1)}, f32[2,2,256,128]{3,2,1,0:T(8,128)S(1)}, u32[]{:S(2)}, u32[]{:S(2)}) collective-permute-start(f32[2,2,256,128]{3,2,1,0:T(8,128)S(1)} %pad_maximum_fusion.4), channel_id=1, source_target_pairs={{2,0},{4,2},{6,4},{8,6},{10,8},{12,10},{14,12},{16,14},{18,16},{20... | collective-permute-start | bytes 1572872 | tf_op jit(solution)/shard_map/ppermute | solution.py:121
  6.5 1.9 %collective-permute-start.3 = (f32[2,2,256,128]{3,2,1,0:T(8,128)S(1)}, f32[2,2,256,128]{3,2,1,0:T(8,128)S(1)}, u32[]{:S(2)}, u32[]{:S(2)}) collective-permute-start(f32[2,2,256,128]{3,2,1,0:T(8,128)S(1)} %pad_maximum_fusion.4), channel_id=1, source_target_pairs={{4,0},{6,2},{8,4},{10,6},{12,8},{14,10},{16,12},{18,14},{20,16},{2... | collective-permute-start | bytes 1572872 | tf_op jit(solution)/shard_map/ppermute | solution.py:121
  8.4 4.3 %collective-permute-start = (f32[2,2,256,128]{3,2,1,0:T(8,128)S(1)}, f32[2,2,256,128]{3,2,1,0:T(8,128)S(1)}, u32[]{:S(2)}, u32[]{:S(2)}) collective-permute-start(f32[2,2,256,128]{3,2,1,0:T(8,128)S(1)} %pad_maximum_fusion.4), channel_id=1, source_target_pairs={{0,4},{2,6},{4,8},{6,10},{8,12},{10,14},{12,16},{14,18},{16,20},{1... | collective-permute-start | bytes 1572872 | tf_op jit(solution)/shard_map/ppermute | solution.py:121
  12.7 2.2 %collective-permute-start.1 = (f32[2,2,256,128]{3,2,1,0:T(8,128)S(1)}, f32[2,2,256,128]{3,2,1,0:T(8,128)S(1)}, u32[]{:S(2)}, u32[]{:S(2)}) collective-permute-start(f32[2,2,256,128]{3,2,1,0:T(8,128)S(1)} %pad_maximum_fusion.4), channel_id=1, source_target_pairs={{0,2},{2,4},{4,6},{6,8},{8,10},{10,12},{12,14},{14,16},{16,18},{18... | collective-permute-start | bytes 1572872 | tf_op jit(solution)/shard_map/ppermute | solution.py:121
  14.9 3.2 %collective-permute-done.2 = f32[2,2,256,128]{3,2,1,0:T(8,128)S(1)} collective-permute-done((f32[2,2,256,128]{3,2,1,0:T(8,128)S(1)}, f32[2,2,256,128]{3,2,1,0:T(8,128)S(1)}, u32[]{:S(2)}, u32[]{:S(2)}) %collective-permute-start.2) | collective-permute-done | bytes 524320 | tf_op jit(solution)/shard_map/ppermute | solution.py:121
  18.1 22.2 %collective-permute-done.3 = f32[2,2,256,128]{3,2,1,0:T(8,128)S(1)} collective-permute-done((f32[2,2,256,128]{3,2,1,0:T(8,128)S(1)}, f32[2,2,256,128]{3,2,1,0:T(8,128)S(1)}, u32[]{:S(2)}, u32[]{:S(2)}) %collective-permute-start.3) | collective-permute-done | bytes 524320 | tf_op jit(solution)/shard_map/ppermute | solution.py:121
  40.3 4.9 %collective-permute-done = f32[2,2,256,128]{3,2,1,0:T(8,128)S(1)} collective-permute-done((f32[2,2,256,128]{3,2,1,0:T(8,128)S(1)}, f32[2,2,256,128]{3,2,1,0:T(8,128)S(1)}, u32[]{:S(2)}, u32[]{:S(2)}) %collective-permute-start) | collective-permute-done | bytes 524320 | tf_op jit(solution)/shard_map/ppermute | solution.py:121
  45.3 1.1 pad_maximum_fusion.1
  46.3 1.9 %collective-permute-start.4 = (f32[8,256,128]{2,1,0:T(8,128)}, f32[8,256,128]{2,1,0:T(8,128)S(1)}, u32[]{:S(2)}, u32[]{:S(2)}) collective-permute-start(f32[8,256,128]{2,1,0:T(8,128)} %pad_maximum_fusion.1), channel_id=1, source_target_pairs={{0,1},{1,0},{2,3},{3,2},{4,5},{5,4},{6,7},{7,6},{8,9},{9,8},{10,11... | collective-permute-start | bytes 3145736 | tf_op jit(solution)/shard_map/ppermute | solution.py:164
  49.3 1.2 %slice_bitcast_fusion.1.f_ref = f32[10,256,128]{2,1,0:T(8,128)} fusion(f32[2,10,256,128]{3,2,1,0:T(8,128)S(1)} %constant_dynamic-update-slice_fusion), kind=kLoop, calls=%fused_computation.1 | loop fusion | bytes 2621440 | tf_op jit(solution)/shard_map/squeeze | solution.py:169
  51.4 1.7 %fusion = (f32[10,256,128]{2,1,0:T(8,128)}, f32[10,256,128]{2,1,0:T(8,128)}) fusion(f32[2,10,256,128]{3,2,1,0:T(8,128)S(1)} %constant_dynamic-update-slice_fusion, f32[4,256,128]{2,1,0:T(8,128)S(1)} %get-tuple-element.5, f32[2,256,128]{2,1,0:T(8,128)S(1)} %copy-done.5, f32[4,256,128]{2,1,0:T(8,128)S(1)} %get-tuple-element.4, pred[]{:T(512)S(6)} %eq.8), kind=kLoop, calls=%fused_computation.3 | loop fusion | flops 1310720 | bytes 5242881 | tf_op jit(solution)/shard_map/jit(_where)/select_n | solution.py:168
  53.1 7.8 %shard_map.131 = f32[2,256,128]{2,1,0:T(8,128)} custom-call(s32[2]{0:T(128)} %pad_add_fusion.meta_ref, f32[10,256,128]{2,1,0:T(8,128)} %slice_bitcast_fusion.1.f_ref, f32[10,256,128]{2,1,0:T(8,128)} %get-tuple-element.3.k_ref, f32[10,256,128]{2,1,0:T(8,128)} %get-tuple-element.2.c_ref), custom_call_target="tpu_custom_call" | custom-call | flops 29491200 | bytes 4194304 | tf_op jit(solution)/shard_map/pallas_call | solution.py:83
  60.9 0.7 broadcast_select_fusion
  61.7 4.2 %collective-permute-start.5 = (f32[2,256,128]{2,1,0:T(8,128)}, f32[2,256,128]{2,1,0:T(8,128)S(1)}, u32[]{:S(2)}, u32[]{:S(2)}) collective-permute-start(f32[2,256,128]{2,1,0:T(8,128)} %broadcast_select_fusion), channel_id=1, source_target_pairs={{1,4},{0,5},{3,6},{2,7},{5,8},{4,9},{7,10},{6,11},{9,12},{8,13},{1... | collective-permute-start | bytes 786440 | tf_op jit(solution)/shard_map/ppermute | solution.py:121
  65.9 1.9 %collective-permute-start.6 = (f32[2,256,128]{2,1,0:T(8,128)}, f32[2,256,128]{2,1,0:T(8,128)S(1)}, u32[]{:S(2)}, u32[]{:S(2)}) collective-permute-start(f32[2,256,128]{2,1,0:T(8,128)} %broadcast_select_fusion), channel_id=1, source_target_pairs={{1,2},{0,3},{3,4},{2,5},{5,6},{4,7},{7,8},{6,9},{9,10},{8,11},{11,... | collective-permute-start | bytes 786440 | tf_op jit(solution)/shard_map/ppermute | solution.py:121
  67.9 4.5 %collective-permute-start.8 = (f32[2,256,128]{2,1,0:T(8,128)}, f32[2,256,128]{2,1,0:T(8,128)S(1)}, u32[]{:S(2)}, u32[]{:S(2)}) collective-permute-start(f32[2,256,128]{2,1,0:T(8,128)} %broadcast_select_fusion), channel_id=1, source_target_pairs={{3,0},{2,1},{5,2},{4,3},{7,4},{6,5},{9,6},{8,7},{11,8},{10,9},{13,... | collective-permute-start | bytes 786440 | tf_op jit(solution)/shard_map/ppermute | solution.py:121
  72.5 1.9 %collective-permute-start.9 = (f32[2,256,128]{2,1,0:T(8,128)}, f32[2,256,128]{2,1,0:T(8,128)S(1)}, u32[]{:S(2)}, u32[]{:S(2)}) collective-permute-start(f32[2,256,128]{2,1,0:T(8,128)} %broadcast_select_fusion), channel_id=1, source_target_pairs={{5,0},{4,1},{7,2},{6,3},{9,4},{8,5},{11,6},{10,7},{13,8},{12,9},{1... | collective-permute-start | bytes 786440 | tf_op jit(solution)/shard_map/ppermute | solution.py:121
  74.7 0.7 copy-done.8
  76.8 1.2 %collective-permute-done.5 = f32[2,256,128]{2,1,0:T(8,128)S(1)} collective-permute-done((f32[2,256,128]{2,1,0:T(8,128)}, f32[2,256,128]{2,1,0:T(8,128)S(1)}, u32[]{:S(2)}, u32[]{:S(2)}) %collective-permute-start.5) | collective-permute-done | bytes 262176 | tf_op jit(solution)/shard_map/ppermute | solution.py:121
  78.1 2.3 %collective-permute-done.8 = f32[2,256,128]{2,1,0:T(8,128)S(1)} collective-permute-done((f32[2,256,128]{2,1,0:T(8,128)}, f32[2,256,128]{2,1,0:T(8,128)S(1)}, u32[]{:S(2)}, u32[]{:S(2)}) %collective-permute-start.8) | collective-permute-done | bytes 262176 | tf_op jit(solution)/shard_map/ppermute | solution.py:121
  80.5 9.2 %collective-permute-done.9 = f32[2,256,128]{2,1,0:T(8,128)S(1)} collective-permute-done((f32[2,256,128]{2,1,0:T(8,128)}, f32[2,256,128]{2,1,0:T(8,128)S(1)}, u32[]{:S(2)}, u32[]{:S(2)}) %collective-permute-start.9) | collective-permute-done | bytes 262176 | tf_op jit(solution)/shard_map/ppermute | solution.py:121
  89.7 1.1 copy-done.3
  90.7 7.8 %shard_map.132 = f32[2,256,128]{2,1,0:T(8,128)} custom-call(s32[2]{0:T(128)} %pad_add_fusion.meta_ref, f32[10,256,128]{2,1,0:T(8,128)} %copy-done.3, f32[10,256,128]{2,1,0:T(8,128)} %get-tuple-element.3.k_ref, f32[10,256,128]{2,1,0:T(8,128)} %get-tuple-element.2.c_ref), custom_call_target="tpu_custom_call" | custom-call | flops 29491200 | bytes 4194304 | tf_op jit(solution)/shard_map/pallas_call | solution.py:83
  98.5 1.7 %subtract_bitcast_fusion = (f32[1,2,256,128]{3,2,1,0:T(8,128)}, f32[256,128]{1,0:T(8,128)S(1)}) fusion(f32[2,256,128]{2,1,0:T(8,128)} %shard_map.132, f32[2,256,128]{2,1,0:T(8,128)S(1)} %copy-done.2), kind=kLoop, calls=%fused_computation.29 | loop fusion | flops 98304 | bytes 917504 | tf_op jit(solution)/shard_map/reshape | solution.py:100
  100.9 1.3 %collective-permute-start.10 = (f32[1,128,64]{1,2,0:T(8,128)S(1)}, f32[1,128,64]{1,2,0:T(8,128)S(1)}, u32[]{:S(2)}, u32[]{:S(2)}) collective-permute-start(f32[1,128,64]{1,2,0:T(8,128)S(1)} %fusion.4), channel_id=1, source_target_pairs={{0,1},{2,3},{4,5},{6,7},{8,9},{10,11},{12,13},{14,15},{16,17},{18,... | collective-permute-start | bytes 98312 | tf_op jit(solution)/shard_map/ppermute | solution.py:121
  102.2 1.3 %collective-permute-start.11 = (f32[1,128,64]{1,2,0:T(8,128)S(1)}, f32[1,128,64]{1,2,0:T(8,128)S(1)}, u32[]{:S(2)}, u32[]{:S(2)}) collective-permute-start(f32[1,128,64]{1,2,0:T(8,128)S(1)} %fusion.4), channel_id=1, source_target_pairs={{2,1},{4,3},{6,5},{8,7},{10,9},{12,11},{14,13},{16,15},{18,17},{20... | collective-permute-start | bytes 98312 | tf_op jit(solution)/shard_map/ppermute | solution.py:121
  103.5 1.3 %collective-permute-start.12 = (f32[1,128,64]{1,2,0:T(8,128)S(1)}, f32[1,128,64]{1,2,0:T(8,128)S(1)}, u32[]{:S(2)}, u32[]{:S(2)}) collective-permute-start(f32[1,128,64]{1,2,0:T(8,128)S(1)} %fusion.4), channel_id=1, source_target_pairs={{0,3},{2,5},{4,7},{6,9},{8,11},{10,13},{12,15},{14,17},{16,19},{18... | collective-permute-start | bytes 98312 | tf_op jit(solution)/shard_map/ppermute | solution.py:121
  105.2 2.3 %collective-permute-done.11 = f32[1,128,64]{1,2,0:T(8,128)S(1)} collective-permute-done((f32[1,128,64]{1,2,0:T(8,128)S(1)}, f32[1,128,64]{1,2,0:T(8,128)S(1)}, u32[]{:S(2)}, u32[]{:S(2)}) %collective-permute-start.11) | collective-permute-done | bytes 32800 | tf_op jit(solution)/shard_map/ppermute | solution.py:121
  107.4 2.2 %collective-permute-done.12 = f32[1,128,64]{1,2,0:T(8,128)S(1)} collective-permute-done((f32[1,128,64]{1,2,0:T(8,128)S(1)}, f32[1,128,64]{1,2,0:T(8,128)S(1)}, u32[]{:S(2)}, u32[]{:S(2)}) %collective-permute-start.12) | collective-permute-done | bytes 32800 | tf_op jit(solution)/shard_map/ppermute | solution.py:121
  110.3 0.7 add_bitcast_fusion
  (53 shorter events, 5.5 us)
Async XLA Ops:
  3.4 14.7 %collective-permute-start.2 = (f32[2,2,256,128]{3,2,1,0:T(8,128)S(1)}, f32[2,2,256,128]{3,2,1,0:T(8,128)S(1)}, u32[]{:S(2)}, u32[]{:S(2)}) collective-permute-start(f32[2,2,256,128]{3,2,1,0:T(8,128)S(1)} %pad_maximum_fusion.4), channel_id=1, source_target_pairs={{2,0},{4,2},{6,4},{8,6},{10,8},{12,10},{14,12},{16,14},{18,16},{20... | collective-permute-start | bytes 1572872 | tf_op jit(solution)/shard_map/ppermute | solution.py:121
  6.5 33.8 %collective-permute-start.3 = (f32[2,2,256,128]{3,2,1,0:T(8,128)S(1)}, f32[2,2,256,128]{3,2,1,0:T(8,128)S(1)}, u32[]{:S(2)}, u32[]{:S(2)}) collective-permute-start(f32[2,2,256,128]{3,2,1,0:T(8,128)S(1)} %pad_maximum_fusion.4), channel_id=1, source_target_pairs={{4,0},{6,2},{8,4},{10,6},{12,8},{14,10},{16,12},{18,14},{20,16},{2... | collective-permute-start | bytes 1572872 | tf_op jit(solution)/shard_map/ppermute | solution.py:121
  8.4 36.8 %collective-permute-start = (f32[2,2,256,128]{3,2,1,0:T(8,128)S(1)}, f32[2,2,256,128]{3,2,1,0:T(8,128)S(1)}, u32[]{:S(2)}, u32[]{:S(2)}) collective-permute-start(f32[2,2,256,128]{3,2,1,0:T(8,128)S(1)} %pad_maximum_fusion.4), channel_id=1, source_target_pairs={{0,4},{2,6},{4,8},{6,10},{8,12},{10,14},{12,16},{14,18},{16,20},{1... | collective-permute-start | bytes 1572872 | tf_op jit(solution)/shard_map/ppermute | solution.py:121
  12.7 32.6 %collective-permute-start.1 = (f32[2,2,256,128]{3,2,1,0:T(8,128)S(1)}, f32[2,2,256,128]{3,2,1,0:T(8,128)S(1)}, u32[]{:S(2)}, u32[]{:S(2)}) collective-permute-start(f32[2,2,256,128]{3,2,1,0:T(8,128)S(1)} %pad_maximum_fusion.4), channel_id=1, source_target_pairs={{0,2},{2,4},{4,6},{6,8},{8,10},{10,12},{12,14},{14,16},{16,18},{18... | collective-permute-start | bytes 1572872 | tf_op jit(solution)/shard_map/ppermute | solution.py:121
  46.3 4.4 %collective-permute-start.4 = (f32[8,256,128]{2,1,0:T(8,128)}, f32[8,256,128]{2,1,0:T(8,128)S(1)}, u32[]{:S(2)}, u32[]{:S(2)}) collective-permute-start(f32[8,256,128]{2,1,0:T(8,128)} %pad_maximum_fusion.1), channel_id=1, source_target_pairs={{0,1},{1,0},{2,3},{3,2},{4,5},{5,4},{6,7},{7,6},{8,9},{9,8},{10,11... | collective-permute-start | bytes 3145736 | tf_op jit(solution)/shard_map/ppermute | solution.py:164
  48.2 0.9 copy-start.4
  50.4 0.9 copy-start.5
  53.1 7.9 %copy-start.10 = (f32[2,256,128]{2,1,0:T(8,128)S(1)}, f32[2,256,128]{2,1,0:T(8,128)}, u32[]{:S(2)}) copy-start(f32[2,256,128]{2,1,0:T(8,128)} %param.12) | copy-start | bytes 786436
  53.1 21.3 %copy-start.1 = (f32[10,256,128]{2,1,0:T(8,128)S(1)}, f32[10,256,128]{2,1,0:T(8,128)}, u32[]{:S(2)}) copy-start(f32[10,256,128]{2,1,0:T(8,128)} %get-tuple-element.3.k_ref) | copy-start | bytes 3932164
  60.9 13.5 %copy-start = (f32[10,256,128]{2,1,0:T(8,128)S(1)}, f32[10,256,128]{2,1,0:T(8,128)}, u32[]{:S(2)}) copy-start(f32[10,256,128]{2,1,0:T(8,128)} %get-tuple-element.2.c_ref) | copy-start | bytes 3932164
  61.7 16.3 %collective-permute-start.5 = (f32[2,256,128]{2,1,0:T(8,128)}, f32[2,256,128]{2,1,0:T(8,128)S(1)}, u32[]{:S(2)}, u32[]{:S(2)}) collective-permute-start(f32[2,256,128]{2,1,0:T(8,128)} %broadcast_select_fusion), channel_id=1, source_target_pairs={{1,4},{0,5},{3,6},{2,7},{5,8},{4,9},{7,10},{6,11},{9,12},{8,13},{1... | collective-permute-start | bytes 786440 | tf_op jit(solution)/shard_map/ppermute | solution.py:121
  65.9 12.1 %collective-permute-start.6 = (f32[2,256,128]{2,1,0:T(8,128)}, f32[2,256,128]{2,1,0:T(8,128)S(1)}, u32[]{:S(2)}, u32[]{:S(2)}) collective-permute-start(f32[2,256,128]{2,1,0:T(8,128)} %broadcast_select_fusion), channel_id=1, source_target_pairs={{1,2},{0,3},{3,4},{2,5},{5,6},{4,7},{7,8},{6,9},{9,10},{8,11},{11,... | collective-permute-start | bytes 786440 | tf_op jit(solution)/shard_map/ppermute | solution.py:121
  67.8 10.2 %collective-permute-start.7 = (f32[2,256,128]{2,1,0:T(8,128)}, f32[2,256,128]{2,1,0:T(8,128)S(1)}, u32[]{:S(2)}, u32[]{:S(2)}) collective-permute-start(f32[2,256,128]{2,1,0:T(8,128)} %broadcast_select_fusion), channel_id=1, source_target_pairs={{1,0},{0,1},{3,2},{2,3},{5,4},{4,5},{7,6},{6,7},{9,8},{8,9},{11,10... | collective-permute-start | bytes 786440 | tf_op jit(solution)/shard_map/ppermute | solution.py:121
  67.9 12.5 %collective-permute-start.8 = (f32[2,256,128]{2,1,0:T(8,128)}, f32[2,256,128]{2,1,0:T(8,128)S(1)}, u32[]{:S(2)}, u32[]{:S(2)}) collective-permute-start(f32[2,256,128]{2,1,0:T(8,128)} %broadcast_select_fusion), channel_id=1, source_target_pairs={{3,0},{2,1},{5,2},{4,3},{7,4},{6,5},{9,6},{8,7},{11,8},{10,9},{13,... | collective-permute-start | bytes 786440 | tf_op jit(solution)/shard_map/ppermute | solution.py:121
  72.5 17.2 %collective-permute-start.9 = (f32[2,256,128]{2,1,0:T(8,128)}, f32[2,256,128]{2,1,0:T(8,128)S(1)}, u32[]{:S(2)}, u32[]{:S(2)}) collective-permute-start(f32[2,256,128]{2,1,0:T(8,128)} %broadcast_select_fusion), channel_id=1, source_target_pairs={{5,0},{4,1},{7,2},{6,3},{9,4},{8,5},{11,6},{10,7},{13,8},{12,9},{1... | collective-permute-start | bytes 786440 | tf_op jit(solution)/shard_map/ppermute | solution.py:121
  74.5 0.8 copy-start.8
  74.6 1.9 %copy-start.7 = (f32[256,128,1]{1,0,2:T(8,128)S(1)}, f32[256,128,1]{1,0,2:T(8,128)}, u32[]{:S(2)}) copy-start(f32[256,128,1]{1,0,2:T(8,128)} %constant.55) | copy-start | bytes 393220
  89.7 1.1 copy-start.3
  90.7 7.8 %copy-start.2 = (f32[2,256,128]{2,1,0:T(8,128)S(1)}, f32[2,256,128]{2,1,0:T(8,128)}, u32[]{:S(2)}) copy-start(f32[2,256,128]{2,1,0:T(8,128)} %shard_map.131) | copy-start | bytes 786436
  90.7 9.5 %copy-start.9 = (f32[128,64]{1,0:T(8,128)S(1)}, f32[128,64]{1,0:T(8,128)}, u32[]{:S(2)}) copy-start(f32[128,64]{1,0:T(8,128)} %constant.45.clone) | copy-start | bytes 98308
  98.5 2.0 %copy-start.6 = (f32[256,128]{1,0:T(8,128)S(1)}, f32[256,128]{1,0:T(8,128)}, u32[]{:S(2)}) copy-start(f32[256,128]{1,0:T(8,128)} %constant.44.clone) | copy-start | bytes 393220
  100.9 4.2 %collective-permute-start.10 = (f32[1,128,64]{1,2,0:T(8,128)S(1)}, f32[1,128,64]{1,2,0:T(8,128)S(1)}, u32[]{:S(2)}, u32[]{:S(2)}) collective-permute-start(f32[1,128,64]{1,2,0:T(8,128)S(1)} %fusion.4), channel_id=1, source_target_pairs={{0,1},{2,3},{4,5},{6,7},{8,9},{10,11},{12,13},{14,15},{16,17},{18,... | collective-permute-start | bytes 98312 | tf_op jit(solution)/shard_map/ppermute | solution.py:121
  102.2 5.2 %collective-permute-start.11 = (f32[1,128,64]{1,2,0:T(8,128)S(1)}, f32[1,128,64]{1,2,0:T(8,128)S(1)}, u32[]{:S(2)}, u32[]{:S(2)}) collective-permute-start(f32[1,128,64]{1,2,0:T(8,128)S(1)} %fusion.4), channel_id=1, source_target_pairs={{2,1},{4,3},{6,5},{8,7},{10,9},{12,11},{14,13},{16,15},{18,17},{20... | collective-permute-start | bytes 98312 | tf_op jit(solution)/shard_map/ppermute | solution.py:121
  103.5 6.1 %collective-permute-start.12 = (f32[1,128,64]{1,2,0:T(8,128)S(1)}, f32[1,128,64]{1,2,0:T(8,128)S(1)}, u32[]{:S(2)}, u32[]{:S(2)}) collective-permute-start(f32[1,128,64]{1,2,0:T(8,128)S(1)} %fusion.4), channel_id=1, source_target_pairs={{0,3},{2,5},{4,7},{6,9},{8,11},{10,13},{12,15},{14,17},{16,19},{18... | collective-permute-start | bytes 98312 | tf_op jit(solution)/shard_map/ppermute | solution.py:121

commit v5 on v3

--- a/solution.py
+++ b/solution.py
@@ -2,11 +2,16 @@
 import jax.numpy as jnp
 import numpy as np
 from jax import lax
+from jax.experimental import pallas as pl
+from jax.experimental.pallas import tpu as pltpu
 from jax.sharding import PartitionSpec as P
+import functools
 
 STEPS = 4
 COARSE_STEPS = STEPS // 4
-HALO = 2
+HALO = 4
+EDGE = 8
+CHUNK = 32
 
 
 def advance(field, conduct, absorb, diffuse_scale, react_scale):
@@ -21,6 +26,107 @@
     inflow = inflow + 0.5 * (conduct_pad[:, 1:-1, 2:] + middle) * (padded[:, 1:-1, 2:] - center)
     inflow = inflow + 0.5 * (conduct_pad[:, 1:-1, :-2] + middle) * (padded[:, 1:-1, :-2] - center)
     return center + diffuse_scale * inflow - react_scale * absorb[1:-1] * center
+
+
+def stencil_chunk(vblk, kblk, vm, vp, km, kp, c0):
+    size = vblk.shape[0]
+    v0 = vblk[EDGE:size - EDGE]
+    k0 = kblk[EDGE:size - EDGE]
+    v_yp = pltpu.roll(vblk, size - 1, 0)[EDGE:size - EDGE]
+    k_yp = pltpu.roll(kblk, size - 1, 0)[EDGE:size - EDGE]
+    v_ym = pltpu.roll(vblk, 1, 0)[EDGE:size - EDGE]
+    k_ym = pltpu.roll(kblk, 1, 0)[EDGE:size - EDGE]
+    cols = v0.shape[1]
+    col = lax.broadcasted_iota(jnp.int32, v0.shape, 1)
+    right = col < cols - 1
+    left = col > 0
+    v_zp = jnp.where(right, pltpu.roll(v0, cols - 1, 1), 0.0)
+    k_zp = jnp.where(right, pltpu.roll(k0, cols - 1, 1), 0.0)
+    v_zm = jnp.where(left, pltpu.roll(v0, 1, 1), 0.0)
+    k_zm = jnp.where(left, pltpu.roll(k0, 1, 1), 0.0)
+    inflow = 0.5 * (kp + k0) * (vp - v0)
+    inflow = inflow + 0.5 * (km + k0) * (vm - v0)
+    inflow = inflow + 0.5 * (k_yp + k0) * (v_yp - v0)
+    inflow = inflow + 0.5 * (k_ym + k0) * (v_ym - v0)
+    inflow = inflow + 0.5 * (k_zp + k0) * (v_zp - v0)
+    inflow = inflow + 0.5 * (k_zm + k0) * (v_zm - v0)
+    return v0 + 0.1 * inflow - 0.1 * c0 * v0
+
+
+def fine_kernel(steps, opening, meta_ref, f_ref, mine_ref, theirs_ref, extra_ref, *rest):
+    if opening:
+        out_ref, send_ref, buf0, buf1, kbuf, cbuf = rest
+    else:
+        out_ref, buf0, buf1, kbuf, cbuf = rest
+    planes, rows, cols = f_ref.shape
+    first = meta_ref[0]
+    total = meta_ref[1]
+    even = meta_ref[2] == 1
+    last_interval = meta_ref[3] == 1
+    zeros = jnp.zeros((EDGE, cols), jnp.float32)
+
+    def fill(p, carry):
+        for buf in (buf0, buf1, kbuf):
+            buf[p, pl.ds(0, EDGE), :] = zeros
+            buf[p, pl.ds(EDGE + rows, EDGE), :] = zeros
+        buf0[p, pl.ds(EDGE, rows), :] = f_ref[p]
+        a = mine_ref[p]
+        b = theirs_ref[p]
+        kbuf[p, pl.ds(EDGE, rows), :] = jnp.where(even, a, b)
+        cbuf[p] = jnp.where(even, b, a)
+        return carry
+
+    lax.fori_loop(0, planes, fill, 0)
+    for step in range(steps):
+        src = buf0 if step % 2 == 0 else buf1
+        dst = buf1 if step % 2 == 0 else buf0
+        final = step == steps - 1
+        lo = step + 1
+        hi = planes - step - 1
+
+        def body(p, carry, src=src, dst=dst, final=final, lo=lo):
+            g = first + p
+            ok = (g >= 0) & (g < total)
+            for r in range(0, rows, CHUNK):
+                base = EDGE + r
+                vblk = src[p, pl.ds(base - EDGE, CHUNK + 2 * EDGE), :]
+                kblk = kbuf[p, pl.ds(base - EDGE, CHUNK + 2 * EDGE), :]
+                vm = src[p - 1, pl.ds(base, CHUNK), :]
+                vp = src[p + 1, pl.ds(base, CHUNK), :]
+                km = kbuf[p - 1, pl.ds(base, CHUNK), :]
+                kp = kbuf[p + 1, pl.ds(base, CHUNK), :]
+                c0 = cbuf[p, pl.ds(r, CHUNK), :]
+                new = stencil_chunk(vblk, kblk, vm, vp, km, kp, c0)
+                if final:
+                    q = p - lo
+                    ex = extra_ref[q, pl.ds(r, CHUNK), :]
+                    if opening:
+                        out_ref[q, pl.ds(r, CHUNK), :] = new
+                        send_ref[q, pl.ds(r, CHUNK), :] = jnp.where(last_interval, ex, new)
+                    else:
+                        out_ref[q, pl.ds(r, CHUNK), :] = new - ex
+                else:
+                    dst[p, pl.ds(base, CHUNK), :] = jnp.where(ok, new, 0.0)
+            return carry
+
+        lax.fori_loop(lo, hi, body, 0)
+
+
+def fine_prop_kernel(field, mine, theirs, extra, meta, steps, opening):
+    planes, rows, cols = field.shape
+    out_planes = planes - 2 * steps
+    cells = rows * cols * sum(planes - 2 * (s + 1) for s in range(steps))
+    part = jax.ShapeDtypeStruct((out_planes, rows, cols), jnp.float32)
+    vmem = pl.BlockSpec(memory_space=pltpu.VMEM)
+    padded = pltpu.VMEM((planes, rows + 2 * EDGE, cols), jnp.float32)
+    return pl.pallas_call(
+        functools.partial(fine_kernel, steps, opening),
+        out_shape=(part, part) if opening else part,
+        in_specs=[pl.BlockSpec(memory_space=pltpu.SMEM)] + [vmem] * 4,
+        out_specs=(vmem, vmem) if opening else vmem,
+        scratch_shapes=[padded, padded, padded, pltpu.VMEM((planes, rows, cols), jnp.float32)],
+        cost_estimate=pl.CostEstimate(flops=45 * cells, transcendentals=0, bytes_accessed=4 * rows * cols * (4 * planes + 2 * out_planes)),
+    )(meta, field, mine, theirs, extra)
 
 
 def pair_matrix(fine):
@@ -101,8 +207,13 @@
         absorb = jnp.where(even, theirs, mine)
         field0 = wide[1]
     else:
+        even = True
         wide = widen(jnp.stack([diffusivity, reaction, start]), 1)
         conduct, absorb, field0 = wide[0], wide[1], wide[2]
+        mine, theirs = conduct, absorb
+    meta = jnp.stack(
+        [me_s * n - halo, jnp.int32(space * n), jnp.int32(even), (me_t == times - 1).astype(jnp.int32)]
+    ).astype(jnp.int32)
     plane_ids = me_s * n - halo + jnp.arange(n + 2 * halo)
     inside = (plane_ids >= 0) & (plane_ids < space * n)
 
@@ -119,11 +230,17 @@
                 field = jnp.where(m, field, 0.0)
         return field
 
-    advanced = fine_prop(field0)
-    payload = jnp.where(me_t == times - 1, initial, advanced)
+    if halo == STEPS:
+        advanced, payload = fine_prop_kernel(field0, mine, theirs, initial, meta, STEPS, True)
+    else:
+        advanced = fine_prop(field0)
+        payload = jnp.where(me_t == times - 1, initial, advanced)
     got2 = gather_planes(payload, ("space", "tm"), prev_pairs, distances)
     relaxed = jnp.concatenate([got2[d] for d in distances], axis=0)[lo:hi]
-    residual = fine_prop(relaxed) - advanced
+    if halo == STEPS:
+        residual = fine_prop_kernel(relaxed, mine, theirs, advanced, meta, STEPS, False)
+    else:
+        residual = fine_prop(relaxed) - advanced
 
     cn = n // 2
     creach = -(-1 // cn)

time: 105 us -> 109 us (1.038)
  Pallas kernels: 0 us -> 15.7 us
  waiting for transfers between devices: 55.9 us -> 46.8 us
  local copies, waits for them, and re-layouts: 2.33 us -> 7.82 us
  other arithmetic: 12.2 us -> 8.06 us
  starting transfers between devices: 29.1 us -> 26.2 us
    pallas_call x0 -> x2, Pallas kernels: none -> 15.7 us  [fine_prop_kernel(): pl.pallas_call(functools.partial(fine_kernel, steps, opening), out_shape=...]
    ppermute x12, waiting for transfers between devices: 54.5 us -> 46.8 us  [gather_planes(): pieces[d] = lax.ppermute(block, axis_names, pairs_of(d))]
    select_n x5 -> x0, other arithmetic: 4.9 us -> none  [the longest x4 4.59 us: fine_prop(): field = jnp.where(m, field, 0.0)]
    ppermute x12, starting transfers between devices: 28.5 us -> 24.3 us  [gather_planes(): pieces[d] = lax.ppermute(block, axis_names, pairs_of(d))]
    unnamed x46 -> x25, local copies, waits for them, and re-layouts: 2.05 us -> 5.08 us
    sub x2 -> x0, other arithmetic: 1.85 us -> none  [advance(): return center + diffuse_scale * inflow - react_scale * absorb[1:-1] * center]
    squeeze x0 -> x1, local copies, waits for them, and re-layouts: none -> 1.66 us  [shards(): mine = wide[0]]
    ppermute x1, waiting for transfers between devices: 1.41 us -> 0.01 us  [shards(): theirs_rim = lax.ppermute(rim, 'tm', partner)]
  transfers between devices with their start and end apart: 13 -> 13, of which waited for: 10 -> 6; matrix products, arithmetic and copies ran while one was open for 2% -> 10% of each run, Pallas kernels for 0% -> 0%
where the time goes in v5:
time: 109 us
  waiting for transfers between devices  46.8 us (43%)
  starting transfers between devices  26.2 us (24%)
  Pallas kernels  15.7 us (14%)
  other arithmetic  8.06 us (7%)
  local copies, waits for them, and re-layouts  7.82 us (7%)
  matrix products  3.04 us (3%)
    ppermute x12, waiting for transfers between devices, gather_planes(): pieces[d] = lax.ppermute(block, axis_names, pairs_of(d))  46.8 us
    ppermute x12, starting transfers between devices, gather_planes(): pieces[d] = lax.ppermute(block, axis_names, pairs_of(d))  24.3 us
    pallas_call x2, Pallas kernels, fine_prop_kernel(): pl.pallas_call(functools.partial(fine_kernel, steps, opening), out_shape=...  15.7 us
    unnamed x25, local copies, waits for them, and re-layouts  5.08 us
    dot_general x6, matrix products, restrict(): jnp.einsum('Yy,mYZ,Zz->myz', rows, planes, cols, precision=lax.Precision....  2.37 us
    reduce_sum x3, other arithmetic, restrict(): planes = field.reshape(first // 2, 2, second, third).sum(axis=1)  2.32 us
  transfers between devices with their start and end apart: 13, of which 6 were waited for; matrix products, arithmetic and copies ran while one was open for 10% of the time, Pallas kernels for 0%

profile of v5, /device:TPU:1, one launch (start us, length us, event | category | flops | bytes accessed | tf_op | source)
XLA Modules:
  0.0 108.6 jit_solution(13045130940588373858)
XLA Ops:
  0.6 1.1 broadcast_select_fusion
  1.7 1.0 pad_maximum_fusion.4
  2.7 1.3 %collective-permute-start.2 = (f32[2,2,256,128]{3,2,1,0:T(8,128)S(1)}, f32[2,2,256,128]{3,2,1,0:T(8,128)S(1)}, u32[]{:S(2)}, u32[]{:S(2)}) collective-permute-start(f32[2,2,256,128]{3,2,1,0:T(8,128)S(1)} %pad_maximum_fusion.4), channel_id=1, source_target_pairs={{2,0},{4,2},{6,4},{8,6},{10,8},{12,10},{14,12},{16,14},{18,16},{20... | collective-permute-start | bytes 1572872 | tf_op jit(solution)/shard_map/ppermute | solution.py:160
  4.0 1.3 %collective-permute-start.3 = (f32[2,2,256,128]{3,2,1,0:T(8,128)S(1)}, f32[2,2,256,128]{3,2,1,0:T(8,128)S(1)}, u32[]{:S(2)}, u32[]{:S(2)}) collective-permute-start(f32[2,2,256,128]{3,2,1,0:T(8,128)S(1)} %pad_maximum_fusion.4), channel_id=1, source_target_pairs={{4,0},{6,2},{8,4},{10,6},{12,8},{14,10},{16,12},{18,14},{20,16},{2... | collective-permute-start | bytes 1572872 | tf_op jit(solution)/shard_map/ppermute | solution.py:160
  5.3 6.4 %collective-permute-start = (f32[2,2,256,128]{3,2,1,0:T(8,128)S(1)}, f32[2,2,256,128]{3,2,1,0:T(8,128)S(1)}, u32[]{:S(2)}, u32[]{:S(2)}) collective-permute-start(f32[2,2,256,128]{3,2,1,0:T(8,128)S(1)} %pad_maximum_fusion.4), channel_id=1, source_target_pairs={{0,4},{2,6},{4,8},{6,10},{8,12},{10,14},{12,16},{14,18},{16,20},{1... | collective-permute-start | bytes 1572872 | tf_op jit(solution)/shard_map/ppermute | solution.py:160
  11.7 2.2 %collective-permute-start.1 = (f32[2,2,256,128]{3,2,1,0:T(8,128)S(1)}, f32[2,2,256,128]{3,2,1,0:T(8,128)S(1)}, u32[]{:S(2)}, u32[]{:S(2)}) collective-permute-start(f32[2,2,256,128]{3,2,1,0:T(8,128)S(1)} %pad_maximum_fusion.4), channel_id=1, source_target_pairs={{0,2},{2,4},{4,6},{6,8},{8,10},{10,12},{12,14},{14,16},{16,18},{18... | collective-permute-start | bytes 1572872 | tf_op jit(solution)/shard_map/ppermute | solution.py:160
  14.0 4.3 %collective-permute-done.2 = f32[2,2,256,128]{3,2,1,0:T(8,128)S(1)} collective-permute-done((f32[2,2,256,128]{3,2,1,0:T(8,128)S(1)}, f32[2,2,256,128]{3,2,1,0:T(8,128)S(1)}, u32[]{:S(2)}, u32[]{:S(2)}) %collective-permute-start.2) | collective-permute-done | bytes 524320 | tf_op jit(solution)/shard_map/ppermute | solution.py:160
  18.3 2.8 %collective-permute-done.3 = f32[2,2,256,128]{3,2,1,0:T(8,128)S(1)} collective-permute-done((f32[2,2,256,128]{3,2,1,0:T(8,128)S(1)}, f32[2,2,256,128]{3,2,1,0:T(8,128)S(1)}, u32[]{:S(2)}, u32[]{:S(2)}) %collective-permute-start.3) | collective-permute-done | bytes 524320 | tf_op jit(solution)/shard_map/ppermute | solution.py:160
  21.1 23.3 %collective-permute-done = f32[2,2,256,128]{3,2,1,0:T(8,128)S(1)} collective-permute-done((f32[2,2,256,128]{3,2,1,0:T(8,128)S(1)}, f32[2,2,256,128]{3,2,1,0:T(8,128)S(1)}, u32[]{:S(2)}, u32[]{:S(2)}) %collective-permute-start) | collective-permute-done | bytes 524320 | tf_op jit(solution)/shard_map/ppermute | solution.py:160
  44.5 1.9 %collective-permute-start.4 = (f32[8,256,128]{2,1,0:T(8,128)S(1)}, f32[8,256,128]{2,1,0:T(8,128)S(1)}, u32[]{:S(2)}, u32[]{:S(2)}) collective-permute-start(f32[8,256,128]{2,1,0:T(8,128)S(1)} %pad_maximum_fusion.1), channel_id=1, source_target_pairs={{0,1},{1,0},{2,3},{3,2},{4,5},{5,4},{6,7},{7,6},{8,9},{9,8},{10,11... | collective-permute-start | bytes 3145736 | tf_op jit(solution)/shard_map/ppermute | solution.py:203
  47.3 1.7 %slice_bitcast_fusion = (f32[10,256,128]{2,1,0:T(8,128)}, f32[10,256,128]{2,1,0:T(8,128)}) fusion(f32[2,10,256,128]{3,2,1,0:T(8,128)S(1)} %constant_dynamic-update-slice_fusion), kind=kLoop, calls=%fused_computation | loop fusion | bytes 5242880 | tf_op jit(solution)/shard_map/squeeze | solution.py:200
  49.0 1.2 %pad_maximum_fusion.theirs_ref = f32[10,256,128]{2,1,0:T(8,128)} fusion(f32[4,256,128]{2,1,0:T(8,128)S(1)} %get-tuple-element.11, f32[2,256,128]{2,1,0:T(8,128)S(1)} %get-tuple-element.12, f32[4,256,128]{2,1,0:T(8,128)S(1)} %get-tuple-element.10), kind=kLoop, calls=%fused_computation.2 | loop fusion | flops 655360 | bytes 2621440 | tf_op jit(solution)/shard_map/concatenate | solution.py:205
  50.2 8.0 %shard_map.131 = (f32[2,256,128]{2,1,0:T(8,128)}, f32[2,256,128]{2,1,0:T(8,128)}) custom-call(s32[4]{0:T(128)} %pad_add_fusion.meta_ref, f32[10,256,128]{2,1,0:T(8,128)} %get-tuple-element.9.f_ref, f32[10,256,128]{2,1,0:T(8,128)} %get-tuple-element.8.mine_ref, f32[10,256,128]{2,1,0:T(8,128)} %pad_maximum_fusion.theirs_ref, f32[2,256,128]{2,1,0:T(8,128)} %extra_ref.1), custom_call_target="tpu_custom_call" | custom-call | flops 29491200 | bytes 5767168 | tf_op jit(solution)/shard_map/pallas_call | solution.py:122
  58.2 4.9 %collective-permute-start.5 = (f32[2,256,128]{2,1,0:T(8,128)}, f32[2,256,128]{2,1,0:T(8,128)}, u32[]{:S(2)}, u32[]{:S(2)}) collective-permute-start(f32[2,256,128]{2,1,0:T(8,128)} %get-tuple-element.5), channel_id=1, source_target_pairs={{1,4},{0,5},{3,6},{2,7},{5,8},{4,9},{7,10},{6,11},{9,12},{8,13},{1... | collective-permute-start | bytes 786440 | tf_op jit(solution)/shard_map/ppermute | solution.py:160
  63.1 2.0 %collective-permute-start.6 = (f32[2,256,128]{2,1,0:T(8,128)}, f32[2,256,128]{2,1,0:T(8,128)}, u32[]{:S(2)}, u32[]{:S(2)}) collective-permute-start(f32[2,256,128]{2,1,0:T(8,128)} %get-tuple-element.5), channel_id=1, source_target_pairs={{1,2},{0,3},{3,4},{2,5},{5,6},{4,7},{7,8},{6,9},{9,10},{8,11},{11,... | collective-permute-start | bytes 786440 | tf_op jit(solution)/shard_map/ppermute | solution.py:160
  65.4 1.3 %collective-permute-start.8 = (f32[2,256,128]{2,1,0:T(8,128)}, f32[2,256,128]{2,1,0:T(8,128)}, u32[]{:S(2)}, u32[]{:S(2)}) collective-permute-start(f32[2,256,128]{2,1,0:T(8,128)} %get-tuple-element.5), channel_id=1, source_target_pairs={{3,0},{2,1},{5,2},{4,3},{7,4},{6,5},{9,6},{8,7},{11,8},{10,9},{13,... | collective-permute-start | bytes 786440 | tf_op jit(solution)/shard_map/ppermute | solution.py:160
  66.7 1.3 %collective-permute-start.9 = (f32[2,256,128]{2,1,0:T(8,128)}, f32[2,256,128]{2,1,0:T(8,128)}, u32[]{:S(2)}, u32[]{:S(2)}) collective-permute-start(f32[2,256,128]{2,1,0:T(8,128)} %get-tuple-element.5), channel_id=1, source_target_pairs={{5,0},{4,1},{7,2},{6,3},{9,4},{8,5},{11,6},{10,7},{13,8},{12,9},{1... | collective-permute-start | bytes 786440 | tf_op jit(solution)/shard_map/ppermute | solution.py:160
  68.0 1.0 slice_select_fusion
  69.0 1.2 %reduce_sum.28 = f32[3,256,128]{2,1,0:T(8,128)S(1)} reduce(f32[3,2,256,128]{3,2,1,0:T(8,128)} %bitcast.47, f32[]{:T(128)} %constant.39.clone.1), dimensions={1}, to_apply=%region_1.2 | reduce | flops 98304 | bytes 1179652 | tf_op jit(solution)/shard_map/reduce_sum | solution.py:139
  71.8 2.1 %collective-permute-done.5 = f32[2,256,128]{2,1,0:T(8,128)} collective-permute-done((f32[2,256,128]{2,1,0:T(8,128)}, f32[2,256,128]{2,1,0:T(8,128)}, u32[]{:S(2)}, u32[]{:S(2)}) %collective-permute-start.5) | collective-permute-done | bytes 262176 | tf_op jit(solution)/shard_map/ppermute | solution.py:160
  73.8 1.0 constant_dynamic-update-slice_fusion.9
  74.8 1.0 constant_dynamic-update-slice_fusion.8
  75.8 1.0 constant_dynamic-update-slice_fusion.7
  76.8 2.8 %collective-permute-done.8 = f32[2,256,128]{2,1,0:T(8,128)} collective-permute-done((f32[2,256,128]{2,1,0:T(8,128)}, f32[2,256,128]{2,1,0:T(8,128)}, u32[]{:S(2)}, u32[]{:S(2)}) %collective-permute-start.8) | collective-permute-done | bytes 262176 | tf_op jit(solution)/shard_map/ppermute | solution.py:160
  79.6 1.0 constant_dynamic-update-slice_fusion.6
  80.6 1.0 constant_dynamic-update-slice_fusion.5.f_ref
  81.5 1.1 copy-done.2
  82.6 7.8 %shard_map.132 = f32[2,256,128]{2,1,0:T(8,128)} custom-call(s32[4]{0:T(128)} %pad_add_fusion.meta_ref, f32[10,256,128]{2,1,0:T(8,128)} %copy-done.2, f32[10,256,128]{2,1,0:T(8,128)} %get-tuple-element.8.mine_ref, f32[10,256,128]{2,1,0:T(8,128)} %pad_maximum_fusion.theirs_ref, f32[2,256,128]{2,1,0:T(8,128)} %get-tuple-element.4.extra_ref), custom_call_target="tpu_custom_call" | custom-call | flops 29491200 | bytes 5767168 | tf_op jit(solution)/shard_map/pallas_call | solution.py:122
  90.4 1.0 reduce_sum.27
  92.1 1.3 %collective-permute-start.10 = (f32[1,128,64]{1,2,0:T(8,128)S(1)}, f32[1,128,64]{1,2,0:T(8,128)S(1)}, u32[]{:S(2)}, u32[]{:S(2)}) collective-permute-start(f32[1,128,64]{1,2,0:T(8,128)S(1)} %fusion.2), channel_id=1, source_target_pairs={{0,1},{2,3},{4,5},{6,7},{8,9},{10,11},{12,13},{14,15},{16,17},{18,... | collective-permute-start | bytes 98312 | tf_op jit(solution)/shard_map/ppermute | solution.py:160
  94.0 1.3 %collective-permute-start.11 = (f32[1,128,64]{1,2,0:T(8,128)S(1)}, f32[1,128,64]{1,2,0:T(8,128)S(1)}, u32[]{:S(2)}, u32[]{:S(2)}) collective-permute-start(f32[1,128,64]{1,2,0:T(8,128)S(1)} %fusion.2), channel_id=1, source_target_pairs={{2,1},{4,3},{6,5},{8,7},{10,9},{12,11},{14,13},{16,15},{18,17},{20... | collective-permute-start | bytes 98312 | tf_op jit(solution)/shard_map/ppermute | solution.py:160
  95.7 11.5 %collective-permute-done.11 = f32[1,128,64]{1,2,0:T(8,128)S(1)} collective-permute-done((f32[1,128,64]{1,2,0:T(8,128)S(1)}, f32[1,128,64]{1,2,0:T(8,128)S(1)}, u32[]{:S(2)}, u32[]{:S(2)}) %collective-permute-start.11) | collective-permute-done | bytes 32800 | tf_op jit(solution)/shard_map/ppermute | solution.py:160
  (47 shorter events, 5.8 us)
Async XLA Ops:
  2.7 15.6 %collective-permute-start.2 = (f32[2,2,256,128]{3,2,1,0:T(8,128)S(1)}, f32[2,2,256,128]{3,2,1,0:T(8,128)S(1)}, u32[]{:S(2)}, u32[]{:S(2)}) collective-permute-start(f32[2,2,256,128]{3,2,1,0:T(8,128)S(1)} %pad_maximum_fusion.4), channel_id=1, source_target_pairs={{2,0},{4,2},{6,4},{8,6},{10,8},{12,10},{14,12},{16,14},{18,16},{20... | collective-permute-start | bytes 1572872 | tf_op jit(solution)/shard_map/ppermute | solution.py:160
  4.0 17.1 %collective-permute-start.3 = (f32[2,2,256,128]{3,2,1,0:T(8,128)S(1)}, f32[2,2,256,128]{3,2,1,0:T(8,128)S(1)}, u32[]{:S(2)}, u32[]{:S(2)}) collective-permute-start(f32[2,2,256,128]{3,2,1,0:T(8,128)S(1)} %pad_maximum_fusion.4), channel_id=1, source_target_pairs={{4,0},{6,2},{8,4},{10,6},{12,8},{14,10},{16,12},{18,14},{20,16},{2... | collective-permute-start | bytes 1572872 | tf_op jit(solution)/shard_map/ppermute | solution.py:160
  5.3 39.1 %collective-permute-start = (f32[2,2,256,128]{3,2,1,0:T(8,128)S(1)}, f32[2,2,256,128]{3,2,1,0:T(8,128)S(1)}, u32[]{:S(2)}, u32[]{:S(2)}) collective-permute-start(f32[2,2,256,128]{3,2,1,0:T(8,128)S(1)} %pad_maximum_fusion.4), channel_id=1, source_target_pairs={{0,4},{2,6},{4,8},{6,10},{8,12},{10,14},{12,16},{14,18},{16,20},{1... | collective-permute-start | bytes 1572872 | tf_op jit(solution)/shard_map/ppermute | solution.py:160
  11.7 32.7 %collective-permute-start.1 = (f32[2,2,256,128]{3,2,1,0:T(8,128)S(1)}, f32[2,2,256,128]{3,2,1,0:T(8,128)S(1)}, u32[]{:S(2)}, u32[]{:S(2)}) collective-permute-start(f32[2,2,256,128]{3,2,1,0:T(8,128)S(1)} %pad_maximum_fusion.4), channel_id=1, source_target_pairs={{0,2},{2,4},{4,6},{6,8},{8,10},{10,12},{12,14},{14,16},{16,18},{18... | collective-permute-start | bytes 1572872 | tf_op jit(solution)/shard_map/ppermute | solution.py:160
  44.5 2.6 %copy-start.4 = (f32[1,2,256,128]{3,2,1,0:T(8,128)S(1)}, f32[1,2,256,128]{3,2,1,0:T(8,128)}, u32[]{:S(2)}) copy-start(f32[1,2,256,128]{3,2,1,0:T(8,128)} %param.13) | copy-start | bytes 786436
  44.5 4.4 %collective-permute-start.4 = (f32[8,256,128]{2,1,0:T(8,128)S(1)}, f32[8,256,128]{2,1,0:T(8,128)S(1)}, u32[]{:S(2)}, u32[]{:S(2)}) collective-permute-start(f32[8,256,128]{2,1,0:T(8,128)S(1)} %pad_maximum_fusion.1), channel_id=1, source_target_pairs={{0,1},{1,0},{2,3},{3,2},{4,5},{5,4},{6,7},{7,6},{8,9},{9,8},{10,11... | collective-permute-start | bytes 3145736 | tf_op jit(solution)/shard_map/ppermute | solution.py:203
  50.2 17.8 %copy-start = (f32[10,256,128]{2,1,0:T(8,128)S(1)}, f32[10,256,128]{2,1,0:T(8,128)}, u32[]{:S(2)}) copy-start(f32[10,256,128]{2,1,0:T(8,128)} %get-tuple-element.8.mine_ref) | copy-start | bytes 3932164
  50.2 17.8 %copy-start.1 = (f32[10,256,128]{2,1,0:T(8,128)S(1)}, f32[10,256,128]{2,1,0:T(8,128)}, u32[]{:S(2)}) copy-start(f32[10,256,128]{2,1,0:T(8,128)} %pad_maximum_fusion.theirs_ref) | copy-start | bytes 3932164
  58.2 15.7 %collective-permute-start.5 = (f32[2,256,128]{2,1,0:T(8,128)}, f32[2,256,128]{2,1,0:T(8,128)}, u32[]{:S(2)}, u32[]{:S(2)}) collective-permute-start(f32[2,256,128]{2,1,0:T(8,128)} %get-tuple-element.5), channel_id=1, source_target_pairs={{1,4},{0,5},{3,6},{2,7},{5,8},{4,9},{7,10},{6,11},{9,12},{8,13},{1... | collective-permute-start | bytes 786440 | tf_op jit(solution)/shard_map/ppermute | solution.py:160
  63.1 11.7 %collective-permute-start.6 = (f32[2,256,128]{2,1,0:T(8,128)}, f32[2,256,128]{2,1,0:T(8,128)}, u32[]{:S(2)}, u32[]{:S(2)}) collective-permute-start(f32[2,256,128]{2,1,0:T(8,128)} %get-tuple-element.5), channel_id=1, source_target_pairs={{1,2},{0,3},{3,4},{2,5},{5,6},{4,7},{7,8},{6,9},{9,10},{8,11},{11,... | collective-permute-start | bytes 786440 | tf_op jit(solution)/shard_map/ppermute | solution.py:160
  65.1 10.7 %collective-permute-start.7 = (f32[2,256,128]{2,1,0:T(8,128)}, f32[2,256,128]{2,1,0:T(8,128)}, u32[]{:S(2)}, u32[]{:S(2)}) collective-permute-start(f32[2,256,128]{2,1,0:T(8,128)} %get-tuple-element.5), channel_id=1, source_target_pairs={{1,0},{0,1},{3,2},{2,3},{5,4},{4,5},{7,6},{6,7},{9,8},{8,9},{11,10... | collective-permute-start | bytes 786440 | tf_op jit(solution)/shard_map/ppermute | solution.py:160
  65.4 14.2 %collective-permute-start.8 = (f32[2,256,128]{2,1,0:T(8,128)}, f32[2,256,128]{2,1,0:T(8,128)}, u32[]{:S(2)}, u32[]{:S(2)}) collective-permute-start(f32[2,256,128]{2,1,0:T(8,128)} %get-tuple-element.5), channel_id=1, source_target_pairs={{3,0},{2,1},{5,2},{4,3},{7,4},{6,5},{9,6},{8,7},{11,8},{10,9},{13,... | collective-permute-start | bytes 786440 | tf_op jit(solution)/shard_map/ppermute | solution.py:160
  66.7 13.9 %collective-permute-start.9 = (f32[2,256,128]{2,1,0:T(8,128)}, f32[2,256,128]{2,1,0:T(8,128)}, u32[]{:S(2)}, u32[]{:S(2)}) collective-permute-start(f32[2,256,128]{2,1,0:T(8,128)} %get-tuple-element.5), channel_id=1, source_target_pairs={{5,0},{4,1},{7,2},{6,3},{9,4},{8,5},{11,6},{10,7},{13,8},{12,9},{1... | collective-permute-start | bytes 786440 | tf_op jit(solution)/shard_map/ppermute | solution.py:160
  69.0 1.3 %copy-start.7 = (f32[128,64,1]{1,0,2:T(8,128)S(1)}, f32[128,64,1]{1,0,2:T(8,128)}, u32[]{:S(2)}) copy-start(f32[128,64,1]{1,0,2:T(8,128)} %constant.54) | copy-start | bytes 98308
  70.3 1.2 %copy-start.6 = (f32[256,128,1]{1,0,2:T(8,128)S(1)}, f32[256,128,1]{1,0,2:T(8,128)}, u32[]{:S(2)}) copy-start(f32[256,128,1]{1,0,2:T(8,128)} %constant.55) | copy-start | bytes 393220
  81.5 1.1 copy-start.2
  82.6 8.8 %copy-start.8 = (f32[128,64]{1,0:T(8,128)S(1)}, f32[128,64]{1,0:T(8,128)}, u32[]{:S(2)}) copy-start(f32[128,64]{1,0:T(8,128)} %constant.45.clone) | copy-start | bytes 98308
  82.6 9.1 %copy-start.5 = (f32[256,128]{1,0:T(8,128)S(1)}, f32[256,128]{1,0:T(8,128)}, u32[]{:S(2)}) copy-start(f32[256,128]{1,0:T(8,128)} %constant.44.clone) | copy-start | bytes 393220
  90.4 17.5 %copy-start.3 = (f32[2,256,128]{2,1,0:T(8,128)S(1)}, f32[2,256,128]{2,1,0:T(8,128)}, u32[]{:S(2)}) copy-start(f32[2,256,128]{2,1,0:T(8,128)} %get-tuple-element.4.extra_ref) | copy-start | bytes 786436
  92.1 3.6 %collective-permute-start.10 = (f32[1,128,64]{1,2,0:T(8,128)S(1)}, f32[1,128,64]{1,2,0:T(8,128)S(1)}, u32[]{:S(2)}, u32[]{:S(2)}) collective-permute-start(f32[1,128,64]{1,2,0:T(8,128)S(1)} %fusion.2), channel_id=1, source_target_pairs={{0,1},{2,3},{4,5},{6,7},{8,9},{10,11},{12,13},{14,15},{16,17},{18,... | collective-permute-start | bytes 98312 | tf_op jit(solution)/shard_map/ppermute | solution.py:160
  93.4 2.3 %collective-permute-start.12 = (f32[1,128,64]{1,2,0:T(8,128)S(1)}, f32[1,128,64]{1,2,0:T(8,128)S(1)}, u32[]{:S(2)}, u32[]{:S(2)}) collective-permute-start(f32[1,128,64]{1,2,0:T(8,128)S(1)} %fusion.2), channel_id=1, source_target_pairs={{0,3},{2,5},{4,7},{6,9},{8,11},{10,13},{12,15},{14,17},{16,19},{18... | collective-permute-start | bytes 98312 | tf_op jit(solution)/shard_map/ppermute | solution.py:160
  94.0 13.2 %collective-permute-start.11 = (f32[1,128,64]{1,2,0:T(8,128)S(1)}, f32[1,128,64]{1,2,0:T(8,128)S(1)}, u32[]{:S(2)}, u32[]{:S(2)}) collective-permute-start(f32[1,128,64]{1,2,0:T(8,128)S(1)} %fusion.2), channel_id=1, source_target_pairs={{2,1},{4,3},{6,5},{8,7},{10,9},{12,11},{14,13},{16,15},{18,17},{20... | collective-permute-start | bytes 98312 | tf_op jit(solution)/shard_map/ppermute | solution.py:160

commit v6 on v2

--- a/solution.py
+++ b/solution.py
@@ -84,7 +84,7 @@
     split = times % 2 == 0
     if split:
         even = me_t % 2 == 0
-        local = jnp.stack([jnp.where(even, diffusivity, reaction), start])
+        local = jnp.where(even, jnp.stack([diffusivity, start]), jnp.stack([reaction, start]))
     else:
         local = jnp.stack([diffusivity, reaction, start])
     got = gather_planes(local, "space", lambda d: None if d == 0 else space_pairs(d), distances)

time: 103 us -> 103 us (level)
  the two profiles are of different devices: /device:TPU:23 before, /device:TPU:1 now
where the time goes in v6:
time: 103 us; the launch traced here: 102 us
  waiting for transfers between devices  35 us (34%)
  starting transfers between devices  33 us (32%)
  other arithmetic  18.2 us (18%)
  local copies, waits for them, and re-layouts  9.25 us (9%)
  matrix products  5.11 us (5%)
  between operations  1.26 us (1%)
    ppermute x12, waiting for transfers between devices, gather_planes(): pieces[d] = lax.ppermute(block, axis_names, pairs_of(d))  33.2 us
    ppermute x12, starting transfers between devices, gather_planes(): pieces[d] = lax.ppermute(block, axis_names, pairs_of(d))  31.1 us
    select_n x5, other arithmetic, fine_prop(): field = jnp.where(m > 0, field, 0.0)  8.33 us
    unnamed x55, local copies, waits for them, and re-layouts  7.55 us
    dot_general x6, matrix products, restrict(): jnp.einsum('Yy,mYZ,Zz->myz', rows, planes, cols, precision=lax.Precision....  4.43 us
    reduce_sum x3, other arithmetic, restrict(): planes = field.reshape(first // 2, 2, second, third).sum(axis=1)  3.95 us
    slice x1, other arithmetic, advance(): return center + diffuse_scale * inflow - react_scale * absorb[1:-1] * center  2.07 us
  transfers between devices with their start and end apart: 13, of which 4 were waited for; matrix products, arithmetic and copies ran while one was open for 11% of the time, Pallas kernels for 0%

profile of v6, /device:TPU:1, one launch (start us, length us, event | category | flops | bytes accessed | tf_op | source)
XLA Modules:
  0.0 101.8 jit_solution(12536328803537691814)
XLA Ops:
  0.7 1.2 %fusion.105 = f32[2,2,256,128]{3,2,1,0:T(8,128)S(1)} fusion(f32[1,2,256,128]{3,2,1,0:T(8,128)} %param.13, f32[1,2,256,128]{3,2,1,0:T(8,128)} %bitcast.67, f32[1,2,256,128]{3,2,1,0:T(8,128)} %bitcast.69, pred[]{:T(512)S(6)} %eq.8), kind=kLoop, calls=%fused_computation.179 | loop fusion | flops 393216 | bytes 1310721 | tf_op jit(solution)/shard_map/jit(_where)/select_n | solution.py:87
  1.9 4.0 %collective-permute-start = (f32[2,2,256,128]{3,2,1,0:T(8,128)S(1)}, f32[2,2,256,128]{3,2,1,0:T(8,128)S(1)}, u32[]{:S(2)}, u32[]{:S(2)}) collective-permute-start(f32[2,2,256,128]{3,2,1,0:T(8,128)S(1)} %fusion.105), channel_id=1, source_target_pairs={{0,4},{2,6},{4,8},{6,10},{8,12},{10,14},{12,16},{14,18},{16,20},{1... | collective-permute-start | bytes 1572872 | tf_op jit(solution)/shard_map/ppermute | solution.py:53
  5.9 3.1 %collective-permute-start.1 = (f32[2,2,256,128]{3,2,1,0:T(8,128)S(1)}, f32[2,2,256,128]{3,2,1,0:T(8,128)S(1)}, u32[]{:S(2)}, u32[]{:S(2)}) collective-permute-start(f32[2,2,256,128]{3,2,1,0:T(8,128)S(1)} %fusion.105), channel_id=1, source_target_pairs={{0,2},{2,4},{4,6},{6,8},{8,10},{10,12},{12,14},{14,16},{16,18},{18... | collective-permute-start | bytes 1572872 | tf_op jit(solution)/shard_map/ppermute | solution.py:53
  9.1 1.3 %collective-permute-start.2 = (f32[2,2,256,128]{3,2,1,0:T(8,128)S(1)}, f32[2,2,256,128]{3,2,1,0:T(8,128)S(1)}, u32[]{:S(2)}, u32[]{:S(2)}) collective-permute-start(f32[2,2,256,128]{3,2,1,0:T(8,128)S(1)} %fusion.105), channel_id=1, source_target_pairs={{2,0},{4,2},{6,4},{8,6},{10,8},{12,10},{14,12},{16,14},{18,16},{20... | collective-permute-start | bytes 1572872 | tf_op jit(solution)/shard_map/ppermute | solution.py:53
  10.4 1.3 %collective-permute-start.3 = (f32[2,2,256,128]{3,2,1,0:T(8,128)S(1)}, f32[2,2,256,128]{3,2,1,0:T(8,128)S(1)}, u32[]{:S(2)}, u32[]{:S(2)}) collective-permute-start(f32[2,2,256,128]{3,2,1,0:T(8,128)S(1)} %fusion.105), channel_id=1, source_target_pairs={{4,0},{6,2},{8,4},{10,6},{12,8},{14,10},{16,12},{18,14},{20,16},{2... | collective-permute-start | bytes 1572872 | tf_op jit(solution)/shard_map/ppermute | solution.py:53
  11.9 20.7 %collective-permute-done.2 = f32[2,2,256,128]{3,2,1,0:T(8,128)S(1)} collective-permute-done((f32[2,2,256,128]{3,2,1,0:T(8,128)S(1)}, f32[2,2,256,128]{3,2,1,0:T(8,128)S(1)}, u32[]{:S(2)}, u32[]{:S(2)}) %collective-permute-start.2) | collective-permute-done | bytes 524320 | tf_op jit(solution)/shard_map/ppermute | solution.py:53
  32.8 1.9 %collective-permute-start.4 = (f32[8,256,128]{2,1,0:T(8,128)S(1)}, f32[8,256,128]{2,1,0:T(8,128)S(1)}, u32[]{:S(2)}, u32[]{:S(2)}) collective-permute-start(f32[8,256,128]{2,1,0:T(8,128)S(1)} %pad_maximum_fusion.7), channel_id=1, source_target_pairs={{0,1},{1,0},{2,3},{3,2},{4,5},{5,4},{6,7},{7,6},{8,9},{9,8},{10,11... | collective-permute-start | bytes 3145736 | tf_op jit(solution)/shard_map/ppermute | solution.py:97
  35.1 1.8 %collective-permute-done.4 = f32[8,256,128]{2,1,0:T(8,128)S(1)} collective-permute-done((f32[8,256,128]{2,1,0:T(8,128)S(1)}, f32[8,256,128]{2,1,0:T(8,128)S(1)}, u32[]{:S(2)}, u32[]{:S(2)}) %collective-permute-start.4) | collective-permute-done | bytes 1048608 | tf_op jit(solution)/shard_map/ppermute | solution.py:97
  39.6 2.2 %fusion.22 = f32[8,256,128]{2,1,0:T(8,128)S(1)} fusion(f32[8,256,128]{2,1,0:T(8,128)S(1)} %slice_bitcast_fusion.1, f32[2,2,256,128]{3,2,1,0:T(8,128)S(1)} %copy-done.9, f32[2,2,256,128]{3,2,1,0:T(8,128)S(1)} %copy-done.18, f32[2,2,256,128]{3,2,1,0:T(8,128)S(1)} %copy-done.7, f32[2,2,256,128]{3,2,1,0:T(8,128)S(1)} %copy-done.5, ...), kind=kLoop, calls=%fused_computation.63 | loop fusion | flops 10747904 | bytes 8912904 | tf_op jit(solution)/shard_map/jit(_where)/select_n | solution.py:116
  41.9 2.1 %fusion.246 = (f32[6,256,128]{2,1,0:T(8,128)}, f32[6,256,128]{2,1,0:T(8,128)S(1)}) fusion(f32[10,256,128]{2,1,0:T(8,128)S(1)} %get-tuple-element.7, f32[6,256,128]{2,1,0:T(8,128)S(1)} %slice.530, f32[6,256,128]{2,1,0:T(8,128)S(1)} %slice.532, f32[8,256,128]{2,1,0:T(8,128)S(1)} %fusion.22, f32[10,256,128]{2,1,0:T(8,128)S(1)} %get-tuple-element.6, ...), kind=kLoop, calls=%fused_computation.361 | loop fusion | flops 6881280 | bytes 7077894 | tf_op jit(solution)/shard_map/slice | solution.py:22
  45.0 1.2 %broadcast_select_fusion = (f32[2,256,128]{2,1,0:T(8,128)}, f32[2,256,128]{2,1,0:T(8,128)}) fusion(f32[2,256,128]{2,1,0:T(8,128)S(1)} %copy-done.23, pred[]{:T(512)S(6)} %eq.9, f32[2,256,128]{2,1,0:T(8,128)S(1)} %slice.544, f32[10,256,128]{2,1,0:T(8,128)S(1)} %get-tuple-element.7, f32[2,256,128]{2,1,0:T(8,128)S(1)} %slice.546, ...), kind=kLoop, calls=%fused_computation.294 | loop fusion | flops 2293760 | bytes 2621441 | tf_op jit(solution)/shard_map/jit(_where)/select_n | solution.py:120
  46.2 13.4 %collective-permute-start.5 = (f32[2,256,128]{2,1,0:T(8,128)}, f32[2,256,128]{2,1,0:T(8,128)}, u32[]{:S(2)}, u32[]{:S(2)}) collective-permute-start(f32[2,256,128]{2,1,0:T(8,128)} %get-tuple-element.4), channel_id=1, source_target_pairs={{1,4},{0,5},{3,6},{2,7},{5,8},{4,9},{7,10},{6,11},{9,12},{8,13},{1... | collective-permute-start | bytes 786440 | tf_op jit(solution)/shard_map/ppermute | solution.py:53
  59.6 2.0 %collective-permute-start.6 = (f32[2,256,128]{2,1,0:T(8,128)}, f32[2,256,128]{2,1,0:T(8,128)}, u32[]{:S(2)}, u32[]{:S(2)}) collective-permute-start(f32[2,256,128]{2,1,0:T(8,128)} %get-tuple-element.4), channel_id=1, source_target_pairs={{1,2},{0,3},{3,4},{2,5},{5,6},{4,7},{7,8},{6,9},{9,10},{8,11},{11,... | collective-permute-start | bytes 786440 | tf_op jit(solution)/shard_map/ppermute | solution.py:53
  61.7 1.3 %collective-permute-start.8 = (f32[2,256,128]{2,1,0:T(8,128)}, f32[2,256,128]{2,1,0:T(8,128)}, u32[]{:S(2)}, u32[]{:S(2)}) collective-permute-start(f32[2,256,128]{2,1,0:T(8,128)} %get-tuple-element.4), channel_id=1, source_target_pairs={{3,0},{2,1},{5,2},{4,3},{7,4},{6,5},{9,6},{8,7},{11,8},{10,9},{13,... | collective-permute-start | bytes 786440 | tf_op jit(solution)/shard_map/ppermute | solution.py:53
  63.0 1.3 %collective-permute-start.9 = (f32[2,256,128]{2,1,0:T(8,128)}, f32[2,256,128]{2,1,0:T(8,128)}, u32[]{:S(2)}, u32[]{:S(2)}) collective-permute-start(f32[2,256,128]{2,1,0:T(8,128)} %get-tuple-element.4), channel_id=1, source_target_pairs={{5,0},{4,1},{7,2},{6,3},{9,4},{8,5},{11,6},{10,7},{13,8},{12,9},{1... | collective-permute-start | bytes 786440 | tf_op jit(solution)/shard_map/ppermute | solution.py:53
  65.1 2.0 %reduce_sum.29 = f32[3,256,128]{2,1,0:T(8,128)} reduce(f32[3,2,256,128]{3,2,1,0:T(8,128)} %bitcast.66, f32[]{:T(128)} %constant.20.clone.1), dimensions={1}, to_apply=%region_2.3 | reduce | flops 98304 | bytes 1179652 | tf_op jit(solution)/shard_map/reduce_sum | solution.py:32
  67.1 1.6 %fusion.249 = f32[64,3,256]{2,0,1:T(8,128)S(1)} fusion(f32[128,64,1]{1,0,2:T(8,128)} %constant.90, f32[3,256,128]{2,1,0:T(8,128)} %reduce_sum.28), kind=kOutput, calls=%fused_computation.364 | convolution fusion | flops 75497472 | bytes 622592 | tf_op jit(solution)/shard_map/Yy,mYZ,Zz->myz/dot_general | solution.py:35
  68.7 1.6 %fusion.250 = f32[64,3,256]{2,0,1:T(8,128)S(1)} fusion(f32[128,64,1]{1,0,2:T(8,128)} %constant.90, f32[3,256,128]{2,1,0:T(8,128)} %reduce_sum.29), kind=kOutput, calls=%fused_computation.365 | convolution fusion | flops 75497472 | bytes 622592 | tf_op jit(solution)/shard_map/Yy,mYZ,Zz->myz/dot_general | solution.py:35
  70.6 1.0 constant_dynamic-update-slice_fusion.9
  71.6 1.0 constant_dynamic-update-slice_fusion.8
  72.6 1.0 constant_dynamic-update-slice_fusion.7
  73.5 1.0 collective-permute-done.8
  74.5 1.0 constant_dynamic-update-slice_fusion.6
  75.5 1.1 %constant_dynamic-update-slice_fusion.5 = f32[10,256,128]{2,1,0:T(8,128)S(1)} fusion(f32[10,256,128]{2,1,0:T(8,128)S(1)} %constant_dynamic-update-slice_fusion.6, f32[2,256,128]{2,1,0:T(8,128)} %collective-permute-done.9), kind=kLoop, calls=%fused_computation.344 | loop fusion | bytes 524288 | tf_op jit(solution)/shard_map/concatenate | solution.py:122
  76.8 3.2 %fusion.38 = f32[8,256,128]{2,1,0:T(8,128)S(1)} fusion(f32[8,256,128]{2,1,0:T(8,128)S(1)} %slice.551, f32[2,256,128]{2,1,0:T(8,128)} %collective-permute-done.9, f32[2,256,128]{2,1,0:T(8,128)} %collective-permute-done.8, f32[2,256,128]{2,1,0:T(8,128)} %collective-permute-done.7, f32[2,256,128]{2,1,0:T(8,128)} %collective-permute-done.6, ...), kind=kLoop, calls=%fused_computation.79 | loop fusion | flops 10747904 | bytes 7602184 | tf_op jit(solution)/shard_map/jit(_where)/select_n | solution.py:116
  80.1 1.2 %fusion.90 = f32[6,256,128]{2,1,0:T(8,128)S(1)} fusion(f32[6,256,128]{2,1,0:T(8,128)S(1)} %slice.552, f32[8,256,128]{2,1,0:T(8,128)S(1)} %fusion.38, pred[6]{0:T(512)(128)(4,1)S(1)} %slice_compare_fusion.1, f32[6,256,128]{2,1,0:T(8,128)S(1)} %slice.532, f32[10,256,128]{2,1,0:T(8,128)S(1)} %get-tuple-element.6, f32[10,256,128]{2,1,0:T(8,128)S(1)} %get-tuple-element.7), kind=kLoop, calls=%fused_computation.156 | loop fusion | flops 6881280 | bytes 6291462 | tf_op jit(solution)/shard_map/jit(_where)/select_n | solution.py:116
  81.4 1.0 copy-done.3
  82.4 0.8 fusion.139
  83.4 1.1 %fusion.243 = (f32[256,128]{1,0:T(8,128)S(1)}, f32[2,256,128]{2,1,0:T(8,128)}) fusion(f32[2,256,128]{2,1,0:T(8,128)S(1)} %copy-done.14, f32[2,256,128]{2,1,0:T(8,128)S(1)} %slice.558, f32[10,256,128]{2,1,0:T(8,128)S(1)} %get-tuple-element.7, f32[2,256,128]{2,1,0:T(8,128)S(1)} %copy-done.16, f32[4,256,128]{2,1,0:T(8,128)S(1)} %fusion.139, ...), kind=kLoop, calls=%fused_computation.360 | loop fusion | flops 2326528 | bytes 2490368 | tf_op jit(solution)/shard_map/reduce_sum | solution.py:32
  85.2 1.3 %collective-permute-start.10 = (f32[1,128,64]{1,2,0:T(8,128)S(1)}, f32[1,128,64]{1,2,0:T(8,128)S(1)}, u32[]{:S(2)}, u32[]{:S(2)}) collective-permute-start(f32[1,128,64]{1,2,0:T(8,128)S(1)} %fusion.4), channel_id=1, source_target_pairs={{0,1},{2,3},{4,5},{6,7},{8,9},{10,11},{12,13},{14,15},{16,17},{18,... | collective-permute-start | bytes 98312 | tf_op jit(solution)/shard_map/ppermute | solution.py:53
  87.2 1.3 %collective-permute-start.11 = (f32[1,128,64]{1,2,0:T(8,128)S(1)}, f32[1,128,64]{1,2,0:T(8,128)S(1)}, u32[]{:S(2)}, u32[]{:S(2)}) collective-permute-start(f32[1,128,64]{1,2,0:T(8,128)S(1)} %fusion.4), channel_id=1, source_target_pairs={{2,1},{4,3},{6,5},{8,7},{10,9},{12,11},{14,13},{16,15},{18,17},{20... | collective-permute-start | bytes 98312 | tf_op jit(solution)/shard_map/ppermute | solution.py:53
  88.9 11.5 %collective-permute-done.11 = f32[1,128,64]{1,2,0:T(8,128)S(1)} collective-permute-done((f32[1,128,64]{1,2,0:T(8,128)S(1)}, f32[1,128,64]{1,2,0:T(8,128)S(1)}, u32[]{:S(2)}, u32[]{:S(2)}) %collective-permute-start.11) | collective-permute-done | bytes 32800 | tf_op jit(solution)/shard_map/ppermute | solution.py:53
  (95 shorter events, 9.2 us)
Async XLA Ops:
  0.6 11.2 %copy-start.12 = (f32[2,256,128]{2,1,0:T(8,128)S(1)}, f32[2,256,128]{2,1,0:T(8,128)}, u32[]{:S(2)}) copy-start(f32[2,256,128]{2,1,0:T(8,128)} %param.14) | copy-start | bytes 786436
  0.6 11.2 %copy-start.13 = (f32[2,256,128]{2,1,0:T(8,128)S(1)}, f32[2,256,128]{2,1,0:T(8,128)}, u32[]{:S(2)}) copy-start(f32[2,256,128]{2,1,0:T(8,128)} %param.15) | copy-start | bytes 786436
  1.9 30.8 %copy-start.17 = (f32[2,2,256,128]{3,2,1,0:T(8,128)}, f32[2,2,256,128]{3,2,1,0:T(8,128)S(1)}, u32[]{:S(2)}) copy-start(f32[2,2,256,128]{3,2,1,0:T(8,128)S(1)} %fusion.105) | copy-start | bytes 1572868
  1.9 30.7 %collective-permute-start = (f32[2,2,256,128]{3,2,1,0:T(8,128)S(1)}, f32[2,2,256,128]{3,2,1,0:T(8,128)S(1)}, u32[]{:S(2)}, u32[]{:S(2)}) collective-permute-start(f32[2,2,256,128]{3,2,1,0:T(8,128)S(1)} %fusion.105), channel_id=1, source_target_pairs={{0,4},{2,6},{4,8},{6,10},{8,12},{10,14},{12,16},{14,18},{16,20},{1... | collective-permute-start | bytes 1572872 | tf_op jit(solution)/shard_map/ppermute | solution.py:53
  5.9 26.7 %collective-permute-start.1 = (f32[2,2,256,128]{3,2,1,0:T(8,128)S(1)}, f32[2,2,256,128]{3,2,1,0:T(8,128)S(1)}, u32[]{:S(2)}, u32[]{:S(2)}) collective-permute-start(f32[2,2,256,128]{3,2,1,0:T(8,128)S(1)} %fusion.105), channel_id=1, source_target_pairs={{0,2},{2,4},{4,6},{6,8},{8,10},{10,12},{12,14},{14,16},{16,18},{18... | collective-permute-start | bytes 1572872 | tf_op jit(solution)/shard_map/ppermute | solution.py:53
  9.1 23.5 %collective-permute-start.2 = (f32[2,2,256,128]{3,2,1,0:T(8,128)S(1)}, f32[2,2,256,128]{3,2,1,0:T(8,128)S(1)}, u32[]{:S(2)}, u32[]{:S(2)}) collective-permute-start(f32[2,2,256,128]{3,2,1,0:T(8,128)S(1)} %fusion.105), channel_id=1, source_target_pairs={{2,0},{4,2},{6,4},{8,6},{10,8},{12,10},{14,12},{16,14},{18,16},{20... | collective-permute-start | bytes 1572872 | tf_op jit(solution)/shard_map/ppermute | solution.py:53
  10.4 22.2 %collective-permute-start.3 = (f32[2,2,256,128]{3,2,1,0:T(8,128)S(1)}, f32[2,2,256,128]{3,2,1,0:T(8,128)S(1)}, u32[]{:S(2)}, u32[]{:S(2)}) collective-permute-start(f32[2,2,256,128]{3,2,1,0:T(8,128)S(1)} %fusion.105), channel_id=1, source_target_pairs={{4,0},{6,2},{8,4},{10,6},{12,8},{14,10},{16,12},{18,14},{20,16},{2... | collective-permute-start | bytes 1572872 | tf_op jit(solution)/shard_map/ppermute | solution.py:53
  32.5 2.4 %copy-start.8 = (f32[2,2,256,128]{3,2,1,0:T(8,128)}, f32[2,2,256,128]{3,2,1,0:T(8,128)S(1)}, u32[]{:S(2)}) copy-start(f32[2,2,256,128]{3,2,1,0:T(8,128)S(1)} %collective-permute-done.2) | copy-start | bytes 1572868
  32.5 2.4 %copy-start.10 = (f32[2,2,256,128]{3,2,1,0:T(8,128)}, f32[2,2,256,128]{3,2,1,0:T(8,128)S(1)}, u32[]{:S(2)}) copy-start(f32[2,2,256,128]{3,2,1,0:T(8,128)S(1)} %collective-permute-done.3) | copy-start | bytes 1572868
  32.6 2.1 %copy-start.4 = (f32[2,2,256,128]{3,2,1,0:T(8,128)}, f32[2,2,256,128]{3,2,1,0:T(8,128)S(1)}, u32[]{:S(2)}) copy-start(f32[2,2,256,128]{3,2,1,0:T(8,128)S(1)} %collective-permute-done) | copy-start | bytes 1572868
  32.6 2.2 %copy-start.6 = (f32[2,2,256,128]{3,2,1,0:T(8,128)}, f32[2,2,256,128]{3,2,1,0:T(8,128)S(1)}, u32[]{:S(2)}) copy-start(f32[2,2,256,128]{3,2,1,0:T(8,128)S(1)} %collective-permute-done.1) | copy-start | bytes 1572868
  32.7 2.1 %copy-start.19 = (f32[1,2,256,128]{3,2,1,0:T(8,128)S(1)}, f32[1,2,256,128]{3,2,1,0:T(8,128)}, u32[]{:S(2)}) copy-start(f32[1,2,256,128]{3,2,1,0:T(8,128)} %param.13) | copy-start | bytes 786436
  32.8 4.2 %collective-permute-start.4 = (f32[8,256,128]{2,1,0:T(8,128)S(1)}, f32[8,256,128]{2,1,0:T(8,128)S(1)}, u32[]{:S(2)}, u32[]{:S(2)}) collective-permute-start(f32[8,256,128]{2,1,0:T(8,128)S(1)} %pad_maximum_fusion.7), channel_id=1, source_target_pairs={{0,1},{1,0},{2,3},{3,2},{4,5},{5,4},{6,7},{7,6},{8,9},{9,8},{10,11... | collective-permute-start | bytes 3145736 | tf_op jit(solution)/shard_map/ppermute | solution.py:97
  37.3 1.4 %copy-start.5 = (f32[2,2,256,128]{3,2,1,0:T(8,128)S(1)}, f32[2,2,256,128]{3,2,1,0:T(8,128)}, u32[]{:S(2)}) copy-start(f32[2,2,256,128]{3,2,1,0:T(8,128)} %copy-done.4) | copy-start | bytes 1572868
  37.3 1.9 %copy-start.7 = (f32[2,2,256,128]{3,2,1,0:T(8,128)S(1)}, f32[2,2,256,128]{3,2,1,0:T(8,128)}, u32[]{:S(2)}) copy-start(f32[2,2,256,128]{3,2,1,0:T(8,128)} %copy-done.6) | copy-start | bytes 1572868
  37.3 2.0 %copy-start.9 = (f32[2,2,256,128]{3,2,1,0:T(8,128)S(1)}, f32[2,2,256,128]{3,2,1,0:T(8,128)}, u32[]{:S(2)}) copy-start(f32[2,2,256,128]{3,2,1,0:T(8,128)} %copy-done.8) | copy-start | bytes 1572868
  37.3 2.1 %copy-start.11 = (f32[2,2,256,128]{3,2,1,0:T(8,128)S(1)}, f32[2,2,256,128]{3,2,1,0:T(8,128)}, u32[]{:S(2)}) copy-start(f32[2,2,256,128]{3,2,1,0:T(8,128)} %copy-done.10) | copy-start | bytes 1572868
  37.3 2.3 %copy-start.18 = (f32[2,2,256,128]{3,2,1,0:T(8,128)S(1)}, f32[2,2,256,128]{3,2,1,0:T(8,128)}, u32[]{:S(2)}) copy-start(f32[2,2,256,128]{3,2,1,0:T(8,128)} %copy-done.17) | copy-start | bytes 1572868
  37.5 6.5 %copy-start.2 = (f32[4,256,128]{2,1,0:T(8,128)}, f32[4,256,128]{2,1,0:T(8,128)S(1)}, u32[]{:S(2)}) copy-start(f32[4,256,128]{2,1,0:T(8,128)S(1)} %slice.539) | copy-start | bytes 1572868
  37.5 7.4 %copy-start.15 = (f32[2,256,128]{2,1,0:T(8,128)}, f32[2,256,128]{2,1,0:T(8,128)S(1)}, u32[]{:S(2)}) copy-start(f32[2,256,128]{2,1,0:T(8,128)S(1)} %slice.546) | copy-start | bytes 786436
  46.2 24.4 %collective-permute-start.5 = (f32[2,256,128]{2,1,0:T(8,128)}, f32[2,256,128]{2,1,0:T(8,128)}, u32[]{:S(2)}, u32[]{:S(2)}) collective-permute-start(f32[2,256,128]{2,1,0:T(8,128)} %get-tuple-element.4), channel_id=1, source_target_pairs={{1,4},{0,5},{3,6},{2,7},{5,8},{4,9},{7,10},{6,11},{9,12},{8,13},{1... | collective-permute-start | bytes 786440 | tf_op jit(solution)/shard_map/ppermute | solution.py:53
  59.6 12.0 %collective-permute-start.6 = (f32[2,256,128]{2,1,0:T(8,128)}, f32[2,256,128]{2,1,0:T(8,128)}, u32[]{:S(2)}, u32[]{:S(2)}) collective-permute-start(f32[2,256,128]{2,1,0:T(8,128)} %get-tuple-element.4), channel_id=1, source_target_pairs={{1,2},{0,3},{3,4},{2,5},{5,6},{4,7},{7,8},{6,9},{9,10},{8,11},{11,... | collective-permute-start | bytes 786440 | tf_op jit(solution)/shard_map/ppermute | solution.py:53
  61.6 11.0 %collective-permute-start.7 = (f32[2,256,128]{2,1,0:T(8,128)}, f32[2,256,128]{2,1,0:T(8,128)}, u32[]{:S(2)}, u32[]{:S(2)}) collective-permute-start(f32[2,256,128]{2,1,0:T(8,128)} %get-tuple-element.4), channel_id=1, source_target_pairs={{1,0},{0,1},{3,2},{2,3},{5,4},{4,5},{7,6},{6,7},{9,8},{8,9},{11,10... | collective-permute-start | bytes 786440 | tf_op jit(solution)/shard_map/ppermute | solution.py:53
  61.7 12.8 %collective-permute-start.8 = (f32[2,256,128]{2,1,0:T(8,128)}, f32[2,256,128]{2,1,0:T(8,128)}, u32[]{:S(2)}, u32[]{:S(2)}) collective-permute-start(f32[2,256,128]{2,1,0:T(8,128)} %get-tuple-element.4), channel_id=1, source_target_pairs={{3,0},{2,1},{5,2},{4,3},{7,4},{6,5},{9,6},{8,7},{11,8},{10,9},{13,... | collective-permute-start | bytes 786440 | tf_op jit(solution)/shard_map/ppermute | solution.py:53
  63.0 12.5 %collective-permute-start.9 = (f32[2,256,128]{2,1,0:T(8,128)}, f32[2,256,128]{2,1,0:T(8,128)}, u32[]{:S(2)}, u32[]{:S(2)}) collective-permute-start(f32[2,256,128]{2,1,0:T(8,128)} %get-tuple-element.4), channel_id=1, source_target_pairs={{5,0},{4,1},{7,2},{6,3},{9,4},{8,5},{11,6},{10,7},{13,8},{12,9},{1... | collective-permute-start | bytes 786440 | tf_op jit(solution)/shard_map/ppermute | solution.py:53
  65.1 5.1 %copy-start.21 = (f32[256,128,1]{1,0,2:T(8,128)S(1)}, f32[256,128,1]{1,0,2:T(8,128)}, u32[]{:S(2)}) copy-start(f32[256,128,1]{1,0,2:T(8,128)} %constant.91) | copy-start | bytes 393220
  75.5 1.3 %copy-start.1 = (f32[8,256,128]{2,1,0:T(8,128)S(1)}, f32[8,256,128]{2,1,0:T(8,128)}, u32[]{:S(2)}) copy-start(f32[8,256,128]{2,1,0:T(8,128)} %copy-done) | copy-start | bytes 3145732
  83.3 1.3 %copy-start.22 = (f32[128,64]{1,0:T(8,128)S(1)}, f32[128,64]{1,0:T(8,128)}, u32[]{:S(2)}) copy-start(f32[128,64]{1,0:T(8,128)} %constant.27.clone) | copy-start | bytes 98308
  83.4 1.4 %copy-start.20 = (f32[256,128]{1,0:T(8,128)S(1)}, f32[256,128]{1,0:T(8,128)}, u32[]{:S(2)}) copy-start(f32[256,128]{1,0:T(8,128)} %constant.26.clone) | copy-start | bytes 393220
  85.2 3.6 %collective-permute-start.10 = (f32[1,128,64]{1,2,0:T(8,128)S(1)}, f32[1,128,64]{1,2,0:T(8,128)S(1)}, u32[]{:S(2)}, u32[]{:S(2)}) collective-permute-start(f32[1,128,64]{1,2,0:T(8,128)S(1)} %fusion.4), channel_id=1, source_target_pairs={{0,1},{2,3},{4,5},{6,7},{8,9},{10,11},{12,13},{14,15},{16,17},{18,... | collective-permute-start | bytes 98312 | tf_op jit(solution)/shard_map/ppermute | solution.py:53
  86.5 2.3 %collective-permute-start.12 = (f32[1,128,64]{1,2,0:T(8,128)S(1)}, f32[1,128,64]{1,2,0:T(8,128)S(1)}, u32[]{:S(2)}, u32[]{:S(2)}) collective-permute-start(f32[1,128,64]{1,2,0:T(8,128)S(1)} %fusion.4), channel_id=1, source_target_pairs={{0,3},{2,5},{4,7},{6,9},{8,11},{10,13},{12,15},{14,17},{16,19},{18... | collective-permute-start | bytes 98312 | tf_op jit(solution)/shard_map/ppermute | solution.py:53
  87.2 13.2 %collective-permute-start.11 = (f32[1,128,64]{1,2,0:T(8,128)S(1)}, f32[1,128,64]{1,2,0:T(8,128)S(1)}, u32[]{:S(2)}, u32[]{:S(2)}) collective-permute-start(f32[1,128,64]{1,2,0:T(8,128)S(1)} %fusion.4), channel_id=1, source_target_pairs={{2,1},{4,3},{6,5},{8,7},{10,9},{12,11},{14,13},{16,15},{18,17},{20... | collective-permute-start | bytes 98312 | tf_op jit(solution)/shard_map/ppermute | solution.py:53
  (5 other events, 4.9 us)

commit v7 on v6

--- a/solution.py
+++ b/solution.py
@@ -71,12 +71,28 @@
 
     def prev_pairs(d):
         return [
-            (joint(s + d, (t - 1) % times), joint(s, t))
+            (joint(s + d, t - 1), joint(s, t))
             for s in range(space)
-            for t in range(times)
+            for t in range(1, times)
             if 0 <= s + d < space
         ]
 
+    def chain_pairs(d):
+        return [
+            (joint(s + d, t - 1), joint(s, t))
+            for s in range(space)
+            for t in range(1, times)
+            if 0 <= s + d < space
+        ]
+
+    def first_pairs(d):
+        if d == 0:
+            return None
+        return [(joint(s + d, times - 1), joint(s, 0)) for s in range(space) if 0 <= s + d < space]
+
+    cn = n // 2
+    creach = -(-1 // cn)
+    cdist = [d for d in range(-creach, creach + 1)]
     start = guesses[0]
     distances = [d for d in range(-reach, reach + 1)]
     lo = reach * n - halo
@@ -116,32 +132,30 @@
                 field = jnp.where(m > 0, field, 0.0)
         return field
 
+    got1 = gather_planes(initial, ("space", "tm"), first_pairs, distances)
+    opening = jnp.concatenate([got1[d] for d in distances], axis=0)[lo:hi]
     advanced = fine_prop(field0)
-    payload = jnp.where(me_t == times - 1, initial, advanced)
-    got2 = gather_planes(payload, ("space", "tm"), prev_pairs, distances)
-    relaxed = jnp.concatenate([got2[d] for d in distances], axis=0)[lo:hi]
-    residual = fine_prop(relaxed) - advanced
+    got2 = gather_planes(advanced, ("space", "tm"), prev_pairs, distances)
+    behind = jnp.concatenate([got2[d] for d in distances], axis=0)[lo:hi]
+    early = fine_prop(opening) - advanced
+    early_source = restrict(early)
+    sent_early = None
+    if times == 2:
+        sent_early = gather_planes(early_source, ("space", "tm"), chain_pairs, cdist)
+        behind, sent_early = lax.optimization_barrier((behind, sent_early))
+    late = fine_prop(behind) - advanced
+    first = me_t == 0
+    residual = jnp.where(first, early, late)
 
-    cn = n // 2
-    creach = -(-1 // cn)
-    cdist = [d for d in range(-creach, creach + 1)]
     coarse_k = restrict(conduct[halo - 2 * creach * cn : halo + n + 2 * creach * cn])
     coarse_c = restrict(absorb[halo - 2 * creach * cn : halo + n + 2 * creach * cn])
     ck = coarse_k[creach * cn - 1 : creach * cn + cn + 1]
     cc = coarse_c[creach * cn - 1 : creach * cn + cn + 1]
-    source = restrict(residual)
-
-    def chain_pairs(d):
-        return [
-            (joint(s + d, t - 1), joint(s, t))
-            for s in range(space)
-            for t in range(1, times)
-            if 0 <= s + d < space
-        ]
+    source = jnp.where(first, early_source, restrict(late))
 
     partial_error = source
     for turn in range(times - 1):
-        got3 = gather_planes(partial_error, ("space", "tm"), chain_pairs, cdist)
+        got3 = sent_early if sent_early is not None else gather_planes(partial_error, ("space", "tm"), chain_pairs, cdist)
         behind = jnp.concatenate([got3[d] for d in cdist], axis=0)
         behind = behind[creach * cn - 1 : creach * cn + cn + 1]
         for number in range(COARSE_STEPS):

time: 103 us -> 121 us (1.17)
  the two profiles are of different devices: /device:TPU:1 before, /device:TPU:12 now
where the time goes in v7:
time: 121 us; the launch traced here: 120 us
  waiting for transfers between devices  39.1 us (32%)
  starting transfers between devices  33.3 us (28%)
  other arithmetic  23.6 us (20%)
  local copies, waits for them, and re-layouts  14.5 us (12%)
  matrix products  8.11 us (7%)
  between operations  1.61 us (1%)
    ppermute x16, waiting for transfers between devices, gather_planes(): pieces[d] = lax.ppermute(block, axis_names, pairs_of(d))  39.1 us
    ppermute x16, starting transfers between devices, gather_planes(): pieces[d] = lax.ppermute(block, axis_names, pairs_of(d))  33.2 us
    unnamed x85, local copies, waits for them, and re-layouts  12.6 us
    select_n x8, other arithmetic, fine_prop(): field = jnp.where(m > 0, field, 0.0)  12.2 us
    dot_general x8, matrix products, restrict(): jnp.einsum('Yy,mYZ,Zz->myz', rows, planes, cols, precision=lax.Precision....  6.68 us
    broadcast_in_dim x2, other arithmetic, shards(): return (corrected[None], residual[None])  3.78 us
    reduce_sum x4, other arithmetic, restrict(): planes = field.reshape(first // 2, 2, second, third).sum(axis=1)  3.02 us
  transfers between devices with their start and end apart: 17, of which 4 were waited for; matrix products, arithmetic and copies ran while one was open for 11% of the time, Pallas kernels for 0%

profile of v7, /device:TPU:12, one launch (start us, length us, event | category | flops | bytes accessed | tf_op | source)
XLA Modules:
  0.0 120.3 jit_solution(8775024796713821206)
XLA Ops:
  0.7 1.2 %fusion.142 = f32[2,2,256,128]{3,2,1,0:T(8,128)S(1)} fusion(f32[1,2,256,128]{3,2,1,0:T(8,128)} %param.15, f32[1,2,256,128]{3,2,1,0:T(8,128)} %bitcast.78, f32[1,2,256,128]{3,2,1,0:T(8,128)} %bitcast.80, pred[]{:T(512)S(6)} %eq.8), kind=kLoop, calls=%fused_computation.235 | loop fusion | flops 393216 | bytes 1310721 | tf_op jit(solution)/shard_map/jit(_where)/select_n | solution.py:103
  1.9 3.4 %collective-permute-start = (f32[2,2,256,128]{3,2,1,0:T(8,128)S(1)}, f32[2,2,256,128]{3,2,1,0:T(8,128)S(1)}, u32[]{:S(2)}, u32[]{:S(2)}) collective-permute-start(f32[2,2,256,128]{3,2,1,0:T(8,128)S(1)} %fusion.142), channel_id=1, source_target_pairs={{0,4},{2,6},{4,8},{6,10},{8,12},{10,14},{12,16},{14,18},{16,20},{1... | collective-permute-start | bytes 1572872 | tf_op jit(solution)/shard_map/ppermute | solution.py:53
  5.4 3.4 %collective-permute-start.1 = (f32[2,2,256,128]{3,2,1,0:T(8,128)S(1)}, f32[2,2,256,128]{3,2,1,0:T(8,128)S(1)}, u32[]{:S(2)}, u32[]{:S(2)}) collective-permute-start(f32[2,2,256,128]{3,2,1,0:T(8,128)S(1)} %fusion.142), channel_id=1, source_target_pairs={{0,2},{2,4},{4,6},{6,8},{8,10},{10,12},{12,14},{14,16},{16,18},{18... | collective-permute-start | bytes 1572872 | tf_op jit(solution)/shard_map/ppermute | solution.py:53
  8.8 3.3 %collective-permute-start.2 = (f32[2,2,256,128]{3,2,1,0:T(8,128)S(1)}, f32[2,2,256,128]{3,2,1,0:T(8,128)S(1)}, u32[]{:S(2)}, u32[]{:S(2)}) collective-permute-start(f32[2,2,256,128]{3,2,1,0:T(8,128)S(1)} %fusion.142), channel_id=1, source_target_pairs={{2,0},{4,2},{6,4},{8,6},{10,8},{12,10},{14,12},{16,14},{18,16},{20... | collective-permute-start | bytes 1572872 | tf_op jit(solution)/shard_map/ppermute | solution.py:53
  12.1 3.3 %collective-permute-start.3 = (f32[2,2,256,128]{3,2,1,0:T(8,128)S(1)}, f32[2,2,256,128]{3,2,1,0:T(8,128)S(1)}, u32[]{:S(2)}, u32[]{:S(2)}) collective-permute-start(f32[2,2,256,128]{3,2,1,0:T(8,128)S(1)} %fusion.142), channel_id=1, source_target_pairs={{4,0},{6,2},{8,4},{10,6},{12,8},{14,10},{16,12},{18,14},{20,16},{2... | collective-permute-start | bytes 1572872 | tf_op jit(solution)/shard_map/ppermute | solution.py:53
  15.4 1.3 %collective-permute-start.5 = (f32[2,256,128]{2,1,0:T(8,128)S(1)}, f32[2,256,128]{2,1,0:T(8,128)}, u32[]{:S(2)}, u32[]{:S(2)}) collective-permute-start(f32[2,256,128]{2,1,0:T(8,128)S(1)} %copy-done.23), channel_id=1, source_target_pairs={{1,4},{3,6},{5,8},{7,10},{9,12},{11,14},{13,16},{15,18},{17,20},{1... | collective-permute-start | bytes 786440 | tf_op jit(solution)/shard_map/ppermute | solution.py:53
  17.6 25.2 %collective-permute-done.5 = f32[2,256,128]{2,1,0:T(8,128)} collective-permute-done((f32[2,256,128]{2,1,0:T(8,128)S(1)}, f32[2,256,128]{2,1,0:T(8,128)}, u32[]{:S(2)}, u32[]{:S(2)}) %collective-permute-start.5) | collective-permute-done | bytes 262176 | tf_op jit(solution)/shard_map/ppermute | solution.py:53
  42.9 1.3 %collective-permute-start.6 = (f32[2,256,128]{2,1,0:T(8,128)S(1)}, f32[2,256,128]{2,1,0:T(8,128)}, u32[]{:S(2)}, u32[]{:S(2)}) collective-permute-start(f32[2,256,128]{2,1,0:T(8,128)S(1)} %copy-done.23), channel_id=1, source_target_pairs={{1,2},{3,4},{5,6},{7,8},{9,10},{11,12},{13,14},{15,16},{17,18},{19... | collective-permute-start | bytes 786440 | tf_op jit(solution)/shard_map/ppermute | solution.py:53
  45.2 6.3 %collective-permute-done.6 = f32[2,256,128]{2,1,0:T(8,128)} collective-permute-done((f32[2,256,128]{2,1,0:T(8,128)S(1)}, f32[2,256,128]{2,1,0:T(8,128)}, u32[]{:S(2)}, u32[]{:S(2)}) %collective-permute-start.6) | collective-permute-done | bytes 262176 | tf_op jit(solution)/shard_map/ppermute | solution.py:53
  51.5 1.3 %collective-permute-start.7 = (f32[2,256,128]{2,1,0:T(8,128)S(1)}, f32[2,256,128]{2,1,0:T(8,128)S(1)}, u32[]{:S(2)}, u32[]{:S(2)}) collective-permute-start(f32[2,256,128]{2,1,0:T(8,128)S(1)} %copy-done.23), channel_id=1, source_target_pairs={{3,0},{5,2},{7,4},{9,6},{11,8},{13,10},{15,12},{17,14},{19,16},{21... | collective-permute-start | bytes 786440 | tf_op jit(solution)/shard_map/ppermute | solution.py:53
  53.9 1.3 %collective-permute-start.8 = (f32[2,256,128]{2,1,0:T(8,128)S(1)}, f32[2,256,128]{2,1,0:T(8,128)S(1)}, u32[]{:S(2)}, u32[]{:S(2)}) collective-permute-start(f32[2,256,128]{2,1,0:T(8,128)S(1)} %copy-done.23), channel_id=1, source_target_pairs={{5,0},{7,2},{9,4},{11,6},{13,8},{15,10},{17,12},{19,14},{21,16},{2... | collective-permute-start | bytes 786440 | tf_op jit(solution)/shard_map/ppermute | solution.py:53
  55.5 3.8 %collective-permute-done.7 = f32[2,256,128]{2,1,0:T(8,128)S(1)} collective-permute-done((f32[2,256,128]{2,1,0:T(8,128)S(1)}, f32[2,256,128]{2,1,0:T(8,128)S(1)}, u32[]{:S(2)}, u32[]{:S(2)}) %collective-permute-start.7) | collective-permute-done | bytes 262176 | tf_op jit(solution)/shard_map/ppermute | solution.py:53
  59.2 3.7 %collective-permute-done.8 = f32[2,256,128]{2,1,0:T(8,128)S(1)} collective-permute-done((f32[2,256,128]{2,1,0:T(8,128)S(1)}, f32[2,256,128]{2,1,0:T(8,128)S(1)}, u32[]{:S(2)}, u32[]{:S(2)}) %collective-permute-start.8) | collective-permute-done | bytes 262176 | tf_op jit(solution)/shard_map/ppermute | solution.py:53
  67.9 2.2 %fusion.24 = f32[8,256,128]{2,1,0:T(8,128)S(1)} fusion(f32[8,256,128]{2,1,0:T(8,128)S(1)} %slice_bitcast_fusion.1, f32[2,2,256,128]{3,2,1,0:T(8,128)S(1)} %copy-done.9, f32[2,2,256,128]{3,2,1,0:T(8,128)S(1)} %copy-done.20, f32[2,2,256,128]{3,2,1,0:T(8,128)S(1)} %copy-done.7, f32[2,2,256,128]{3,2,1,0:T(8,128)S(1)} %copy-done.5, ...), kind=kLoop, calls=%fused_computation.78 | loop fusion | flops 10747904 | bytes 9961480 | tf_op jit(solution)/shard_map/jit(_where)/select_n | solution.py:132
  70.1 1.4 %fusion.92 = f32[6,256,128]{2,1,0:T(8,128)S(1)} fusion(f32[6,256,128]{2,1,0:T(8,128)S(1)} %slice.683, f32[8,256,128]{2,1,0:T(8,128)S(1)} %fusion.24, pred[6]{0:T(512)(128)(4,1)S(1)} %slice_compare_fusion.1, f32[10,256,128]{2,1,0:T(8,128)S(1)} %get-tuple-element.16, f32[10,256,128]{2,1,0:T(8,128)S(1)} %get-tuple-element.15, f32[6,256,128]{2,1,0:T(8,128)S(1)} %slice.685), kind=kLoop, calls=%fused_computation.175 | loop fusion | flops 6881280 | bytes 7077894 | tf_op jit(solution)/shard_map/jit(_where)/select_n | solution.py:132
  72.5 3.1 %fusion.40 = f32[8,256,128]{2,1,0:T(8,128)S(1)} fusion(f32[8,256,128]{2,1,0:T(8,128)S(1)} %slice.704, f32[2,256,128]{2,1,0:T(8,128)S(1)} %collective-permute-done.8, f32[2,256,128]{2,1,0:T(8,128)S(1)} %collective-permute-done.7, f32[2,256,128]{2,1,0:T(8,128)S(1)} %copy-done.24, f32[2,256,128]{2,1,0:T(8,128)} %collective-permute-done.6, ...), kind=kLoop, calls=%fused_computation.94 | loop fusion | flops 10747904 | bytes 8650760 | tf_op jit(solution)/shard_map/jit(_where)/select_n | solution.py:132
  75.7 1.4 %fusion.108 = f32[6,256,128]{2,1,0:T(8,128)S(1)} fusion(f32[6,256,128]{2,1,0:T(8,128)S(1)} %slice.705, f32[8,256,128]{2,1,0:T(8,128)S(1)} %fusion.40, pred[6]{0:T(512)(128)(4,1)S(1)} %slice_compare_fusion.1, f32[10,256,128]{2,1,0:T(8,128)S(1)} %get-tuple-element.16, f32[10,256,128]{2,1,0:T(8,128)S(1)} %get-tuple-element.15, f32[6,256,128]{2,1,0:T(8,128)S(1)} %slice.685), kind=kLoop, calls=%fused_computation.191 | loop fusion | flops 6881280 | bytes 7077894 | tf_op jit(solution)/shard_map/jit(_where)/select_n | solution.py:132
  78.2 2.2 %fusion.319 = (f32[256,128]{1,0:T(8,128)}, f32[2,256,128]{2,1,0:T(8,128)}, f32[2,256,128]{2,1,0:T(8,128)}) fusion(f32[2,256,128]{2,1,0:T(8,128)S(1)} %slice.711, f32[10,256,128]{2,1,0:T(8,128)S(1)} %get-tuple-element.16, f32[2,256,128]{2,1,0:T(8,128)S(1)} %slice.699, f32[4,256,128]{2,1,0:T(8,128)S(1)} %fusion.176, ...), kind=kLoop, calls=%fused_computation.463 | loop fusion | flops 4227072 | bytes 3538944 | tf_op jit(solution)/shard_map/reduce_sum | solution.py:32
  80.4 2.1 %collective-permute-start.9 = (f32[2,256,128]{2,1,0:T(8,128)}, f32[2,256,128]{2,1,0:T(8,128)}, u32[]{:S(2)}, u32[]{:S(2)}) collective-permute-start(f32[2,256,128]{2,1,0:T(8,128)} %get-tuple-element.14), channel_id=1, source_target_pairs={{0,5},{2,7},{4,9},{6,11},{8,13},{10,15},{12,17},{14,19},{16,21},{1... | collective-permute-start | bytes 786440 | tf_op jit(solution)/shard_map/ppermute | solution.py:53
  82.5 2.0 %collective-permute-start.10 = (f32[2,256,128]{2,1,0:T(8,128)}, f32[2,256,128]{2,1,0:T(8,128)}, u32[]{:S(2)}, u32[]{:S(2)}) collective-permute-start(f32[2,256,128]{2,1,0:T(8,128)} %get-tuple-element.14), channel_id=1, source_target_pairs={{0,3},{2,5},{4,7},{6,9},{8,11},{10,13},{12,15},{14,17},{16,19},{18... | collective-permute-start | bytes 786440 | tf_op jit(solution)/shard_map/ppermute | solution.py:53
  84.5 2.0 %collective-permute-start.11 = (f32[2,256,128]{2,1,0:T(8,128)}, f32[2,256,128]{2,1,0:T(8,128)}, u32[]{:S(2)}, u32[]{:S(2)}) collective-permute-start(f32[2,256,128]{2,1,0:T(8,128)} %get-tuple-element.14), channel_id=1, source_target_pairs={{0,1},{2,3},{4,5},{6,7},{8,9},{10,11},{12,13},{14,15},{16,17},{18,... | collective-permute-start | bytes 786440 | tf_op jit(solution)/shard_map/ppermute | solution.py:53
  86.5 2.0 %collective-permute-start.12 = (f32[2,256,128]{2,1,0:T(8,128)}, f32[2,256,128]{2,1,0:T(8,128)}, u32[]{:S(2)}, u32[]{:S(2)}) collective-permute-start(f32[2,256,128]{2,1,0:T(8,128)} %get-tuple-element.14), channel_id=1, source_target_pairs={{2,1},{4,3},{6,5},{8,7},{10,9},{12,11},{14,13},{16,15},{18,17},{20... | collective-permute-start | bytes 786440 | tf_op jit(solution)/shard_map/ppermute | solution.py:53
  88.5 2.0 %collective-permute-start.13 = (f32[2,256,128]{2,1,0:T(8,128)}, f32[2,256,128]{2,1,0:T(8,128)}, u32[]{:S(2)}, u32[]{:S(2)}) collective-permute-start(f32[2,256,128]{2,1,0:T(8,128)} %get-tuple-element.14), channel_id=1, source_target_pairs={{4,1},{6,3},{8,5},{10,7},{12,9},{14,11},{16,13},{18,15},{20,17},{2... | collective-permute-start | bytes 786440 | tf_op jit(solution)/shard_map/ppermute | solution.py:53
  91.3 1.6 %fusion.326 = f32[64,3,256]{2,0,1:T(8,128)S(1)} fusion(f32[128,64,1]{1,0,2:T(8,128)} %constant.97, f32[3,256,128]{2,1,0:T(8,128)} %reduce_sum.38), kind=kOutput, calls=%fused_computation.468 | convolution fusion | flops 75497472 | bytes 622592 | tf_op jit(solution)/shard_map/Yy,mYZ,Zz->myz/dot_general | solution.py:35
  92.9 1.2 %fusion.3 = f32[3,128,64]{1,2,0:T(8,128)S(1)} fusion(f32[64,3,256]{2,0,1:T(8,128)S(1)} %fusion.326, f32[256,128,1]{1,0,2:T(8,128)} %constant.98), kind=kOutput, calls=%fused_computation.55 | convolution fusion | flops 75522048 | bytes 425984 | tf_op jit(solution)/shard_map/Yy,mYZ,Zz->myz/dot_general | solution.py:35
  95.7 1.3 %collective-permute-start.14 = (f32[1,128,64]{1,2,0:T(8,128)S(1)}, f32[1,128,64]{1,2,0:T(8,128)S(1)}, u32[]{:S(2)}, u32[]{:S(2)}) collective-permute-start(f32[1,128,64]{1,2,0:T(8,128)S(1)} %fusion.5), channel_id=1, source_target_pairs={{0,3},{2,5},{4,7},{6,9},{8,11},{10,13},{12,15},{14,17},{16,19},{18... | collective-permute-start | bytes 98312 | tf_op jit(solution)/shard_map/ppermute | solution.py:53
  98.0 1.3 %collective-permute-start.15 = (f32[1,128,64]{1,2,0:T(8,128)S(1)}, f32[1,128,64]{1,2,0:T(8,128)S(1)}, u32[]{:S(2)}, u32[]{:S(2)}) collective-permute-start(f32[1,128,64]{1,2,0:T(8,128)S(1)} %fusion.5), channel_id=1, source_target_pairs={{0,1},{2,3},{4,5},{6,7},{8,9},{10,11},{12,13},{14,15},{16,17},{18,... | collective-permute-start | bytes 98312 | tf_op jit(solution)/shard_map/ppermute | solution.py:53
  100.3 1.9 %collective-permute-start.16 = (f32[1,128,64]{1,2,0:T(8,128)S(1)}, f32[1,128,64]{1,2,0:T(8,128)}, u32[]{:S(2)}, u32[]{:S(2)}) collective-permute-start(f32[1,128,64]{1,2,0:T(8,128)S(1)} %fusion.5), channel_id=1, source_target_pairs={{2,1},{4,3},{6,5},{8,7},{10,9},{12,11},{14,13},{16,15},{18,17},{20... | collective-permute-start | bytes 98312 | tf_op jit(solution)/shard_map/ppermute | solution.py:53
  106.6 1.8 %fusion.56 = f32[8,256,128]{2,1,0:T(8,128)S(1)} fusion(f32[8,256,128]{2,1,0:T(8,128)S(1)} %slice.635, f32[10,256,128]{2,1,0:T(8,128)S(1)} %constant_dynamic-update-slice_fusion.10, f32[10,256,128]{2,1,0:T(8,128)S(1)} %get-tuple-element.16, pred[8]{0:T(512)(128)(4,1)S(1)} %slice_compare_fusion, f32[10,256,128]{2,1,0:T(8,128)S(1)} %get-tuple-element.15, ...), kind=kLoop, calls=%fused_computation.110 | loop fusion | flops 9175040 | bytes 9437192 | tf_op jit(solution)/shard_map/jit(_where)/select_n | solution.py:132
  108.4 2.0 %fusion.322 = (f32[6,256,128]{2,1,0:T(8,128)}, f32[6,256,128]{2,1,0:T(8,128)S(1)}) fusion(f32[10,256,128]{2,1,0:T(8,128)S(1)} %get-tuple-element.16, f32[6,256,128]{2,1,0:T(8,128)S(1)} %slice.714, f32[6,256,128]{2,1,0:T(8,128)S(1)} %slice.685, f32[8,256,128]{2,1,0:T(8,128)S(1)} %fusion.56, f32[10,256,128]{2,1,0:T(8,128)S(1)} %get-tuple-element.15, ...), kind=kLoop, calls=%fused_computation.464 | loop fusion | flops 6881280 | bytes 7864326 | tf_op jit(solution)/shard_map/slice | solution.py:22
  112.5 2.1 %select_bitcast_fusion = (f32[1,2,256,128]{3,2,1,0:T(8,128)}, f32[2,256,128]{2,1,0:T(8,128)S(1)}) fusion(f32[2,256,128]{2,1,0:T(8,128)S(1)} %copy-done.25, pred[]{:T(512)S(6)} %eq.9, f32[2,256,128]{2,1,0:T(8,128)} %get-tuple-element.14, f32[2,256,128]{2,1,0:T(8,128)S(1)} %slice.720, f32[10,256,128]{2,1,0:T(8,128)S(1)} %get-tuple-element.16, ...), kind=kLoop, calls=%fused_computation.391 | loop fusion | flops 2359296 | bytes 3145729 | tf_op jit(solution)/shard_map/broadcast_in_dim | solution.py:165
  118.6 1.7 %add_bitcast_fusion = f32[1,2,256,128]{3,2,1,0:T(8,128)} fusion(f32[2,256,128]{2,1,0:T(8,128)} %get-tuple-element.14, f32[256,128]{1,0:T(8,128)S(1)} %fusion.328), kind=kLoop, calls=%fused_computation.392 | loop fusion | flops 65536 | bytes 655360 | tf_op jit(solution)/shard_map/broadcast_in_dim | solution.py:165
  (146 shorter events, 24.6 us)
Async XLA Ops:
  0.6 16.3 %copy-start.15 = (f32[2,256,128]{2,1,0:T(8,128)S(1)}, f32[2,256,128]{2,1,0:T(8,128)}, u32[]{:S(2)}) copy-start(f32[2,256,128]{2,1,0:T(8,128)} %param.16) | copy-start | bytes 786436
  0.6 16.3 %copy-start.16 = (f32[2,256,128]{2,1,0:T(8,128)S(1)}, f32[2,256,128]{2,1,0:T(8,128)}, u32[]{:S(2)}) copy-start(f32[2,256,128]{2,1,0:T(8,128)} %param.17) | copy-start | bytes 786436
  0.6 14.8 %copy-start.23 = (f32[2,256,128]{2,1,0:T(8,128)S(1)}, f32[2,256,128]{2,1,0:T(8,128)}, u32[]{:S(2)}) copy-start(f32[2,256,128]{2,1,0:T(8,128)} %param.14) | copy-start | bytes 786436
  1.9 53.3 %copy-start.19 = (f32[2,2,256,128]{3,2,1,0:T(8,128)}, f32[2,2,256,128]{3,2,1,0:T(8,128)S(1)}, u32[]{:S(2)}) copy-start(f32[2,2,256,128]{3,2,1,0:T(8,128)S(1)} %fusion.142) | copy-start | bytes 1572868
  1.9 53.3 %collective-permute-start = (f32[2,2,256,128]{3,2,1,0:T(8,128)S(1)}, f32[2,2,256,128]{3,2,1,0:T(8,128)S(1)}, u32[]{:S(2)}, u32[]{:S(2)}) collective-permute-start(f32[2,2,256,128]{3,2,1,0:T(8,128)S(1)} %fusion.142), channel_id=1, source_target_pairs={{0,4},{2,6},{4,8},{6,10},{8,12},{10,14},{12,16},{14,18},{16,20},{1... | collective-permute-start | bytes 1572872 | tf_op jit(solution)/shard_map/ppermute | solution.py:53
  5.4 49.9 %collective-permute-start.1 = (f32[2,2,256,128]{3,2,1,0:T(8,128)S(1)}, f32[2,2,256,128]{3,2,1,0:T(8,128)S(1)}, u32[]{:S(2)}, u32[]{:S(2)}) collective-permute-start(f32[2,2,256,128]{3,2,1,0:T(8,128)S(1)} %fusion.142), channel_id=1, source_target_pairs={{0,2},{2,4},{4,6},{6,8},{8,10},{10,12},{12,14},{14,16},{16,18},{18... | collective-permute-start | bytes 1572872 | tf_op jit(solution)/shard_map/ppermute | solution.py:53
  8.8 45.1 %collective-permute-start.2 = (f32[2,2,256,128]{3,2,1,0:T(8,128)S(1)}, f32[2,2,256,128]{3,2,1,0:T(8,128)S(1)}, u32[]{:S(2)}, u32[]{:S(2)}) collective-permute-start(f32[2,2,256,128]{3,2,1,0:T(8,128)S(1)} %fusion.142), channel_id=1, source_target_pairs={{2,0},{4,2},{6,4},{8,6},{10,8},{12,10},{14,12},{16,14},{18,16},{20... | collective-permute-start | bytes 1572872 | tf_op jit(solution)/shard_map/ppermute | solution.py:53
  12.1 43.0 %collective-permute-start.3 = (f32[2,2,256,128]{3,2,1,0:T(8,128)S(1)}, f32[2,2,256,128]{3,2,1,0:T(8,128)S(1)}, u32[]{:S(2)}, u32[]{:S(2)}) collective-permute-start(f32[2,2,256,128]{3,2,1,0:T(8,128)S(1)} %fusion.142), channel_id=1, source_target_pairs={{4,0},{6,2},{8,4},{10,6},{12,8},{14,10},{16,12},{18,14},{20,16},{2... | collective-permute-start | bytes 1572872 | tf_op jit(solution)/shard_map/ppermute | solution.py:53
  15.4 27.4 %collective-permute-start.5 = (f32[2,256,128]{2,1,0:T(8,128)S(1)}, f32[2,256,128]{2,1,0:T(8,128)}, u32[]{:S(2)}, u32[]{:S(2)}) collective-permute-start(f32[2,256,128]{2,1,0:T(8,128)S(1)} %copy-done.23), channel_id=1, source_target_pairs={{1,4},{3,6},{5,8},{7,10},{9,12},{11,14},{13,16},{15,18},{17,20},{1... | collective-permute-start | bytes 786440 | tf_op jit(solution)/shard_map/ppermute | solution.py:53
  42.9 8.7 %collective-permute-start.6 = (f32[2,256,128]{2,1,0:T(8,128)S(1)}, f32[2,256,128]{2,1,0:T(8,128)}, u32[]{:S(2)}, u32[]{:S(2)}) collective-permute-start(f32[2,256,128]{2,1,0:T(8,128)S(1)} %copy-done.23), channel_id=1, source_target_pairs={{1,2},{3,4},{5,6},{7,8},{9,10},{11,12},{13,14},{15,16},{17,18},{19... | collective-permute-start | bytes 786440 | tf_op jit(solution)/shard_map/ppermute | solution.py:53
  51.5 7.7 %collective-permute-start.7 = (f32[2,256,128]{2,1,0:T(8,128)S(1)}, f32[2,256,128]{2,1,0:T(8,128)S(1)}, u32[]{:S(2)}, u32[]{:S(2)}) collective-permute-start(f32[2,256,128]{2,1,0:T(8,128)S(1)} %copy-done.23), channel_id=1, source_target_pairs={{3,0},{5,2},{7,4},{9,6},{11,8},{13,10},{15,12},{17,14},{19,16},{21... | collective-permute-start | bytes 786440 | tf_op jit(solution)/shard_map/ppermute | solution.py:53
  53.8 10.2 %copy-start.8 = (f32[2,2,256,128]{3,2,1,0:T(8,128)}, f32[2,2,256,128]{3,2,1,0:T(8,128)S(1)}, u32[]{:S(2)}) copy-start(f32[2,2,256,128]{3,2,1,0:T(8,128)S(1)} %collective-permute-done.2) | copy-start | bytes 1572868
  53.9 9.1 %collective-permute-start.8 = (f32[2,256,128]{2,1,0:T(8,128)S(1)}, f32[2,256,128]{2,1,0:T(8,128)S(1)}, u32[]{:S(2)}, u32[]{:S(2)}) collective-permute-start(f32[2,256,128]{2,1,0:T(8,128)S(1)} %copy-done.23), channel_id=1, source_target_pairs={{5,0},{7,2},{9,4},{11,6},{13,8},{15,10},{17,12},{19,14},{21,16},{2... | collective-permute-start | bytes 786440 | tf_op jit(solution)/shard_map/ppermute | solution.py:53
  55.2 9.0 %copy-start.10 = (f32[2,2,256,128]{3,2,1,0:T(8,128)}, f32[2,2,256,128]{3,2,1,0:T(8,128)S(1)}, u32[]{:S(2)}) copy-start(f32[2,2,256,128]{3,2,1,0:T(8,128)S(1)} %collective-permute-done.3) | copy-start | bytes 1572868
  55.2 7.8 %copy-start.4 = (f32[2,2,256,128]{3,2,1,0:T(8,128)}, f32[2,2,256,128]{3,2,1,0:T(8,128)S(1)}, u32[]{:S(2)}) copy-start(f32[2,2,256,128]{3,2,1,0:T(8,128)S(1)} %collective-permute-done) | copy-start | bytes 1572868
  55.3 7.9 %copy-start.6 = (f32[2,2,256,128]{3,2,1,0:T(8,128)}, f32[2,2,256,128]{3,2,1,0:T(8,128)S(1)}, u32[]{:S(2)}) copy-start(f32[2,2,256,128]{3,2,1,0:T(8,128)S(1)} %collective-permute-done.1) | copy-start | bytes 1572868
  55.4 8.9 %collective-permute-start.4 = (f32[8,256,128]{2,1,0:T(8,128)S(1)}, f32[8,256,128]{2,1,0:T(8,128)S(1)}, u32[]{:S(2)}, u32[]{:S(2)}) collective-permute-start(f32[8,256,128]{2,1,0:T(8,128)S(1)} %pad_maximum_fusion.7), channel_id=1, source_target_pairs={{0,1},{1,0},{2,3},{3,2},{4,5},{5,4},{6,7},{7,6},{8,9},{9,8},{10,11... | collective-permute-start | bytes 3145736 | tf_op jit(solution)/shard_map/ppermute | solution.py:113
  65.5 6.9 %copy-start = (f32[8,256,128]{2,1,0:T(8,128)}, f32[8,256,128]{2,1,0:T(8,128)S(1)}, u32[]{:S(2)}) copy-start(f32[8,256,128]{2,1,0:T(8,128)S(1)} %slice.680) | copy-start | bytes 3145732
  65.7 11.4 %copy-start.2 = (f32[4,256,128]{2,1,0:T(8,128)}, f32[4,256,128]{2,1,0:T(8,128)S(1)}, u32[]{:S(2)}) copy-start(f32[4,256,128]{2,1,0:T(8,128)S(1)} %slice.692) | copy-start | bytes 1572868
  65.7 12.2 %copy-start.17 = (f32[2,256,128]{2,1,0:T(8,128)}, f32[2,256,128]{2,1,0:T(8,128)S(1)}, u32[]{:S(2)}) copy-start(f32[2,256,128]{2,1,0:T(8,128)S(1)} %slice.699) | copy-start | bytes 786436
  72.4 3.2 %copy-start.12 = (f32[4,256,128]{2,1,0:T(8,128)}, f32[4,256,128]{2,1,0:T(8,128)S(1)}, u32[]{:S(2)}) copy-start(f32[4,256,128]{2,1,0:T(8,128)S(1)} %fusion.160) | copy-start | bytes 1572868
  80.4 14.9 %copy-start.21 = (f32[256,128]{1,0:T(8,128)S(1)}, f32[256,128]{1,0:T(8,128)}, u32[]{:S(2)}) copy-start(f32[256,128]{1,0:T(8,128)} %constant.26.clone) | copy-start | bytes 393220
  80.4 15.3 %collective-permute-start.9 = (f32[2,256,128]{2,1,0:T(8,128)}, f32[2,256,128]{2,1,0:T(8,128)}, u32[]{:S(2)}, u32[]{:S(2)}) collective-permute-start(f32[2,256,128]{2,1,0:T(8,128)} %get-tuple-element.14), channel_id=1, source_target_pairs={{0,5},{2,7},{4,9},{6,11},{8,13},{10,15},{12,17},{14,19},{16,21},{1... | collective-permute-start | bytes 786440 | tf_op jit(solution)/shard_map/ppermute | solution.py:53
  82.5 15.5 %collective-permute-start.10 = (f32[2,256,128]{2,1,0:T(8,128)}, f32[2,256,128]{2,1,0:T(8,128)}, u32[]{:S(2)}, u32[]{:S(2)}) collective-permute-start(f32[2,256,128]{2,1,0:T(8,128)} %get-tuple-element.14), channel_id=1, source_target_pairs={{0,3},{2,5},{4,7},{6,9},{8,11},{10,13},{12,15},{14,17},{16,19},{18... | collective-permute-start | bytes 786440 | tf_op jit(solution)/shard_map/ppermute | solution.py:53
  84.5 15.8 %collective-permute-start.11 = (f32[2,256,128]{2,1,0:T(8,128)}, f32[2,256,128]{2,1,0:T(8,128)}, u32[]{:S(2)}, u32[]{:S(2)}) collective-permute-start(f32[2,256,128]{2,1,0:T(8,128)} %get-tuple-element.14), channel_id=1, source_target_pairs={{0,1},{2,3},{4,5},{6,7},{8,9},{10,11},{12,13},{14,15},{16,17},{18,... | collective-permute-start | bytes 786440 | tf_op jit(solution)/shard_map/ppermute | solution.py:53
  86.5 16.7 %collective-permute-start.12 = (f32[2,256,128]{2,1,0:T(8,128)}, f32[2,256,128]{2,1,0:T(8,128)}, u32[]{:S(2)}, u32[]{:S(2)}) collective-permute-start(f32[2,256,128]{2,1,0:T(8,128)} %get-tuple-element.14), channel_id=1, source_target_pairs={{2,1},{4,3},{6,5},{8,7},{10,9},{12,11},{14,13},{16,15},{18,17},{20... | collective-permute-start | bytes 786440 | tf_op jit(solution)/shard_map/ppermute | solution.py:53
  88.5 15.7 %collective-permute-start.13 = (f32[2,256,128]{2,1,0:T(8,128)}, f32[2,256,128]{2,1,0:T(8,128)}, u32[]{:S(2)}, u32[]{:S(2)}) collective-permute-start(f32[2,256,128]{2,1,0:T(8,128)} %get-tuple-element.14), channel_id=1, source_target_pairs={{4,1},{6,3},{8,5},{10,7},{12,9},{14,11},{16,13},{18,15},{20,17},{2... | collective-permute-start | bytes 786440 | tf_op jit(solution)/shard_map/ppermute | solution.py:53
  94.1 10.1 %copy-start.29 = (f32[3,128,64]{1,2,0:T(8,128)}, f32[3,128,64]{1,2,0:T(8,128)S(1)}, u32[]{:S(2)}) copy-start(f32[3,128,64]{1,2,0:T(8,128)S(1)} %fusion.3) | copy-start | bytes 294916
  95.7 9.5 %copy-start.32 = (f32[1,128,64]{1,2,0:T(8,128)}, f32[1,128,64]{1,2,0:T(8,128)S(1)}, u32[]{:S(2)}) copy-start(f32[1,128,64]{1,2,0:T(8,128)S(1)} %fusion.5) | copy-start | bytes 98308
  95.7 9.5 %collective-permute-start.14 = (f32[1,128,64]{1,2,0:T(8,128)S(1)}, f32[1,128,64]{1,2,0:T(8,128)S(1)}, u32[]{:S(2)}, u32[]{:S(2)}) collective-permute-start(f32[1,128,64]{1,2,0:T(8,128)S(1)} %fusion.5), channel_id=1, source_target_pairs={{0,3},{2,5},{4,7},{6,9},{8,11},{10,13},{12,15},{14,17},{16,19},{18... | collective-permute-start | bytes 98312 | tf_op jit(solution)/shard_map/ppermute | solution.py:53
  98.0 7.3 %collective-permute-start.15 = (f32[1,128,64]{1,2,0:T(8,128)S(1)}, f32[1,128,64]{1,2,0:T(8,128)S(1)}, u32[]{:S(2)}, u32[]{:S(2)}) collective-permute-start(f32[1,128,64]{1,2,0:T(8,128)S(1)} %fusion.5), channel_id=1, source_target_pairs={{0,1},{2,3},{4,5},{6,7},{8,9},{10,11},{12,13},{14,15},{16,17},{18,... | collective-permute-start | bytes 98312 | tf_op jit(solution)/shard_map/ppermute | solution.py:53
  100.3 6.2 %collective-permute-start.16 = (f32[1,128,64]{1,2,0:T(8,128)S(1)}, f32[1,128,64]{1,2,0:T(8,128)}, u32[]{:S(2)}, u32[]{:S(2)}) collective-permute-start(f32[1,128,64]{1,2,0:T(8,128)S(1)} %fusion.5), channel_id=1, source_target_pairs={{2,1},{4,3},{6,5},{8,7},{10,9},{12,11},{14,13},{16,15},{18,17},{20... | collective-permute-start | bytes 98312 | tf_op jit(solution)/shard_map/ppermute | solution.py:53
  (24 other events, 37.4 us)

commit v8 on v6

--- a/solution.py
+++ b/solution.py
@@ -117,7 +117,7 @@
         return field
 
     advanced = fine_prop(field0)
-    payload = jnp.where(me_t == times - 1, initial, advanced)
+    payload = lax.cond(me_t == times - 1, lambda: initial, lambda: advanced)
     got2 = gather_planes(payload, ("space", "tm"), prev_pairs, distances)
     relaxed = jnp.concatenate([got2[d] for d in distances], axis=0)[lo:hi]
     residual = fine_prop(relaxed) - advanced

time: 103 us -> 103 us (level)
  the two profiles are of different devices: /device:TPU:1 before, /device:TPU:5 now
where the time goes in v8:
time: 103 us
  waiting for transfers between devices  39.6 us (38%)
  starting transfers between devices  27.9 us (27%)
  other arithmetic  17.4 us (17%)
  local copies, waits for them, and re-layouts  11.3 us (11%)
  matrix products  5.1 us (5%)
  between operations  1.29 us (1%)
    ppermute x12, waiting for transfers between devices, gather_planes(): pieces[d] = lax.ppermute(block, axis_names, pairs_of(d))  37.7 us
    ppermute x12, starting transfers between devices, gather_planes(): pieces[d] = lax.ppermute(block, axis_names, pairs_of(d))  25.8 us
    select_n x5, other arithmetic, fine_prop(): field = jnp.where(m > 0, field, 0.0)  8.36 us
    unnamed x55, local copies, waits for them, and re-layouts  8.03 us
    dot_general x6, matrix products, restrict(): jnp.einsum('Yy,mYZ,Zz->myz', rows, planes, cols, precision=lax.Precision....  4.43 us
    reduce_sum x3, other arithmetic, restrict(): planes = field.reshape(first // 2, 2, second, third).sum(axis=1)  3.95 us
    ppermute x1, starting transfers between devices, shards(): theirs_rim = lax.ppermute(rim, 'tm', partner)  2.18 us
  transfers between devices with their start and end apart: 13, of which 6 were waited for; matrix products, arithmetic and copies ran while one was open for 11% of the time, Pallas kernels for 0%

profile of v8, /device:TPU:5, one launch (start us, length us, event | category | flops | bytes accessed | tf_op | source)
XLA Modules:
  0.0 102.6 jit_solution(17758831801770811)
XLA Ops:
  0.7 1.2 %fusion.105 = f32[2,2,256,128]{3,2,1,0:T(8,128)S(1)} fusion(f32[1,2,256,128]{3,2,1,0:T(8,128)} %param.15, f32[1,2,256,128]{3,2,1,0:T(8,128)} %bitcast.67, f32[1,2,256,128]{3,2,1,0:T(8,128)} %bitcast.69, pred[]{:T(512)S(6)} %eq.8), kind=kLoop, calls=%fused_computation.179 | loop fusion | flops 393216 | bytes 1310721 | tf_op jit(solution)/shard_map/jit(_where)/select_n | solution.py:87
  1.9 3.1 %collective-permute-start = (f32[2,2,256,128]{3,2,1,0:T(8,128)S(1)}, f32[2,2,256,128]{3,2,1,0:T(8,128)S(1)}, u32[]{:S(2)}, u32[]{:S(2)}) collective-permute-start(f32[2,2,256,128]{3,2,1,0:T(8,128)S(1)} %fusion.105), channel_id=1, source_target_pairs={{0,4},{2,6},{4,8},{6,10},{8,12},{10,14},{12,16},{14,18},{16,20},{1... | collective-permute-start | bytes 1572872 | tf_op jit(solution)/shard_map/ppermute | solution.py:53
  5.0 3.1 %collective-permute-start.1 = (f32[2,2,256,128]{3,2,1,0:T(8,128)S(1)}, f32[2,2,256,128]{3,2,1,0:T(8,128)S(1)}, u32[]{:S(2)}, u32[]{:S(2)}) collective-permute-start(f32[2,2,256,128]{3,2,1,0:T(8,128)S(1)} %fusion.105), channel_id=1, source_target_pairs={{0,2},{2,4},{4,6},{6,8},{8,10},{10,12},{12,14},{14,16},{16,18},{18... | collective-permute-start | bytes 1572872 | tf_op jit(solution)/shard_map/ppermute | solution.py:53
  8.2 3.1 %collective-permute-start.2 = (f32[2,2,256,128]{3,2,1,0:T(8,128)S(1)}, f32[2,2,256,128]{3,2,1,0:T(8,128)S(1)}, u32[]{:S(2)}, u32[]{:S(2)}) collective-permute-start(f32[2,2,256,128]{3,2,1,0:T(8,128)S(1)} %fusion.105), channel_id=1, source_target_pairs={{2,0},{4,2},{6,4},{8,6},{10,8},{12,10},{14,12},{16,14},{18,16},{20... | collective-permute-start | bytes 1572872 | tf_op jit(solution)/shard_map/ppermute | solution.py:53
  11.2 1.9 %collective-permute-start.3 = (f32[2,2,256,128]{3,2,1,0:T(8,128)S(1)}, f32[2,2,256,128]{3,2,1,0:T(8,128)S(1)}, u32[]{:S(2)}, u32[]{:S(2)}) collective-permute-start(f32[2,2,256,128]{3,2,1,0:T(8,128)S(1)} %fusion.105), channel_id=1, source_target_pairs={{4,0},{6,2},{8,4},{10,6},{12,8},{14,10},{16,12},{18,14},{20,16},{2... | collective-permute-start | bytes 1572872 | tf_op jit(solution)/shard_map/ppermute | solution.py:53
  13.4 16.3 %collective-permute-done.2 = f32[2,2,256,128]{3,2,1,0:T(8,128)S(1)} collective-permute-done((f32[2,2,256,128]{3,2,1,0:T(8,128)S(1)}, f32[2,2,256,128]{3,2,1,0:T(8,128)S(1)}, u32[]{:S(2)}, u32[]{:S(2)}) %collective-permute-start.2) | collective-permute-done | bytes 524320 | tf_op jit(solution)/shard_map/ppermute | solution.py:53
  29.7 11.0 %collective-permute-done.3 = f32[2,2,256,128]{3,2,1,0:T(8,128)S(1)} collective-permute-done((f32[2,2,256,128]{3,2,1,0:T(8,128)S(1)}, f32[2,2,256,128]{3,2,1,0:T(8,128)S(1)}, u32[]{:S(2)}, u32[]{:S(2)}) %collective-permute-start.3) | collective-permute-done | bytes 524320 | tf_op jit(solution)/shard_map/ppermute | solution.py:53
  40.9 2.2 %collective-permute-start.4 = (f32[8,256,128]{2,1,0:T(8,128)S(1)}, f32[8,256,128]{2,1,0:T(8,128)S(1)}, u32[]{:S(2)}, u32[]{:S(2)}) collective-permute-start(f32[8,256,128]{2,1,0:T(8,128)S(1)} %pad_maximum_fusion.7), channel_id=1, source_target_pairs={{0,1},{1,0},{2,3},{3,2},{4,5},{5,4},{6,7},{7,6},{8,9},{9,8},{10,11... | collective-permute-start | bytes 3145736 | tf_op jit(solution)/shard_map/ppermute | solution.py:97
  43.5 1.8 %collective-permute-done.4 = f32[8,256,128]{2,1,0:T(8,128)S(1)} collective-permute-done((f32[8,256,128]{2,1,0:T(8,128)S(1)}, f32[8,256,128]{2,1,0:T(8,128)S(1)}, u32[]{:S(2)}, u32[]{:S(2)}) %collective-permute-start.4) | collective-permute-done | bytes 1048608 | tf_op jit(solution)/shard_map/ppermute | solution.py:97
  48.1 2.2 %fusion.22 = f32[8,256,128]{2,1,0:T(8,128)S(1)} fusion(f32[8,256,128]{2,1,0:T(8,128)S(1)} %slice_bitcast_fusion.1, f32[2,2,256,128]{3,2,1,0:T(8,128)S(1)} %copy-done.9, f32[2,2,256,128]{3,2,1,0:T(8,128)S(1)} %copy-done.19, f32[2,2,256,128]{3,2,1,0:T(8,128)S(1)} %copy-done.7, f32[2,2,256,128]{3,2,1,0:T(8,128)S(1)} %copy-done.5, ...), kind=kLoop, calls=%fused_computation.63 | loop fusion | flops 10747904 | bytes 8912904 | tf_op jit(solution)/shard_map/jit(_where)/select_n | solution.py:116
  50.4 2.0 %fusion.245 = (f32[6,256,128]{2,1,0:T(8,128)}, f32[6,256,128]{2,1,0:T(8,128)S(1)}) fusion(f32[10,256,128]{2,1,0:T(8,128)S(1)} %get-tuple-element.13, f32[6,256,128]{2,1,0:T(8,128)S(1)} %slice.530, f32[6,256,128]{2,1,0:T(8,128)S(1)} %slice.532, f32[8,256,128]{2,1,0:T(8,128)S(1)} %fusion.22, f32[10,256,128]{2,1,0:T(8,128)S(1)} %get-tuple-element.12, ...), kind=kLoop, calls=%fused_computation.360 | loop fusion | flops 6881280 | bytes 7077894 | tf_op jit(solution)/shard_map/slice | solution.py:22
  54.4 1.7 %conditional.1 = (f32[2,256,128]{2,1,0:T(8,128)}) conditional(s32[]{:T(128)} %convert_element_type.30, f32[2,256,128]{2,1,0:T(8,128)S(1)} %fusion.172, (f32[2,256,128]{2,1,0:T(8,128)}) %tuple.15), branch_computations={%region_0.1_spmd, %region_1.2_spmd} | conditional | bytes 524296 | solution.py:120
  54.4 1.7 %copy.20 = f32[2,256,128]{2,1,0:T(8,128)} copy(f32[2,256,128]{2,1,0:T(8,128)} %get-tuple-element.9) | data formatting | bytes 524288 | tf_op jit(solution)/shard_map/cond
  56.1 1.9 %collective-permute-start.5 = (f32[2,256,128]{2,1,0:T(8,128)}, f32[2,256,128]{2,1,0:T(8,128)}, u32[]{:S(2)}, u32[]{:S(2)}) collective-permute-start(f32[2,256,128]{2,1,0:T(8,128)} %get-tuple-element.18), channel_id=1, source_target_pairs={{1,4},{0,5},{3,6},{2,7},{5,8},{4,9},{7,10},{6,11},{9,12},{8,13},{1... | collective-permute-start | bytes 786440 | tf_op jit(solution)/shard_map/ppermute | solution.py:53
  58.0 3.3 %collective-permute-start.6 = (f32[2,256,128]{2,1,0:T(8,128)}, f32[2,256,128]{2,1,0:T(8,128)}, u32[]{:S(2)}, u32[]{:S(2)}) collective-permute-start(f32[2,256,128]{2,1,0:T(8,128)} %get-tuple-element.18), channel_id=1, source_target_pairs={{1,2},{0,3},{3,4},{2,5},{5,6},{4,7},{7,8},{6,9},{9,10},{8,11},{11,... | collective-permute-start | bytes 786440 | tf_op jit(solution)/shard_map/ppermute | solution.py:53
  61.4 3.4 %collective-permute-start.8 = (f32[2,256,128]{2,1,0:T(8,128)}, f32[2,256,128]{2,1,0:T(8,128)}, u32[]{:S(2)}, u32[]{:S(2)}) collective-permute-start(f32[2,256,128]{2,1,0:T(8,128)} %get-tuple-element.18), channel_id=1, source_target_pairs={{3,0},{2,1},{5,2},{4,3},{7,4},{6,5},{9,6},{8,7},{11,8},{10,9},{13,... | collective-permute-start | bytes 786440 | tf_op jit(solution)/shard_map/ppermute | solution.py:53
  64.8 1.9 %collective-permute-start.9 = (f32[2,256,128]{2,1,0:T(8,128)}, f32[2,256,128]{2,1,0:T(8,128)}, u32[]{:S(2)}, u32[]{:S(2)}) collective-permute-start(f32[2,256,128]{2,1,0:T(8,128)} %get-tuple-element.18), channel_id=1, source_target_pairs={{5,0},{4,1},{7,2},{6,3},{9,4},{8,5},{11,6},{10,7},{13,8},{12,9},{1... | collective-permute-start | bytes 786440 | tf_op jit(solution)/shard_map/ppermute | solution.py:53
  66.8 2.0 %reduce_sum.29 = f32[3,256,128]{2,1,0:T(8,128)} reduce(f32[3,2,256,128]{3,2,1,0:T(8,128)} %bitcast.66, f32[]{:T(128)} %constant.20.clone.1), dimensions={1}, to_apply=%region_4.5 | reduce | flops 98304 | bytes 1179652 | tf_op jit(solution)/shard_map/reduce_sum | solution.py:32
  69.6 1.6 %fusion.249 = f32[64,3,256]{2,0,1:T(8,128)S(1)} fusion(f32[128,64,1]{1,0,2:T(8,128)} %constant.90, f32[3,256,128]{2,1,0:T(8,128)} %reduce_sum.29), kind=kOutput, calls=%fused_computation.364 | convolution fusion | flops 75497472 | bytes 622592 | tf_op jit(solution)/shard_map/Yy,mYZ,Zz->myz/dot_general | solution.py:35
  71.1 1.6 %fusion.248 = f32[64,3,256]{2,0,1:T(8,128)S(1)} fusion(f32[128,64,1]{1,0,2:T(8,128)} %constant.90, f32[3,256,128]{2,1,0:T(8,128)} %reduce_sum.28), kind=kOutput, calls=%fused_computation.363 | convolution fusion | flops 75497472 | bytes 622592 | tf_op jit(solution)/shard_map/Yy,mYZ,Zz->myz/dot_general | solution.py:35
  74.0 1.0 constant_dynamic-update-slice_fusion.8
  75.0 1.0 constant_dynamic-update-slice_fusion.7
  77.0 5.9 %collective-permute-done.9 = f32[2,256,128]{2,1,0:T(8,128)} collective-permute-done((f32[2,256,128]{2,1,0:T(8,128)}, f32[2,256,128]{2,1,0:T(8,128)}, u32[]{:S(2)}, u32[]{:S(2)}) %collective-permute-start.9) | collective-permute-done | bytes 262176 | tf_op jit(solution)/shard_map/ppermute | solution.py:53
  84.0 3.3 %fusion.38 = f32[8,256,128]{2,1,0:T(8,128)S(1)} fusion(f32[8,256,128]{2,1,0:T(8,128)S(1)} %slice.551, f32[2,256,128]{2,1,0:T(8,128)} %collective-permute-done.9, f32[2,256,128]{2,1,0:T(8,128)} %collective-permute-done.8, f32[2,256,128]{2,1,0:T(8,128)} %collective-permute-done.7, f32[2,256,128]{2,1,0:T(8,128)} %collective-permute-done.6, ...), kind=kLoop, calls=%fused_computation.79 | loop fusion | flops 10747904 | bytes 7602184 | tf_op jit(solution)/shard_map/jit(_where)/select_n | solution.py:116
  87.3 1.2 %fusion.90 = f32[6,256,128]{2,1,0:T(8,128)S(1)} fusion(f32[6,256,128]{2,1,0:T(8,128)S(1)} %slice.552, f32[8,256,128]{2,1,0:T(8,128)S(1)} %fusion.38, pred[6]{0:T(512)(128)(4,1)S(1)} %slice_compare_fusion.1, f32[6,256,128]{2,1,0:T(8,128)S(1)} %slice.532, f32[10,256,128]{2,1,0:T(8,128)S(1)} %get-tuple-element.12, f32[10,256,128]{2,1,0:T(8,128)S(1)} %get-tuple-element.13), kind=kLoop, calls=%fused_computation.156 | loop fusion | flops 6881280 | bytes 6291462 | tf_op jit(solution)/shard_map/jit(_where)/select_n | solution.py:116
  88.6 1.0 copy-done.3
  90.6 1.2 %fusion.243 = (f32[256,128]{1,0:T(8,128)S(1)}, f32[2,256,128]{2,1,0:T(8,128)}) fusion(f32[2,256,128]{2,1,0:T(8,128)S(1)} %copy-done.13, f32[2,256,128]{2,1,0:T(8,128)S(1)} %slice.558, f32[10,256,128]{2,1,0:T(8,128)S(1)} %get-tuple-element.13, f32[2,256,128]{2,1,0:T(8,128)S(1)} %copy-done.17, f32[4,256,128]{2,1,0:T(8,128)S(1)} %fusion.139, ...), kind=kLoop, calls=%fused_computation.359 | loop fusion | flops 2326528 | bytes 2490368 | tf_op jit(solution)/shard_map/reduce_sum | solution.py:32
  92.4 1.3 %collective-permute-start.10 = (f32[1,128,64]{1,2,0:T(8,128)S(1)}, f32[1,128,64]{1,2,0:T(8,128)S(1)}, u32[]{:S(2)}, u32[]{:S(2)}) collective-permute-start(f32[1,128,64]{1,2,0:T(8,128)S(1)} %fusion.4), channel_id=1, source_target_pairs={{0,1},{2,3},{4,5},{6,7},{8,9},{10,11},{12,13},{14,15},{16,17},{18,... | collective-permute-start | bytes 98312 | tf_op jit(solution)/shard_map/ppermute | solution.py:53
  93.7 1.3 %collective-permute-start.11 = (f32[1,128,64]{1,2,0:T(8,128)S(1)}, f32[1,128,64]{1,2,0:T(8,128)S(1)}, u32[]{:S(2)}, u32[]{:S(2)}) collective-permute-start(f32[1,128,64]{1,2,0:T(8,128)S(1)} %fusion.4), channel_id=1, source_target_pairs={{2,1},{4,3},{6,5},{8,7},{10,9},{12,11},{14,13},{16,15},{18,17},{20... | collective-permute-start | bytes 98312 | tf_op jit(solution)/shard_map/ppermute | solution.py:53
  95.0 1.3 %collective-permute-start.12 = (f32[1,128,64]{1,2,0:T(8,128)S(1)}, f32[1,128,64]{1,2,0:T(8,128)S(1)}, u32[]{:S(2)}, u32[]{:S(2)}) collective-permute-start(f32[1,128,64]{1,2,0:T(8,128)S(1)} %fusion.4), channel_id=1, source_target_pairs={{0,3},{2,5},{4,7},{6,9},{8,11},{10,13},{12,15},{14,17},{16,19},{18... | collective-permute-start | bytes 98312 | tf_op jit(solution)/shard_map/ppermute | solution.py:53
  96.7 2.3 %collective-permute-done.11 = f32[1,128,64]{1,2,0:T(8,128)S(1)} collective-permute-done((f32[1,128,64]{1,2,0:T(8,128)S(1)}, f32[1,128,64]{1,2,0:T(8,128)S(1)}, u32[]{:S(2)}, u32[]{:S(2)}) %collective-permute-start.11) | collective-permute-done | bytes 32800 | tf_op jit(solution)/shard_map/ppermute | solution.py:53
  99.0 2.2 %collective-permute-done.12 = f32[1,128,64]{1,2,0:T(8,128)S(1)} collective-permute-done((f32[1,128,64]{1,2,0:T(8,128)S(1)}, f32[1,128,64]{1,2,0:T(8,128)S(1)}, u32[]{:S(2)}, u32[]{:S(2)}) %collective-permute-start.12) | collective-permute-done | bytes 32800 | tf_op jit(solution)/shard_map/ppermute | solution.py:53
  (97 shorter events, 13.0 us)
Async XLA Ops:
  0.6 12.7 %copy-start.14 = (f32[2,256,128]{2,1,0:T(8,128)S(1)}, f32[2,256,128]{2,1,0:T(8,128)}, u32[]{:S(2)}) copy-start(f32[2,256,128]{2,1,0:T(8,128)} %param.16) | copy-start | bytes 786436
  0.6 12.7 %copy-start.15 = (f32[2,256,128]{2,1,0:T(8,128)S(1)}, f32[2,256,128]{2,1,0:T(8,128)}, u32[]{:S(2)}) copy-start(f32[2,256,128]{2,1,0:T(8,128)} %param.17) | copy-start | bytes 786436
  1.9 39.0 %copy-start.18 = (f32[2,2,256,128]{3,2,1,0:T(8,128)}, f32[2,2,256,128]{3,2,1,0:T(8,128)S(1)}, u32[]{:S(2)}) copy-start(f32[2,2,256,128]{3,2,1,0:T(8,128)S(1)} %fusion.105) | copy-start | bytes 1572868
  1.9 38.9 %collective-permute-start = (f32[2,2,256,128]{3,2,1,0:T(8,128)S(1)}, f32[2,2,256,128]{3,2,1,0:T(8,128)S(1)}, u32[]{:S(2)}, u32[]{:S(2)}) collective-permute-start(f32[2,2,256,128]{3,2,1,0:T(8,128)S(1)} %fusion.105), channel_id=1, source_target_pairs={{0,4},{2,6},{4,8},{6,10},{8,12},{10,14},{12,16},{14,18},{16,20},{1... | collective-permute-start | bytes 1572872 | tf_op jit(solution)/shard_map/ppermute | solution.py:53
  5.0 35.7 %collective-permute-start.1 = (f32[2,2,256,128]{3,2,1,0:T(8,128)S(1)}, f32[2,2,256,128]{3,2,1,0:T(8,128)S(1)}, u32[]{:S(2)}, u32[]{:S(2)}) collective-permute-start(f32[2,2,256,128]{3,2,1,0:T(8,128)S(1)} %fusion.105), channel_id=1, source_target_pairs={{0,2},{2,4},{4,6},{6,8},{8,10},{10,12},{12,14},{14,16},{16,18},{18... | collective-permute-start | bytes 1572872 | tf_op jit(solution)/shard_map/ppermute | solution.py:53
  8.2 21.5 %collective-permute-start.2 = (f32[2,2,256,128]{3,2,1,0:T(8,128)S(1)}, f32[2,2,256,128]{3,2,1,0:T(8,128)S(1)}, u32[]{:S(2)}, u32[]{:S(2)}) collective-permute-start(f32[2,2,256,128]{3,2,1,0:T(8,128)S(1)} %fusion.105), channel_id=1, source_target_pairs={{2,0},{4,2},{6,4},{8,6},{10,8},{12,10},{14,12},{16,14},{18,16},{20... | collective-permute-start | bytes 1572872 | tf_op jit(solution)/shard_map/ppermute | solution.py:53
  11.2 29.5 %collective-permute-start.3 = (f32[2,2,256,128]{3,2,1,0:T(8,128)S(1)}, f32[2,2,256,128]{3,2,1,0:T(8,128)S(1)}, u32[]{:S(2)}, u32[]{:S(2)}) collective-permute-start(f32[2,2,256,128]{3,2,1,0:T(8,128)S(1)} %fusion.105), channel_id=1, source_target_pairs={{4,0},{6,2},{8,4},{10,6},{12,8},{14,10},{16,12},{18,14},{20,16},{2... | collective-permute-start | bytes 1572872 | tf_op jit(solution)/shard_map/ppermute | solution.py:53
  29.7 13.7 %copy-start.8 = (f32[2,2,256,128]{3,2,1,0:T(8,128)}, f32[2,2,256,128]{3,2,1,0:T(8,128)S(1)}, u32[]{:S(2)}) copy-start(f32[2,2,256,128]{3,2,1,0:T(8,128)S(1)} %collective-permute-done.2) | copy-start | bytes 1572868
  40.7 2.7 %copy-start.10 = (f32[2,2,256,128]{3,2,1,0:T(8,128)}, f32[2,2,256,128]{3,2,1,0:T(8,128)S(1)}, u32[]{:S(2)}) copy-start(f32[2,2,256,128]{3,2,1,0:T(8,128)S(1)} %collective-permute-done.3) | copy-start | bytes 1572868
  40.7 2.4 %copy-start.4 = (f32[2,2,256,128]{3,2,1,0:T(8,128)}, f32[2,2,256,128]{3,2,1,0:T(8,128)S(1)}, u32[]{:S(2)}) copy-start(f32[2,2,256,128]{3,2,1,0:T(8,128)S(1)} %collective-permute-done) | copy-start | bytes 1572868
  40.8 2.5 %copy-start.6 = (f32[2,2,256,128]{3,2,1,0:T(8,128)}, f32[2,2,256,128]{3,2,1,0:T(8,128)S(1)}, u32[]{:S(2)}) copy-start(f32[2,2,256,128]{3,2,1,0:T(8,128)S(1)} %collective-permute-done.1) | copy-start | bytes 1572868
  40.9 2.4 %copy-start.20 = (f32[1,2,256,128]{3,2,1,0:T(8,128)S(1)}, f32[1,2,256,128]{3,2,1,0:T(8,128)}, u32[]{:S(2)}) copy-start(f32[1,2,256,128]{3,2,1,0:T(8,128)} %param.15) | copy-start | bytes 786436
  40.9 4.5 %collective-permute-start.4 = (f32[8,256,128]{2,1,0:T(8,128)S(1)}, f32[8,256,128]{2,1,0:T(8,128)S(1)}, u32[]{:S(2)}, u32[]{:S(2)}) collective-permute-start(f32[8,256,128]{2,1,0:T(8,128)S(1)} %pad_maximum_fusion.7), channel_id=1, source_target_pairs={{0,1},{1,0},{2,3},{3,2},{4,5},{5,4},{6,7},{7,6},{8,9},{9,8},{10,11... | collective-permute-start | bytes 3145736 | tf_op jit(solution)/shard_map/ppermute | solution.py:97
  45.8 1.4 %copy-start.5 = (f32[2,2,256,128]{3,2,1,0:T(8,128)S(1)}, f32[2,2,256,128]{3,2,1,0:T(8,128)}, u32[]{:S(2)}) copy-start(f32[2,2,256,128]{3,2,1,0:T(8,128)} %copy-done.4) | copy-start | bytes 1572868
  45.8 1.9 %copy-start.7 = (f32[2,2,256,128]{3,2,1,0:T(8,128)S(1)}, f32[2,2,256,128]{3,2,1,0:T(8,128)}, u32[]{:S(2)}) copy-start(f32[2,2,256,128]{3,2,1,0:T(8,128)} %copy-done.6) | copy-start | bytes 1572868
  45.8 2.0 %copy-start.9 = (f32[2,2,256,128]{3,2,1,0:T(8,128)S(1)}, f32[2,2,256,128]{3,2,1,0:T(8,128)}, u32[]{:S(2)}) copy-start(f32[2,2,256,128]{3,2,1,0:T(8,128)} %copy-done.8) | copy-start | bytes 1572868
  45.8 2.1 %copy-start.11 = (f32[2,2,256,128]{3,2,1,0:T(8,128)S(1)}, f32[2,2,256,128]{3,2,1,0:T(8,128)}, u32[]{:S(2)}) copy-start(f32[2,2,256,128]{3,2,1,0:T(8,128)} %copy-done.10) | copy-start | bytes 1572868
  45.8 2.3 %copy-start.19 = (f32[2,2,256,128]{3,2,1,0:T(8,128)S(1)}, f32[2,2,256,128]{3,2,1,0:T(8,128)}, u32[]{:S(2)}) copy-start(f32[2,2,256,128]{3,2,1,0:T(8,128)} %copy-done.18) | copy-start | bytes 1572868
  45.9 6.5 %copy-start.2 = (f32[4,256,128]{2,1,0:T(8,128)}, f32[4,256,128]{2,1,0:T(8,128)S(1)}, u32[]{:S(2)}) copy-start(f32[4,256,128]{2,1,0:T(8,128)S(1)} %slice.539) | copy-start | bytes 1572868
  46.0 7.3 %copy-start.16 = (f32[2,256,128]{2,1,0:T(8,128)}, f32[2,256,128]{2,1,0:T(8,128)S(1)}, u32[]{:S(2)}) copy-start(f32[2,256,128]{2,1,0:T(8,128)S(1)} %slice.546) | copy-start | bytes 786436
  56.1 17.0 %collective-permute-start.5 = (f32[2,256,128]{2,1,0:T(8,128)}, f32[2,256,128]{2,1,0:T(8,128)}, u32[]{:S(2)}, u32[]{:S(2)}) collective-permute-start(f32[2,256,128]{2,1,0:T(8,128)} %get-tuple-element.18), channel_id=1, source_target_pairs={{1,4},{0,5},{3,6},{2,7},{5,8},{4,9},{7,10},{6,11},{9,12},{8,13},{1... | collective-permute-start | bytes 786440 | tf_op jit(solution)/shard_map/ppermute | solution.py:53
  58.0 16.0 %collective-permute-start.6 = (f32[2,256,128]{2,1,0:T(8,128)}, f32[2,256,128]{2,1,0:T(8,128)}, u32[]{:S(2)}, u32[]{:S(2)}) collective-permute-start(f32[2,256,128]{2,1,0:T(8,128)} %get-tuple-element.18), channel_id=1, source_target_pairs={{1,2},{0,3},{3,4},{2,5},{5,6},{4,7},{7,8},{6,9},{9,10},{8,11},{11,... | collective-permute-start | bytes 786440 | tf_op jit(solution)/shard_map/ppermute | solution.py:53
  61.3 13.7 %collective-permute-start.7 = (f32[2,256,128]{2,1,0:T(8,128)}, f32[2,256,128]{2,1,0:T(8,128)}, u32[]{:S(2)}, u32[]{:S(2)}) collective-permute-start(f32[2,256,128]{2,1,0:T(8,128)} %get-tuple-element.18), channel_id=1, source_target_pairs={{1,0},{0,1},{3,2},{2,3},{5,4},{4,5},{7,6},{6,7},{9,8},{8,9},{11,10... | collective-permute-start | bytes 786440 | tf_op jit(solution)/shard_map/ppermute | solution.py:53
  61.4 14.6 %collective-permute-start.8 = (f32[2,256,128]{2,1,0:T(8,128)}, f32[2,256,128]{2,1,0:T(8,128)}, u32[]{:S(2)}, u32[]{:S(2)}) collective-permute-start(f32[2,256,128]{2,1,0:T(8,128)} %get-tuple-element.18), channel_id=1, source_target_pairs={{3,0},{2,1},{5,2},{4,3},{7,4},{6,5},{9,6},{8,7},{11,8},{10,9},{13,... | collective-permute-start | bytes 786440 | tf_op jit(solution)/shard_map/ppermute | solution.py:53
  64.8 18.1 %collective-permute-start.9 = (f32[2,256,128]{2,1,0:T(8,128)}, f32[2,256,128]{2,1,0:T(8,128)}, u32[]{:S(2)}, u32[]{:S(2)}) collective-permute-start(f32[2,256,128]{2,1,0:T(8,128)} %get-tuple-element.18), channel_id=1, source_target_pairs={{5,0},{4,1},{7,2},{6,3},{9,4},{8,5},{11,6},{10,7},{13,8},{12,9},{1... | collective-permute-start | bytes 786440 | tf_op jit(solution)/shard_map/ppermute | solution.py:53
  68.7 4.0 %copy-start.22 = (f32[256,128,1]{1,0,2:T(8,128)S(1)}, f32[256,128,1]{1,0,2:T(8,128)}, u32[]{:S(2)}) copy-start(f32[256,128,1]{1,0,2:T(8,128)} %constant.91) | copy-start | bytes 393220
  77.0 7.0 %copy-start.1 = (f32[8,256,128]{2,1,0:T(8,128)S(1)}, f32[8,256,128]{2,1,0:T(8,128)}, u32[]{:S(2)}) copy-start(f32[8,256,128]{2,1,0:T(8,128)} %copy-done) | copy-start | bytes 3145732
  90.6 1.2 %copy-start.23 = (f32[128,64]{1,0:T(8,128)S(1)}, f32[128,64]{1,0:T(8,128)}, u32[]{:S(2)}) copy-start(f32[128,64]{1,0:T(8,128)} %constant.27.clone) | copy-start | bytes 98308
  90.6 1.4 %copy-start.21 = (f32[256,128]{1,0:T(8,128)S(1)}, f32[256,128]{1,0:T(8,128)}, u32[]{:S(2)}) copy-start(f32[256,128]{1,0:T(8,128)} %constant.26.clone) | copy-start | bytes 393220
  92.4 4.2 %collective-permute-start.10 = (f32[1,128,64]{1,2,0:T(8,128)S(1)}, f32[1,128,64]{1,2,0:T(8,128)S(1)}, u32[]{:S(2)}, u32[]{:S(2)}) collective-permute-start(f32[1,128,64]{1,2,0:T(8,128)S(1)} %fusion.4), channel_id=1, source_target_pairs={{0,1},{2,3},{4,5},{6,7},{8,9},{10,11},{12,13},{14,15},{16,17},{18,... | collective-permute-start | bytes 98312 | tf_op jit(solution)/shard_map/ppermute | solution.py:53
  93.7 5.2 %collective-permute-start.11 = (f32[1,128,64]{1,2,0:T(8,128)S(1)}, f32[1,128,64]{1,2,0:T(8,128)S(1)}, u32[]{:S(2)}, u32[]{:S(2)}) collective-permute-start(f32[1,128,64]{1,2,0:T(8,128)S(1)} %fusion.4), channel_id=1, source_target_pairs={{2,1},{4,3},{6,5},{8,7},{10,9},{12,11},{14,13},{16,15},{18,17},{20... | collective-permute-start | bytes 98312 | tf_op jit(solution)/shard_map/ppermute | solution.py:53
  95.0 6.1 %collective-permute-start.12 = (f32[1,128,64]{1,2,0:T(8,128)S(1)}, f32[1,128,64]{1,2,0:T(8,128)S(1)}, u32[]{:S(2)}, u32[]{:S(2)}) collective-permute-start(f32[1,128,64]{1,2,0:T(8,128)S(1)} %fusion.4), channel_id=1, source_target_pairs={{0,3},{2,5},{4,7},{6,9},{8,11},{10,13},{12,15},{14,17},{16,19},{18... | collective-permute-start | bytes 98312 | tf_op jit(solution)/shard_map/ppermute | solution.py:53
  (5 other events, 4.7 us)

commit v9 on v1

--- a/solution.py
+++ b/solution.py
@@ -78,14 +78,50 @@
         ]
 
     start = guesses[0]
-    local = jnp.stack([diffusivity, reaction, start])
     distances = [d for d in range(-reach, reach + 1)]
-    got = gather_planes(local, "space", lambda d: None if d == 0 else space_pairs(d), distances)
-    wide = jnp.concatenate([got[d] for d in distances], axis=1)
     lo = reach * n - halo
     hi = reach * n + n + halo
-    wide = wide[:, lo:hi]
-    conduct, absorb, field0 = wide[0], wide[1], wide[2]
+    split = times % 2 == 0
+    if split:
+        even = me_t % 2 == 0
+        partner = [(t, t ^ 1) for t in range(times)]
+        other = lax.ppermute(start, "tm", partner)
+        local = jnp.where(
+            even,
+            jnp.stack([start, other, diffusivity, reaction]),
+            jnp.stack([other, start, diffusivity, reaction]),
+        )
+
+        def side_pairs(d):
+            pairs = []
+            for s in range(space):
+                for t in range(times):
+                    src_s = s - d if t % 2 == 0 else s + d
+                    if 0 <= src_s < space:
+                        pairs.append((joint(src_s, t), joint(s, t)))
+            return pairs
+
+        near = [lax.ppermute(local, ("space", "tm"), side_pairs(d)) for d in range(1, reach + 1)]
+        keep = jnp.where(
+            even,
+            jnp.stack([jnp.stack([blk[1], blk[2], blk[3]]) for blk in near]),
+            jnp.stack([jnp.stack([blk[0], blk[2], blk[3]]) for blk in near]),
+        )
+        handed = lax.ppermute(keep, "tm", partner)
+        own_g = jnp.where(even, jnp.stack([blk[0] for blk in near]), jnp.stack([blk[1] for blk in near]))
+        own_kc = jnp.stack([jnp.stack([blk[2], blk[3]]) for blk in near])
+        here = jnp.concatenate([own_g[:, None], own_kc], axis=1)
+        left = jnp.where(even, here, handed)
+        right = jnp.where(even, handed, here)
+        centre = jnp.stack([start, diffusivity, reaction])
+        pieces = [left[reach - 1 - i] for i in range(reach)] + [centre] + [right[i] for i in range(reach)]
+        wide = jnp.concatenate(pieces, axis=1)[:, lo:hi]
+        field0, conduct, absorb = wide[0], wide[1], wide[2]
+    else:
+        local = jnp.stack([diffusivity, reaction, start])
+        got = gather_planes(local, "space", lambda d: None if d == 0 else space_pairs(d), distances)
+        wide = jnp.concatenate([got[d] for d in distances], axis=1)[:, lo:hi]
+        conduct, absorb, field0 = wide[0], wide[1], wide[2]
     plane_ids = me_s * n - halo + jnp.arange(n + 2 * halo)
     inside = ((plane_ids >= 0) & (plane_ids < space * n)).astype(jnp.float32)[:, None, None]
 

time: 120 us -> 110 us (0.917)
  the two profiles are of different devices: /device:TPU:7 before, /device:TPU:1 now
where the time goes in v9:
time: 110 us; the launch traced here: 108 us
  starting transfers between devices  34 us (31%)
  waiting for transfers between devices  33.1 us (30%)
  other arithmetic  23.6 us (21%)
  local copies, waits for them, and re-layouts  11 us (10%)
  matrix products  5.11 us (5%)
  between operations  1.24 us (1%)
    ppermute x2, waiting for transfers between devices, shards(): lax.ppermute(local, ('space', 'tm'), side_pairs(d))  22 us
    ppermute x8, starting transfers between devices, gather_planes(): pieces[d] = lax.ppermute(block, axis_names, pairs_of(d))  16.1 us
    ppermute x1, starting transfers between devices, shards(): handed = lax.ppermute(keep, 'tm', partner)  15.2 us
    select_n x6, other arithmetic, fine_prop(): field = jnp.where(m > 0, field, 0.0)  11.3 us
    ppermute x8, waiting for transfers between devices, gather_planes(): pieces[d] = lax.ppermute(block, axis_names, pairs_of(d))  7.45 us
    unnamed x45, local copies, waits for them, and re-layouts  6.83 us
    reduce_sum x3, other arithmetic, restrict(): planes = field.reshape(first // 2, 2, second, third).sum(axis=1)  5.12 us
    dot_general x6, matrix products, restrict(): jnp.einsum('Yy,mYZ,Zz->myz', rows, planes, cols, precision=lax.Precision....  4.43 us
  transfers between devices with their start and end apart: 12, of which 6 were waited for; matrix products, arithmetic and copies ran while one was open for 12% of the time, Pallas kernels for 0%

profile of v9, /device:TPU:1, one launch (start us, length us, event | category | flops | bytes accessed | tf_op | source)
XLA Modules:
  0.0 108.1 jit_solution(5247911450478910250)
XLA Ops:
  0.8 1.7 %collective-permute-done = f32[2,256,128]{2,1,0:T(8,128)S(1)} collective-permute-done((f32[2,256,128]{2,1,0:T(8,128)}, f32[2,256,128]{2,1,0:T(8,128)S(1)}, u32[]{:S(2)}, u32[]{:S(2)}) %collective-permute-start) | collective-permute-done | bytes 262176 | tf_op jit(solution)/shard_map/ppermute | solution.py:88
  2.4 1.3 %fusion.5 = f32[4,2,256,128]{3,2,1,0:T(8,128)S(1)} fusion(f32[1,2,256,128]{3,2,1,0:T(8,128)} %bitcast.202, f32[1,2,256,128]{3,2,1,0:T(8,128)} %bitcast.213, f32[1,2,256,128]{3,2,1,0:T(8,128)S(1)} %bitcast.228, f32[1,2,256,128]{3,2,1,0:T(8,128)} %param.13, pred[]{:T(512)S(6)} %eq.8), kind=kLoop, calls=%fused_computation.53 | loop fusion | flops 1835008 | bytes 2097153 | tf_op jit(solution)/shard_map/jit(_where)/select_n | solution.py:89
  3.7 1.3 %collective-permute-start.2 = (f32[4,2,256,128]{3,2,1,0:T(8,128)S(1)}, f32[4,2,256,128]{3,2,1,0:T(8,128)S(1)}, u32[]{:S(2)}, u32[]{:S(2)}) collective-permute-start(f32[4,2,256,128]{3,2,1,0:T(8,128)S(1)} %fusion.5), channel_id=1, source_target_pairs={{5,1},{7,3},{0,4},{9,5},{2,6},{11,7},{4,8},{13,9},{6,10},{15,11},{... | collective-permute-start | bytes 3145736 | tf_op jit(solution)/shard_map/ppermute | solution.py:104
  5.0 1.3 %collective-permute-start.1 = (f32[4,2,256,128]{3,2,1,0:T(8,128)S(1)}, f32[4,2,256,128]{3,2,1,0:T(8,128)S(1)}, u32[]{:S(2)}, u32[]{:S(2)}) collective-permute-start(f32[4,2,256,128]{3,2,1,0:T(8,128)S(1)} %fusion.5), channel_id=1, source_target_pairs={{3,1},{0,2},{5,3},{2,4},{7,5},{4,6},{9,7},{6,8},{11,9},{8,10},{13,... | collective-permute-start | bytes 3145736 | tf_op jit(solution)/shard_map/ppermute | solution.py:104
  6.3 13.9 %collective-permute-done.2 = f32[4,2,256,128]{3,2,1,0:T(8,128)S(1)} collective-permute-done((f32[4,2,256,128]{3,2,1,0:T(8,128)S(1)}, f32[4,2,256,128]{3,2,1,0:T(8,128)S(1)}, u32[]{:S(2)}, u32[]{:S(2)}) %collective-permute-start.2) | collective-permute-done | bytes 1048608 | tf_op jit(solution)/shard_map/ppermute | solution.py:104
  20.3 8.1 %collective-permute-done.1 = f32[4,2,256,128]{3,2,1,0:T(8,128)S(1)} collective-permute-done((f32[4,2,256,128]{3,2,1,0:T(8,128)S(1)}, f32[4,2,256,128]{3,2,1,0:T(8,128)S(1)}, u32[]{:S(2)}, u32[]{:S(2)}) %collective-permute-start.1) | collective-permute-done | bytes 1048608 | tf_op jit(solution)/shard_map/ppermute | solution.py:104
  29.7 15.2 %collective-permute-start.3 = (f32[2,3,2,256,128]{4,3,2,1,0:T(8,128)S(1)}, f32[2,3,2,256,128]{4,3,2,1,0:T(8,128)}, u32[]{:S(2)}, u32[]{:S(2)}) collective-permute-start(f32[2,3,2,256,128]{4,3,2,1,0:T(8,128)S(1)} %maximum_select_fusion), channel_id=1, source_target_pairs={{0,1},{1,0},{2,3},{3,2},{4,5},{5,4},{6,7},{7,6},{8,9},{9,8},{10,11... | collective-permute-start | bytes 4718600 | tf_op jit(solution)/shard_map/ppermute | solution.py:110
  45.1 1.0 maximum_select_fusion.1
  46.1 1.9 %collective-permute-done.3 = f32[2,3,2,256,128]{4,3,2,1,0:T(8,128)} collective-permute-done((f32[2,3,2,256,128]{4,3,2,1,0:T(8,128)S(1)}, f32[2,3,2,256,128]{4,3,2,1,0:T(8,128)}, u32[]{:S(2)}, u32[]{:S(2)}) %collective-permute-start.3) | collective-permute-done | bytes 1572896 | tf_op jit(solution)/shard_map/ppermute | solution.py:110
  48.0 1.7 %fusion.3 = (f32[2,3,2,256,128]{4,3,2,1,0:T(8,128)S(1)}, f32[2,3,2,256,128]{4,3,2,1,0:T(8,128)S(1)}) fusion(f32[2,3,2,256,128]{4,3,2,1,0:T(8,128)} %collective-permute-done.3, f32[1,2,2,256,128]{4,3,2,1,0:T(8,128)S(1)} %get-tuple-element.27, f32[1,2,2,256,128]{4,3,2,1,0:T(8,128)S(1)} %get-tuple-element.25, ...), kind=kLoop, calls=%fused_computation.51 | loop fusion | flops 1572864 | bytes 6291457 | tf_op jit(solution)/shard_map/jit(_where)/select_n | solution.py:115
  51.4 1.5 %fusion.254 = (f32[1,6,256,128]{3,2,1,0:T(8,128)}, f32[6,256,128]{2,1,0:T(8,128)S(1)}, f32[1,6,256,128]{3,2,1,0:T(8,128)}) fusion(f32[3,6,256,128]{3,2,1,0:T(8,128)S(1)} %pad_maximum_fusion.2), kind=kLoop, calls=%fused_computation.389 | loop fusion | bytes 3932160 | tf_op jit(solution)/shard_map/slice | solution.py:22
  53.9 1.1 copy-done.12
  55.4 1.9 %fusion.23 = f32[8,256,128]{2,1,0:T(8,128)S(1)} fusion(f32[8,256,128]{2,1,0:T(8,128)S(1)} %get-tuple-element.7, f32[3,8,256,128]{3,2,1,0:T(8,128)S(1)} %get-tuple-element.14, f32[3,8,256,128]{3,2,1,0:T(8,128)S(1)} %get-tuple-element.13, f32[3,10,256,128]{3,2,1,0:T(8,128)S(1)} %constant_dynamic-update-slice_fusion, pred[8]{0:T(512)(128)(4,1)S(1)} %slice_compare_fusion, ...), kind=kLoop, calls=%fused_computation.71 | loop fusion | flops 9175040 | bytes 8388616 | tf_op jit(solution)/shard_map/jit(_where)/select_n | solution.py:136
  57.4 1.4 %fusion.76 = f32[6,256,128]{2,1,0:T(8,128)S(1)} fusion(f32[6,256,128]{2,1,0:T(8,128)S(1)} %slice.639, f32[8,256,128]{2,1,0:T(8,128)S(1)} %fusion.23, pred[6]{0:T(512)(128)(4,1)S(1)} %slice_compare_fusion.1, f32[6,256,128]{2,1,0:T(8,128)S(1)} %get-tuple-element.11, f32[3,2,256,128]{3,2,1,0:T(8,128)S(1)} %get-tuple-element.15, ...), kind=kLoop, calls=%fused_computation.145 | loop fusion | flops 8847360 | bytes 8650758 | tf_op jit(solution)/shard_map/jit(_where)/select_n | solution.py:136
  59.8 1.1 %broadcast_select_fusion = (f32[2,256,128]{2,1,0:T(8,128)}, f32[2,256,128]{2,1,0:T(8,128)S(1)}) fusion(f32[2,256,128]{2,1,0:T(8,128)S(1)} %copy-done.17, pred[]{:T(512)S(6)} %eq.9, f32[2,256,128]{2,1,0:T(8,128)S(1)} %slice.647, f32[2,256,128]{2,1,0:T(8,128)S(1)} %copy-done, f32[2,256,128]{2,1,0:T(8,128)S(1)} %copy-done.1, f32[4,256,128]{2,1,0:T(8,128)S(1)} %fusion.126, ...), kind=kLoop, calls=%fused_computation.319 | loop fusion | flops 2686976 | bytes 4456449 | tf_op jit(solution)/shard_map/jit(_where)/select_n | solution.py:140
  61.0 1.4 %collective-permute-start.8 = (f32[2,256,128]{2,1,0:T(8,128)}, f32[2,256,128]{2,1,0:T(8,128)}, u32[]{:S(2)}, u32[]{:S(2)}) collective-permute-start(f32[2,256,128]{2,1,0:T(8,128)} %get-tuple-element.4), channel_id=1, source_target_pairs={{5,0},{4,1},{7,2},{6,3},{9,4},{8,5},{11,6},{10,7},{13,8},{12,9},{1... | collective-permute-start | bytes 786440 | tf_op jit(solution)/shard_map/ppermute | solution.py:53
  62.4 1.3 %collective-permute-start.7 = (f32[2,256,128]{2,1,0:T(8,128)}, f32[2,256,128]{2,1,0:T(8,128)}, u32[]{:S(2)}, u32[]{:S(2)}) collective-permute-start(f32[2,256,128]{2,1,0:T(8,128)} %get-tuple-element.4), channel_id=1, source_target_pairs={{3,0},{2,1},{5,2},{4,3},{7,4},{6,5},{9,6},{8,7},{11,8},{10,9},{13,... | collective-permute-start | bytes 786440 | tf_op jit(solution)/shard_map/ppermute | solution.py:53
  64.1 5.0 %collective-permute-start.5 = (f32[2,256,128]{2,1,0:T(8,128)}, f32[2,256,128]{2,1,0:T(8,128)}, u32[]{:S(2)}, u32[]{:S(2)}) collective-permute-start(f32[2,256,128]{2,1,0:T(8,128)} %get-tuple-element.4), channel_id=1, source_target_pairs={{1,2},{0,3},{3,4},{2,5},{5,6},{4,7},{7,8},{6,9},{9,10},{8,11},{11,... | collective-permute-start | bytes 786440 | tf_op jit(solution)/shard_map/ppermute | solution.py:53
  69.1 4.8 %collective-permute-start.4 = (f32[2,256,128]{2,1,0:T(8,128)}, f32[2,256,128]{2,1,0:T(8,128)}, u32[]{:S(2)}, u32[]{:S(2)}) collective-permute-start(f32[2,256,128]{2,1,0:T(8,128)} %get-tuple-element.4), channel_id=1, source_target_pairs={{1,4},{0,5},{3,6},{2,7},{5,8},{4,9},{7,10},{6,11},{9,12},{8,13},{1... | collective-permute-start | bytes 786440 | tf_op jit(solution)/shard_map/ppermute | solution.py:53
  73.9 2.0 %reduce_sum.29 = f32[3,256,128]{2,1,0:T(8,128)} reduce(f32[3,2,256,128]{3,2,1,0:T(8,128)} %bitcast.226, f32[]{:T(128)} %constant.20.clone.1), dimensions={1}, to_apply=%region_2.3 | reduce | flops 98304 | bytes 1179652 | tf_op jit(solution)/shard_map/reduce_sum | solution.py:32
  75.9 2.0 %reduce_sum.28 = f32[3,256,128]{2,1,0:T(8,128)} reduce(f32[3,2,256,128]{3,2,1,0:T(8,128)} %bitcast.225, f32[]{:T(128)} %constant.20.clone.1), dimensions={1}, to_apply=%region_1.2 | reduce | flops 98304 | bytes 1179652 | tf_op jit(solution)/shard_map/reduce_sum | solution.py:32
  77.9 1.6 %fusion.257 = f32[64,3,256]{2,0,1:T(8,128)S(1)} fusion(f32[128,64,1]{1,0,2:T(8,128)} %constant.90, f32[3,256,128]{2,1,0:T(8,128)} %reduce_sum.29), kind=kOutput, calls=%fused_computation.392 | convolution fusion | flops 75497472 | bytes 622592 | tf_op jit(solution)/shard_map/Yy,mYZ,Zz->myz/dot_general | solution.py:35
  79.5 1.6 %fusion.256 = f32[64,3,256]{2,0,1:T(8,128)S(1)} fusion(f32[128,64,1]{1,0,2:T(8,128)} %constant.90, f32[3,256,128]{2,1,0:T(8,128)} %reduce_sum.28), kind=kOutput, calls=%fused_computation.391 | convolution fusion | flops 75497472 | bytes 622592 | tf_op jit(solution)/shard_map/Yy,mYZ,Zz->myz/dot_general | solution.py:35
  81.4 2.6 %collective-permute-done.4 = f32[2,256,128]{2,1,0:T(8,128)} collective-permute-done((f32[2,256,128]{2,1,0:T(8,128)}, f32[2,256,128]{2,1,0:T(8,128)}, u32[]{:S(2)}, u32[]{:S(2)}) %collective-permute-start.4) | collective-permute-done | bytes 262176 | tf_op jit(solution)/shard_map/ppermute | solution.py:53
  86.0 1.0 constant_dynamic-update-slice_fusion.6
  86.9 1.0 constant_dynamic-update-slice_fusion.5
  89.0 3.8 %fusion.39 = f32[8,256,128]{2,1,0:T(8,128)S(1)} fusion(f32[8,256,128]{2,1,0:T(8,128)S(1)} %slice.650, f32[2,256,128]{2,1,0:T(8,128)} %collective-permute-done.8, f32[2,256,128]{2,1,0:T(8,128)} %collective-permute-done.7, f32[2,256,128]{2,1,0:T(8,128)} %collective-permute-done.6, f32[2,256,128]{2,1,0:T(8,128)} %collective-permute-done.5, ...), kind=kLoop, calls=%fused_computation.87 | loop fusion | flops 10747904 | bytes 7602184 | tf_op jit(solution)/shard_map/jit(_where)/select_n | solution.py:136
  92.9 2.5 %fusion.92 = f32[6,256,128]{2,1,0:T(8,128)S(1)} fusion(f32[6,256,128]{2,1,0:T(8,128)S(1)} %slice.651, f32[8,256,128]{2,1,0:T(8,128)S(1)} %fusion.39, pred[6]{0:T(512)(128)(4,1)S(1)} %slice_compare_fusion.1, f32[6,256,128]{2,1,0:T(8,128)S(1)} %copy-done.11, f32[3,2,256,128]{3,2,1,0:T(8,128)S(1)} %get-tuple-element.15, ...), kind=kLoop, calls=%fused_computation.161 | loop fusion | flops 8847360 | bytes 8650758 | tf_op jit(solution)/shard_map/jit(_where)/select_n | solution.py:136
  96.4 1.1 %fusion.251 = (f32[256,128]{1,0:T(8,128)S(1)}, f32[2,256,128]{2,1,0:T(8,128)}) fusion(f32[2,256,128]{2,1,0:T(8,128)S(1)} %get-tuple-element.5, f32[2,256,128]{2,1,0:T(8,128)S(1)} %slice.657, f32[2,256,128]{2,1,0:T(8,128)S(1)} %copy-done, f32[2,256,128]{2,1,0:T(8,128)S(1)} %copy-done.1, f32[4,256,128]{2,1,0:T(8,128)S(1)} %fusion.142, ...), kind=kLoop, calls=%fused_computation.388 | loop fusion | flops 2719744 | bytes 4325376 | tf_op jit(solution)/shard_map/reduce_sum | solution.py:32
  98.9 1.3 %collective-permute-start.10 = (f32[1,128,64]{1,2,0:T(8,128)S(1)}, f32[1,128,64]{1,2,0:T(8,128)S(1)}, u32[]{:S(2)}, u32[]{:S(2)}) collective-permute-start(f32[1,128,64]{1,2,0:T(8,128)S(1)} %fusion.2), channel_id=1, source_target_pairs={{2,1},{4,3},{6,5},{8,7},{10,9},{12,11},{14,13},{16,15},{18,17},{20... | collective-permute-start | bytes 98312 | tf_op jit(solution)/shard_map/ppermute | solution.py:53
  100.2 1.3 %collective-permute-start.9 = (f32[1,128,64]{1,2,0:T(8,128)S(1)}, f32[1,128,64]{1,2,0:T(8,128)S(1)}, u32[]{:S(2)}, u32[]{:S(2)}) collective-permute-start(f32[1,128,64]{1,2,0:T(8,128)S(1)} %fusion.2), channel_id=1, source_target_pairs={{0,1},{2,3},{4,5},{6,7},{8,9},{10,11},{12,13},{14,15},{16,17},{18,... | collective-permute-start | bytes 98312 | tf_op jit(solution)/shard_map/ppermute | solution.py:53
  101.8 4.8 %collective-permute-done.10 = f32[1,128,64]{1,2,0:T(8,128)S(1)} collective-permute-done((f32[1,128,64]{1,2,0:T(8,128)S(1)}, f32[1,128,64]{1,2,0:T(8,128)S(1)}, u32[]{:S(2)}, u32[]{:S(2)}) %collective-permute-start.10) | collective-permute-done | bytes 32800 | tf_op jit(solution)/shard_map/ppermute | solution.py:53
  (88 shorter events, 13.5 us)
Async XLA Ops:
  0.6 1.8 %collective-permute-start = (f32[2,256,128]{2,1,0:T(8,128)}, f32[2,256,128]{2,1,0:T(8,128)S(1)}, u32[]{:S(2)}, u32[]{:S(2)}) collective-permute-start(f32[2,256,128]{2,1,0:T(8,128)} %bitcast.224), channel_id=1, source_target_pairs={{0,1},{1,0},{2,3},{3,2},{4,5},{5,4},{6,7},{7,6},{8,9},{9,8},{10,11... | collective-permute-start | bytes 786440 | tf_op jit(solution)/shard_map/ppermute | solution.py:88
  3.7 16.5 %collective-permute-start.2 = (f32[4,2,256,128]{3,2,1,0:T(8,128)S(1)}, f32[4,2,256,128]{3,2,1,0:T(8,128)S(1)}, u32[]{:S(2)}, u32[]{:S(2)}) collective-permute-start(f32[4,2,256,128]{3,2,1,0:T(8,128)S(1)} %fusion.5), channel_id=1, source_target_pairs={{5,1},{7,3},{0,4},{9,5},{2,6},{11,7},{4,8},{13,9},{6,10},{15,11},{... | collective-permute-start | bytes 3145736 | tf_op jit(solution)/shard_map/ppermute | solution.py:104
  5.0 23.4 %collective-permute-start.1 = (f32[4,2,256,128]{3,2,1,0:T(8,128)S(1)}, f32[4,2,256,128]{3,2,1,0:T(8,128)S(1)}, u32[]{:S(2)}, u32[]{:S(2)}) collective-permute-start(f32[4,2,256,128]{3,2,1,0:T(8,128)S(1)} %fusion.5), channel_id=1, source_target_pairs={{3,1},{0,2},{5,3},{2,4},{7,5},{4,6},{9,7},{6,8},{11,9},{8,10},{13,... | collective-permute-start | bytes 3145736 | tf_op jit(solution)/shard_map/ppermute | solution.py:104
  29.7 18.4 %collective-permute-start.3 = (f32[2,3,2,256,128]{4,3,2,1,0:T(8,128)S(1)}, f32[2,3,2,256,128]{4,3,2,1,0:T(8,128)}, u32[]{:S(2)}, u32[]{:S(2)}) collective-permute-start(f32[2,3,2,256,128]{4,3,2,1,0:T(8,128)S(1)} %maximum_select_fusion), channel_id=1, source_target_pairs={{0,1},{1,0},{2,3},{3,2},{4,5},{5,4},{6,7},{7,6},{8,9},{9,8},{10,11... | collective-permute-start | bytes 4718600 | tf_op jit(solution)/shard_map/ppermute | solution.py:110
  49.8 1.0 copy-start
  49.8 1.0 copy-start.1
  49.8 1.3 %copy-start.2 = (f32[1,2,256,128]{3,2,1,0:T(8,128)S(1)}, f32[1,2,256,128]{3,2,1,0:T(8,128)}, u32[]{:S(2)}) copy-start(f32[1,2,256,128]{3,2,1,0:T(8,128)} %param.13) | copy-start | bytes 786436
  50.0 7.4 %copy-start.4 = (f32[3,2,256,128]{3,2,1,0:T(8,128)}, f32[3,2,256,128]{3,2,1,0:T(8,128)S(1)}, u32[]{:S(2)}) copy-start(f32[3,2,256,128]{3,2,1,0:T(8,128)S(1)} %get-tuple-element.17) | copy-start | bytes 2359300
  51.2 7.7 %copy-start.13 = (f32[4,256,128]{2,1,0:T(8,128)}, f32[4,256,128]{2,1,0:T(8,128)S(1)}, u32[]{:S(2)}) copy-start(f32[4,256,128]{2,1,0:T(8,128)S(1)} %maximum_bitcast_fusion.5) | copy-start | bytes 1572868
  51.3 6.0 %copy-start.3 = (f32[3,6,256,128]{3,2,1,0:T(8,128)}, f32[3,6,256,128]{3,2,1,0:T(8,128)S(1)}, u32[]{:S(2)}) copy-start(f32[3,6,256,128]{3,2,1,0:T(8,128)S(1)} %pad_maximum_fusion.2) | copy-start | bytes 7077892
  52.9 4.5 %copy-start.10 = (f32[6,256,128]{2,1,0:T(8,128)}, f32[6,256,128]{2,1,0:T(8,128)S(1)}, u32[]{:S(2)}) copy-start(f32[6,256,128]{2,1,0:T(8,128)S(1)} %get-tuple-element.11) | copy-start | bytes 2359300
  53.1 1.9 %copy-start.12 = (f32[3,10,256,128]{3,2,1,0:T(8,128)}, f32[3,10,256,128]{3,2,1,0:T(8,128)S(1)}, u32[]{:S(2)}) copy-start(f32[3,10,256,128]{3,2,1,0:T(8,128)S(1)} %constant_dynamic-update-slice_fusion) | copy-start | bytes 11796484
  53.4 2.0 %copy-start.8 = (f32[8,256,128]{2,1,0:T(8,128)}, f32[8,256,128]{2,1,0:T(8,128)S(1)}, u32[]{:S(2)}) copy-start(f32[8,256,128]{2,1,0:T(8,128)S(1)} %get-tuple-element.6) | copy-start | bytes 3145732
  53.9 3.3 %copy-start.6 = (f32[3,8,256,128]{3,2,1,0:T(8,128)}, f32[3,8,256,128]{3,2,1,0:T(8,128)S(1)}, u32[]{:S(2)}) copy-start(f32[3,8,256,128]{3,2,1,0:T(8,128)S(1)} %get-tuple-element.13) | copy-start | bytes 9437188
  53.9 3.4 %copy-start.7 = (f32[3,8,256,128]{3,2,1,0:T(8,128)}, f32[3,8,256,128]{3,2,1,0:T(8,128)S(1)}, u32[]{:S(2)}) copy-start(f32[3,8,256,128]{3,2,1,0:T(8,128)S(1)} %get-tuple-element.14) | copy-start | bytes 9437188
  58.9 1.0 copy-start.17
  61.0 20.0 %copy-start.16 = (f32[256,128,1]{1,0,2:T(8,128)S(1)}, f32[256,128,1]{1,0,2:T(8,128)}, u32[]{:S(2)}) copy-start(f32[256,128,1]{1,0,2:T(8,128)} %constant.91) | copy-start | bytes 393220
  61.0 26.9 %collective-permute-start.8 = (f32[2,256,128]{2,1,0:T(8,128)}, f32[2,256,128]{2,1,0:T(8,128)}, u32[]{:S(2)}, u32[]{:S(2)}) collective-permute-start(f32[2,256,128]{2,1,0:T(8,128)} %get-tuple-element.4), channel_id=1, source_target_pairs={{5,0},{4,1},{7,2},{6,3},{9,4},{8,5},{11,6},{10,7},{13,8},{12,9},{1... | collective-permute-start | bytes 786440 | tf_op jit(solution)/shard_map/ppermute | solution.py:53
  62.4 24.5 %collective-permute-start.7 = (f32[2,256,128]{2,1,0:T(8,128)}, f32[2,256,128]{2,1,0:T(8,128)}, u32[]{:S(2)}, u32[]{:S(2)}) collective-permute-start(f32[2,256,128]{2,1,0:T(8,128)} %get-tuple-element.4), channel_id=1, source_target_pairs={{3,0},{2,1},{5,2},{4,3},{7,4},{6,5},{9,6},{8,7},{11,8},{10,9},{13,... | collective-permute-start | bytes 786440 | tf_op jit(solution)/shard_map/ppermute | solution.py:53
  63.7 22.2 %collective-permute-start.6 = (f32[2,256,128]{2,1,0:T(8,128)}, f32[2,256,128]{2,1,0:T(8,128)}, u32[]{:S(2)}, u32[]{:S(2)}) collective-permute-start(f32[2,256,128]{2,1,0:T(8,128)} %get-tuple-element.4), channel_id=1, source_target_pairs={{1,0},{0,1},{3,2},{2,3},{5,4},{4,5},{7,6},{6,7},{9,8},{8,9},{11,10... | collective-permute-start | bytes 786440 | tf_op jit(solution)/shard_map/ppermute | solution.py:53
  64.1 20.8 %collective-permute-start.5 = (f32[2,256,128]{2,1,0:T(8,128)}, f32[2,256,128]{2,1,0:T(8,128)}, u32[]{:S(2)}, u32[]{:S(2)}) collective-permute-start(f32[2,256,128]{2,1,0:T(8,128)} %get-tuple-element.4), channel_id=1, source_target_pairs={{1,2},{0,3},{3,4},{2,5},{5,6},{4,7},{7,8},{6,9},{9,10},{8,11},{11,... | collective-permute-start | bytes 786440 | tf_op jit(solution)/shard_map/ppermute | solution.py:53
  69.1 14.9 %collective-permute-start.4 = (f32[2,256,128]{2,1,0:T(8,128)}, f32[2,256,128]{2,1,0:T(8,128)}, u32[]{:S(2)}, u32[]{:S(2)}) collective-permute-start(f32[2,256,128]{2,1,0:T(8,128)} %get-tuple-element.4), channel_id=1, source_target_pairs={{1,4},{0,5},{3,6},{2,7},{5,8},{4,9},{7,10},{6,11},{9,12},{8,13},{1... | collective-permute-start | bytes 786440 | tf_op jit(solution)/shard_map/ppermute | solution.py:53
  81.4 7.6 %copy-start.9 = (f32[8,256,128]{2,1,0:T(8,128)S(1)}, f32[8,256,128]{2,1,0:T(8,128)}, u32[]{:S(2)}) copy-start(f32[8,256,128]{2,1,0:T(8,128)} %copy-done.8) | copy-start | bytes 3145732
  89.0 3.9 %copy-start.5 = (f32[3,2,256,128]{3,2,1,0:T(8,128)S(1)}, f32[3,2,256,128]{3,2,1,0:T(8,128)}, u32[]{:S(2)}) copy-start(f32[3,2,256,128]{3,2,1,0:T(8,128)} %copy-done.4) | copy-start | bytes 2359300
  89.0 3.9 %copy-start.11 = (f32[6,256,128]{2,1,0:T(8,128)S(1)}, f32[6,256,128]{2,1,0:T(8,128)}, u32[]{:S(2)}) copy-start(f32[6,256,128]{2,1,0:T(8,128)} %copy-done.10) | copy-start | bytes 2359300
  92.9 2.6 %copy-start.14 = (f32[4,256,128]{2,1,0:T(8,128)S(1)}, f32[4,256,128]{2,1,0:T(8,128)}, u32[]{:S(2)}) copy-start(f32[4,256,128]{2,1,0:T(8,128)} %copy-done.13) | copy-start | bytes 1572868
  96.4 1.2 %copy-start.18 = (f32[128,64]{1,0:T(8,128)S(1)}, f32[128,64]{1,0:T(8,128)}, u32[]{:S(2)}) copy-start(f32[128,64]{1,0:T(8,128)} %constant.27.clone) | copy-start | bytes 98308
  96.4 1.4 %copy-start.15 = (f32[256,128]{1,0:T(8,128)S(1)}, f32[256,128]{1,0:T(8,128)}, u32[]{:S(2)}) copy-start(f32[256,128]{1,0:T(8,128)} %constant.26.clone) | copy-start | bytes 393220
  98.2 3.6 %collective-permute-start.11 = (f32[1,128,64]{1,2,0:T(8,128)S(1)}, f32[1,128,64]{1,2,0:T(8,128)S(1)}, u32[]{:S(2)}, u32[]{:S(2)}) collective-permute-start(f32[1,128,64]{1,2,0:T(8,128)S(1)} %fusion.2), channel_id=1, source_target_pairs={{0,3},{2,5},{4,7},{6,9},{8,11},{10,13},{12,15},{14,17},{16,19},{18... | collective-permute-start | bytes 98312 | tf_op jit(solution)/shard_map/ppermute | solution.py:53
  98.9 7.8 %collective-permute-start.10 = (f32[1,128,64]{1,2,0:T(8,128)S(1)}, f32[1,128,64]{1,2,0:T(8,128)S(1)}, u32[]{:S(2)}, u32[]{:S(2)}) collective-permute-start(f32[1,128,64]{1,2,0:T(8,128)S(1)} %fusion.2), channel_id=1, source_target_pairs={{2,1},{4,3},{6,5},{8,7},{10,9},{12,11},{14,13},{16,15},{18,17},{20... | collective-permute-start | bytes 98312 | tf_op jit(solution)/shard_map/ppermute | solution.py:53
  100.2 6.5 %collective-permute-start.9 = (f32[1,128,64]{1,2,0:T(8,128)S(1)}, f32[1,128,64]{1,2,0:T(8,128)S(1)}, u32[]{:S(2)}, u32[]{:S(2)}) collective-permute-start(f32[1,128,64]{1,2,0:T(8,128)S(1)} %fusion.2), channel_id=1, source_target_pairs={{0,1},{2,3},{4,5},{6,7},{8,9},{10,11},{12,13},{14,15},{16,17},{18,... | collective-permute-start | bytes 98312 | tf_op jit(solution)/shard_map/ppermute | solution.py:53

commit v10 on v6

--- a/solution.py
+++ b/solution.py
@@ -32,7 +32,7 @@
     planes = field.reshape(first // 2, 2, second, third).sum(axis=1)
     rows = pair_matrix(second)
     cols = pair_matrix(third)
-    out = jnp.einsum("Yy,mYZ,Zz->myz", rows, planes, cols, precision=lax.Precision.HIGHEST)
+    out = jnp.einsum("Yy,mYZ,Zz->myz", rows, planes, cols, precision=lax.Precision.HIGH)
     return out * 0.125
 
 
@@ -40,7 +40,7 @@
     first, second, third = field.shape
     rows = pair_matrix(second * 2)
     cols = pair_matrix(third * 2)
-    out = jnp.einsum("Yy,myz,Zz->mYZ", rows, field, cols, precision=lax.Precision.HIGHEST)
+    out = jnp.einsum("Yy,myz,Zz->mYZ", rows, field, cols, precision=lax.Precision.HIGH)
     return jnp.repeat(out, 2, axis=0)
 
 

time: 103 us -> 102 us (level)
  transfers between devices with their start and end apart: 13 -> 13, of which waited for: 4 -> 5; matrix products, arithmetic and copies ran while one was open for 11% -> 10% of each run, Pallas kernels for 0% -> 0%
where the time goes in v10:
time: 102 us; the launch traced here: 101 us
  waiting for transfers between devices  35.5 us (35%)
  starting transfers between devices  33 us (32%)
  other arithmetic  18.2 us (18%)
  local copies, waits for them, and re-layouts  9.25 us (9%)
  matrix products  4.29 us (4%)
  between operations  1.28 us (1%)
    ppermute x12, waiting for transfers between devices, gather_planes(): pieces[d] = lax.ppermute(block, axis_names, pairs_of(d))  33.7 us
    ppermute x12, starting transfers between devices, gather_planes(): pieces[d] = lax.ppermute(block, axis_names, pairs_of(d))  31.1 us
    select_n x5, other arithmetic, fine_prop(): field = jnp.where(m > 0, field, 0.0)  8.33 us
    unnamed x55, local copies, waits for them, and re-layouts  7.55 us
    reduce_sum x3, other arithmetic, restrict(): planes = field.reshape(first // 2, 2, second, third).sum(axis=1)  3.95 us
    dot_general x6, matrix products, restrict(): jnp.einsum('Yy,mYZ,Zz->myz', rows, planes, cols, precision=lax.Precision....  3.75 us
    slice x1, other arithmetic, advance(): return center + diffuse_scale * inflow - react_scale * absorb[1:-1] * center  2.07 us
  transfers between devices with their start and end apart: 13, of which 5 were waited for; matrix products, arithmetic and copies ran while one was open for 10% of the time, Pallas kernels for 0%

profile of v10, /device:TPU:1, one launch (start us, length us, event | category | flops | bytes accessed | tf_op | source)
XLA Modules:
  0.0 101.5 jit_solution(5728735654871621199)
XLA Ops:
  0.7 1.2 %fusion.105 = f32[2,2,256,128]{3,2,1,0:T(8,128)S(1)} fusion(f32[1,2,256,128]{3,2,1,0:T(8,128)} %param.13, f32[1,2,256,128]{3,2,1,0:T(8,128)} %bitcast.67, f32[1,2,256,128]{3,2,1,0:T(8,128)} %bitcast.69, pred[]{:T(512)S(6)} %eq.8), kind=kLoop, calls=%fused_computation.179 | loop fusion | flops 393216 | bytes 1310721 | tf_op jit(solution)/shard_map/jit(_where)/select_n | solution.py:87
  1.9 4.0 %collective-permute-start = (f32[2,2,256,128]{3,2,1,0:T(8,128)S(1)}, f32[2,2,256,128]{3,2,1,0:T(8,128)S(1)}, u32[]{:S(2)}, u32[]{:S(2)}) collective-permute-start(f32[2,2,256,128]{3,2,1,0:T(8,128)S(1)} %fusion.105), channel_id=1, source_target_pairs={{0,4},{2,6},{4,8},{6,10},{8,12},{10,14},{12,16},{14,18},{16,20},{1... | collective-permute-start | bytes 1572872 | tf_op jit(solution)/shard_map/ppermute | solution.py:53
  5.9 3.1 %collective-permute-start.1 = (f32[2,2,256,128]{3,2,1,0:T(8,128)S(1)}, f32[2,2,256,128]{3,2,1,0:T(8,128)S(1)}, u32[]{:S(2)}, u32[]{:S(2)}) collective-permute-start(f32[2,2,256,128]{3,2,1,0:T(8,128)S(1)} %fusion.105), channel_id=1, source_target_pairs={{0,2},{2,4},{4,6},{6,8},{8,10},{10,12},{12,14},{14,16},{16,18},{18... | collective-permute-start | bytes 1572872 | tf_op jit(solution)/shard_map/ppermute | solution.py:53
  9.1 1.3 %collective-permute-start.2 = (f32[2,2,256,128]{3,2,1,0:T(8,128)S(1)}, f32[2,2,256,128]{3,2,1,0:T(8,128)S(1)}, u32[]{:S(2)}, u32[]{:S(2)}) collective-permute-start(f32[2,2,256,128]{3,2,1,0:T(8,128)S(1)} %fusion.105), channel_id=1, source_target_pairs={{2,0},{4,2},{6,4},{8,6},{10,8},{12,10},{14,12},{16,14},{18,16},{20... | collective-permute-start | bytes 1572872 | tf_op jit(solution)/shard_map/ppermute | solution.py:53
  10.4 1.3 %collective-permute-start.3 = (f32[2,2,256,128]{3,2,1,0:T(8,128)S(1)}, f32[2,2,256,128]{3,2,1,0:T(8,128)S(1)}, u32[]{:S(2)}, u32[]{:S(2)}) collective-permute-start(f32[2,2,256,128]{3,2,1,0:T(8,128)S(1)} %fusion.105), channel_id=1, source_target_pairs={{4,0},{6,2},{8,4},{10,6},{12,8},{14,10},{16,12},{18,14},{20,16},{2... | collective-permute-start | bytes 1572872 | tf_op jit(solution)/shard_map/ppermute | solution.py:53
  11.9 20.7 %collective-permute-done.2 = f32[2,2,256,128]{3,2,1,0:T(8,128)S(1)} collective-permute-done((f32[2,2,256,128]{3,2,1,0:T(8,128)S(1)}, f32[2,2,256,128]{3,2,1,0:T(8,128)S(1)}, u32[]{:S(2)}, u32[]{:S(2)}) %collective-permute-start.2) | collective-permute-done | bytes 524320 | tf_op jit(solution)/shard_map/ppermute | solution.py:53
  32.8 1.9 %collective-permute-start.4 = (f32[8,256,128]{2,1,0:T(8,128)S(1)}, f32[8,256,128]{2,1,0:T(8,128)S(1)}, u32[]{:S(2)}, u32[]{:S(2)}) collective-permute-start(f32[8,256,128]{2,1,0:T(8,128)S(1)} %pad_maximum_fusion.7), channel_id=1, source_target_pairs={{0,1},{1,0},{2,3},{3,2},{4,5},{5,4},{6,7},{7,6},{8,9},{9,8},{10,11... | collective-permute-start | bytes 3145736 | tf_op jit(solution)/shard_map/ppermute | solution.py:97
  35.1 1.8 %collective-permute-done.4 = f32[8,256,128]{2,1,0:T(8,128)S(1)} collective-permute-done((f32[8,256,128]{2,1,0:T(8,128)S(1)}, f32[8,256,128]{2,1,0:T(8,128)S(1)}, u32[]{:S(2)}, u32[]{:S(2)}) %collective-permute-start.4) | collective-permute-done | bytes 1048608 | tf_op jit(solution)/shard_map/ppermute | solution.py:97
  39.6 2.2 %fusion.22 = f32[8,256,128]{2,1,0:T(8,128)S(1)} fusion(f32[8,256,128]{2,1,0:T(8,128)S(1)} %slice_bitcast_fusion.1, f32[2,2,256,128]{3,2,1,0:T(8,128)S(1)} %copy-done.9, f32[2,2,256,128]{3,2,1,0:T(8,128)S(1)} %copy-done.18, f32[2,2,256,128]{3,2,1,0:T(8,128)S(1)} %copy-done.7, f32[2,2,256,128]{3,2,1,0:T(8,128)S(1)} %copy-done.5, ...), kind=kLoop, calls=%fused_computation.63 | loop fusion | flops 10747904 | bytes 8912904 | tf_op jit(solution)/shard_map/jit(_where)/select_n | solution.py:116
  41.9 2.1 %fusion.246 = (f32[6,256,128]{2,1,0:T(8,128)}, f32[6,256,128]{2,1,0:T(8,128)S(1)}) fusion(f32[10,256,128]{2,1,0:T(8,128)S(1)} %get-tuple-element.7, f32[6,256,128]{2,1,0:T(8,128)S(1)} %slice.530, f32[6,256,128]{2,1,0:T(8,128)S(1)} %slice.532, f32[8,256,128]{2,1,0:T(8,128)S(1)} %fusion.22, f32[10,256,128]{2,1,0:T(8,128)S(1)} %get-tuple-element.6, ...), kind=kLoop, calls=%fused_computation.361 | loop fusion | flops 6881280 | bytes 7077894 | tf_op jit(solution)/shard_map/slice | solution.py:22
  45.0 1.2 %broadcast_select_fusion = (f32[2,256,128]{2,1,0:T(8,128)}, f32[2,256,128]{2,1,0:T(8,128)}) fusion(f32[2,256,128]{2,1,0:T(8,128)S(1)} %copy-done.23, pred[]{:T(512)S(6)} %eq.9, f32[2,256,128]{2,1,0:T(8,128)S(1)} %slice.544, f32[10,256,128]{2,1,0:T(8,128)S(1)} %get-tuple-element.7, f32[2,256,128]{2,1,0:T(8,128)S(1)} %slice.546, ...), kind=kLoop, calls=%fused_computation.294 | loop fusion | flops 2293760 | bytes 2621441 | tf_op jit(solution)/shard_map/jit(_where)/select_n | solution.py:120
  46.2 13.4 %collective-permute-start.5 = (f32[2,256,128]{2,1,0:T(8,128)}, f32[2,256,128]{2,1,0:T(8,128)}, u32[]{:S(2)}, u32[]{:S(2)}) collective-permute-start(f32[2,256,128]{2,1,0:T(8,128)} %get-tuple-element.4), channel_id=1, source_target_pairs={{1,4},{0,5},{3,6},{2,7},{5,8},{4,9},{7,10},{6,11},{9,12},{8,13},{1... | collective-permute-start | bytes 786440 | tf_op jit(solution)/shard_map/ppermute | solution.py:53
  59.6 2.0 %collective-permute-start.6 = (f32[2,256,128]{2,1,0:T(8,128)}, f32[2,256,128]{2,1,0:T(8,128)}, u32[]{:S(2)}, u32[]{:S(2)}) collective-permute-start(f32[2,256,128]{2,1,0:T(8,128)} %get-tuple-element.4), channel_id=1, source_target_pairs={{1,2},{0,3},{3,4},{2,5},{5,6},{4,7},{7,8},{6,9},{9,10},{8,11},{11,... | collective-permute-start | bytes 786440 | tf_op jit(solution)/shard_map/ppermute | solution.py:53
  61.7 1.3 %collective-permute-start.8 = (f32[2,256,128]{2,1,0:T(8,128)}, f32[2,256,128]{2,1,0:T(8,128)}, u32[]{:S(2)}, u32[]{:S(2)}) collective-permute-start(f32[2,256,128]{2,1,0:T(8,128)} %get-tuple-element.4), channel_id=1, source_target_pairs={{3,0},{2,1},{5,2},{4,3},{7,4},{6,5},{9,6},{8,7},{11,8},{10,9},{13,... | collective-permute-start | bytes 786440 | tf_op jit(solution)/shard_map/ppermute | solution.py:53
  63.0 1.3 %collective-permute-start.9 = (f32[2,256,128]{2,1,0:T(8,128)}, f32[2,256,128]{2,1,0:T(8,128)}, u32[]{:S(2)}, u32[]{:S(2)}) collective-permute-start(f32[2,256,128]{2,1,0:T(8,128)} %get-tuple-element.4), channel_id=1, source_target_pairs={{5,0},{4,1},{7,2},{6,3},{9,4},{8,5},{11,6},{10,7},{13,8},{12,9},{1... | collective-permute-start | bytes 786440 | tf_op jit(solution)/shard_map/ppermute | solution.py:53
  65.1 2.0 %reduce_sum.29 = f32[3,256,128]{2,1,0:T(8,128)} reduce(f32[3,2,256,128]{3,2,1,0:T(8,128)} %bitcast.66, f32[]{:T(128)} %constant.20.clone.1), dimensions={1}, to_apply=%region_2.3 | reduce | flops 98304 | bytes 1179652 | tf_op jit(solution)/shard_map/reduce_sum | solution.py:32
  67.1 1.4 %fusion.249 = f32[64,3,256]{2,0,1:T(8,128)S(1)} fusion(f32[128,64,1]{1,0,2:T(8,128)} %constant.90, f32[3,256,128]{2,1,0:T(8,128)} %reduce_sum.28), kind=kOutput, calls=%fused_computation.364 | convolution fusion | flops 37748736 | bytes 622592 | tf_op jit(solution)/shard_map/Yy,mYZ,Zz->myz/dot_general | solution.py:35
  68.5 1.4 %fusion.250 = f32[64,3,256]{2,0,1:T(8,128)S(1)} fusion(f32[128,64,1]{1,0,2:T(8,128)} %constant.90, f32[3,256,128]{2,1,0:T(8,128)} %reduce_sum.29), kind=kOutput, calls=%fused_computation.365 | convolution fusion | flops 37748736 | bytes 622592 | tf_op jit(solution)/shard_map/Yy,mYZ,Zz->myz/dot_general | solution.py:35
  70.6 1.0 constant_dynamic-update-slice_fusion.9
  71.6 1.0 constant_dynamic-update-slice_fusion.8
  72.6 1.0 constant_dynamic-update-slice_fusion.7
  73.5 1.0 collective-permute-done.8
  74.5 1.0 constant_dynamic-update-slice_fusion.6
  75.5 1.1 %constant_dynamic-update-slice_fusion.5 = f32[10,256,128]{2,1,0:T(8,128)S(1)} fusion(f32[10,256,128]{2,1,0:T(8,128)S(1)} %constant_dynamic-update-slice_fusion.6, f32[2,256,128]{2,1,0:T(8,128)} %collective-permute-done.9), kind=kLoop, calls=%fused_computation.344 | loop fusion | bytes 524288 | tf_op jit(solution)/shard_map/concatenate | solution.py:122
  76.8 3.2 %fusion.38 = f32[8,256,128]{2,1,0:T(8,128)S(1)} fusion(f32[8,256,128]{2,1,0:T(8,128)S(1)} %slice.551, f32[2,256,128]{2,1,0:T(8,128)} %collective-permute-done.9, f32[2,256,128]{2,1,0:T(8,128)} %collective-permute-done.8, f32[2,256,128]{2,1,0:T(8,128)} %collective-permute-done.7, f32[2,256,128]{2,1,0:T(8,128)} %collective-permute-done.6, ...), kind=kLoop, calls=%fused_computation.79 | loop fusion | flops 10747904 | bytes 7602184 | tf_op jit(solution)/shard_map/jit(_where)/select_n | solution.py:116
  80.1 1.2 %fusion.90 = f32[6,256,128]{2,1,0:T(8,128)S(1)} fusion(f32[6,256,128]{2,1,0:T(8,128)S(1)} %slice.552, f32[8,256,128]{2,1,0:T(8,128)S(1)} %fusion.38, pred[6]{0:T(512)(128)(4,1)S(1)} %slice_compare_fusion.1, f32[6,256,128]{2,1,0:T(8,128)S(1)} %slice.532, f32[10,256,128]{2,1,0:T(8,128)S(1)} %get-tuple-element.6, f32[10,256,128]{2,1,0:T(8,128)S(1)} %get-tuple-element.7), kind=kLoop, calls=%fused_computation.156 | loop fusion | flops 6881280 | bytes 6291462 | tf_op jit(solution)/shard_map/jit(_where)/select_n | solution.py:116
  81.4 1.0 copy-done.3
  82.4 0.8 fusion.139
  83.4 1.1 %fusion.243 = (f32[256,128]{1,0:T(8,128)S(1)}, f32[2,256,128]{2,1,0:T(8,128)}) fusion(f32[2,256,128]{2,1,0:T(8,128)S(1)} %copy-done.14, f32[2,256,128]{2,1,0:T(8,128)S(1)} %slice.558, f32[10,256,128]{2,1,0:T(8,128)S(1)} %get-tuple-element.7, f32[2,256,128]{2,1,0:T(8,128)S(1)} %copy-done.16, f32[4,256,128]{2,1,0:T(8,128)S(1)} %fusion.139, ...), kind=kLoop, calls=%fused_computation.360 | loop fusion | flops 2326528 | bytes 2490368 | tf_op jit(solution)/shard_map/reduce_sum | solution.py:32
  85.1 1.3 %collective-permute-start.10 = (f32[1,128,64]{1,2,0:T(8,128)S(1)}, f32[1,128,64]{1,2,0:T(8,128)S(1)}, u32[]{:S(2)}, u32[]{:S(2)}) collective-permute-start(f32[1,128,64]{1,2,0:T(8,128)S(1)} %fusion.4), channel_id=1, source_target_pairs={{0,1},{2,3},{4,5},{6,7},{8,9},{10,11},{12,13},{14,15},{16,17},{18,... | collective-permute-start | bytes 98312 | tf_op jit(solution)/shard_map/ppermute | solution.py:53
  87.0 1.3 %collective-permute-start.11 = (f32[1,128,64]{1,2,0:T(8,128)S(1)}, f32[1,128,64]{1,2,0:T(8,128)S(1)}, u32[]{:S(2)}, u32[]{:S(2)}) collective-permute-start(f32[1,128,64]{1,2,0:T(8,128)S(1)} %fusion.4), channel_id=1, source_target_pairs={{2,1},{4,3},{6,5},{8,7},{10,9},{12,11},{14,13},{16,15},{18,17},{20... | collective-permute-start | bytes 98312 | tf_op jit(solution)/shard_map/ppermute | solution.py:53
  88.6 11.6 %collective-permute-done.11 = f32[1,128,64]{1,2,0:T(8,128)S(1)} collective-permute-done((f32[1,128,64]{1,2,0:T(8,128)S(1)}, f32[1,128,64]{1,2,0:T(8,128)S(1)}, u32[]{:S(2)}, u32[]{:S(2)}) %collective-permute-start.11) | collective-permute-done | bytes 32800 | tf_op jit(solution)/shard_map/ppermute | solution.py:53
  (95 shorter events, 9.1 us)
Async XLA Ops:
  0.6 11.2 %copy-start.12 = (f32[2,256,128]{2,1,0:T(8,128)S(1)}, f32[2,256,128]{2,1,0:T(8,128)}, u32[]{:S(2)}) copy-start(f32[2,256,128]{2,1,0:T(8,128)} %param.14) | copy-start | bytes 786436
  0.6 11.2 %copy-start.13 = (f32[2,256,128]{2,1,0:T(8,128)S(1)}, f32[2,256,128]{2,1,0:T(8,128)}, u32[]{:S(2)}) copy-start(f32[2,256,128]{2,1,0:T(8,128)} %param.15) | copy-start | bytes 786436
  1.9 30.8 %copy-start.17 = (f32[2,2,256,128]{3,2,1,0:T(8,128)}, f32[2,2,256,128]{3,2,1,0:T(8,128)S(1)}, u32[]{:S(2)}) copy-start(f32[2,2,256,128]{3,2,1,0:T(8,128)S(1)} %fusion.105) | copy-start | bytes 1572868
  1.9 30.7 %collective-permute-start = (f32[2,2,256,128]{3,2,1,0:T(8,128)S(1)}, f32[2,2,256,128]{3,2,1,0:T(8,128)S(1)}, u32[]{:S(2)}, u32[]{:S(2)}) collective-permute-start(f32[2,2,256,128]{3,2,1,0:T(8,128)S(1)} %fusion.105), channel_id=1, source_target_pairs={{0,4},{2,6},{4,8},{6,10},{8,12},{10,14},{12,16},{14,18},{16,20},{1... | collective-permute-start | bytes 1572872 | tf_op jit(solution)/shard_map/ppermute | solution.py:53
  5.9 26.7 %collective-permute-start.1 = (f32[2,2,256,128]{3,2,1,0:T(8,128)S(1)}, f32[2,2,256,128]{3,2,1,0:T(8,128)S(1)}, u32[]{:S(2)}, u32[]{:S(2)}) collective-permute-start(f32[2,2,256,128]{3,2,1,0:T(8,128)S(1)} %fusion.105), channel_id=1, source_target_pairs={{0,2},{2,4},{4,6},{6,8},{8,10},{10,12},{12,14},{14,16},{16,18},{18... | collective-permute-start | bytes 1572872 | tf_op jit(solution)/shard_map/ppermute | solution.py:53
  9.1 23.5 %collective-permute-start.2 = (f32[2,2,256,128]{3,2,1,0:T(8,128)S(1)}, f32[2,2,256,128]{3,2,1,0:T(8,128)S(1)}, u32[]{:S(2)}, u32[]{:S(2)}) collective-permute-start(f32[2,2,256,128]{3,2,1,0:T(8,128)S(1)} %fusion.105), channel_id=1, source_target_pairs={{2,0},{4,2},{6,4},{8,6},{10,8},{12,10},{14,12},{16,14},{18,16},{20... | collective-permute-start | bytes 1572872 | tf_op jit(solution)/shard_map/ppermute | solution.py:53
  10.4 22.2 %collective-permute-start.3 = (f32[2,2,256,128]{3,2,1,0:T(8,128)S(1)}, f32[2,2,256,128]{3,2,1,0:T(8,128)S(1)}, u32[]{:S(2)}, u32[]{:S(2)}) collective-permute-start(f32[2,2,256,128]{3,2,1,0:T(8,128)S(1)} %fusion.105), channel_id=1, source_target_pairs={{4,0},{6,2},{8,4},{10,6},{12,8},{14,10},{16,12},{18,14},{20,16},{2... | collective-permute-start | bytes 1572872 | tf_op jit(solution)/shard_map/ppermute | solution.py:53
  32.5 2.4 %copy-start.8 = (f32[2,2,256,128]{3,2,1,0:T(8,128)}, f32[2,2,256,128]{3,2,1,0:T(8,128)S(1)}, u32[]{:S(2)}) copy-start(f32[2,2,256,128]{3,2,1,0:T(8,128)S(1)} %collective-permute-done.2) | copy-start | bytes 1572868
  32.5 2.4 %copy-start.10 = (f32[2,2,256,128]{3,2,1,0:T(8,128)}, f32[2,2,256,128]{3,2,1,0:T(8,128)S(1)}, u32[]{:S(2)}) copy-start(f32[2,2,256,128]{3,2,1,0:T(8,128)S(1)} %collective-permute-done.3) | copy-start | bytes 1572868
  32.6 2.1 %copy-start.4 = (f32[2,2,256,128]{3,2,1,0:T(8,128)}, f32[2,2,256,128]{3,2,1,0:T(8,128)S(1)}, u32[]{:S(2)}) copy-start(f32[2,2,256,128]{3,2,1,0:T(8,128)S(1)} %collective-permute-done) | copy-start | bytes 1572868
  32.6 2.2 %copy-start.6 = (f32[2,2,256,128]{3,2,1,0:T(8,128)}, f32[2,2,256,128]{3,2,1,0:T(8,128)S(1)}, u32[]{:S(2)}) copy-start(f32[2,2,256,128]{3,2,1,0:T(8,128)S(1)} %collective-permute-done.1) | copy-start | bytes 1572868
  32.7 2.1 %copy-start.19 = (f32[1,2,256,128]{3,2,1,0:T(8,128)S(1)}, f32[1,2,256,128]{3,2,1,0:T(8,128)}, u32[]{:S(2)}) copy-start(f32[1,2,256,128]{3,2,1,0:T(8,128)} %param.13) | copy-start | bytes 786436
  32.8 4.2 %collective-permute-start.4 = (f32[8,256,128]{2,1,0:T(8,128)S(1)}, f32[8,256,128]{2,1,0:T(8,128)S(1)}, u32[]{:S(2)}, u32[]{:S(2)}) collective-permute-start(f32[8,256,128]{2,1,0:T(8,128)S(1)} %pad_maximum_fusion.7), channel_id=1, source_target_pairs={{0,1},{1,0},{2,3},{3,2},{4,5},{5,4},{6,7},{7,6},{8,9},{9,8},{10,11... | collective-permute-start | bytes 3145736 | tf_op jit(solution)/shard_map/ppermute | solution.py:97
  37.3 1.4 %copy-start.5 = (f32[2,2,256,128]{3,2,1,0:T(8,128)S(1)}, f32[2,2,256,128]{3,2,1,0:T(8,128)}, u32[]{:S(2)}) copy-start(f32[2,2,256,128]{3,2,1,0:T(8,128)} %copy-done.4) | copy-start | bytes 1572868
  37.3 1.9 %copy-start.7 = (f32[2,2,256,128]{3,2,1,0:T(8,128)S(1)}, f32[2,2,256,128]{3,2,1,0:T(8,128)}, u32[]{:S(2)}) copy-start(f32[2,2,256,128]{3,2,1,0:T(8,128)} %copy-done.6) | copy-start | bytes 1572868
  37.3 2.0 %copy-start.9 = (f32[2,2,256,128]{3,2,1,0:T(8,128)S(1)}, f32[2,2,256,128]{3,2,1,0:T(8,128)}, u32[]{:S(2)}) copy-start(f32[2,2,256,128]{3,2,1,0:T(8,128)} %copy-done.8) | copy-start | bytes 1572868
  37.3 2.1 %copy-start.11 = (f32[2,2,256,128]{3,2,1,0:T(8,128)S(1)}, f32[2,2,256,128]{3,2,1,0:T(8,128)}, u32[]{:S(2)}) copy-start(f32[2,2,256,128]{3,2,1,0:T(8,128)} %copy-done.10) | copy-start | bytes 1572868
  37.3 2.3 %copy-start.18 = (f32[2,2,256,128]{3,2,1,0:T(8,128)S(1)}, f32[2,2,256,128]{3,2,1,0:T(8,128)}, u32[]{:S(2)}) copy-start(f32[2,2,256,128]{3,2,1,0:T(8,128)} %copy-done.17) | copy-start | bytes 1572868
  37.5 6.5 %copy-start.2 = (f32[4,256,128]{2,1,0:T(8,128)}, f32[4,256,128]{2,1,0:T(8,128)S(1)}, u32[]{:S(2)}) copy-start(f32[4,256,128]{2,1,0:T(8,128)S(1)} %slice.539) | copy-start | bytes 1572868
  37.5 7.4 %copy-start.15 = (f32[2,256,128]{2,1,0:T(8,128)}, f32[2,256,128]{2,1,0:T(8,128)S(1)}, u32[]{:S(2)}) copy-start(f32[2,256,128]{2,1,0:T(8,128)S(1)} %slice.546) | copy-start | bytes 786436
  46.2 24.4 %collective-permute-start.5 = (f32[2,256,128]{2,1,0:T(8,128)}, f32[2,256,128]{2,1,0:T(8,128)}, u32[]{:S(2)}, u32[]{:S(2)}) collective-permute-start(f32[2,256,128]{2,1,0:T(8,128)} %get-tuple-element.4), channel_id=1, source_target_pairs={{1,4},{0,5},{3,6},{2,7},{5,8},{4,9},{7,10},{6,11},{9,12},{8,13},{1... | collective-permute-start | bytes 786440 | tf_op jit(solution)/shard_map/ppermute | solution.py:53
  59.6 12.0 %collective-permute-start.6 = (f32[2,256,128]{2,1,0:T(8,128)}, f32[2,256,128]{2,1,0:T(8,128)}, u32[]{:S(2)}, u32[]{:S(2)}) collective-permute-start(f32[2,256,128]{2,1,0:T(8,128)} %get-tuple-element.4), channel_id=1, source_target_pairs={{1,2},{0,3},{3,4},{2,5},{5,6},{4,7},{7,8},{6,9},{9,10},{8,11},{11,... | collective-permute-start | bytes 786440 | tf_op jit(solution)/shard_map/ppermute | solution.py:53
  61.6 11.0 %collective-permute-start.7 = (f32[2,256,128]{2,1,0:T(8,128)}, f32[2,256,128]{2,1,0:T(8,128)}, u32[]{:S(2)}, u32[]{:S(2)}) collective-permute-start(f32[2,256,128]{2,1,0:T(8,128)} %get-tuple-element.4), channel_id=1, source_target_pairs={{1,0},{0,1},{3,2},{2,3},{5,4},{4,5},{7,6},{6,7},{9,8},{8,9},{11,10... | collective-permute-start | bytes 786440 | tf_op jit(solution)/shard_map/ppermute | solution.py:53
  61.7 12.8 %collective-permute-start.8 = (f32[2,256,128]{2,1,0:T(8,128)}, f32[2,256,128]{2,1,0:T(8,128)}, u32[]{:S(2)}, u32[]{:S(2)}) collective-permute-start(f32[2,256,128]{2,1,0:T(8,128)} %get-tuple-element.4), channel_id=1, source_target_pairs={{3,0},{2,1},{5,2},{4,3},{7,4},{6,5},{9,6},{8,7},{11,8},{10,9},{13,... | collective-permute-start | bytes 786440 | tf_op jit(solution)/shard_map/ppermute | solution.py:53
  63.0 12.5 %collective-permute-start.9 = (f32[2,256,128]{2,1,0:T(8,128)}, f32[2,256,128]{2,1,0:T(8,128)}, u32[]{:S(2)}, u32[]{:S(2)}) collective-permute-start(f32[2,256,128]{2,1,0:T(8,128)} %get-tuple-element.4), channel_id=1, source_target_pairs={{5,0},{4,1},{7,2},{6,3},{9,4},{8,5},{11,6},{10,7},{13,8},{12,9},{1... | collective-permute-start | bytes 786440 | tf_op jit(solution)/shard_map/ppermute | solution.py:53
  65.1 4.8 %copy-start.21 = (f32[256,128,1]{1,0,2:T(8,128)S(1)}, f32[256,128,1]{1,0,2:T(8,128)}, u32[]{:S(2)}) copy-start(f32[256,128,1]{1,0,2:T(8,128)} %constant.91) | copy-start | bytes 393220
  75.5 1.3 %copy-start.1 = (f32[8,256,128]{2,1,0:T(8,128)S(1)}, f32[8,256,128]{2,1,0:T(8,128)}, u32[]{:S(2)}) copy-start(f32[8,256,128]{2,1,0:T(8,128)} %copy-done) | copy-start | bytes 3145732
  83.3 1.3 %copy-start.22 = (f32[128,64]{1,0:T(8,128)S(1)}, f32[128,64]{1,0:T(8,128)}, u32[]{:S(2)}) copy-start(f32[128,64]{1,0:T(8,128)} %constant.27.clone) | copy-start | bytes 98308
  83.4 1.4 %copy-start.20 = (f32[256,128]{1,0:T(8,128)S(1)}, f32[256,128]{1,0:T(8,128)}, u32[]{:S(2)}) copy-start(f32[256,128]{1,0:T(8,128)} %constant.26.clone) | copy-start | bytes 393220
  85.1 3.5 %collective-permute-start.10 = (f32[1,128,64]{1,2,0:T(8,128)S(1)}, f32[1,128,64]{1,2,0:T(8,128)S(1)}, u32[]{:S(2)}, u32[]{:S(2)}) collective-permute-start(f32[1,128,64]{1,2,0:T(8,128)S(1)} %fusion.4), channel_id=1, source_target_pairs={{0,1},{2,3},{4,5},{6,7},{8,9},{10,11},{12,13},{14,15},{16,17},{18,... | collective-permute-start | bytes 98312 | tf_op jit(solution)/shard_map/ppermute | solution.py:53
  86.4 2.3 %collective-permute-start.12 = (f32[1,128,64]{1,2,0:T(8,128)S(1)}, f32[1,128,64]{1,2,0:T(8,128)S(1)}, u32[]{:S(2)}, u32[]{:S(2)}) collective-permute-start(f32[1,128,64]{1,2,0:T(8,128)S(1)} %fusion.4), channel_id=1, source_target_pairs={{0,3},{2,5},{4,7},{6,9},{8,11},{10,13},{12,15},{14,17},{16,19},{18... | collective-permute-start | bytes 98312 | tf_op jit(solution)/shard_map/ppermute | solution.py:53
  87.0 13.2 %collective-permute-start.11 = (f32[1,128,64]{1,2,0:T(8,128)S(1)}, f32[1,128,64]{1,2,0:T(8,128)S(1)}, u32[]{:S(2)}, u32[]{:S(2)}) collective-permute-start(f32[1,128,64]{1,2,0:T(8,128)S(1)} %fusion.4), channel_id=1, source_target_pairs={{2,1},{4,3},{6,5},{8,7},{10,9},{12,11},{14,13},{16,15},{18,17},{20... | collective-permute-start | bytes 98312 | tf_op jit(solution)/shard_map/ppermute | solution.py:53
  (5 other events, 4.9 us)

commit v11 on v6

--- a/solution.py
+++ b/solution.py
@@ -105,8 +105,8 @@
     plane_ids = me_s * n - halo + jnp.arange(n + 2 * halo)
     inside = ((plane_ids >= 0) & (plane_ids < space * n)).astype(jnp.float32)[:, None, None]
 
-    def fine_prop(field):
-        for number in range(STEPS):
+    def fine_prop(field, first_step=0):
+        for number in range(first_step, STEPS):
             cut = number
             k = conduct[cut : conduct.shape[0] - cut]
             c = absorb[cut : absorb.shape[0] - cut]
@@ -119,8 +119,18 @@
     advanced = fine_prop(field0)
     payload = jnp.where(me_t == times - 1, initial, advanced)
     got2 = gather_planes(payload, ("space", "tm"), prev_pairs, distances)
-    relaxed = jnp.concatenate([got2[d] for d in distances], axis=0)[lo:hi]
-    residual = fine_prop(relaxed) - advanced
+    if lo == 0 and n == 2 and halo == 4:
+        blocks = [got2[d] for d in distances]
+        flat = [blk[i] for blk in blocks for i in range(n)]
+        outs = []
+        for p0, p1 in [(1, 2), (2, 4), (4, 6), (6, 8), (8, 9)]:
+            window = jnp.stack(flat[p0 - 1 : p1 + 1])
+            piece = advance(window, conduct[p0 - 1 : p1 + 1], absorb[p0 - 1 : p1 + 1], 0.1, 0.1)
+            outs.append(jnp.where(inside[p0:p1] > 0, piece, 0.0))
+        residual = fine_prop(jnp.concatenate(outs, axis=0), first_step=1) - advanced
+    else:
+        relaxed = jnp.concatenate([got2[d] for d in distances], axis=0)[lo:hi]
+        residual = fine_prop(relaxed) - advanced
 
     cn = n // 2
     creach = -(-1 // cn)

time: 103 us -> 108 us (1.049)
  other arithmetic: 18.2 us -> 25 us
  waiting for transfers between devices: 35 us -> 31.5 us
  starting transfers between devices: 33 us -> 35.3 us
  local copies, waits for them, and re-layouts: 9.25 us -> 7.06 us
  between operations: 1.26 us -> 2.59 us
    select_n x1 -> x5, other arithmetic: 0.2 us -> 7.32 us  [the longest x4 7.11 us: shards(): outs.append(jnp.where(inside[p0:p1] > 0, piece, 0.0))]
    unnamed x55 -> x49, local copies, waits for them, and re-layouts: 7.55 us -> 3.13 us
    ppermute x12, waiting for transfers between devices: 33.2 us -> 29.6 us  [gather_planes(): pieces[d] = lax.ppermute(block, axis_names, pairs_of(d))]
    slice x0 -> x4, local copies, waits for them, and re-layouts: none -> 3.4 us  [the longest x3 2.81 us: shards(): flat = [blk[i] for blk in blocks for i in range(n)]]
    select_n x5 -> x4, other arithmetic: 8.33 us -> 5.27 us  [fine_prop(): field = jnp.where(m > 0, field, 0.0)]
    ppermute x12, starting transfers between devices: 31.1 us -> 33.4 us  [gather_planes(): pieces[d] = lax.ppermute(block, axis_names, pairs_of(d))]
    slice x0 -> x1, other arithmetic: none -> 2.15 us  [advance(): middle = conduct[1:-1]]
  transfers between devices with their start and end apart: 13 -> 13, of which waited for: 4 -> 4; matrix products, arithmetic and copies ran while one was open for 11% -> 12% of each run, Pallas kernels for 0% -> 0%
where the time goes in v11:
time: 108 us; the launch traced here: 107 us
  starting transfers between devices  35.3 us (33%)
  waiting for transfers between devices  31.5 us (29%)
  other arithmetic  25 us (23%)
  local copies, waits for them, and re-layouts  7.06 us (7%)
  matrix products  5.11 us (5%)
  between operations  2.59 us (2%)
    ppermute x12, starting transfers between devices, gather_planes(): pieces[d] = lax.ppermute(block, axis_names, pairs_of(d))  33.4 us
    ppermute x12, waiting for transfers between devices, gather_planes(): pieces[d] = lax.ppermute(block, axis_names, pairs_of(d))  29.6 us
    select_n x4, other arithmetic, shards(): outs.append(jnp.where(inside[p0:p1] > 0, piece, 0.0))  7.11 us
    select_n x4, other arithmetic, fine_prop(): field = jnp.where(m > 0, field, 0.0)  5.27 us
    dot_general x6, matrix products, restrict(): jnp.einsum('Yy,mYZ,Zz->myz', rows, planes, cols, precision=lax.Precision....  4.43 us
    reduce_sum x3, other arithmetic, restrict(): planes = field.reshape(first // 2, 2, second, third).sum(axis=1)  3.94 us
    unnamed x49, local copies, waits for them, and re-layouts  3.13 us
    slice x3, local copies, waits for them, and re-layouts, shards(): flat = [blk[i] for blk in blocks for i in range(n)]  2.81 us
  transfers between devices with their start and end apart: 13, of which 4 were waited for; matrix products, arithmetic and copies ran while one was open for 12% of the time, Pallas kernels for 0%

profile of v11, /device:TPU:1, one launch (start us, length us, event | category | flops | bytes accessed | tf_op | source)
XLA Modules:
  0.0 106.6 jit_solution(16856956764680214099)
XLA Ops:
  0.7 1.2 %fusion.89 = f32[2,2,256,128]{3,2,1,0:T(8,128)S(1)} fusion(f32[1,2,256,128]{3,2,1,0:T(8,128)} %param.13, f32[1,2,256,128]{3,2,1,0:T(8,128)} %bitcast.69, f32[1,2,256,128]{3,2,1,0:T(8,128)} %bitcast.71, pred[]{:T(512)S(6)} %eq.8), kind=kLoop, calls=%fused_computation.182 | loop fusion | flops 393216 | bytes 1310721 | tf_op jit(solution)/shard_map/jit(_where)/select_n | solution.py:87
  1.9 4.0 %collective-permute-start = (f32[2,2,256,128]{3,2,1,0:T(8,128)S(1)}, f32[2,2,256,128]{3,2,1,0:T(8,128)S(1)}, u32[]{:S(2)}, u32[]{:S(2)}) collective-permute-start(f32[2,2,256,128]{3,2,1,0:T(8,128)S(1)} %fusion.89), channel_id=1, source_target_pairs={{0,4},{2,6},{4,8},{6,10},{8,12},{10,14},{12,16},{14,18},{16,20},{1... | collective-permute-start | bytes 1572872 | tf_op jit(solution)/shard_map/ppermute | solution.py:53
  5.9 3.1 %collective-permute-start.1 = (f32[2,2,256,128]{3,2,1,0:T(8,128)S(1)}, f32[2,2,256,128]{3,2,1,0:T(8,128)S(1)}, u32[]{:S(2)}, u32[]{:S(2)}) collective-permute-start(f32[2,2,256,128]{3,2,1,0:T(8,128)S(1)} %fusion.89), channel_id=1, source_target_pairs={{0,2},{2,4},{4,6},{6,8},{8,10},{10,12},{12,14},{14,16},{16,18},{18... | collective-permute-start | bytes 1572872 | tf_op jit(solution)/shard_map/ppermute | solution.py:53
  9.1 1.3 %collective-permute-start.2 = (f32[2,2,256,128]{3,2,1,0:T(8,128)S(1)}, f32[2,2,256,128]{3,2,1,0:T(8,128)S(1)}, u32[]{:S(2)}, u32[]{:S(2)}) collective-permute-start(f32[2,2,256,128]{3,2,1,0:T(8,128)S(1)} %fusion.89), channel_id=1, source_target_pairs={{2,0},{4,2},{6,4},{8,6},{10,8},{12,10},{14,12},{16,14},{18,16},{20... | collective-permute-start | bytes 1572872 | tf_op jit(solution)/shard_map/ppermute | solution.py:53
  10.4 1.3 %collective-permute-start.3 = (f32[2,2,256,128]{3,2,1,0:T(8,128)S(1)}, f32[2,2,256,128]{3,2,1,0:T(8,128)S(1)}, u32[]{:S(2)}, u32[]{:S(2)}) collective-permute-start(f32[2,2,256,128]{3,2,1,0:T(8,128)S(1)} %fusion.89), channel_id=1, source_target_pairs={{4,0},{6,2},{8,4},{10,6},{12,8},{14,10},{16,12},{18,14},{20,16},{2... | collective-permute-start | bytes 1572872 | tf_op jit(solution)/shard_map/ppermute | solution.py:53
  14.4 18.2 %collective-permute-done.2 = f32[2,2,256,128]{3,2,1,0:T(8,128)S(1)} collective-permute-done((f32[2,2,256,128]{3,2,1,0:T(8,128)S(1)}, f32[2,2,256,128]{3,2,1,0:T(8,128)S(1)}, u32[]{:S(2)}, u32[]{:S(2)}) %collective-permute-start.2) | collective-permute-done | bytes 524320 | tf_op jit(solution)/shard_map/ppermute | solution.py:53
  32.8 1.9 %collective-permute-start.4 = (f32[8,256,128]{2,1,0:T(8,128)S(1)}, f32[8,256,128]{2,1,0:T(8,128)S(1)}, u32[]{:S(2)}, u32[]{:S(2)}) collective-permute-start(f32[8,256,128]{2,1,0:T(8,128)S(1)} %pad_maximum_fusion.7), channel_id=1, source_target_pairs={{0,1},{1,0},{2,3},{3,2},{4,5},{5,4},{6,7},{7,6},{8,9},{9,8},{10,11... | collective-permute-start | bytes 3145736 | tf_op jit(solution)/shard_map/ppermute | solution.py:97
  35.1 1.8 %collective-permute-done.4 = f32[8,256,128]{2,1,0:T(8,128)S(1)} collective-permute-done((f32[8,256,128]{2,1,0:T(8,128)S(1)}, f32[8,256,128]{2,1,0:T(8,128)S(1)}, u32[]{:S(2)}, u32[]{:S(2)}) %collective-permute-start.4) | collective-permute-done | bytes 1048608 | tf_op jit(solution)/shard_map/ppermute | solution.py:97
  39.3 2.2 %fusion.15 = f32[8,256,128]{2,1,0:T(8,128)S(1)} fusion(f32[8,256,128]{2,1,0:T(8,128)S(1)} %slice_bitcast_fusion.1, f32[8,256,128]{2,1,0:T(8,128)S(1)} %slice.831, f32[10,256,128]{2,1,0:T(8,128)S(1)} %get-tuple-element.6, f32[2,2,256,128]{3,2,1,0:T(8,128)S(1)} %copy-done.7, f32[2,2,256,128]{3,2,1,0:T(8,128)S(1)} %copy-done.16, ...), kind=kLoop, calls=%fused_computation.52 | loop fusion | flops 10747904 | bytes 8912904 | tf_op jit(solution)/shard_map/jit(_where)/select_n | solution.py:116
  41.5 2.0 %fusion.371 = (f32[6,256,128]{2,1,0:T(8,128)}, f32[6,256,128]{2,1,0:T(8,128)S(1)}) fusion(f32[10,256,128]{2,1,0:T(8,128)S(1)} %get-tuple-element.6, f32[6,256,128]{2,1,0:T(8,128)S(1)} %slice.834, f32[6,256,128]{2,1,0:T(8,128)S(1)} %slice.836, f32[8,256,128]{2,1,0:T(8,128)S(1)} %fusion.15, f32[10,256,128]{2,1,0:T(8,128)S(1)} %get-tuple-element.7, ...), kind=kLoop, calls=%fused_computation.539 | loop fusion | flops 6881280 | bytes 7077894 | tf_op jit(solution)/shard_map/slice | solution.py:22
  44.5 1.2 %broadcast_select_fusion = (f32[2,256,128]{2,1,0:T(8,128)}, f32[2,256,128]{2,1,0:T(8,128)}) fusion(f32[2,256,128]{2,1,0:T(8,128)S(1)} %copy-done.20, pred[]{:T(512)S(6)} %eq.9, f32[2,256,128]{2,1,0:T(8,128)S(1)} %slice.848, f32[10,256,128]{2,1,0:T(8,128)S(1)} %get-tuple-element.6, f32[2,256,128]{2,1,0:T(8,128)S(1)} %slice.850, ...), kind=kLoop, calls=%fused_computation.474 | loop fusion | flops 2293760 | bytes 2883585 | tf_op jit(solution)/shard_map/jit(_where)/select_n | solution.py:120
  45.8 1.3 %collective-permute-start.8 = (f32[2,256,128]{2,1,0:T(8,128)}, f32[2,256,128]{2,1,0:T(8,128)}, u32[]{:S(2)}, u32[]{:S(2)}) collective-permute-start(f32[2,256,128]{2,1,0:T(8,128)} %get-tuple-element.4), channel_id=1, source_target_pairs={{3,0},{2,1},{5,2},{4,3},{7,4},{6,5},{9,6},{8,7},{11,8},{10,9},{13,... | collective-permute-start | bytes 786440 | tf_op jit(solution)/shard_map/ppermute | solution.py:53
  47.0 10.8 %collective-permute-start.5 = (f32[2,256,128]{2,1,0:T(8,128)}, f32[2,256,128]{2,1,0:T(8,128)}, u32[]{:S(2)}, u32[]{:S(2)}) collective-permute-start(f32[2,256,128]{2,1,0:T(8,128)} %get-tuple-element.4), channel_id=1, source_target_pairs={{1,2},{0,3},{3,4},{2,5},{5,6},{4,7},{7,8},{6,9},{9,10},{8,11},{11,... | collective-permute-start | bytes 786440 | tf_op jit(solution)/shard_map/ppermute | solution.py:53
  57.9 7.0 %collective-permute-start.7 = (f32[2,256,128]{2,1,0:T(8,128)}, f32[2,256,128]{2,1,0:T(8,128)}, u32[]{:S(2)}, u32[]{:S(2)}) collective-permute-start(f32[2,256,128]{2,1,0:T(8,128)} %get-tuple-element.4), channel_id=1, source_target_pairs={{1,4},{0,5},{3,6},{2,7},{5,8},{4,9},{7,10},{6,11},{9,12},{8,13},{1... | collective-permute-start | bytes 786440 | tf_op jit(solution)/shard_map/ppermute | solution.py:53
  64.9 1.3 %collective-permute-start.9 = (f32[2,256,128]{2,1,0:T(8,128)}, f32[2,256,128]{2,1,0:T(8,128)}, u32[]{:S(2)}, u32[]{:S(2)}) collective-permute-start(f32[2,256,128]{2,1,0:T(8,128)} %get-tuple-element.4), channel_id=1, source_target_pairs={{5,0},{4,1},{7,2},{6,3},{9,4},{8,5},{11,6},{10,7},{13,8},{12,9},{1... | collective-permute-start | bytes 786440 | tf_op jit(solution)/shard_map/ppermute | solution.py:53
  67.1 2.0 %reduce_sum.29 = f32[3,256,128]{2,1,0:T(8,128)} reduce(f32[3,2,256,128]{3,2,1,0:T(8,128)} %bitcast.68, f32[]{:T(128)} %constant.22.clone.1), dimensions={1}, to_apply=%region_2.3 | reduce | flops 98304 | bytes 1179652 | tf_op jit(solution)/shard_map/reduce_sum | solution.py:32
  69.1 1.6 %fusion.377 = f32[64,3,256]{2,0,1:T(8,128)S(1)} fusion(f32[128,64,1]{1,0,2:T(8,128)} %constant.113, f32[3,256,128]{2,1,0:T(8,128)} %reduce_sum.28), kind=kOutput, calls=%fused_computation.545 | convolution fusion | flops 75497472 | bytes 622592 | tf_op jit(solution)/shard_map/Yy,mYZ,Zz->myz/dot_general | solution.py:35
  70.6 1.6 %fusion.378 = f32[64,3,256]{2,0,1:T(8,128)S(1)} fusion(f32[128,64,1]{1,0,2:T(8,128)} %constant.113, f32[3,256,128]{2,1,0:T(8,128)} %reduce_sum.29), kind=kOutput, calls=%fused_computation.546 | convolution fusion | flops 75497472 | bytes 622592 | tf_op jit(solution)/shard_map/Yy,mYZ,Zz->myz/dot_general | solution.py:35
  72.6 1.0 fusion.374
  73.6 5.3 %collective-permute-done.7 = f32[2,256,128]{2,1,0:T(8,128)} collective-permute-done((f32[2,256,128]{2,1,0:T(8,128)}, f32[2,256,128]{2,1,0:T(8,128)}, u32[]{:S(2)}, u32[]{:S(2)}) %collective-permute-start.7) | collective-permute-done | bytes 262176 | tf_op jit(solution)/shard_map/ppermute | solution.py:53
  79.8 0.9 slice.864
  80.8 1.3 %fusion.278 = (f32[1,256,128]{2,1,0:T(8,128)S(1)}, f32[1,256,128]{2,1,0:T(8,128)S(1)}, f32[1,256,128]{2,1,0:T(8,128)S(1)}) fusion(f32[1,256,128]{2,1,0:T(8,128)S(1)} %slice.864, f32[1,256,128]{2,1,0:T(8,128)S(1)} %slice.868, f32[10,256,128]{2,1,0:T(8,128)S(1)} %get-tuple-element.6, f32[2,256,128]{2,1,0:T(8,128)} %collective-permute-done.8, ...), kind=kLoop, calls=%fused_computation.414 | loop fusion | flops 1146880 | bytes 1572865 | tf_op jit(solution)/shard_map/jit(_where)/select_n | solution.py:129
  82.1 1.3 %fusion.302 = (f32[1,256,128]{2,1,0:T(8,128)S(1)}, f32[1,256,128]{2,1,0:T(8,128)S(1)}) fusion(f32[1,256,128]{2,1,0:T(8,128)S(1)} %slice.858, f32[1,256,128]{2,1,0:T(8,128)S(1)} %get-tuple-element.11, f32[10,256,128]{2,1,0:T(8,128)S(1)} %get-tuple-element.6, f32[2,256,128]{2,1,0:T(8,128)} %collective-permute-done.7, ...), kind=kLoop, calls=%fused_computation.438 | loop fusion | flops 1146880 | bytes 1310721 | tf_op jit(solution)/shard_map/jit(_where)/select_n | solution.py:129
  83.4 2.1 %fusion.372 = (f32[2,256,128]{2,1,0:T(8,128)S(1)}, f32[2,256,128]{2,1,0:T(8,128)S(1)}) fusion(f32[10,256,128]{2,1,0:T(8,128)S(1)} %get-tuple-element.7, f32[2,256,128]{2,1,0:T(8,128)} %collective-permute-done.6, f32[10,256,128]{2,1,0:T(8,128)S(1)} %get-tuple-element.6, f32[2,256,128]{2,1,0:T(8,128)S(1)} %copy-done.11, ...), kind=kLoop, calls=%fused_computation.540 | loop fusion | flops 2424832 | bytes 2621442 | tf_op jit(solution)/shard_map/slice | solution.py:13
  85.5 2.4 %fusion.173 = (f32[2,256,128]{2,1,0:T(8,128)S(1)}, f32[2,256,128]{2,1,0:T(8,128)S(1)}) fusion(f32[2,256,128]{2,1,0:T(8,128)} %collective-permute-done.5, f32[2,256,128]{2,1,0:T(8,128)S(1)} %get-tuple-element.14, f32[10,256,128]{2,1,0:T(8,128)S(1)} %get-tuple-element.6, f32[1,256,128]{2,1,0:T(8,128)S(1)} %slice.858, ...), kind=kLoop, calls=%fused_computation.291 | loop fusion | flops 2424832 | bytes 2359298 | tf_op jit(solution)/shard_map/jit(_where)/select_n | solution.py:129
  87.9 2.2 %fusion.213 = f32[2,256,128]{2,1,0:T(8,128)S(1)} fusion(f32[2,256,128]{2,1,0:T(8,128)} %collective-permute-done.8, f32[2,256,128]{2,1,0:T(8,128)S(1)} %get-tuple-element.13, f32[10,256,128]{2,1,0:T(8,128)S(1)} %get-tuple-element.6, f32[1,256,128]{2,1,0:T(8,128)S(1)} %get-tuple-element.22, f32[1,256,128]{2,1,0:T(8,128)S(1)} %slice.864, ...), kind=kLoop, calls=%fused_computation.331 | loop fusion | flops 2424832 | bytes 1835010 | tf_op jit(solution)/shard_map/jit(_where)/select_n | solution.py:129
  90.1 1.5 %fusion.72 = f32[6,256,128]{2,1,0:T(8,128)S(1)} fusion(f32[6,256,128]{2,1,0:T(8,128)S(1)} %pad_maximum_fusion.14, f32[2,256,128]{2,1,0:T(8,128)S(1)} %fusion.213, f32[2,256,128]{2,1,0:T(8,128)S(1)} %get-tuple-element.15, f32[2,256,128]{2,1,0:T(8,128)S(1)} %get-tuple-element.12, f32[1,256,128]{2,1,0:T(8,128)S(1)} %get-tuple-element.19, ...), kind=kLoop, calls=%fused_computation.152 | loop fusion | flops 8060928 | bytes 5767174 | tf_op jit(solution)/shard_map/jit(_where)/select_n | solution.py:116
  91.7 1.0 copy-done.1
  93.6 1.1 %fusion.368 = (f32[256,128]{1,0:T(8,128)S(1)}, f32[2,256,128]{2,1,0:T(8,128)}) fusion(f32[2,256,128]{2,1,0:T(8,128)S(1)} %copy-done.14, f32[2,256,128]{2,1,0:T(8,128)S(1)} %slice.882, f32[10,256,128]{2,1,0:T(8,128)S(1)} %get-tuple-element.6, f32[2,256,128]{2,1,0:T(8,128)S(1)} %copy-done.11, f32[4,256,128]{2,1,0:T(8,128)S(1)} %fusion.123, ...), kind=kLoop, calls=%fused_computation.538 | loop fusion | flops 2326528 | bytes 2752512 | tf_op jit(solution)/shard_map/reduce_sum | solution.py:32
  95.4 1.3 %collective-permute-start.10 = (f32[1,128,64]{1,2,0:T(8,128)S(1)}, f32[1,128,64]{1,2,0:T(8,128)S(1)}, u32[]{:S(2)}, u32[]{:S(2)}) collective-permute-start(f32[1,128,64]{1,2,0:T(8,128)S(1)} %fusion.4), channel_id=1, source_target_pairs={{0,1},{2,3},{4,5},{6,7},{8,9},{10,11},{12,13},{14,15},{16,17},{18,... | collective-permute-start | bytes 98312 | tf_op jit(solution)/shard_map/ppermute | solution.py:53
  97.4 1.3 %collective-permute-start.11 = (f32[1,128,64]{1,2,0:T(8,128)S(1)}, f32[1,128,64]{1,2,0:T(8,128)S(1)}, u32[]{:S(2)}, u32[]{:S(2)}) collective-permute-start(f32[1,128,64]{1,2,0:T(8,128)S(1)} %fusion.4), channel_id=1, source_target_pairs={{2,1},{4,3},{6,5},{8,7},{10,9},{12,11},{14,13},{16,15},{18,17},{20... | collective-permute-start | bytes 98312 | tf_op jit(solution)/shard_map/ppermute | solution.py:53
  99.0 6.1 %collective-permute-done.11 = f32[1,128,64]{1,2,0:T(8,128)S(1)} collective-permute-done((f32[1,128,64]{1,2,0:T(8,128)S(1)}, f32[1,128,64]{1,2,0:T(8,128)S(1)}, u32[]{:S(2)}, u32[]{:S(2)}) %collective-permute-start.11) | collective-permute-done | bytes 32800 | tf_op jit(solution)/shard_map/ppermute | solution.py:53
  (97 shorter events, 11.5 us)
Async XLA Ops:
  0.6 13.7 %copy-start.12 = (f32[2,256,128]{2,1,0:T(8,128)S(1)}, f32[2,256,128]{2,1,0:T(8,128)}, u32[]{:S(2)}) copy-start(f32[2,256,128]{2,1,0:T(8,128)} %param.14) | copy-start | bytes 786436
  0.6 13.7 %copy-start.13 = (f32[2,256,128]{2,1,0:T(8,128)S(1)}, f32[2,256,128]{2,1,0:T(8,128)}, u32[]{:S(2)}) copy-start(f32[2,256,128]{2,1,0:T(8,128)} %param.15) | copy-start | bytes 786436
  1.9 30.8 %copy-start.15 = (f32[2,2,256,128]{3,2,1,0:T(8,128)}, f32[2,2,256,128]{3,2,1,0:T(8,128)S(1)}, u32[]{:S(2)}) copy-start(f32[2,2,256,128]{3,2,1,0:T(8,128)S(1)} %fusion.89) | copy-start | bytes 1572868
  1.9 30.7 %collective-permute-start = (f32[2,2,256,128]{3,2,1,0:T(8,128)S(1)}, f32[2,2,256,128]{3,2,1,0:T(8,128)S(1)}, u32[]{:S(2)}, u32[]{:S(2)}) collective-permute-start(f32[2,2,256,128]{3,2,1,0:T(8,128)S(1)} %fusion.89), channel_id=1, source_target_pairs={{0,4},{2,6},{4,8},{6,10},{8,12},{10,14},{12,16},{14,18},{16,20},{1... | collective-permute-start | bytes 1572872 | tf_op jit(solution)/shard_map/ppermute | solution.py:53
  5.9 26.7 %collective-permute-start.1 = (f32[2,2,256,128]{3,2,1,0:T(8,128)S(1)}, f32[2,2,256,128]{3,2,1,0:T(8,128)S(1)}, u32[]{:S(2)}, u32[]{:S(2)}) collective-permute-start(f32[2,2,256,128]{3,2,1,0:T(8,128)S(1)} %fusion.89), channel_id=1, source_target_pairs={{0,2},{2,4},{4,6},{6,8},{8,10},{10,12},{12,14},{14,16},{16,18},{18... | collective-permute-start | bytes 1572872 | tf_op jit(solution)/shard_map/ppermute | solution.py:53
  9.1 23.5 %collective-permute-start.2 = (f32[2,2,256,128]{3,2,1,0:T(8,128)S(1)}, f32[2,2,256,128]{3,2,1,0:T(8,128)S(1)}, u32[]{:S(2)}, u32[]{:S(2)}) collective-permute-start(f32[2,2,256,128]{3,2,1,0:T(8,128)S(1)} %fusion.89), channel_id=1, source_target_pairs={{2,0},{4,2},{6,4},{8,6},{10,8},{12,10},{14,12},{16,14},{18,16},{20... | collective-permute-start | bytes 1572872 | tf_op jit(solution)/shard_map/ppermute | solution.py:53
  10.4 22.2 %collective-permute-start.3 = (f32[2,2,256,128]{3,2,1,0:T(8,128)S(1)}, f32[2,2,256,128]{3,2,1,0:T(8,128)S(1)}, u32[]{:S(2)}, u32[]{:S(2)}) collective-permute-start(f32[2,2,256,128]{3,2,1,0:T(8,128)S(1)} %fusion.89), channel_id=1, source_target_pairs={{4,0},{6,2},{8,4},{10,6},{12,8},{14,10},{16,12},{18,14},{20,16},{2... | collective-permute-start | bytes 1572872 | tf_op jit(solution)/shard_map/ppermute | solution.py:53
  32.5 2.4 %copy-start.6 = (f32[2,2,256,128]{3,2,1,0:T(8,128)}, f32[2,2,256,128]{3,2,1,0:T(8,128)S(1)}, u32[]{:S(2)}) copy-start(f32[2,2,256,128]{3,2,1,0:T(8,128)S(1)} %collective-permute-done.2) | copy-start | bytes 1572868
  32.5 2.4 %copy-start.8 = (f32[2,2,256,128]{3,2,1,0:T(8,128)}, f32[2,2,256,128]{3,2,1,0:T(8,128)S(1)}, u32[]{:S(2)}) copy-start(f32[2,2,256,128]{3,2,1,0:T(8,128)S(1)} %collective-permute-done.3) | copy-start | bytes 1572868
  32.6 2.1 %copy-start.2 = (f32[2,2,256,128]{3,2,1,0:T(8,128)}, f32[2,2,256,128]{3,2,1,0:T(8,128)S(1)}, u32[]{:S(2)}) copy-start(f32[2,2,256,128]{3,2,1,0:T(8,128)S(1)} %collective-permute-done) | copy-start | bytes 1572868
  32.6 2.2 %copy-start.4 = (f32[2,2,256,128]{3,2,1,0:T(8,128)}, f32[2,2,256,128]{3,2,1,0:T(8,128)S(1)}, u32[]{:S(2)}) copy-start(f32[2,2,256,128]{3,2,1,0:T(8,128)S(1)} %collective-permute-done.1) | copy-start | bytes 1572868
  32.7 2.1 %copy-start.17 = (f32[1,2,256,128]{3,2,1,0:T(8,128)S(1)}, f32[1,2,256,128]{3,2,1,0:T(8,128)}, u32[]{:S(2)}) copy-start(f32[1,2,256,128]{3,2,1,0:T(8,128)} %param.13) | copy-start | bytes 786436
  32.8 4.2 %collective-permute-start.4 = (f32[8,256,128]{2,1,0:T(8,128)S(1)}, f32[8,256,128]{2,1,0:T(8,128)S(1)}, u32[]{:S(2)}, u32[]{:S(2)}) collective-permute-start(f32[8,256,128]{2,1,0:T(8,128)S(1)} %pad_maximum_fusion.7), channel_id=1, source_target_pairs={{0,1},{1,0},{2,3},{3,2},{4,5},{5,4},{6,7},{7,6},{8,9},{9,8},{10,11... | collective-permute-start | bytes 3145736 | tf_op jit(solution)/shard_map/ppermute | solution.py:97
  37.3 1.5 %copy-start.5 = (f32[2,2,256,128]{3,2,1,0:T(8,128)S(1)}, f32[2,2,256,128]{3,2,1,0:T(8,128)}, u32[]{:S(2)}) copy-start(f32[2,2,256,128]{3,2,1,0:T(8,128)} %copy-done.4) | copy-start | bytes 1572868
  37.3 1.6 %copy-start.7 = (f32[2,2,256,128]{3,2,1,0:T(8,128)S(1)}, f32[2,2,256,128]{3,2,1,0:T(8,128)}, u32[]{:S(2)}) copy-start(f32[2,2,256,128]{3,2,1,0:T(8,128)} %copy-done.6) | copy-start | bytes 1572868
  37.3 1.8 %copy-start.9 = (f32[2,2,256,128]{3,2,1,0:T(8,128)S(1)}, f32[2,2,256,128]{3,2,1,0:T(8,128)}, u32[]{:S(2)}) copy-start(f32[2,2,256,128]{3,2,1,0:T(8,128)} %copy-done.8) | copy-start | bytes 1572868
  37.3 1.9 %copy-start.16 = (f32[2,2,256,128]{3,2,1,0:T(8,128)S(1)}, f32[2,2,256,128]{3,2,1,0:T(8,128)}, u32[]{:S(2)}) copy-start(f32[2,2,256,128]{3,2,1,0:T(8,128)} %copy-done.15) | copy-start | bytes 1572868
  37.4 6.1 %copy-start = (f32[4,256,128]{2,1,0:T(8,128)}, f32[4,256,128]{2,1,0:T(8,128)S(1)}, u32[]{:S(2)}) copy-start(f32[4,256,128]{2,1,0:T(8,128)S(1)} %slice.843) | copy-start | bytes 1572868
  37.5 7.0 %copy-start.10 = (f32[2,256,128]{2,1,0:T(8,128)}, f32[2,256,128]{2,1,0:T(8,128)S(1)}, u32[]{:S(2)}) copy-start(f32[2,256,128]{2,1,0:T(8,128)S(1)} %slice.850) | copy-start | bytes 786436
  45.8 35.0 %collective-permute-start.8 = (f32[2,256,128]{2,1,0:T(8,128)}, f32[2,256,128]{2,1,0:T(8,128)}, u32[]{:S(2)}, u32[]{:S(2)}) collective-permute-start(f32[2,256,128]{2,1,0:T(8,128)} %get-tuple-element.4), channel_id=1, source_target_pairs={{3,0},{2,1},{5,2},{4,3},{7,4},{6,5},{9,6},{8,7},{11,8},{10,9},{13,... | collective-permute-start | bytes 786440 | tf_op jit(solution)/shard_map/ppermute | solution.py:53
  47.0 35.0 %collective-permute-start.5 = (f32[2,256,128]{2,1,0:T(8,128)}, f32[2,256,128]{2,1,0:T(8,128)}, u32[]{:S(2)}, u32[]{:S(2)}) collective-permute-start(f32[2,256,128]{2,1,0:T(8,128)} %get-tuple-element.4), channel_id=1, source_target_pairs={{1,2},{0,3},{3,4},{2,5},{5,6},{4,7},{7,8},{6,9},{9,10},{8,11},{11,... | collective-permute-start | bytes 786440 | tf_op jit(solution)/shard_map/ppermute | solution.py:53
  57.8 14.8 %collective-permute-start.6 = (f32[2,256,128]{2,1,0:T(8,128)}, f32[2,256,128]{2,1,0:T(8,128)}, u32[]{:S(2)}, u32[]{:S(2)}) collective-permute-start(f32[2,256,128]{2,1,0:T(8,128)} %get-tuple-element.4), channel_id=1, source_target_pairs={{1,0},{0,1},{3,2},{2,3},{5,4},{4,5},{7,6},{6,7},{9,8},{8,9},{11,10... | collective-permute-start | bytes 786440 | tf_op jit(solution)/shard_map/ppermute | solution.py:53
  57.9 21.0 %collective-permute-start.7 = (f32[2,256,128]{2,1,0:T(8,128)}, f32[2,256,128]{2,1,0:T(8,128)}, u32[]{:S(2)}, u32[]{:S(2)}) collective-permute-start(f32[2,256,128]{2,1,0:T(8,128)} %get-tuple-element.4), channel_id=1, source_target_pairs={{1,4},{0,5},{3,6},{2,7},{5,8},{4,9},{7,10},{6,11},{9,12},{8,13},{1... | collective-permute-start | bytes 786440 | tf_op jit(solution)/shard_map/ppermute | solution.py:53
  64.9 14.9 %collective-permute-start.9 = (f32[2,256,128]{2,1,0:T(8,128)}, f32[2,256,128]{2,1,0:T(8,128)}, u32[]{:S(2)}, u32[]{:S(2)}) collective-permute-start(f32[2,256,128]{2,1,0:T(8,128)} %get-tuple-element.4), channel_id=1, source_target_pairs={{5,0},{4,1},{7,2},{6,3},{9,4},{8,5},{11,6},{10,7},{13,8},{12,9},{1... | collective-permute-start | bytes 786440 | tf_op jit(solution)/shard_map/ppermute | solution.py:53
  67.1 5.2 %copy-start.19 = (f32[256,128,1]{1,0,2:T(8,128)S(1)}, f32[256,128,1]{1,0,2:T(8,128)}, u32[]{:S(2)}) copy-start(f32[256,128,1]{1,0,2:T(8,128)} %constant.114) | copy-start | bytes 393220
  80.8 2.6 %copy-start.11 = (f32[2,256,128]{2,1,0:T(8,128)S(1)}, f32[2,256,128]{2,1,0:T(8,128)}, u32[]{:S(2)}) copy-start(f32[2,256,128]{2,1,0:T(8,128)} %copy-done.10) | copy-start | bytes 786436
  80.8 2.6 %copy-start.22 = (pred[2]{0:T(512)(128)(4,1)S(1)}, pred[2]{0:T(512)(128)(4,1)}, u32[]{:S(2)}) copy-start(pred[2]{0:T(512)(128)(4,1)} %get-tuple-element.27) | copy-start | bytes 10
  93.6 1.1 %copy-start.21 = (f32[128,64]{1,0:T(8,128)S(1)}, f32[128,64]{1,0:T(8,128)}, u32[]{:S(2)}) copy-start(f32[128,64]{1,0:T(8,128)} %constant.30.clone) | copy-start | bytes 98308
  93.6 1.4 %copy-start.18 = (f32[256,128]{1,0:T(8,128)S(1)}, f32[256,128]{1,0:T(8,128)}, u32[]{:S(2)}) copy-start(f32[256,128]{1,0:T(8,128)} %constant.29.clone) | copy-start | bytes 393220
  95.4 3.6 %collective-permute-start.10 = (f32[1,128,64]{1,2,0:T(8,128)S(1)}, f32[1,128,64]{1,2,0:T(8,128)S(1)}, u32[]{:S(2)}, u32[]{:S(2)}) collective-permute-start(f32[1,128,64]{1,2,0:T(8,128)S(1)} %fusion.4), channel_id=1, source_target_pairs={{0,1},{2,3},{4,5},{6,7},{8,9},{10,11},{12,13},{14,15},{16,17},{18,... | collective-permute-start | bytes 98312 | tf_op jit(solution)/shard_map/ppermute | solution.py:53
  96.7 2.3 %collective-permute-start.12 = (f32[1,128,64]{1,2,0:T(8,128)S(1)}, f32[1,128,64]{1,2,0:T(8,128)S(1)}, u32[]{:S(2)}, u32[]{:S(2)}) collective-permute-start(f32[1,128,64]{1,2,0:T(8,128)S(1)} %fusion.4), channel_id=1, source_target_pairs={{0,3},{2,5},{4,7},{6,9},{8,11},{10,13},{12,15},{14,17},{16,19},{18... | collective-permute-start | bytes 98312 | tf_op jit(solution)/shard_map/ppermute | solution.py:53
  97.4 7.8 %collective-permute-start.11 = (f32[1,128,64]{1,2,0:T(8,128)S(1)}, f32[1,128,64]{1,2,0:T(8,128)S(1)}, u32[]{:S(2)}, u32[]{:S(2)}) collective-permute-start(f32[1,128,64]{1,2,0:T(8,128)S(1)} %fusion.4), channel_id=1, source_target_pairs={{2,1},{4,3},{6,5},{8,7},{10,9},{12,11},{14,13},{16,15},{18,17},{20... | collective-permute-start | bytes 98312 | tf_op jit(solution)/shard_map/ppermute | solution.py:53
  (4 other events, 4.0 us)

commit v12 on v6

--- a/solution.py
+++ b/solution.py
@@ -92,11 +92,8 @@
     wide = wide[:, lo:hi]
     if split:
         mine = wide[0]
-        rim = jnp.concatenate([mine[:halo], mine[halo + n :]], axis=0)
         partner = [(t, t ^ 1) for t in range(times)]
-        theirs_rim = lax.ppermute(rim, "tm", partner)
-        theirs_own = jnp.where(even, reaction, diffusivity)
-        theirs = jnp.concatenate([theirs_rim[:halo], theirs_own, theirs_rim[halo:]], axis=0)
+        theirs = lax.ppermute(mine, "tm", partner)
         conduct = jnp.where(even, mine, theirs)
         absorb = jnp.where(even, theirs, mine)
         field0 = wide[1]

time: 103 us -> 107 us (1.039)
  local copies, waits for them, and re-layouts: 9.25 us -> 12.6 us
  other arithmetic: 18.2 us -> 19.6 us
    unnamed x55 -> x57, local copies, waits for them, and re-layouts: 7.55 us -> 9.71 us
    ppermute x12, waiting for transfers between devices: 33.2 us -> 31.3 us  [gather_planes(): pieces[d] = lax.ppermute(block, axis_names, pairs_of(d))]
    select_n x1, other arithmetic: 0.2 us -> 1.9 us  [shards(): conduct = jnp.where(even, mine, theirs)]
    squeeze x0 -> x1, local copies, waits for them, and re-layouts: none -> 1.27 us  [shards(): mine = wide[0]]
  transfers between devices with their start and end apart: 13 -> 13, of which waited for: 4 -> 4; matrix products, arithmetic and copies ran while one was open for 11% -> 10% of each run, Pallas kernels for 0% -> 0%
where the time goes in v12:
time: 107 us; the launch traced here: 106 us
  waiting for transfers between devices  34 us (32%)
  starting transfers between devices  33.7 us (31%)
  other arithmetic  19.6 us (18%)
  local copies, waits for them, and re-layouts  12.6 us (12%)
  matrix products  5.11 us (5%)
  between operations  1.23 us (1%)
    ppermute x12, starting transfers between devices, gather_planes(): pieces[d] = lax.ppermute(block, axis_names, pairs_of(d))  31.9 us
    ppermute x12, waiting for transfers between devices, gather_planes(): pieces[d] = lax.ppermute(block, axis_names, pairs_of(d))  31.3 us
    unnamed x57, local copies, waits for them, and re-layouts  9.71 us
    select_n x5, other arithmetic, fine_prop(): field = jnp.where(m > 0, field, 0.0)  8.31 us
    dot_general x6, matrix products, restrict(): jnp.einsum('Yy,mYZ,Zz->myz', rows, planes, cols, precision=lax.Precision....  4.44 us
    reduce_sum x3, other arithmetic, restrict(): planes = field.reshape(first // 2, 2, second, third).sum(axis=1)  3.96 us
    ppermute x1, waiting for transfers between devices, shards(): theirs = lax.ppermute(mine, 'tm', partner)  2.69 us
  transfers between devices with their start and end apart: 13, of which 4 were waited for; matrix products, arithmetic and copies ran while one was open for 10% of the time, Pallas kernels for 0%

profile of v12, /device:TPU:1, one launch (start us, length us, event | category | flops | bytes accessed | tf_op | source)
XLA Modules:
  0.0 106.2 jit_solution(14159025763814534077)
XLA Ops:
  0.6 1.2 %fusion.103 = f32[2,2,256,128]{3,2,1,0:T(8,128)S(1)} fusion(f32[1,2,256,128]{3,2,1,0:T(8,128)} %param.13, f32[1,2,256,128]{3,2,1,0:T(8,128)} %bitcast.63, f32[1,2,256,128]{3,2,1,0:T(8,128)} %bitcast.65, pred[]{:T(512)S(6)} %eq.8), kind=kLoop, calls=%fused_computation.177 | loop fusion | flops 393216 | bytes 1310721 | tf_op jit(solution)/shard_map/jit(_where)/select_n | solution.py:87
  1.8 4.1 %collective-permute-start = (f32[2,2,256,128]{3,2,1,0:T(8,128)S(1)}, f32[2,2,256,128]{3,2,1,0:T(8,128)S(1)}, u32[]{:S(2)}, u32[]{:S(2)}) collective-permute-start(f32[2,2,256,128]{3,2,1,0:T(8,128)S(1)} %fusion.103), channel_id=1, source_target_pairs={{0,4},{2,6},{4,8},{6,10},{8,12},{10,14},{12,16},{14,18},{16,20},{1... | collective-permute-start | bytes 1572872 | tf_op jit(solution)/shard_map/ppermute | solution.py:53
  6.0 3.1 %collective-permute-start.1 = (f32[2,2,256,128]{3,2,1,0:T(8,128)S(1)}, f32[2,2,256,128]{3,2,1,0:T(8,128)S(1)}, u32[]{:S(2)}, u32[]{:S(2)}) collective-permute-start(f32[2,2,256,128]{3,2,1,0:T(8,128)S(1)} %fusion.103), channel_id=1, source_target_pairs={{0,2},{2,4},{4,6},{6,8},{8,10},{10,12},{12,14},{14,16},{16,18},{18... | collective-permute-start | bytes 1572872 | tf_op jit(solution)/shard_map/ppermute | solution.py:53
  9.1 1.3 %collective-permute-start.2 = (f32[2,2,256,128]{3,2,1,0:T(8,128)S(1)}, f32[2,2,256,128]{3,2,1,0:T(8,128)S(1)}, u32[]{:S(2)}, u32[]{:S(2)}) collective-permute-start(f32[2,2,256,128]{3,2,1,0:T(8,128)S(1)} %fusion.103), channel_id=1, source_target_pairs={{2,0},{4,2},{6,4},{8,6},{10,8},{12,10},{14,12},{16,14},{18,16},{20... | collective-permute-start | bytes 1572872 | tf_op jit(solution)/shard_map/ppermute | solution.py:53
  10.4 1.3 %collective-permute-start.3 = (f32[2,2,256,128]{3,2,1,0:T(8,128)S(1)}, f32[2,2,256,128]{3,2,1,0:T(8,128)S(1)}, u32[]{:S(2)}, u32[]{:S(2)}) collective-permute-start(f32[2,2,256,128]{3,2,1,0:T(8,128)S(1)} %fusion.103), channel_id=1, source_target_pairs={{4,0},{6,2},{8,4},{10,6},{12,8},{14,10},{16,12},{18,14},{20,16},{2... | collective-permute-start | bytes 1572872 | tf_op jit(solution)/shard_map/ppermute | solution.py:53
  11.7 16.0 %collective-permute-done = f32[2,2,256,128]{3,2,1,0:T(8,128)S(1)} collective-permute-done((f32[2,2,256,128]{3,2,1,0:T(8,128)S(1)}, f32[2,2,256,128]{3,2,1,0:T(8,128)S(1)}, u32[]{:S(2)}, u32[]{:S(2)}) %collective-permute-start) | collective-permute-done | bytes 524320 | tf_op jit(solution)/shard_map/ppermute | solution.py:53
  28.5 4.1 %collective-permute-done.2 = f32[2,2,256,128]{3,2,1,0:T(8,128)S(1)} collective-permute-done((f32[2,2,256,128]{3,2,1,0:T(8,128)S(1)}, f32[2,2,256,128]{3,2,1,0:T(8,128)S(1)}, u32[]{:S(2)}, u32[]{:S(2)}) %collective-permute-start.2) | collective-permute-done | bytes 524320 | tf_op jit(solution)/shard_map/ppermute | solution.py:53
  34.3 1.3 %slice_bitcast_fusion = f32[10,256,128]{2,1,0:T(8,128)} fusion(f32[2,10,256,128]{3,2,1,0:T(8,128)S(1)} %constant_dynamic-update-slice_fusion), kind=kLoop, calls=%fused_computation.36 | loop fusion | bytes 2621440 | tf_op jit(solution)/shard_map/squeeze | solution.py:94
  35.6 1.8 %collective-permute-start.4 = (f32[10,256,128]{2,1,0:T(8,128)}, f32[10,256,128]{2,1,0:T(8,128)}, u32[]{:S(2)}, u32[]{:S(2)}) collective-permute-start(f32[10,256,128]{2,1,0:T(8,128)} %slice_bitcast_fusion), channel_id=1, source_target_pairs={{0,1},{1,0},{2,3},{3,2},{4,5},{5,4},{6,7},{7,6},{8,9},{9,8},{10,11... | collective-permute-start | bytes 3932168 | tf_op jit(solution)/shard_map/ppermute | solution.py:96
  37.7 2.7 %collective-permute-done.4 = f32[10,256,128]{2,1,0:T(8,128)} collective-permute-done((f32[10,256,128]{2,1,0:T(8,128)}, f32[10,256,128]{2,1,0:T(8,128)}, u32[]{:S(2)}, u32[]{:S(2)}) %collective-permute-start.4) | collective-permute-done | bytes 1310752 | tf_op jit(solution)/shard_map/ppermute | solution.py:96
  40.4 1.9 %broadcast_select_fusion.1 = (f32[10,256,128]{2,1,0:T(8,128)S(1)}, f32[10,256,128]{2,1,0:T(8,128)S(1)}) fusion(f32[10,256,128]{2,1,0:T(8,128)} %collective-permute-done.4, pred[]{:T(512)S(6)} %eq.8, f32[2,10,256,128]{3,2,1,0:T(8,128)} %copy-done.2), kind=kLoop, calls=%fused_computation.174 | loop fusion | flops 655360 | bytes 5242881 | tf_op jit(solution)/shard_map/jit(_where)/select_n | solution.py:97
  44.7 2.2 %fusion.20 = f32[8,256,128]{2,1,0:T(8,128)S(1)} fusion(f32[8,256,128]{2,1,0:T(8,128)S(1)} %slice_bitcast_fusion.1, f32[2,2,256,128]{3,2,1,0:T(8,128)S(1)} %copy-done.15, f32[2,2,256,128]{3,2,1,0:T(8,128)S(1)} %copy-done.9, f32[2,2,256,128]{3,2,1,0:T(8,128)S(1)} %copy-done.13, f32[2,2,256,128]{3,2,1,0:T(8,128)S(1)} %copy-done.11, ...), kind=kLoop, calls=%fused_computation.60 | loop fusion | flops 10747904 | bytes 8912904 | tf_op jit(solution)/shard_map/jit(_where)/select_n | solution.py:113
  47.0 2.1 %fusion.242 = (f32[6,256,128]{2,1,0:T(8,128)}, f32[6,256,128]{2,1,0:T(8,128)S(1)}) fusion(f32[10,256,128]{2,1,0:T(8,128)S(1)} %get-tuple-element.7, f32[6,256,128]{2,1,0:T(8,128)S(1)} %slice.500, f32[6,256,128]{2,1,0:T(8,128)S(1)} %slice.502, f32[8,256,128]{2,1,0:T(8,128)S(1)} %fusion.20, f32[10,256,128]{2,1,0:T(8,128)S(1)} %get-tuple-element.6, ...), kind=kLoop, calls=%fused_computation.354 | loop fusion | flops 6881280 | bytes 7077894 | tf_op jit(solution)/shard_map/slice | solution.py:22
  50.0 1.2 %broadcast_select_fusion.2 = (f32[2,256,128]{2,1,0:T(8,128)}, f32[2,256,128]{2,1,0:T(8,128)}) fusion(f32[2,256,128]{2,1,0:T(8,128)S(1)} %copy-done.24, pred[]{:T(512)S(6)} %eq.9, f32[2,256,128]{2,1,0:T(8,128)S(1)} %slice.514, f32[10,256,128]{2,1,0:T(8,128)S(1)} %get-tuple-element.7, f32[2,256,128]{2,1,0:T(8,128)S(1)} %slice.516, ...), kind=kLoop, calls=%fused_computation.288 | loop fusion | flops 2293760 | bytes 2621441 | tf_op jit(solution)/shard_map/jit(_where)/select_n | solution.py:117
  51.3 12.6 %collective-permute-start.5 = (f32[2,256,128]{2,1,0:T(8,128)}, f32[2,256,128]{2,1,0:T(8,128)}, u32[]{:S(2)}, u32[]{:S(2)}) collective-permute-start(f32[2,256,128]{2,1,0:T(8,128)} %get-tuple-element.4), channel_id=1, source_target_pairs={{1,4},{0,5},{3,6},{2,7},{5,8},{4,9},{7,10},{6,11},{9,12},{8,13},{1... | collective-permute-start | bytes 786440 | tf_op jit(solution)/shard_map/ppermute | solution.py:53
  63.9 3.2 %collective-permute-start.6 = (f32[2,256,128]{2,1,0:T(8,128)}, f32[2,256,128]{2,1,0:T(8,128)}, u32[]{:S(2)}, u32[]{:S(2)}) collective-permute-start(f32[2,256,128]{2,1,0:T(8,128)} %get-tuple-element.4), channel_id=1, source_target_pairs={{1,2},{0,3},{3,4},{2,5},{5,6},{4,7},{7,8},{6,9},{9,10},{8,11},{11,... | collective-permute-start | bytes 786440 | tf_op jit(solution)/shard_map/ppermute | solution.py:53
  67.4 1.3 %collective-permute-start.8 = (f32[2,256,128]{2,1,0:T(8,128)}, f32[2,256,128]{2,1,0:T(8,128)}, u32[]{:S(2)}, u32[]{:S(2)}) collective-permute-start(f32[2,256,128]{2,1,0:T(8,128)} %get-tuple-element.4), channel_id=1, source_target_pairs={{3,0},{2,1},{5,2},{4,3},{7,4},{6,5},{9,6},{8,7},{11,8},{10,9},{13,... | collective-permute-start | bytes 786440 | tf_op jit(solution)/shard_map/ppermute | solution.py:53
  68.7 1.3 %collective-permute-start.9 = (f32[2,256,128]{2,1,0:T(8,128)}, f32[2,256,128]{2,1,0:T(8,128)}, u32[]{:S(2)}, u32[]{:S(2)}) collective-permute-start(f32[2,256,128]{2,1,0:T(8,128)} %get-tuple-element.4), channel_id=1, source_target_pairs={{5,0},{4,1},{7,2},{6,3},{9,4},{8,5},{11,6},{10,7},{13,8},{12,9},{1... | collective-permute-start | bytes 786440 | tf_op jit(solution)/shard_map/ppermute | solution.py:53
  70.8 2.0 %reduce_sum.29 = f32[3,256,128]{2,1,0:T(8,128)} reduce(f32[3,2,256,128]{3,2,1,0:T(8,128)} %bitcast.62, f32[]{:T(128)} %constant.20.clone.1), dimensions={1}, to_apply=%region_2.3 | reduce | flops 98304 | bytes 1179652 | tf_op jit(solution)/shard_map/reduce_sum | solution.py:32
  72.8 1.6 %fusion.244 = f32[64,3,256]{2,0,1:T(8,128)S(1)} fusion(f32[128,64,1]{1,0,2:T(8,128)} %constant.90, f32[3,256,128]{2,1,0:T(8,128)} %reduce_sum.28), kind=kOutput, calls=%fused_computation.356 | convolution fusion | flops 75497472 | bytes 622592 | tf_op jit(solution)/shard_map/Yy,mYZ,Zz->myz/dot_general | solution.py:35
  74.4 1.6 %fusion.245 = f32[64,3,256]{2,0,1:T(8,128)S(1)} fusion(f32[128,64,1]{1,0,2:T(8,128)} %constant.90, f32[3,256,128]{2,1,0:T(8,128)} %reduce_sum.29), kind=kOutput, calls=%fused_computation.357 | convolution fusion | flops 75497472 | bytes 622592 | tf_op jit(solution)/shard_map/Yy,mYZ,Zz->myz/dot_general | solution.py:35
  77.3 1.0 constant_dynamic-update-slice_fusion.8
  78.3 1.0 constant_dynamic-update-slice_fusion.7
  79.3 1.0 constant_dynamic-update-slice_fusion.6
  80.3 1.1 constant_dynamic-update-slice_fusion.5
  81.6 3.2 %fusion.36 = f32[8,256,128]{2,1,0:T(8,128)S(1)} fusion(f32[8,256,128]{2,1,0:T(8,128)S(1)} %slice.521, f32[2,256,128]{2,1,0:T(8,128)} %collective-permute-done.9, f32[2,256,128]{2,1,0:T(8,128)} %collective-permute-done.8, f32[2,256,128]{2,1,0:T(8,128)} %collective-permute-done.7, f32[2,256,128]{2,1,0:T(8,128)} %collective-permute-done.6, ...), kind=kLoop, calls=%fused_computation.76 | loop fusion | flops 10747904 | bytes 7602184 | tf_op jit(solution)/shard_map/jit(_where)/select_n | solution.py:113
  84.9 1.2 %fusion.88 = f32[6,256,128]{2,1,0:T(8,128)S(1)} fusion(f32[6,256,128]{2,1,0:T(8,128)S(1)} %slice.522, f32[8,256,128]{2,1,0:T(8,128)S(1)} %fusion.36, pred[6]{0:T(512)(128)(4,1)S(1)} %slice_compare_fusion.1, f32[6,256,128]{2,1,0:T(8,128)S(1)} %slice.502, f32[10,256,128]{2,1,0:T(8,128)S(1)} %get-tuple-element.6, f32[10,256,128]{2,1,0:T(8,128)S(1)} %get-tuple-element.7), kind=kLoop, calls=%fused_computation.152 | loop fusion | flops 6881280 | bytes 6291462 | tf_op jit(solution)/shard_map/jit(_where)/select_n | solution.py:113
  86.2 1.0 copy-done.4
  88.2 1.2 %fusion.239 = (f32[256,128]{1,0:T(8,128)S(1)}, f32[2,256,128]{2,1,0:T(8,128)}) fusion(f32[2,256,128]{2,1,0:T(8,128)S(1)} %copy-done.5, f32[2,256,128]{2,1,0:T(8,128)S(1)} %slice.528, f32[10,256,128]{2,1,0:T(8,128)S(1)} %get-tuple-element.7, f32[2,256,128]{2,1,0:T(8,128)S(1)} %copy-done.7, f32[4,256,128]{2,1,0:T(8,128)S(1)} %fusion.137, ...), kind=kLoop, calls=%fused_computation.353 | loop fusion | flops 2326528 | bytes 2490368 | tf_op jit(solution)/shard_map/reduce_sum | solution.py:32
  90.0 1.3 %collective-permute-start.10 = (f32[1,128,64]{1,2,0:T(8,128)S(1)}, f32[1,128,64]{1,2,0:T(8,128)S(1)}, u32[]{:S(2)}, u32[]{:S(2)}) collective-permute-start(f32[1,128,64]{1,2,0:T(8,128)S(1)} %fusion.2), channel_id=1, source_target_pairs={{0,1},{2,3},{4,5},{6,7},{8,9},{10,11},{12,13},{14,15},{16,17},{18,... | collective-permute-start | bytes 98312 | tf_op jit(solution)/shard_map/ppermute | solution.py:53
  92.0 1.3 %collective-permute-start.11 = (f32[1,128,64]{1,2,0:T(8,128)S(1)}, f32[1,128,64]{1,2,0:T(8,128)S(1)}, u32[]{:S(2)}, u32[]{:S(2)}) collective-permute-start(f32[1,128,64]{1,2,0:T(8,128)S(1)} %fusion.2), channel_id=1, source_target_pairs={{2,1},{4,3},{6,5},{8,7},{10,9},{12,11},{14,13},{16,15},{18,17},{20... | collective-permute-start | bytes 98312 | tf_op jit(solution)/shard_map/ppermute | solution.py:53
  93.6 11.2 %collective-permute-done.11 = f32[1,128,64]{1,2,0:T(8,128)S(1)} collective-permute-done((f32[1,128,64]{1,2,0:T(8,128)S(1)}, f32[1,128,64]{1,2,0:T(8,128)S(1)}, u32[]{:S(2)}, u32[]{:S(2)}) %collective-permute-start.11) | collective-permute-done | bytes 32800 | tf_op jit(solution)/shard_map/ppermute | solution.py:53
  (93 shorter events, 12.8 us)
Async XLA Ops:
  1.8 26.2 %copy-start.8 = (f32[2,2,256,128]{3,2,1,0:T(8,128)}, f32[2,2,256,128]{3,2,1,0:T(8,128)S(1)}, u32[]{:S(2)}) copy-start(f32[2,2,256,128]{3,2,1,0:T(8,128)S(1)} %fusion.103) | copy-start | bytes 1572868
  1.8 26.1 %copy-start.18 = (f32[1,2,256,128]{3,2,1,0:T(8,128)S(1)}, f32[1,2,256,128]{3,2,1,0:T(8,128)}, u32[]{:S(2)}) copy-start(f32[1,2,256,128]{3,2,1,0:T(8,128)} %param.13) | copy-start | bytes 786436
  1.8 26.1 %copy-start.19 = (f32[2,256,128]{2,1,0:T(8,128)S(1)}, f32[2,256,128]{2,1,0:T(8,128)}, u32[]{:S(2)}) copy-start(f32[2,256,128]{2,1,0:T(8,128)} %param.14) | copy-start | bytes 786436
  1.8 26.1 %copy-start.20 = (f32[2,256,128]{2,1,0:T(8,128)S(1)}, f32[2,256,128]{2,1,0:T(8,128)}, u32[]{:S(2)}) copy-start(f32[2,256,128]{2,1,0:T(8,128)} %param.15) | copy-start | bytes 786436
  1.8 25.9 %collective-permute-start = (f32[2,2,256,128]{3,2,1,0:T(8,128)S(1)}, f32[2,2,256,128]{3,2,1,0:T(8,128)S(1)}, u32[]{:S(2)}, u32[]{:S(2)}) collective-permute-start(f32[2,2,256,128]{3,2,1,0:T(8,128)S(1)} %fusion.103), channel_id=1, source_target_pairs={{0,4},{2,6},{4,8},{6,10},{8,12},{10,14},{12,16},{14,18},{16,20},{1... | collective-permute-start | bytes 1572872 | tf_op jit(solution)/shard_map/ppermute | solution.py:53
  6.0 21.8 %collective-permute-start.1 = (f32[2,2,256,128]{3,2,1,0:T(8,128)S(1)}, f32[2,2,256,128]{3,2,1,0:T(8,128)S(1)}, u32[]{:S(2)}, u32[]{:S(2)}) collective-permute-start(f32[2,2,256,128]{3,2,1,0:T(8,128)S(1)} %fusion.103), channel_id=1, source_target_pairs={{0,2},{2,4},{4,6},{6,8},{8,10},{10,12},{12,14},{14,16},{16,18},{18... | collective-permute-start | bytes 1572872 | tf_op jit(solution)/shard_map/ppermute | solution.py:53
  9.1 23.5 %collective-permute-start.2 = (f32[2,2,256,128]{3,2,1,0:T(8,128)S(1)}, f32[2,2,256,128]{3,2,1,0:T(8,128)S(1)}, u32[]{:S(2)}, u32[]{:S(2)}) collective-permute-start(f32[2,2,256,128]{3,2,1,0:T(8,128)S(1)} %fusion.103), channel_id=1, source_target_pairs={{2,0},{4,2},{6,4},{8,6},{10,8},{12,10},{14,12},{16,14},{18,16},{20... | collective-permute-start | bytes 1572872 | tf_op jit(solution)/shard_map/ppermute | solution.py:53
  10.4 22.2 %collective-permute-start.3 = (f32[2,2,256,128]{3,2,1,0:T(8,128)S(1)}, f32[2,2,256,128]{3,2,1,0:T(8,128)S(1)}, u32[]{:S(2)}, u32[]{:S(2)}) collective-permute-start(f32[2,2,256,128]{3,2,1,0:T(8,128)S(1)} %fusion.103), channel_id=1, source_target_pairs={{4,0},{6,2},{8,4},{10,6},{12,8},{14,10},{16,12},{18,14},{20,16},{2... | collective-permute-start | bytes 1572872 | tf_op jit(solution)/shard_map/ppermute | solution.py:53
  27.8 4.8 %copy-start.12 = (f32[2,2,256,128]{3,2,1,0:T(8,128)}, f32[2,2,256,128]{3,2,1,0:T(8,128)S(1)}, u32[]{:S(2)}) copy-start(f32[2,2,256,128]{3,2,1,0:T(8,128)S(1)} %collective-permute-done.1) | copy-start | bytes 1572868
  34.3 3.3 %copy-start.2 = (f32[2,10,256,128]{3,2,1,0:T(8,128)}, f32[2,10,256,128]{3,2,1,0:T(8,128)S(1)}, u32[]{:S(2)}) copy-start(f32[2,10,256,128]{3,2,1,0:T(8,128)S(1)} %constant_dynamic-update-slice_fusion) | copy-start | bytes 7864324
  35.6 4.8 %collective-permute-start.4 = (f32[10,256,128]{2,1,0:T(8,128)}, f32[10,256,128]{2,1,0:T(8,128)}, u32[]{:S(2)}, u32[]{:S(2)}) collective-permute-start(f32[10,256,128]{2,1,0:T(8,128)} %slice_bitcast_fusion), channel_id=1, source_target_pairs={{0,1},{1,0},{2,3},{3,2},{4,5},{5,4},{6,7},{7,6},{8,9},{9,8},{10,11... | collective-permute-start | bytes 3932168 | tf_op jit(solution)/shard_map/ppermute | solution.py:96
  42.4 1.4 %copy-start.9 = (f32[2,2,256,128]{3,2,1,0:T(8,128)S(1)}, f32[2,2,256,128]{3,2,1,0:T(8,128)}, u32[]{:S(2)}) copy-start(f32[2,2,256,128]{3,2,1,0:T(8,128)} %copy-done.8) | copy-start | bytes 1572868
  42.4 1.9 %copy-start.11 = (f32[2,2,256,128]{3,2,1,0:T(8,128)S(1)}, f32[2,2,256,128]{3,2,1,0:T(8,128)}, u32[]{:S(2)}) copy-start(f32[2,2,256,128]{3,2,1,0:T(8,128)} %copy-done.10) | copy-start | bytes 1572868
  42.4 2.0 %copy-start.13 = (f32[2,2,256,128]{3,2,1,0:T(8,128)S(1)}, f32[2,2,256,128]{3,2,1,0:T(8,128)}, u32[]{:S(2)}) copy-start(f32[2,2,256,128]{3,2,1,0:T(8,128)} %copy-done.12) | copy-start | bytes 1572868
  42.4 2.1 %copy-start.15 = (f32[2,2,256,128]{3,2,1,0:T(8,128)S(1)}, f32[2,2,256,128]{3,2,1,0:T(8,128)}, u32[]{:S(2)}) copy-start(f32[2,2,256,128]{3,2,1,0:T(8,128)} %copy-done.14) | copy-start | bytes 1572868
  42.4 2.3 %copy-start.17 = (f32[2,2,256,128]{3,2,1,0:T(8,128)S(1)}, f32[2,2,256,128]{3,2,1,0:T(8,128)}, u32[]{:S(2)}) copy-start(f32[2,2,256,128]{3,2,1,0:T(8,128)} %copy-done.16) | copy-start | bytes 1572868
  42.5 6.5 %copy-start.3 = (f32[4,256,128]{2,1,0:T(8,128)}, f32[4,256,128]{2,1,0:T(8,128)S(1)}, u32[]{:S(2)}) copy-start(f32[4,256,128]{2,1,0:T(8,128)S(1)} %slice.509) | copy-start | bytes 1572868
  42.6 7.4 %copy-start.6 = (f32[2,256,128]{2,1,0:T(8,128)}, f32[2,256,128]{2,1,0:T(8,128)S(1)}, u32[]{:S(2)}) copy-start(f32[2,256,128]{2,1,0:T(8,128)S(1)} %slice.516) | copy-start | bytes 786436
  51.3 25.1 %collective-permute-start.5 = (f32[2,256,128]{2,1,0:T(8,128)}, f32[2,256,128]{2,1,0:T(8,128)}, u32[]{:S(2)}, u32[]{:S(2)}) collective-permute-start(f32[2,256,128]{2,1,0:T(8,128)} %get-tuple-element.4), channel_id=1, source_target_pairs={{1,4},{0,5},{3,6},{2,7},{5,8},{4,9},{7,10},{6,11},{9,12},{8,13},{1... | collective-permute-start | bytes 786440 | tf_op jit(solution)/shard_map/ppermute | solution.py:53
  63.9 13.4 %collective-permute-start.6 = (f32[2,256,128]{2,1,0:T(8,128)}, f32[2,256,128]{2,1,0:T(8,128)}, u32[]{:S(2)}, u32[]{:S(2)}) collective-permute-start(f32[2,256,128]{2,1,0:T(8,128)} %get-tuple-element.4), channel_id=1, source_target_pairs={{1,2},{0,3},{3,4},{2,5},{5,6},{4,7},{7,8},{6,9},{9,10},{8,11},{11,... | collective-permute-start | bytes 786440 | tf_op jit(solution)/shard_map/ppermute | solution.py:53
  67.1 11.2 %collective-permute-start.7 = (f32[2,256,128]{2,1,0:T(8,128)}, f32[2,256,128]{2,1,0:T(8,128)}, u32[]{:S(2)}, u32[]{:S(2)}) collective-permute-start(f32[2,256,128]{2,1,0:T(8,128)} %get-tuple-element.4), channel_id=1, source_target_pairs={{1,0},{0,1},{3,2},{2,3},{5,4},{4,5},{7,6},{6,7},{9,8},{8,9},{11,10... | collective-permute-start | bytes 786440 | tf_op jit(solution)/shard_map/ppermute | solution.py:53
  67.4 11.8 %collective-permute-start.8 = (f32[2,256,128]{2,1,0:T(8,128)}, f32[2,256,128]{2,1,0:T(8,128)}, u32[]{:S(2)}, u32[]{:S(2)}) collective-permute-start(f32[2,256,128]{2,1,0:T(8,128)} %get-tuple-element.4), channel_id=1, source_target_pairs={{3,0},{2,1},{5,2},{4,3},{7,4},{6,5},{9,6},{8,7},{11,8},{10,9},{13,... | collective-permute-start | bytes 786440 | tf_op jit(solution)/shard_map/ppermute | solution.py:53
  68.7 11.5 %collective-permute-start.9 = (f32[2,256,128]{2,1,0:T(8,128)}, f32[2,256,128]{2,1,0:T(8,128)}, u32[]{:S(2)}, u32[]{:S(2)}) collective-permute-start(f32[2,256,128]{2,1,0:T(8,128)} %get-tuple-element.4), channel_id=1, source_target_pairs={{5,0},{4,1},{7,2},{6,3},{9,4},{8,5},{11,6},{10,7},{13,8},{12,9},{1... | collective-permute-start | bytes 786440 | tf_op jit(solution)/shard_map/ppermute | solution.py:53
  70.8 5.1 %copy-start.22 = (f32[256,128,1]{1,0,2:T(8,128)S(1)}, f32[256,128,1]{1,0,2:T(8,128)}, u32[]{:S(2)}) copy-start(f32[256,128,1]{1,0,2:T(8,128)} %constant.91) | copy-start | bytes 393220
  80.3 1.3 %copy-start.1 = (f32[8,256,128]{2,1,0:T(8,128)S(1)}, f32[8,256,128]{2,1,0:T(8,128)}, u32[]{:S(2)}) copy-start(f32[8,256,128]{2,1,0:T(8,128)} %copy-done) | copy-start | bytes 3145732
  86.1 1.0 copy-start.4
  87.2 1.0 copy-start.7
  88.0 1.3 %copy-start.23 = (f32[128,64]{1,0:T(8,128)S(1)}, f32[128,64]{1,0:T(8,128)}, u32[]{:S(2)}) copy-start(f32[128,64]{1,0:T(8,128)} %constant.27.clone) | copy-start | bytes 98308
  88.2 1.4 %copy-start.21 = (f32[256,128]{1,0:T(8,128)S(1)}, f32[256,128]{1,0:T(8,128)}, u32[]{:S(2)}) copy-start(f32[256,128]{1,0:T(8,128)} %constant.26.clone) | copy-start | bytes 393220
  90.0 3.6 %collective-permute-start.10 = (f32[1,128,64]{1,2,0:T(8,128)S(1)}, f32[1,128,64]{1,2,0:T(8,128)S(1)}, u32[]{:S(2)}, u32[]{:S(2)}) collective-permute-start(f32[1,128,64]{1,2,0:T(8,128)S(1)} %fusion.2), channel_id=1, source_target_pairs={{0,1},{2,3},{4,5},{6,7},{8,9},{10,11},{12,13},{14,15},{16,17},{18,... | collective-permute-start | bytes 98312 | tf_op jit(solution)/shard_map/ppermute | solution.py:53
  91.3 2.3 %collective-permute-start.12 = (f32[1,128,64]{1,2,0:T(8,128)S(1)}, f32[1,128,64]{1,2,0:T(8,128)S(1)}, u32[]{:S(2)}, u32[]{:S(2)}) collective-permute-start(f32[1,128,64]{1,2,0:T(8,128)S(1)} %fusion.2), channel_id=1, source_target_pairs={{0,3},{2,5},{4,7},{6,9},{8,11},{10,13},{12,15},{14,17},{16,19},{18... | collective-permute-start | bytes 98312 | tf_op jit(solution)/shard_map/ppermute | solution.py:53
  92.0 12.8 %collective-permute-start.11 = (f32[1,128,64]{1,2,0:T(8,128)S(1)}, f32[1,128,64]{1,2,0:T(8,128)S(1)}, u32[]{:S(2)}, u32[]{:S(2)}) collective-permute-start(f32[1,128,64]{1,2,0:T(8,128)S(1)} %fusion.2), channel_id=1, source_target_pairs={{2,1},{4,3},{6,5},{8,7},{10,9},{12,11},{14,13},{16,15},{18,17},{20... | collective-permute-start | bytes 98312 | tf_op jit(solution)/shard_map/ppermute | solution.py:53
  (6 other events, 5.3 us)

commit v13 on v8

--- a/solution.py
+++ b/solution.py
@@ -105,8 +105,8 @@
     plane_ids = me_s * n - halo + jnp.arange(n + 2 * halo)
     inside = ((plane_ids >= 0) & (plane_ids < space * n)).astype(jnp.float32)[:, None, None]
 
-    def fine_prop(field):
-        for number in range(STEPS):
+    def fine_prop(field, steps=STEPS):
+        for number in range(steps):
             cut = number
             k = conduct[cut : conduct.shape[0] - cut]
             c = absorb[cut : absorb.shape[0] - cut]
@@ -116,8 +116,12 @@
                 field = jnp.where(m > 0, field, 0.0)
         return field
 
-    advanced = fine_prop(field0)
-    payload = lax.cond(me_t == times - 1, lambda: initial, lambda: advanced)
+    before_last = fine_prop(field0, STEPS - 1)
+    last_k = conduct[STEPS - 1 : conduct.shape[0] - STEPS + 1]
+    last_c = absorb[STEPS - 1 : absorb.shape[0] - STEPS + 1]
+    payload = jnp.where(me_t == times - 1, initial, advance(before_last, last_k, last_c, 0.1, 0.1))
+    kept = lax.optimization_barrier(before_last)
+    advanced = advance(kept, last_k, last_c, 0.1, 0.1)
     got2 = gather_planes(payload, ("space", "tm"), prev_pairs, distances)
     relaxed = jnp.concatenate([got2[d] for d in distances], axis=0)[lo:hi]
     residual = fine_prop(relaxed) - advanced

time: 103 us -> 103 us (level)
  the two profiles are of different devices: /device:TPU:5 before, /device:TPU:1 now
where the time goes in v13:
time: 103 us; the launch traced here: 102 us
  waiting for transfers between devices  37.9 us (37%)
  starting transfers between devices  33.1 us (32%)
  other arithmetic  16.5 us (16%)
  local copies, waits for them, and re-layouts  9.47 us (9%)
  matrix products  4.08 us (4%)
  between operations  1.34 us (1%)
    ppermute x12, waiting for transfers between devices, gather_planes(): pieces[d] = lax.ppermute(block, axis_names, pairs_of(d))  36.1 us
    ppermute x12, starting transfers between devices, gather_planes(): pieces[d] = lax.ppermute(block, axis_names, pairs_of(d))  31.2 us
    select_n x5, other arithmetic, fine_prop(): field = jnp.where(m > 0, field, 0.0)  8.3 us
    unnamed x71, local copies, waits for them, and re-layouts  7.7 us
    dot_general x6, matrix products, restrict(): jnp.einsum('Yy,mYZ,Zz->myz', rows, planes, cols, precision=lax.Precision....  3.41 us
    reduce_sum x3, other arithmetic, restrict(): planes = field.reshape(first // 2, 2, second, third).sum(axis=1)  2.35 us
  transfers between devices with their start and end apart: 13, of which 5 were waited for; matrix products, arithmetic and copies ran while one was open for 8% of the time, Pallas kernels for 0%

profile of v13, /device:TPU:1, one launch (start us, length us, event | category | flops | bytes accessed | tf_op | source)
XLA Modules:
  0.0 102.4 jit_solution(2835742713346495335)
XLA Ops:
  0.7 1.2 %fusion.105 = f32[2,2,256,128]{3,2,1,0:T(8,128)S(1)} fusion(f32[1,2,256,128]{3,2,1,0:T(8,128)} %param.13, f32[1,2,256,128]{3,2,1,0:T(8,128)} %bitcast.67, f32[1,2,256,128]{3,2,1,0:T(8,128)} %bitcast.69, pred[]{:T(512)S(6)} %eq.8), kind=kLoop, calls=%fused_computation.183 | loop fusion | flops 393216 | bytes 1310721 | tf_op jit(solution)/shard_map/jit(_where)/select_n | solution.py:87
  1.9 4.0 %collective-permute-start = (f32[2,2,256,128]{3,2,1,0:T(8,128)S(1)}, f32[2,2,256,128]{3,2,1,0:T(8,128)S(1)}, u32[]{:S(2)}, u32[]{:S(2)}) collective-permute-start(f32[2,2,256,128]{3,2,1,0:T(8,128)S(1)} %fusion.105), channel_id=1, source_target_pairs={{0,4},{2,6},{4,8},{6,10},{8,12},{10,14},{12,16},{14,18},{16,20},{1... | collective-permute-start | bytes 1572872 | tf_op jit(solution)/shard_map/ppermute | solution.py:53
  5.9 3.1 %collective-permute-start.1 = (f32[2,2,256,128]{3,2,1,0:T(8,128)S(1)}, f32[2,2,256,128]{3,2,1,0:T(8,128)S(1)}, u32[]{:S(2)}, u32[]{:S(2)}) collective-permute-start(f32[2,2,256,128]{3,2,1,0:T(8,128)S(1)} %fusion.105), channel_id=1, source_target_pairs={{0,2},{2,4},{4,6},{6,8},{8,10},{10,12},{12,14},{14,16},{16,18},{18... | collective-permute-start | bytes 1572872 | tf_op jit(solution)/shard_map/ppermute | solution.py:53
  9.1 1.3 %collective-permute-start.2 = (f32[2,2,256,128]{3,2,1,0:T(8,128)S(1)}, f32[2,2,256,128]{3,2,1,0:T(8,128)S(1)}, u32[]{:S(2)}, u32[]{:S(2)}) collective-permute-start(f32[2,2,256,128]{3,2,1,0:T(8,128)S(1)} %fusion.105), channel_id=1, source_target_pairs={{2,0},{4,2},{6,4},{8,6},{10,8},{12,10},{14,12},{16,14},{18,16},{20... | collective-permute-start | bytes 1572872 | tf_op jit(solution)/shard_map/ppermute | solution.py:53
  10.4 1.3 %collective-permute-start.3 = (f32[2,2,256,128]{3,2,1,0:T(8,128)S(1)}, f32[2,2,256,128]{3,2,1,0:T(8,128)S(1)}, u32[]{:S(2)}, u32[]{:S(2)}) collective-permute-start(f32[2,2,256,128]{3,2,1,0:T(8,128)S(1)} %fusion.105), channel_id=1, source_target_pairs={{4,0},{6,2},{8,4},{10,6},{12,8},{14,10},{16,12},{18,14},{20,16},{2... | collective-permute-start | bytes 1572872 | tf_op jit(solution)/shard_map/ppermute | solution.py:53
  11.9 20.7 %collective-permute-done.2 = f32[2,2,256,128]{3,2,1,0:T(8,128)S(1)} collective-permute-done((f32[2,2,256,128]{3,2,1,0:T(8,128)S(1)}, f32[2,2,256,128]{3,2,1,0:T(8,128)S(1)}, u32[]{:S(2)}, u32[]{:S(2)}) %collective-permute-start.2) | collective-permute-done | bytes 524320 | tf_op jit(solution)/shard_map/ppermute | solution.py:53
  32.8 1.9 %collective-permute-start.4 = (f32[8,256,128]{2,1,0:T(8,128)S(1)}, f32[8,256,128]{2,1,0:T(8,128)S(1)}, u32[]{:S(2)}, u32[]{:S(2)}) collective-permute-start(f32[8,256,128]{2,1,0:T(8,128)S(1)} %pad_maximum_fusion.7), channel_id=1, source_target_pairs={{0,1},{1,0},{2,3},{3,2},{4,5},{5,4},{6,7},{7,6},{8,9},{9,8},{10,11... | collective-permute-start | bytes 3145736 | tf_op jit(solution)/shard_map/ppermute | solution.py:97
  35.1 1.8 %collective-permute-done.4 = f32[8,256,128]{2,1,0:T(8,128)S(1)} collective-permute-done((f32[8,256,128]{2,1,0:T(8,128)S(1)}, f32[8,256,128]{2,1,0:T(8,128)S(1)}, u32[]{:S(2)}, u32[]{:S(2)}) %collective-permute-start.4) | collective-permute-done | bytes 1048608 | tf_op jit(solution)/shard_map/ppermute | solution.py:97
  39.6 2.2 %fusion.22 = f32[8,256,128]{2,1,0:T(8,128)S(1)} fusion(f32[8,256,128]{2,1,0:T(8,128)S(1)} %slice_bitcast_fusion.1, f32[2,2,256,128]{3,2,1,0:T(8,128)S(1)} %copy-done.11, f32[2,2,256,128]{3,2,1,0:T(8,128)S(1)} %copy-done.20, f32[2,2,256,128]{3,2,1,0:T(8,128)S(1)} %copy-done.9, f32[2,2,256,128]{3,2,1,0:T(8,128)S(1)} %copy-done.7, ...), kind=kLoop, calls=%fused_computation.63 | loop fusion | flops 10747904 | bytes 8912904 | tf_op jit(solution)/shard_map/jit(_where)/select_n | solution.py:116
  41.9 1.2 %fusion.74 = f32[6,256,128]{2,1,0:T(8,128)S(1)} fusion(f32[6,256,128]{2,1,0:T(8,128)S(1)} %slice.566, f32[8,256,128]{2,1,0:T(8,128)S(1)} %fusion.22, pred[6]{0:T(512)(128)(4,1)S(1)} %slice_compare_fusion.1, f32[6,256,128]{2,1,0:T(8,128)S(1)} %slice.568, f32[10,256,128]{2,1,0:T(8,128)S(1)} %get-tuple-element.5, f32[10,256,128]{2,1,0:T(8,128)S(1)} %get-tuple-element.6), kind=kLoop, calls=%fused_computation.144 | loop fusion | flops 6881280 | bytes 6291462 | tf_op jit(solution)/shard_map/jit(_where)/select_n | solution.py:116
  43.2 0.8 fusion.123
  44.1 1.2 %fusion.188 = f32[2,256,128]{2,1,0:T(8,128)} fusion(f32[2,256,128]{2,1,0:T(8,128)S(1)} %copy-done.31, f32[2,256,128]{2,1,0:T(8,128)S(1)} %slice.587, f32[4,256,128]{2,1,0:T(8,128)S(1)} %fusion.123, f32[10,256,128]{2,1,0:T(8,128)S(1)} %get-tuple-element.6, pred[]{:T(512)S(6)} %eq.9, f32[10,256,128]{2,1,0:T(8,128)S(1)} %get-tuple-element.5, ...), kind=kLoop, calls=%fused_computation.275 | loop fusion | flops 2293760 | bytes 2621441 | tf_op jit(solution)/shard_map/jit(_where)/select_n | solution.py:122
  45.3 13.5 %collective-permute-start.5 = (f32[2,256,128]{2,1,0:T(8,128)}, f32[2,256,128]{2,1,0:T(8,128)}, u32[]{:S(2)}, u32[]{:S(2)}) collective-permute-start(f32[2,256,128]{2,1,0:T(8,128)} %fusion.188), channel_id=1, source_target_pairs={{1,4},{0,5},{3,6},{2,7},{5,8},{4,9},{7,10},{6,11},{9,12},{8,13},{1... | collective-permute-start | bytes 786440 | tf_op jit(solution)/shard_map/ppermute | solution.py:53
  58.8 2.0 %collective-permute-start.6 = (f32[2,256,128]{2,1,0:T(8,128)}, f32[2,256,128]{2,1,0:T(8,128)}, u32[]{:S(2)}, u32[]{:S(2)}) collective-permute-start(f32[2,256,128]{2,1,0:T(8,128)} %fusion.188), channel_id=1, source_target_pairs={{1,2},{0,3},{3,4},{2,5},{5,6},{4,7},{7,8},{6,9},{9,10},{8,11},{11,... | collective-permute-start | bytes 786440 | tf_op jit(solution)/shard_map/ppermute | solution.py:53
  61.0 1.3 %collective-permute-start.8 = (f32[2,256,128]{2,1,0:T(8,128)}, f32[2,256,128]{2,1,0:T(8,128)}, u32[]{:S(2)}, u32[]{:S(2)}) collective-permute-start(f32[2,256,128]{2,1,0:T(8,128)} %fusion.188), channel_id=1, source_target_pairs={{3,0},{2,1},{5,2},{4,3},{7,4},{6,5},{9,6},{8,7},{11,8},{10,9},{13,... | collective-permute-start | bytes 786440 | tf_op jit(solution)/shard_map/ppermute | solution.py:53
  62.2 1.3 %collective-permute-start.9 = (f32[2,256,128]{2,1,0:T(8,128)}, f32[2,256,128]{2,1,0:T(8,128)}, u32[]{:S(2)}, u32[]{:S(2)}) collective-permute-start(f32[2,256,128]{2,1,0:T(8,128)} %fusion.188), channel_id=1, source_target_pairs={{5,0},{4,1},{7,2},{6,3},{9,4},{8,5},{11,6},{10,7},{13,8},{12,9},{1... | collective-permute-start | bytes 786440 | tf_op jit(solution)/shard_map/ppermute | solution.py:53
  63.5 0.8 reduce_sum.28
  64.4 1.6 %fusion.268 = f32[64,3,256]{2,0,1:T(8,128)S(1)} fusion(f32[128,64,1]{1,0,2:T(8,128)} %constant.92, f32[3,256,128]{2,1,0:T(8,128)} %reduce_sum.28), kind=kOutput, calls=%fused_computation.388 | convolution fusion | flops 75497472 | bytes 622592 | tf_op jit(solution)/shard_map/Yy,mYZ,Zz->myz/dot_general | solution.py:35
  66.3 3.6 %collective-permute-done.5 = f32[2,256,128]{2,1,0:T(8,128)} collective-permute-done((f32[2,256,128]{2,1,0:T(8,128)}, f32[2,256,128]{2,1,0:T(8,128)}, u32[]{:S(2)}, u32[]{:S(2)}) %collective-permute-start.5) | collective-permute-done | bytes 262176 | tf_op jit(solution)/shard_map/ppermute | solution.py:53
  69.8 1.0 constant_dynamic-update-slice_fusion.9
  70.8 1.0 constant_dynamic-update-slice_fusion.8
  71.8 1.0 constant_dynamic-update-slice_fusion.7
  72.8 1.0 collective-permute-done.8
  73.8 1.0 constant_dynamic-update-slice_fusion.6
  74.8 1.1 %constant_dynamic-update-slice_fusion.5 = f32[10,256,128]{2,1,0:T(8,128)S(1)} fusion(f32[10,256,128]{2,1,0:T(8,128)S(1)} %constant_dynamic-update-slice_fusion.6, f32[2,256,128]{2,1,0:T(8,128)} %collective-permute-done.9), kind=kLoop, calls=%fused_computation.368 | loop fusion | bytes 524288 | tf_op jit(solution)/shard_map/concatenate | solution.py:126
  76.0 3.2 %fusion.38 = f32[8,256,128]{2,1,0:T(8,128)S(1)} fusion(f32[8,256,128]{2,1,0:T(8,128)S(1)} %slice.590, f32[2,256,128]{2,1,0:T(8,128)} %collective-permute-done.9, f32[2,256,128]{2,1,0:T(8,128)} %collective-permute-done.8, f32[2,256,128]{2,1,0:T(8,128)} %collective-permute-done.7, f32[2,256,128]{2,1,0:T(8,128)} %collective-permute-done.6, ...), kind=kLoop, calls=%fused_computation.79 | loop fusion | flops 10747904 | bytes 7602184 | tf_op jit(solution)/shard_map/jit(_where)/select_n | solution.py:116
  79.4 2.1 %fusion.265 = (f32[6,256,128]{2,1,0:T(8,128)}, f32[6,256,128]{2,1,0:T(8,128)S(1)}) fusion(f32[10,256,128]{2,1,0:T(8,128)S(1)} %get-tuple-element.6, f32[6,256,128]{2,1,0:T(8,128)S(1)} %slice.591, f32[6,256,128]{2,1,0:T(8,128)S(1)} %slice.568, f32[8,256,128]{2,1,0:T(8,128)S(1)} %fusion.38, f32[10,256,128]{2,1,0:T(8,128)S(1)} %get-tuple-element.5, ...), kind=kLoop, calls=%fused_computation.385 | loop fusion | flops 6881280 | bytes 7077894 | tf_op jit(solution)/shard_map/slice | solution.py:22
  81.5 1.0 copy-done.5
  83.6 1.5 %fusion.262 = (f32[256,128]{1,0:T(8,128)S(1)}, f32[2,256,128]{2,1,0:T(8,128)}, f32[2,256,128]{2,1,0:T(8,128)}) fusion(f32[2,256,128]{2,1,0:T(8,128)S(1)} %slice.597, f32[10,256,128]{2,1,0:T(8,128)S(1)} %get-tuple-element.6, f32[2,256,128]{2,1,0:T(8,128)S(1)} %copy-done.18, f32[4,256,128]{2,1,0:T(8,128)S(1)} %fusion.139, ...), kind=kLoop, calls=%fused_computation.384 | loop fusion | flops 4227072 | bytes 3538944 | tf_op jit(solution)/shard_map/reduce_sum | solution.py:32
  85.8 1.3 %collective-permute-start.10 = (f32[1,128,64]{1,2,0:T(8,128)S(1)}, f32[1,128,64]{1,2,0:T(8,128)S(1)}, u32[]{:S(2)}, u32[]{:S(2)}) collective-permute-start(f32[1,128,64]{1,2,0:T(8,128)S(1)} %fusion.4), channel_id=1, source_target_pairs={{0,1},{2,3},{4,5},{6,7},{8,9},{10,11},{12,13},{14,15},{16,17},{18,... | collective-permute-start | bytes 98312 | tf_op jit(solution)/shard_map/ppermute | solution.py:53
  87.8 1.3 %collective-permute-start.11 = (f32[1,128,64]{1,2,0:T(8,128)S(1)}, f32[1,128,64]{1,2,0:T(8,128)S(1)}, u32[]{:S(2)}, u32[]{:S(2)}) collective-permute-start(f32[1,128,64]{1,2,0:T(8,128)S(1)} %fusion.4), channel_id=1, source_target_pairs={{2,1},{4,3},{6,5},{8,7},{10,9},{12,11},{14,13},{16,15},{18,17},{20... | collective-permute-start | bytes 98312 | tf_op jit(solution)/shard_map/ppermute | solution.py:53
  90.1 10.8 %collective-permute-done.11 = f32[1,128,64]{1,2,0:T(8,128)S(1)} collective-permute-done((f32[1,128,64]{1,2,0:T(8,128)S(1)}, f32[1,128,64]{1,2,0:T(8,128)S(1)}, u32[]{:S(2)}, u32[]{:S(2)}) %collective-permute-start.11) | collective-permute-done | bytes 32800 | tf_op jit(solution)/shard_map/ppermute | solution.py:53
  (114 shorter events, 9.1 us)
Async XLA Ops:
  0.6 11.2 %copy-start.15 = (f32[2,256,128]{2,1,0:T(8,128)S(1)}, f32[2,256,128]{2,1,0:T(8,128)}, u32[]{:S(2)}) copy-start(f32[2,256,128]{2,1,0:T(8,128)} %param.14) | copy-start | bytes 786436
  0.6 11.2 %copy-start.16 = (f32[2,256,128]{2,1,0:T(8,128)S(1)}, f32[2,256,128]{2,1,0:T(8,128)}, u32[]{:S(2)}) copy-start(f32[2,256,128]{2,1,0:T(8,128)} %param.15) | copy-start | bytes 786436
  1.9 30.8 %copy-start.19 = (f32[2,2,256,128]{3,2,1,0:T(8,128)}, f32[2,2,256,128]{3,2,1,0:T(8,128)S(1)}, u32[]{:S(2)}) copy-start(f32[2,2,256,128]{3,2,1,0:T(8,128)S(1)} %fusion.105) | copy-start | bytes 1572868
  1.9 30.7 %collective-permute-start = (f32[2,2,256,128]{3,2,1,0:T(8,128)S(1)}, f32[2,2,256,128]{3,2,1,0:T(8,128)S(1)}, u32[]{:S(2)}, u32[]{:S(2)}) collective-permute-start(f32[2,2,256,128]{3,2,1,0:T(8,128)S(1)} %fusion.105), channel_id=1, source_target_pairs={{0,4},{2,6},{4,8},{6,10},{8,12},{10,14},{12,16},{14,18},{16,20},{1... | collective-permute-start | bytes 1572872 | tf_op jit(solution)/shard_map/ppermute | solution.py:53
  5.9 26.7 %collective-permute-start.1 = (f32[2,2,256,128]{3,2,1,0:T(8,128)S(1)}, f32[2,2,256,128]{3,2,1,0:T(8,128)S(1)}, u32[]{:S(2)}, u32[]{:S(2)}) collective-permute-start(f32[2,2,256,128]{3,2,1,0:T(8,128)S(1)} %fusion.105), channel_id=1, source_target_pairs={{0,2},{2,4},{4,6},{6,8},{8,10},{10,12},{12,14},{14,16},{16,18},{18... | collective-permute-start | bytes 1572872 | tf_op jit(solution)/shard_map/ppermute | solution.py:53
  9.1 23.5 %collective-permute-start.2 = (f32[2,2,256,128]{3,2,1,0:T(8,128)S(1)}, f32[2,2,256,128]{3,2,1,0:T(8,128)S(1)}, u32[]{:S(2)}, u32[]{:S(2)}) collective-permute-start(f32[2,2,256,128]{3,2,1,0:T(8,128)S(1)} %fusion.105), channel_id=1, source_target_pairs={{2,0},{4,2},{6,4},{8,6},{10,8},{12,10},{14,12},{16,14},{18,16},{20... | collective-permute-start | bytes 1572872 | tf_op jit(solution)/shard_map/ppermute | solution.py:53
  10.4 22.2 %collective-permute-start.3 = (f32[2,2,256,128]{3,2,1,0:T(8,128)S(1)}, f32[2,2,256,128]{3,2,1,0:T(8,128)S(1)}, u32[]{:S(2)}, u32[]{:S(2)}) collective-permute-start(f32[2,2,256,128]{3,2,1,0:T(8,128)S(1)} %fusion.105), channel_id=1, source_target_pairs={{4,0},{6,2},{8,4},{10,6},{12,8},{14,10},{16,12},{18,14},{20,16},{2... | collective-permute-start | bytes 1572872 | tf_op jit(solution)/shard_map/ppermute | solution.py:53
  32.5 2.4 %copy-start.10 = (f32[2,2,256,128]{3,2,1,0:T(8,128)}, f32[2,2,256,128]{3,2,1,0:T(8,128)S(1)}, u32[]{:S(2)}) copy-start(f32[2,2,256,128]{3,2,1,0:T(8,128)S(1)} %collective-permute-done.2) | copy-start | bytes 1572868
  32.5 2.4 %copy-start.12 = (f32[2,2,256,128]{3,2,1,0:T(8,128)}, f32[2,2,256,128]{3,2,1,0:T(8,128)S(1)}, u32[]{:S(2)}) copy-start(f32[2,2,256,128]{3,2,1,0:T(8,128)S(1)} %collective-permute-done.3) | copy-start | bytes 1572868
  32.6 2.2 %copy-start.8 = (f32[2,2,256,128]{3,2,1,0:T(8,128)}, f32[2,2,256,128]{3,2,1,0:T(8,128)S(1)}, u32[]{:S(2)}) copy-start(f32[2,2,256,128]{3,2,1,0:T(8,128)S(1)} %collective-permute-done.1) | copy-start | bytes 1572868
  32.8 4.2 %collective-permute-start.4 = (f32[8,256,128]{2,1,0:T(8,128)S(1)}, f32[8,256,128]{2,1,0:T(8,128)S(1)}, u32[]{:S(2)}, u32[]{:S(2)}) collective-permute-start(f32[8,256,128]{2,1,0:T(8,128)S(1)} %pad_maximum_fusion.7), channel_id=1, source_target_pairs={{0,1},{1,0},{2,3},{3,2},{4,5},{5,4},{6,7},{7,6},{8,9},{9,8},{10,11... | collective-permute-start | bytes 3145736 | tf_op jit(solution)/shard_map/ppermute | solution.py:97
  37.3 2.1 %copy-start.13 = (f32[2,2,256,128]{3,2,1,0:T(8,128)S(1)}, f32[2,2,256,128]{3,2,1,0:T(8,128)}, u32[]{:S(2)}) copy-start(f32[2,2,256,128]{3,2,1,0:T(8,128)} %copy-done.12) | copy-start | bytes 1572868
  37.3 2.3 %copy-start.20 = (f32[2,2,256,128]{3,2,1,0:T(8,128)S(1)}, f32[2,2,256,128]{3,2,1,0:T(8,128)}, u32[]{:S(2)}) copy-start(f32[2,2,256,128]{3,2,1,0:T(8,128)} %copy-done.19) | copy-start | bytes 1572868
  37.5 5.7 %copy-start.4 = (f32[4,256,128]{2,1,0:T(8,128)}, f32[4,256,128]{2,1,0:T(8,128)S(1)}, u32[]{:S(2)}) copy-start(f32[4,256,128]{2,1,0:T(8,128)S(1)} %slice.575) | copy-start | bytes 1572868
  37.5 6.6 %copy-start.17 = (f32[2,256,128]{2,1,0:T(8,128)}, f32[2,256,128]{2,1,0:T(8,128)S(1)}, u32[]{:S(2)}) copy-start(f32[2,256,128]{2,1,0:T(8,128)S(1)} %slice.582) | copy-start | bytes 786436
  45.3 20.6 %copy-start.24 = (f32[256,128,1]{1,0,2:T(8,128)S(1)}, f32[256,128,1]{1,0,2:T(8,128)}, u32[]{:S(2)}) copy-start(f32[256,128,1]{1,0,2:T(8,128)} %constant.93) | copy-start | bytes 393220
  45.3 24.6 %collective-permute-start.5 = (f32[2,256,128]{2,1,0:T(8,128)}, f32[2,256,128]{2,1,0:T(8,128)}, u32[]{:S(2)}, u32[]{:S(2)}) collective-permute-start(f32[2,256,128]{2,1,0:T(8,128)} %fusion.188), channel_id=1, source_target_pairs={{1,4},{0,5},{3,6},{2,7},{5,8},{4,9},{7,10},{6,11},{9,12},{8,13},{1... | collective-permute-start | bytes 786440 | tf_op jit(solution)/shard_map/ppermute | solution.py:53
  58.8 12.0 %collective-permute-start.6 = (f32[2,256,128]{2,1,0:T(8,128)}, f32[2,256,128]{2,1,0:T(8,128)}, u32[]{:S(2)}, u32[]{:S(2)}) collective-permute-start(f32[2,256,128]{2,1,0:T(8,128)} %fusion.188), channel_id=1, source_target_pairs={{1,2},{0,3},{3,4},{2,5},{5,6},{4,7},{7,8},{6,9},{9,10},{8,11},{11,... | collective-permute-start | bytes 786440 | tf_op jit(solution)/shard_map/ppermute | solution.py:53
  60.8 11.0 %collective-permute-start.7 = (f32[2,256,128]{2,1,0:T(8,128)}, f32[2,256,128]{2,1,0:T(8,128)}, u32[]{:S(2)}, u32[]{:S(2)}) collective-permute-start(f32[2,256,128]{2,1,0:T(8,128)} %fusion.188), channel_id=1, source_target_pairs={{1,0},{0,1},{3,2},{2,3},{5,4},{4,5},{7,6},{6,7},{9,8},{8,9},{11,10... | collective-permute-start | bytes 786440 | tf_op jit(solution)/shard_map/ppermute | solution.py:53
  61.0 12.8 %collective-permute-start.8 = (f32[2,256,128]{2,1,0:T(8,128)}, f32[2,256,128]{2,1,0:T(8,128)}, u32[]{:S(2)}, u32[]{:S(2)}) collective-permute-start(f32[2,256,128]{2,1,0:T(8,128)} %fusion.188), channel_id=1, source_target_pairs={{3,0},{2,1},{5,2},{4,3},{7,4},{6,5},{9,6},{8,7},{11,8},{10,9},{13,... | collective-permute-start | bytes 786440 | tf_op jit(solution)/shard_map/ppermute | solution.py:53
  62.2 12.5 %collective-permute-start.9 = (f32[2,256,128]{2,1,0:T(8,128)}, f32[2,256,128]{2,1,0:T(8,128)}, u32[]{:S(2)}, u32[]{:S(2)}) collective-permute-start(f32[2,256,128]{2,1,0:T(8,128)} %fusion.188), channel_id=1, source_target_pairs={{5,0},{4,1},{7,2},{6,3},{9,4},{8,5},{11,6},{10,7},{13,8},{12,9},{1... | collective-permute-start | bytes 786440 | tf_op jit(solution)/shard_map/ppermute | solution.py:53
  66.3 8.5 %copy-start.26 = (f32[3,128,64]{1,2,0:T(8,128)}, f32[3,128,64]{1,2,0:T(8,128)S(1)}, u32[]{:S(2)}) copy-start(f32[3,128,64]{1,2,0:T(8,128)S(1)} %fusion.3) | copy-start | bytes 294916
  83.6 5.4 %copy-start.14 = (f32[6,256,128]{2,1,0:T(8,128)S(1)}, f32[6,256,128]{2,1,0:T(8,128)}, u32[]{:S(2)}) copy-start(f32[6,256,128]{2,1,0:T(8,128)} %get-tuple-element.7) | copy-start | bytes 2359300
  85.1 4.1 %copy-start.28 = (f32[128,64,1]{1,0,2:T(8,128)S(1)}, f32[128,64,1]{1,0,2:T(8,128)}, u32[]{:S(2)}) copy-start(f32[128,64,1]{1,0,2:T(8,128)} %constant.92) | copy-start | bytes 98308
  85.1 4.6 %copy-start.25 = (f32[256,128,1]{1,0,2:T(8,128)S(1)}, f32[256,128,1]{1,0,2:T(8,128)}, u32[]{:S(2)}) copy-start(f32[256,128,1]{1,0,2:T(8,128)} %constant.93) | copy-start | bytes 393220
  85.4 15.5 %copy-start.27 = (f32[3,128,64]{1,2,0:T(8,128)S(1)}, f32[3,128,64]{1,2,0:T(8,128)}, u32[]{:S(2)}) copy-start(f32[3,128,64]{1,2,0:T(8,128)} %copy-done.26) | copy-start | bytes 294916
  85.4 15.5 %slice-start.1 = ((f32[3,128,64]{1,2,0:T(8,128)}), f32[1,128,64]{1,2,0:T(8,128)S(1)}, s32[]{:S(2)}) async-start(f32[3,128,64]{1,2,0:T(8,128)} %copy-done.26), calls=%async_computation.1 | async-start | bytes 65536 | tf_op jit(solution)/shard_map/slice | solution.py:13
  85.8 4.3 %collective-permute-start.10 = (f32[1,128,64]{1,2,0:T(8,128)S(1)}, f32[1,128,64]{1,2,0:T(8,128)S(1)}, u32[]{:S(2)}, u32[]{:S(2)}) collective-permute-start(f32[1,128,64]{1,2,0:T(8,128)S(1)} %fusion.4), channel_id=1, source_target_pairs={{0,1},{2,3},{4,5},{6,7},{8,9},{10,11},{12,13},{14,15},{16,17},{18,... | collective-permute-start | bytes 98312 | tf_op jit(solution)/shard_map/ppermute | solution.py:53
  87.1 3.0 %collective-permute-start.12 = (f32[1,128,64]{1,2,0:T(8,128)S(1)}, f32[1,128,64]{1,2,0:T(8,128)S(1)}, u32[]{:S(2)}, u32[]{:S(2)}) collective-permute-start(f32[1,128,64]{1,2,0:T(8,128)S(1)} %fusion.4), channel_id=1, source_target_pairs={{0,3},{2,5},{4,7},{6,9},{8,11},{10,13},{12,15},{14,17},{16,19},{18... | collective-permute-start | bytes 98312 | tf_op jit(solution)/shard_map/ppermute | solution.py:53
  87.8 13.1 %collective-permute-start.11 = (f32[1,128,64]{1,2,0:T(8,128)S(1)}, f32[1,128,64]{1,2,0:T(8,128)S(1)}, u32[]{:S(2)}, u32[]{:S(2)}) collective-permute-start(f32[1,128,64]{1,2,0:T(8,128)S(1)} %fusion.4), channel_id=1, source_target_pairs={{2,1},{4,3},{6,5},{8,7},{10,9},{12,11},{14,13},{16,15},{18,17},{20... | collective-permute-start | bytes 98312 | tf_op jit(solution)/shard_map/ppermute | solution.py:53
  89.1 12.1 %copy-start.30 = (f32[128,64]{1,0:T(8,128)S(1)}, f32[128,64]{1,0:T(8,128)}, u32[]{:S(2)}) copy-start(f32[128,64]{1,0:T(8,128)} %constant.27.clone) | copy-start | bytes 98308
  89.1 12.5 %copy-start.22 = (f32[2,256,128]{2,1,0:T(8,128)S(1)}, f32[2,256,128]{2,1,0:T(8,128)}, u32[]{:S(2)}) copy-start(f32[2,256,128]{2,1,0:T(8,128)} %get-tuple-element.4) | copy-start | bytes 786436
  (15 other events, 21.6 us)
